TPU v7x, 32 devices: a whole 2x2x4 slice. The times are simulated.
32 devices in a mesh: ctx: 8 (over z, y), tp: 4 (over x, core).
Axes of the slice: x: 2, y: 2, z: 4, core: 2. Of those that a mesh axis runs over, the one named last changes fastest.
Arguments:
- features: bfloat16 [2048, 8192], P('ctx', 'tp'), may hold values from -6 to 6
- input_map: bfloat16 [2048, 512], P('ctx', 'tp'), may hold values from -1.5 to 1.5
- output_map: bfloat16 [2048, 512], P('ctx', 'tp'), may hold values from -1.5 to 1.5
- gate_in: bfloat16 [2048, 8192], P('ctx', 'tp'), may hold values from -6 to 6
- conv_feat: float32 [4, 8192], P(None, 'tp'), may hold values from -3 to 3
- conv_input: float32 [4, 512], P(None, 'tp'), may hold values from -3 to 3
- conv_output: float32 [4, 512], P(None, 'tp'), may hold values from -3 to 3
- step_size: float32 [2048, 128], P('ctx', 'tp'), may hold values from 0.1 to 1
- log_decay: float32 [2048, 128], P('ctx', 'tp'), may hold values from -1 to 0, as said below
- skip_gain: float32 [128], P('tp'), may hold values from 0.5 to 2
- norm_gain: float32 [8192], P('tp'), may hold values from 0.5 to 1.5
- out_weight: bfloat16 [8192, 4096], P('tp', 'ctx'), may hold values from -0.0625 to 0.0625
Outputs:
- layer_out: bfloat16 [2048, 4096], P('ctx', 'tp')
Inputs may be any that keep to these rules, and one draw needn't show every extreme that they name: log_decay is negative.
All inputs are finite; a program needn't handle non-finite values.
Results may differ from a plain program's by a relative error of at most 0.0066.
Values may be sent and summed in bfloat16 or wider, within the bound.
No kernel may reach another device: no remote copies, remote signals or barrier semaphores. Data moves between devices by JAX's collectives and lax.ppermute only.
A program may use at most 192 MiB of HBM per device.

v0:
```python
import jax
import jax.numpy as jnp
from jax import lax
from jax.sharding import PartitionSpec as P

N = 128
BLOCK = 256


def prefix(part, axis, combine, identity):
    place = lax.axis_index(axis)
    gathered = jax.tree.map(lambda a: lax.all_gather(a, axis), part)
    state = jax.tree.map(lambda a, e: jnp.zeros_like(a) + jnp.asarray(e, a.dtype), part, identity)

    def one(hop, state):
        return combine(
            state, jax.tree.map(lambda a: lax.dynamic_index_in_dim(a, hop, 0, False), gathered)
        )

    return lax.fori_loop(0, place, one, state)


def shifted(value, axis, steps):
    count = lax.axis_size(axis)
    first, last = (max(0, -steps), min(count, count - steps))
    return lax.ppermute(value, axis, [(source, source + steps) for source in range(first, last)])


def local_conv(packed, kernel, tok_rows):
    tail_len = kernel.shape[0] - 1
    padded = jnp.pad(packed.astype(jnp.float32), ((tail_len, 0), (0, 0)))
    pre_act = jnp.zeros((tok_rows, kernel.shape[1]), jnp.float32)
    for tap_index in range(kernel.shape[0]):
        pre_act = pre_act + kernel[tap_index] * padded[tap_index : tap_index + tok_rows]
    return pre_act


def edge_partial(tail_rows, kernel):
    tail_len = kernel.shape[0] - 1
    tail_vals = tail_rows.astype(jnp.float32)
    outputs = []
    for row_index in range(tail_len):
        accum = jnp.zeros((kernel.shape[1],), jnp.float32)
        for tap_index in range(tail_len - row_index):
            accum = accum + kernel[tap_index] * tail_vals[row_index + tap_index]
        outputs.append(accum)
    return jnp.stack(outputs, axis=0)


def intra_block(scaled, b_rows, c_rows, cum_log):
    scores = jnp.einsum("tgn,sgn->gts", c_rows, b_rows, preferred_element_type=jnp.float32)
    cum_cols = jnp.moveaxis(cum_log, 0, -1)
    log_gap = cum_cols[..., :, None] - cum_cols[..., None, :]
    block_len = cum_log.shape[0]
    causal = jnp.arange(block_len)[:, None] >= jnp.arange(block_len)[None, :]
    decays = jnp.exp(jnp.where(causal, log_gap, -jnp.inf))
    weights = (scores[:, None] * decays).astype(jnp.bfloat16)
    return jnp.einsum("gjts,sgjp->tgjp", weights, scaled, preferred_element_type=jnp.float32)


def block_state(scaled, b_rows, cum_log):
    end_decay = jnp.exp(cum_log[-1][None] - cum_log)
    b_weighted = (b_rows.astype(jnp.float32)[:, :, None, :] * end_decay[..., None]).astype(
        jnp.bfloat16
    )
    return jnp.einsum("sgjp,sgjn->gjpn", scaled, b_weighted, preferred_element_type=jnp.float32)


def inter_block(c_rows, cum_log, state_carry):
    rounded = state_carry.astype(jnp.bfloat16)
    inner = jnp.einsum("tgn,gjpn->tgjp", c_rows, rounded, preferred_element_type=jnp.float32)
    return inner * jnp.exp(cum_log)[..., None]


def combine(first_part, second_part):
    decay_first, state_first = first_part
    decay_second, state_second = second_part
    return (decay_first * decay_second, decay_second[..., None, None] * state_first + state_second)


def prefix_states(dev_decay, dev_state):
    identity = (jnp.ones_like(dev_decay), jnp.zeros_like(dev_state))
    _, incoming = prefix((dev_decay, dev_state), "ctx", combine, identity)
    return incoming


def on_device(
    features,
    input_map,
    output_map,
    gate_in,
    conv_feat,
    conv_input,
    conv_output,
    step_size,
    log_decay,
    skip_gain,
    norm_gain,
    out_weight,
):
    tok_rows, width_x = features.shape
    width_b = input_map.shape[1]
    head_count = step_size.shape[1]
    head_dim = width_x // head_count
    groups_here = width_b // N
    per_group = head_count // groups_here
    tail_len = conv_feat.shape[0] - 1
    n_blocks = tok_rows // BLOCK
    packed = jnp.concatenate([features, input_map, output_map], axis=1)
    kernel = jnp.concatenate([conv_feat, conv_input, conv_output], axis=1)
    pre_act = local_conv(packed, kernel, tok_rows)
    tail_rows = shifted(packed[tok_rows - tail_len :], "ctx", 1)
    edge_sums = edge_partial(tail_rows, kernel)
    pre_act = pre_act + jnp.pad(edge_sums, ((0, tok_rows - tail_len), (0, 0)))
    conv_out = jax.nn.silu(pre_act).astype(jnp.bfloat16)
    x_conv = conv_out[:, :width_x]
    b_conv = conv_out[:, width_x : width_x + width_b]
    c_conv = conv_out[:, width_x + width_b :]
    x_heads = x_conv.astype(jnp.float32).reshape(tok_rows, groups_here, per_group, head_dim)
    scaled = (x_heads * step_size.reshape(tok_rows, groups_here, per_group)[..., None]).astype(
        jnp.bfloat16
    )

    def blocked(value_entries):
        return value_entries.reshape((n_blocks, BLOCK) + value_entries.shape[1:])

    scaled_b = blocked(scaled)
    b_rows = blocked(b_conv.reshape(tok_rows, groups_here, N))
    c_rows = blocked(c_conv.reshape(tok_rows, groups_here, N))
    cum_log = jnp.cumsum(blocked(log_decay.reshape(tok_rows, groups_here, per_group)), axis=1)
    blk_states = jax.vmap(block_state)(scaled_b, b_rows, cum_log)
    blk_decay = jnp.exp(cum_log[:, -1])

    def fold_local(state_carry, block_in):
        decay_b, state_b = block_in
        return (decay_b[..., None, None] * state_carry + state_b, None)

    dev_state, _ = lax.scan(
        fold_local, jnp.zeros(blk_states.shape[1:], jnp.float32), (blk_decay, blk_states)
    )
    dev_decay = jnp.prod(blk_decay, axis=0)
    incoming = prefix_states(dev_decay, dev_state)

    def advance(state_carry, block_in):
        scaled_k, b_k, c_k, cum_k, decay_k, state_k = block_in
        block_y = intra_block(scaled_k, b_k, c_k, cum_k) + inter_block(c_k, cum_k, state_carry)
        return (decay_k[..., None, None] * state_carry + state_k, block_y)

    _, ssm_y = lax.scan(
        advance, incoming, (scaled_b, b_rows, c_rows, cum_log, blk_decay, blk_states)
    )
    mixed_y = ssm_y.reshape(tok_rows, groups_here, per_group, head_dim)
    mixed_y = mixed_y + skip_gain.reshape(groups_here, per_group)[..., None] * x_heads
    gated_y = mixed_y.reshape(tok_rows, width_x) * jax.nn.silu(gate_in.astype(jnp.float32))
    grouped = gated_y.reshape(tok_rows, groups_here, width_x // groups_here)
    inv_root = lax.rsqrt(jnp.mean(grouped * grouped, axis=-1, keepdims=True) + 1e-05)
    hidden = ((grouped * inv_root).reshape(tok_rows, width_x) * norm_gain).astype(jnp.bfloat16)
    partial_out = jnp.dot(
        hidden,
        lax.all_gather(out_weight, "ctx", axis=1, tiled=True),
        preferred_element_type=jnp.float32,
    )
    return lax.psum_scatter(partial_out, "tp", scatter_dimension=1, tiled=True).astype(jnp.bfloat16)


def solution(mesh):
    placed = (
        P("ctx", "tp"),
        P("ctx", "tp"),
        P("ctx", "tp"),
        P("ctx", "tp"),
        P(None, "tp"),
        P(None, "tp"),
        P(None, "tp"),
        P("ctx", "tp"),
        P("ctx", "tp"),
        P("tp"),
        P("tp"),
        P("tp", "ctx"),
    )
    return jax.shard_map(
        on_device, mesh=mesh, in_specs=placed, out_specs=P("ctx", "tp"), check_vma=False
    )
```

profile of v0, /device:TPU:2, one launch (start us, length us, event | category | flops | bytes accessed | tf_op | source)
XLA Modules:
  0.0 436.8 jit_solution(13638195077279787356)
XLA Ops:
  6.5 0.0 copy-start
  6.5 0.0 copy-start.11
  6.6 0.0 all-gather.7.cloned.1.call-start
  6.6 1.4 constant_dynamic-update-slice_fusion.5
  8.0 0.0 copy-done.4
  8.0 0.0 copy-done.5
  8.0 1.0 copy-done.2
  9.1 3.4 collective-permute-start
  12.5 0.6 reduce-window.6
  13.1 0.2 slice_reduce_fusion
  13.3 0.1 copy.50
  13.5 0.2 bitcast_exponential_fusion
  13.8 0.1 subtract_exponential_fusion
  13.9 0.0 copy-done.10
  14.0 1.4 convert_element_type.56
  15.4 0.1 copy.53
  15.4 0.0 collective-permute-done
  15.5 0.1 slice_reduce_fusion.4
  15.6 1.5 multiply_convert_fusion.3
  17.2 1.7 slice_convert_fusion
  18.9 0.0 copy-start.6
  18.9 1.9 copy.47
  20.8 0.0 copy-done.6
  20.8 2.5 fusion.17
  23.3 0.0 all-gather.7.cloned.1.call-update
  23.3 0.0 all-gather.5.cloned.1.call-start
  23.3 0.7 all-gather.5.cloned.1.call-update
  24.0 0.0 reduce-scatter.2.cloned.1.call-start
  24.1 0.7 copy.51
  24.8 0.7 copy.56
  25.5 20.5 %all-gather = f32[8,1,1,32]{3,2,1,0:T(1,128)S(1)} all-gather(f32[1,1,1,32]{3,2,1,0:T(1,128)S(1)} %get-tuple-element.131), channel_id=2, replica_groups=mesh['ctx'=8,'tp'=4] {'ctx'}, dimensions={0}, use_global_device_ids=true | all-gather | bytes 1152 | tf_op jit(solution)/shard_map/all_gather | solution.py:12
  46.0 1.1 fusion.25
  47.1 101.3 %all-gather.7.cloned.1.call-done = f32[256,64,128]{2,1,0:T(8,128)} async-done(((f32[32,64,128]{2,1,0:T(8,128)}), f32[256,64,128]{2,1,0:T(8,128)}) %all-gather.7.cloned.1.call-update) | async-done | bytes 8388624 | tf_op jit(solution)/shard_map/all_gather | solution.py:12
  148.4 0.1 broadcast.92
  148.5 0.0 copy-start.7
  148.6 0.0 copy-start.13
  148.6 1.3 fusion.21
  149.9 3.7 fusion.14
  153.6 2.0 copy.58
  155.7 0.0 copy-done.3
  155.7 0.0 copy-start.12
  155.7 0.8 multiply_reduce_fusion
  156.5 219.6 %all-gather.5.cloned.1.call-done = bf16[2048,4096]{1,0:T(8,128)(2,1)} async-done(((bf16[2048,512]{1,0:T(8,128)(2,1)}), bf16[2048,4096]{1,0:T(8,128)(2,1)}) %all-gather.5.cloned.1.call-update) | async-done | bytes 16777232 | tf_op jit(solution)/shard_map/all_gather | solution.py:160
  376.0 0.0 copy-done.12
  376.0 10.6 %fusion.18 = f32[256,4096]{1,0:T(8,128)} fusion(bf16[2048,4096]{1,0:T(8,128)(2,1)} %all-gather.5.cloned.1.call-done, f32[2048]{0:T(1024)S(1)} %copy-done.12, f32[256]{0:T(256)S(1)} %add_rsqrt_fusion, f32[256,2048]{1,0:T(8,128)S(1)} %copy.58, bf16[256,2048]{1,0:T(8,128)(2,1)S(1)} %copy-done.3), kind=kOutput, calls=%fused_computation.33 | convolution fusion | flops 4299685888 | bytes 24126464 | tf_op jit(solution)/shard_map/dot_general | solution.py:158
  386.6 0.0 reduce-scatter.2.cloned.1.call-update
  386.6 41.6 %reduce-scatter.2.cloned.1.call-done = f32[256,1024]{1,0:T(8,128)} async-done(((f32[256,4096]{1,0:T(8,128)}), f32[256,1024]{1,0:T(8,128)}) %reduce-scatter.2.cloned.1.call-update) | async-done | bytes 1048592 | tf_op jit(solution)/shard_map/reduce_scatter | solution.py:163
  428.2 2.1 convert_element_type.67
  (33 shorter events, 0.3 us)
Async XLA Ops:
  6.5 6.0 %copy-start = (f32[256,32]{0,1:T(8,128)S(1)}, f32[256,32]{0,1:T(8,128)}, u32[]{:S(2)}) copy-start(f32[256,32]{0,1:T(8,128)} %param.22) | copy-start | bytes 98308
  6.5 1.4 copy-start.4
  6.5 1.5 copy-start.5
  6.5 7.2 %copy-start.9 = (f32[4,2048]{1,0:T(4,128)S(1)}, f32[4,2048]{1,0:T(4,128)}, u32[]{:S(2)}) copy-start(f32[4,2048]{1,0:T(4,128)} %param.18) | copy-start | bytes 98308
  6.5 7.4 %copy-start.10 = (f32[4,128]{1,0:T(4,128)S(1)}, f32[4,128]{1,0:T(4,128)}, u32[]{:S(2)}) copy-start(f32[4,128]{1,0:T(4,128)} %param.19) | copy-start | bytes 6148
  6.5 7.4 %copy-start.11 = (f32[4,128]{1,0:T(4,128)S(1)}, f32[4,128]{1,0:T(4,128)}, u32[]{:S(2)}) copy-start(f32[4,128]{1,0:T(4,128)} %param.20) | copy-start | bytes 6148
  6.6 141.9 %all-gather.7.cloned.1.call-start = ((), (), s32[]{:S(2)}) async-start(), calls=%async_computation.3 | async-start | bytes 9437184 | tf_op jit(solution)/shard_map/all_gather | solution.py:12
  8.0 1.0 copy-start.2
  9.1 6.4 %collective-permute-start = (bf16[3,2304]{1,0:T(4,128)(2,1)S(1)}, bf16[3,2304]{1,0:T(4,128)(2,1)S(1)}, u32[]{:S(2)}, u32[]{:S(2)}) collective-permute-start(bf16[3,2304]{1,0:T(4,128)(2,1)S(1)} %slice.83), channel_id=1, source_target_pairs={{0,4},{4,8},{8,12},{12,16},{16,20},{20,24},{24,28},{1,5},{5,9},{9,... | collective-permute-start | bytes 41480 | tf_op jit(solution)/shard_map/ppermute | solution.py:26
  17.1 1.7 copy-start.1
  18.9 1.9 copy-start.6
  23.3 352.7 %all-gather.5.cloned.1.call-start = ((), (), s32[]{:S(2)}) async-start(), calls=%async_computation.1 | async-start | bytes 18874368 | tf_op jit(solution)/shard_map/all_gather | solution.py:160
  24.0 404.1 %reduce-scatter.2.cloned.1.call-start = ((), (), s32[]{:S(2)}) async-start(), calls=%async_computation.2 | async-start | bytes 5242880 | tf_op jit(solution)/shard_map/reduce_scatter | solution.py:163
  148.5 1.3 copy-start.7
  148.6 1.3 copy-start.8
  148.6 1.3 copy-start.13
  153.6 2.0 copy-start.3
  155.7 220.3 %copy-start.12 = (f32[2048]{0:T(1024)S(1)}, f32[2048]{0:T(1024)}, u32[]{:S(2)}) copy-start(f32[2048]{0:T(1024)} %param.24) | copy-start | bytes 24580
Sparse Core Ops, SparseCore 0:
  23.4 124.9 all-gather.6
  150.5 225.5 all-gather.4
  386.7 41.4 reduce-scatter.1
where the time goes:
time: 440 us; the launch traced here: 437 us
  waiting for transfers between devices  363 us (82%)
  blocking collectives  20.5 us (5%)
  matrix products  19.1 us (4%)
  between operations  13.5 us (3%)
  other arithmetic  8.7 us (2%)
  local copies, waits for them, and re-layouts  8.28 us (2%)
    all_gather x1, waiting for transfers between devices, on_device(): lax.all_gather(out_weight, 'ctx', axis=1, tiled=True)  220 us
    all_gather x1, waiting for transfers between devices, prefix(): gathered = jax.tree.map(lambda a: lax.all_gather(a, axis), part)  101 us
    reduce_scatter x1, waiting for transfers between devices, on_device(): lax.psum_scatter(partial_out, 'tp', scatter_dimension=1, tiled=True)  41.6 us
    all_gather x1, blocking collectives, prefix(): gathered = jax.tree.map(lambda a: lax.all_gather(a, axis), part)  20.5 us
    dot_general x1, matrix products, on_device(): jnp.dot(hidden, lax.all_gather(out_weight, 'ctx', axis=1, tiled=True), pr...  10.6 us
  transfers between devices with their start and end apart: 4, of which 3 were waited for; matrix products, arithmetic and copies ran while one was open for 3% of the time, Pallas kernels for 0%

commit v1 on v0

--- a/solution.py
+++ b/solution.py
@@ -5,19 +5,6 @@
 
 N = 128
 BLOCK = 256
-
-
-def prefix(part, axis, combine, identity):
-    place = lax.axis_index(axis)
-    gathered = jax.tree.map(lambda a: lax.all_gather(a, axis), part)
-    state = jax.tree.map(lambda a, e: jnp.zeros_like(a) + jnp.asarray(e, a.dtype), part, identity)
-
-    def one(hop, state):
-        return combine(
-            state, jax.tree.map(lambda a: lax.dynamic_index_in_dim(a, hop, 0, False), gathered)
-        )
-
-    return lax.fori_loop(0, place, one, state)
 
 
 def shifted(value, axis, steps):
@@ -79,9 +66,21 @@
 
 
 def prefix_states(dev_decay, dev_state):
-    identity = (jnp.ones_like(dev_decay), jnp.zeros_like(dev_state))
-    _, incoming = prefix((dev_decay, dev_state), "ctx", combine, identity)
-    return incoming
+    count = lax.axis_size("ctx")
+    own = (dev_decay, dev_state)
+    if count == 1:
+        return jnp.zeros_like(dev_state)
+    got = shifted(own, "ctx", 1)
+    before = got
+    upto = combine(got, own)
+    step = 2
+    while step < count:
+        got = shifted(upto, "ctx", step)
+        before = combine(got, before)
+        if step * 2 < count:
+            upto = combine(got, upto)
+        step *= 2
+    return before[1]
 
 
 def on_device(

time: 440 us -> 389 us (0.88)
  waiting for transfers between devices: 363 us -> 266 us
  starting transfers between devices: 3.54 us -> 76.5 us
  blocking collectives: 20.5 us -> 0 us
    all_gather x1 -> x0, waiting for transfers between devices: 101 us -> none  [prefix(): gathered = jax.tree.map(lambda a: lax.all_gather(a, axis), part)]
    ppermute x1 -> x6, waiting for transfers between devices: 0.01 us -> 91.9 us  [shifted(): lax.ppermute(value, axis, [(source, source + steps) for source in range(f...]
    all_gather x1, waiting for transfers between devices: 220 us -> 132 us  [on_device(): lax.all_gather(out_weight, 'ctx', axis=1, tiled=True)]
    ppermute x1 -> x6, starting transfers between devices: 3.42 us -> 76.4 us  [shifted(): lax.ppermute(value, axis, [(source, source + steps) for source in range(f...]
    all_gather x1 -> x0, blocking collectives: 20.5 us -> none  [prefix(): gathered = jax.tree.map(lambda a: lax.all_gather(a, axis), part)]
  transfers between devices with their start and end apart: 4 -> 8, of which waited for: 3 -> 6; matrix products, arithmetic and copies ran while one was open for 3% -> 4% of each run, Pallas kernels for 0% -> 0%
where the time goes in v1:
time: 389 us; the launch traced here: 386 us
  waiting for transfers between devices  266 us (68%)
  starting transfers between devices  76.5 us (20%)
  matrix products  16.3 us (4%)
  between operations  13.8 us (4%)
  other arithmetic  7.57 us (2%)
  local copies, waits for them, and re-layouts  5.64 us (1%)
    all_gather x1, waiting for transfers between devices, on_device(): lax.all_gather(out_weight, 'ctx', axis=1, tiled=True)  132 us
    ppermute x6, waiting for transfers between devices, shifted(): lax.ppermute(value, axis, [(source, source + steps) for source in range(f...  91.9 us
    ppermute x6, starting transfers between devices, shifted(): lax.ppermute(value, axis, [(source, source + steps) for source in range(f...  76.4 us
    reduce_scatter x1, waiting for transfers between devices, on_device(): lax.psum_scatter(partial_out, 'tp', scatter_dimension=1, tiled=True)  41.1 us
    dot_general x1, matrix products, on_device(): jnp.dot(hidden, lax.all_gather(out_weight, 'ctx', axis=1, tiled=True), pr...  10.6 us
  transfers between devices with their start and end apart: 8, of which 6 were waited for; matrix products, arithmetic and copies ran while one was open for 4% of the time, Pallas kernels for 0%

profile of v1, /device:TPU:2, one launch (start us, length us, event | category | flops | bytes accessed | tf_op | source)
XLA Modules:
  0.0 385.6 jit_solution(2838211451355489667)
XLA Ops:
  6.5 0.0 copy-start
  6.5 0.0 copy-start.7
  6.6 0.0 all-gather.2.cloned.1.call-start
  6.6 0.7 all-gather.2.cloned.1.call-update
  7.3 0.0 reduce-scatter.2.cloned.1.call-start
  7.3 0.4 copy-done.1
  7.8 0.1 constant_dynamic-update-slice_fusion.5
  7.9 3.4 collective-permute-start
  11.4 0.6 reduce-window.6
  12.0 0.2 slice_reduce_fusion
  12.2 0.1 copy.30
  12.3 0.0 copy-done.7
  12.4 0.1 broadcast.89
  12.4 0.1 fusion.35
  12.5 0.5 exponential_reduce_fusion
  13.1 0.1 subtract_exponential_fusion
  13.2 0.0 copy-done.8
  13.2 0.2 convert_element_type.56
  13.4 0.0 collective-permute-done
  13.4 0.1 slice_reduce_fusion.5
  13.6 1.5 multiply_convert_fusion.3
  15.1 1.6 slice_convert_fusion
  16.7 2.1 copy.27
  18.8 1.4 fusion.18
  20.3 3.8 collective-permute-start.3
  24.1 41.9 %collective-permute-done.3 = f32[1,32,64,128]{3,2,1,0:T(8,128)S(1)} collective-permute-done((f32[1,32,64,128]{3,2,1,0:T(8,128)S(1)}, f32[1,32,64,128]{3,2,1,0:T(8,128)S(1)}, u32[]{:S(2)}, u32[]{:S(2)}) %collective-permute-start.3) | collective-permute-done | bytes 1048608 | tf_op jit(solution)/shard_map/ppermute | solution.py:13
  66.0 0.2 multiply_add_fusion.1
  66.2 8.4 %collective-permute-start.4 = (f32[1,32,64,128]{3,2,1,0:T(8,128)S(1)}, f32[1,32,64,128]{3,2,1,0:T(8,128)S(1)}, u32[]{:S(2)}, u32[]{:S(2)}) collective-permute-start(f32[1,32,64,128]{3,2,1,0:T(8,128)S(1)} %multiply_add_fusion.1), channel_id=1, source_target_pairs={{0,8},{4,12},{8,16},{12,20},{16,24},{20,28},{1,9},{5,13},{9,17},{1... | collective-permute-start | bytes 3145736 | tf_op jit(solution)/shard_map/ppermute | solution.py:13
  74.6 12.0 %collective-permute-start.1 = (f32[1,32]{1,0:T(1,128)S(1)}, f32[1,32]{1,0:T(1,128)S(1)}, u32[]{:S(2)}, u32[]{:S(2)}) collective-permute-start(f32[1,32]{1,0:T(1,128)S(1)} %bitcast.73), channel_id=1, source_target_pairs={{0,4},{4,8},{8,12},{12,16},{16,20},{20,24},{24,28},{1,5},{5,9},{9,... | collective-permute-start | bytes 392 | tf_op jit(solution)/shard_map/ppermute | solution.py:13
  86.6 1.2 collective-permute-done.1
  87.9 6.9 %collective-permute-done.4 = f32[1,32,64,128]{3,2,1,0:T(8,128)S(1)} collective-permute-done((f32[1,32,64,128]{3,2,1,0:T(8,128)S(1)}, f32[1,32,64,128]{3,2,1,0:T(8,128)S(1)}, u32[]{:S(2)}, u32[]{:S(2)}) %collective-permute-start.4) | collective-permute-done | bytes 1048608 | tf_op jit(solution)/shard_map/ppermute | solution.py:13
  94.8 0.2 multiply_add_fusion
  95.0 45.4 %collective-permute-start.5 = (f32[1,32,64,128]{3,2,1,0:T(8,128)S(1)}, f32[1,32,64,128]{3,2,1,0:T(8,128)S(1)}, u32[]{:S(2)}, u32[]{:S(2)}) collective-permute-start(f32[1,32,64,128]{3,2,1,0:T(8,128)S(1)} %multiply_add_fusion), channel_id=1, source_target_pairs={{0,16},{4,20},{8,24},{12,28},{1,17},{5,21},{9,25},{13,29},{2,18},{... | collective-permute-start | bytes 3145736 | tf_op jit(solution)/shard_map/ppermute | solution.py:13
  140.4 3.4 collective-permute-start.2
  143.8 41.9 %collective-permute-done.2 = f32[1,32]{1,0:T(1,128)S(1)} collective-permute-done((f32[1,32]{1,0:T(1,128)S(1)}, f32[1,32]{1,0:T(1,128)S(1)}, u32[]{:S(2)}, u32[]{:S(2)}) %collective-permute-start.2) | collective-permute-done | bytes 160 | tf_op jit(solution)/shard_map/ppermute | solution.py:13
  185.7 0.2 fusion.27
  185.9 0.0 copy-start.9
  185.9 2.1 fusion
  188.0 0.0 collective-permute-done.5
  188.0 2.1 fusion.14
  190.1 2.0 copy.32
  192.1 0.0 copy-start.10
  192.1 0.8 multiply_reduce_fusion
  192.9 132.1 %all-gather.2.cloned.1.call-done = bf16[2048,4096]{1,0:T(8,128)(2,1)} async-done(((bf16[2048,512]{1,0:T(8,128)(2,1)}), bf16[2048,4096]{1,0:T(8,128)(2,1)}) %all-gather.2.cloned.1.call-update) | async-done | bytes 16777232 | tf_op jit(solution)/shard_map/all_gather | solution.py:159
  325.0 10.6 %fusion.19 = f32[256,4096]{1,0:T(8,128)} fusion(bf16[2048,4096]{1,0:T(8,128)(2,1)} %all-gather.2.cloned.1.call-done, f32[2048]{0:T(1024)S(1)} %copy-done.10, f32[256]{0:T(256)S(1)} %add_rsqrt_fusion, f32[256,2048]{1,0:T(8,128)S(1)} %copy.32, bf16[256,2048]{1,0:T(8,128)(2,1)S(1)} %copy-done.2), kind=kOutput, calls=%fused_computation.32 | convolution fusion | flops 4299685888 | bytes 24126464 | tf_op jit(solution)/shard_map/dot_general | solution.py:157
  335.5 0.0 reduce-scatter.2.cloned.1.call-update
  335.6 41.1 %reduce-scatter.2.cloned.1.call-done = f32[256,1024]{1,0:T(8,128)} async-done(((f32[256,4096]{1,0:T(8,128)}), f32[256,1024]{1,0:T(8,128)}) %reduce-scatter.2.cloned.1.call-update) | async-done | bytes 1048592 | tf_op jit(solution)/shard_map/reduce_scatter | solution.py:162
  376.6 2.1 convert_element_type.67
  (36 shorter events, 0.3 us)
Async XLA Ops:
  6.5 4.8 %copy-start = (f32[256,32]{0,1:T(8,128)S(1)}, f32[256,32]{0,1:T(8,128)}, u32[]{:S(2)}) copy-start(f32[256,32]{0,1:T(8,128)} %param.20) | copy-start | bytes 98308
  6.5 1.2 copy-start.1
  6.5 1.3 copy-start.3
  6.5 1.3 copy-start.4
  6.5 5.8 %copy-start.6 = (f32[4,2048]{1,0:T(4,128)S(1)}, f32[4,2048]{1,0:T(4,128)}, u32[]{:S(2)}) copy-start(f32[4,2048]{1,0:T(4,128)} %param.16) | copy-start | bytes 98308
  6.5 5.8 %copy-start.7 = (f32[4,128]{1,0:T(4,128)S(1)}, f32[4,128]{1,0:T(4,128)}, u32[]{:S(2)}) copy-start(f32[4,128]{1,0:T(4,128)} %param.17) | copy-start | bytes 6148
  6.6 6.6 %copy-start.8 = (f32[4,128]{1,0:T(4,128)S(1)}, f32[4,128]{1,0:T(4,128)}, u32[]{:S(2)}) copy-start(f32[4,128]{1,0:T(4,128)} %param.18) | copy-start | bytes 6148
  6.6 318.4 %all-gather.2.cloned.1.call-start = ((), (), s32[]{:S(2)}) async-start(), calls=%async_computation.1 | async-start | bytes 18874368 | tf_op jit(solution)/shard_map/all_gather | solution.py:159
  7.3 369.3 %reduce-scatter.2.cloned.1.call-start = ((), (), s32[]{:S(2)}) async-start(), calls=%async_computation.2 | async-start | bytes 5242880 | tf_op jit(solution)/shard_map/reduce_scatter | solution.py:162
  7.9 5.5 %collective-permute-start = (bf16[3,2304]{1,0:T(4,128)(2,1)S(1)}, bf16[3,2304]{1,0:T(4,128)(2,1)S(1)}, u32[]{:S(2)}, u32[]{:S(2)}) collective-permute-start(bf16[3,2304]{1,0:T(4,128)(2,1)S(1)} %slice.83), channel_id=1, source_target_pairs={{0,4},{4,8},{8,12},{12,16},{16,20},{20,24},{24,28},{1,5},{5,9},{9,... | collective-permute-start | bytes 41480 | tf_op jit(solution)/shard_map/ppermute | solution.py:13
  16.7 2.1 copy-start.5
  20.3 45.7 %collective-permute-start.3 = (f32[1,32,64,128]{3,2,1,0:T(8,128)S(1)}, f32[1,32,64,128]{3,2,1,0:T(8,128)S(1)}, u32[]{:S(2)}, u32[]{:S(2)}) collective-permute-start(f32[1,32,64,128]{3,2,1,0:T(8,128)S(1)} %fusion.18), channel_id=1, source_target_pairs={{0,4},{4,8},{8,12},{12,16},{16,20},{20,24},{24,28},{1,5},{5,9},{9,... | collective-permute-start | bytes 3145736 | tf_op jit(solution)/shard_map/ppermute | solution.py:13
  66.2 28.6 %collective-permute-start.4 = (f32[1,32,64,128]{3,2,1,0:T(8,128)S(1)}, f32[1,32,64,128]{3,2,1,0:T(8,128)S(1)}, u32[]{:S(2)}, u32[]{:S(2)}) collective-permute-start(f32[1,32,64,128]{3,2,1,0:T(8,128)S(1)} %multiply_add_fusion.1), channel_id=1, source_target_pairs={{0,8},{4,12},{8,16},{12,20},{16,24},{20,28},{1,9},{5,13},{9,17},{1... | collective-permute-start | bytes 3145736 | tf_op jit(solution)/shard_map/ppermute | solution.py:13
  74.6 13.3 %collective-permute-start.1 = (f32[1,32]{1,0:T(1,128)S(1)}, f32[1,32]{1,0:T(1,128)S(1)}, u32[]{:S(2)}, u32[]{:S(2)}) collective-permute-start(f32[1,32]{1,0:T(1,128)S(1)} %bitcast.73), channel_id=1, source_target_pairs={{0,4},{4,8},{8,12},{12,16},{16,20},{20,24},{24,28},{1,5},{5,9},{9,... | collective-permute-start | bytes 392 | tf_op jit(solution)/shard_map/ppermute | solution.py:13
  95.0 93.0 %collective-permute-start.5 = (f32[1,32,64,128]{3,2,1,0:T(8,128)S(1)}, f32[1,32,64,128]{3,2,1,0:T(8,128)S(1)}, u32[]{:S(2)}, u32[]{:S(2)}) collective-permute-start(f32[1,32,64,128]{3,2,1,0:T(8,128)S(1)} %multiply_add_fusion), channel_id=1, source_target_pairs={{0,16},{4,20},{8,24},{12,28},{1,17},{5,21},{9,25},{13,29},{2,18},{... | collective-permute-start | bytes 3145736 | tf_op jit(solution)/shard_map/ppermute | solution.py:13
  140.4 45.3 %collective-permute-start.2 = (f32[1,32]{1,0:T(1,128)S(1)}, f32[1,32]{1,0:T(1,128)S(1)}, u32[]{:S(2)}, u32[]{:S(2)}) collective-permute-start(f32[1,32]{1,0:T(1,128)S(1)} %bitcast_multiply_fusion.1), channel_id=1, source_target_pairs={{0,8},{4,12},{8,16},{12,20},{16,24},{20,28},{1,9},{5,13},{9,17},{1... | collective-permute-start | bytes 392 | tf_op jit(solution)/shard_map/ppermute | solution.py:13
  185.9 2.1 copy-start.9
  190.0 2.0 copy-start.2
  192.1 132.9 %copy-start.10 = (f32[2048]{0:T(1024)S(1)}, f32[2048]{0:T(1024)}, u32[]{:S(2)}) copy-start(f32[2048]{0:T(1024)} %param.22) | copy-start | bytes 24580
Sparse Core Ops, SparseCore 0:
  9.4 315.5 all-gather.1
  335.7 40.8 reduce-scatter.1

commit v2 on v1

--- a/solution.py
+++ b/solution.py
@@ -1,3 +1,5 @@
+import functools
+
 import jax
 import jax.numpy as jnp
 from jax import lax
@@ -7,8 +9,7 @@
 BLOCK = 256
 
 
-def shifted(value, axis, steps):
-    count = lax.axis_size(axis)
+def shifted(value, axis, steps, count):
     first, last = (max(0, -steps), min(count, count - steps))
     return lax.ppermute(value, axis, [(source, source + steps) for source in range(first, last)])
 
@@ -65,17 +66,16 @@
     return (decay_first * decay_second, decay_second[..., None, None] * state_first + state_second)
 
 
-def prefix_states(dev_decay, dev_state):
-    count = lax.axis_size("ctx")
+def prefix_states(dev_decay, dev_state, axis, count):
     own = (dev_decay, dev_state)
     if count == 1:
         return jnp.zeros_like(dev_state)
-    got = shifted(own, "ctx", 1)
+    got = shifted(own, axis, 1, count)
     before = got
     upto = combine(got, own)
     step = 2
     while step < count:
-        got = shifted(upto, "ctx", step)
+        got = shifted(upto, axis, step, count)
         before = combine(got, before)
         if step * 2 < count:
             upto = combine(got, upto)
@@ -84,6 +84,7 @@
 
 
 def on_device(
+    layout,
     features,
     input_map,
     output_map,
@@ -108,7 +109,8 @@
     packed = jnp.concatenate([features, input_map, output_map], axis=1)
     kernel = jnp.concatenate([conv_feat, conv_input, conv_output], axis=1)
     pre_act = local_conv(packed, kernel, tok_rows)
-    tail_rows = shifted(packed[tok_rows - tail_len :], "ctx", 1)
+    ctx_axes, ctx_count, outer_axis, inner_axis, tp_count = layout
+    tail_rows = shifted(packed[tok_rows - tail_len :], ctx_axes, 1, ctx_count)
     edge_sums = edge_partial(tail_rows, kernel)
     pre_act = pre_act + jnp.pad(edge_sums, ((0, tok_rows - tail_len), (0, 0)))
     conv_out = jax.nn.silu(pre_act).astype(jnp.bfloat16)
@@ -138,7 +140,7 @@
         fold_local, jnp.zeros(blk_states.shape[1:], jnp.float32), (blk_decay, blk_states)
     )
     dev_decay = jnp.prod(blk_decay, axis=0)
-    incoming = prefix_states(dev_decay, dev_state)
+    incoming = prefix_states(dev_decay, dev_state, ctx_axes, ctx_count)
 
     def advance(state_carry, block_in):
         scaled_k, b_k, c_k, cum_k, decay_k, state_k = block_in
@@ -154,29 +156,53 @@
     grouped = gated_y.reshape(tok_rows, groups_here, width_x // groups_here)
     inv_root = lax.rsqrt(jnp.mean(grouped * grouped, axis=-1, keepdims=True) + 1e-05)
     hidden = ((grouped * inv_root).reshape(tok_rows, width_x) * norm_gain).astype(jnp.bfloat16)
-    partial_out = jnp.dot(
-        hidden,
-        lax.all_gather(out_weight, "ctx", axis=1, tiled=True),
-        preferred_element_type=jnp.float32,
-    )
-    return lax.psum_scatter(partial_out, "tp", scatter_dimension=1, tiled=True).astype(jnp.bfloat16)
+    if outer_axis is None:
+        partial_out = jnp.dot(
+            hidden,
+            lax.all_gather(out_weight, ctx_axes, axis=1, tiled=True),
+            preferred_element_type=jnp.float32,
+        )
+        return lax.psum_scatter(partial_out, "tp", scatter_dimension=1, tiled=True).astype(
+            jnp.bfloat16
+        )
+    rows_all = lax.all_gather(hidden, outer_axis, axis=0, tiled=True)
+    cols_all = lax.all_gather(out_weight, inner_axis, axis=1, tiled=True)
+    partial_out = jnp.dot(rows_all, cols_all, preferred_element_type=jnp.float32)
+    reduced = lax.psum_scatter(partial_out, "tp", scatter_dimension=0, tiled=True)
+    swap = [(o * tp_count + t, t * tp_count + o) for o in range(tp_count) for t in range(tp_count)]
+    return lax.ppermute(reduced.astype(jnp.bfloat16), (outer_axis, "tp"), swap)
 
 
 def solution(mesh):
+    ctx_count = mesh.shape["ctx"]
+    tp_count = mesh.shape["tp"]
+    if ctx_count % tp_count == 0:
+        inner = ctx_count // tp_count
+        grid = mesh.devices.reshape(tp_count, inner, tp_count)
+        mesh = jax.sharding.Mesh(grid, ("outer", "inner", "tp"))
+        ctx_axes = ("outer", "inner")
+        layout = (ctx_axes, ctx_count, "outer", "inner", tp_count)
+    else:
+        ctx_axes = "ctx"
+        layout = (ctx_axes, ctx_count, None, None, tp_count)
     placed = (
-        P("ctx", "tp"),
-        P("ctx", "tp"),
-        P("ctx", "tp"),
-        P("ctx", "tp"),
+        P(ctx_axes, "tp"),
+        P(ctx_axes, "tp"),
+        P(ctx_axes, "tp"),
+        P(ctx_axes, "tp"),
         P(None, "tp"),
         P(None, "tp"),
         P(None, "tp"),
-        P("ctx", "tp"),
-        P("ctx", "tp"),
+        P(ctx_axes, "tp"),
+        P(ctx_axes, "tp"),
         P("tp"),
         P("tp"),
-        P("tp", "ctx"),
+        P("tp", ctx_axes),
     )
     return jax.shard_map(
-        on_device, mesh=mesh, in_specs=placed, out_specs=P("ctx", "tp"), check_vma=False
-    )
+        functools.partial(on_device, layout),
+        mesh=mesh,
+        in_specs=placed,
+        out_specs=P(ctx_axes, "tp"),
+        check_vma=False,
+    )

time: 389 us -> 314 us (0.81)
  starting transfers between devices: 76.5 us -> 31.1 us
  waiting for transfers between devices: 266 us -> 233 us
    ppermute x6, starting transfers between devices: 76.4 us -> 25.6 us  [shifted(): lax.ppermute(value, axis, [(source, source + steps) for source in range(f...]
    all_gather x1 -> x2, waiting for transfers between devices: 132 us -> 103 us  [the longest x1 103 us: on_device(): rows_all = lax.all_gather(hidden, outer_axis, axis=0, tiled=True)]
    ppermute x6, waiting for transfers between devices: 91.9 us -> 63.6 us  [shifted(): lax.ppermute(value, axis, [(source, source + steps) for source in range(f...]
    ppermute x0 -> x1, waiting for transfers between devices: none -> 24 us  [on_device(): return lax.ppermute(reduced.astype(jnp.bfloat16), (outer_axis, 'tp'), swap)]
    ppermute x0 -> x1, starting transfers between devices: none -> 5.42 us  [on_device(): return lax.ppermute(reduced.astype(jnp.bfloat16), (outer_axis, 'tp'), swap)]
  transfers between devices with their start and end apart: 8 -> 10, of which waited for: 6 -> 7; matrix products, arithmetic and copies ran while one was open for 4% -> 5% of each run, Pallas kernels for 0% -> 0%
where the time goes in v2:
time: 314 us
  waiting for transfers between devices  233 us (74%)
  starting transfers between devices  31.1 us (10%)
  matrix products  18.7 us (6%)
  between operations  13.5 us (4%)
  other arithmetic  10.8 us (3%)
  local copies, waits for them, and re-layouts  7.14 us (2%)
    all_gather x1, waiting for transfers between devices, on_device(): rows_all = lax.all_gather(hidden, outer_axis, axis=0, tiled=True)  103 us
    ppermute x6, waiting for transfers between devices, shifted(): lax.ppermute(value, axis, [(source, source + steps) for source in range(f...  63.6 us
    reduce_scatter x1, waiting for transfers between devices, on_device(): lax.psum_scatter(partial_out, 'tp', scatter_dimension=0, tiled=True)  42.1 us
    ppermute x6, starting transfers between devices, shifted(): lax.ppermute(value, axis, [(source, source + steps) for source in range(f...  25.6 us
    ppermute x1, waiting for transfers between devices, on_device(): return lax.ppermute(reduced.astype(jnp.bfloat16), (outer_axis, 'tp'), swap)  24 us
    dot_general x1, matrix products, on_device(): jnp.dot(rows_all, cols_all, preferred_element_type=jnp.float32)  9.93 us
  transfers between devices with their start and end apart: 10, of which 7 were waited for; matrix products, arithmetic and copies ran while one was open for 5% of the time, Pallas kernels for 0%

profile of v2, /device:TPU:2, one launch (start us, length us, event | category | flops | bytes accessed | tf_op | source)
XLA Modules:
  0.0 313.9 jit_solution(12602130731376251955)
XLA Ops:
  6.6 0.0 all-gather.5.cloned.1.call-start
  6.6 1.4 constant_dynamic-update-slice_fusion.5
  8.1 3.4 %collective-permute-start = (bf16[3,2304]{1,0:T(4,128)(2,1)S(1)}, bf16[3,2304]{1,0:T(4,128)(2,1)S(1)}, u32[]{:S(2)}, u32[]{:S(2)}) collective-permute-start(bf16[3,2304]{1,0:T(4,128)(2,1)S(1)} %slice.83), channel_id=1, source_target_pairs={{0,4},{4,8},{8,12},{12,16},{16,20},{20,24},{24,28},{1,5},{5,9},{9,... | collective-permute-start | bytes 41480 | tf_op jit(solution)/shard_map/ppermute | solution.py:14
  11.5 0.6 reduce-window.6
  12.1 0.2 slice_reduce_fusion
  12.3 0.1 copy.30
  12.4 0.1 broadcast.89
  12.5 0.7 fusion.31
  13.2 0.5 exponential_reduce_fusion
  13.8 0.1 subtract_exponential_fusion
  14.0 0.2 convert_element_type.56
  14.2 0.1 slice_reduce_fusion.5
  14.3 1.5 multiply_convert_fusion.3
  15.8 1.6 slice_convert_fusion
  17.5 1.9 copy.27
  19.4 3.2 %fusion.18 = f32[1,32,64,128]{3,2,1,0:T(8,128)} fusion(f32[256,32]{0,1:T(8,128)S(1)} %bitcast.69, f32[256,128]{1,0:T(8,128)S(1)} %slice_convert_fusion.1, f32[32]{0:T(128)S(1)} %get-tuple-element.59, f32[256,32,64]{0,2,1:T(8,128)S(1)} %bitcast.61, f32[256,32]{0,1:T(8,128)} %param.19), kind=kOutput, calls=%fused_computation.31 | convolution fusion | flops 137625600 | bytes 3342464 | tf_op jit(solution)/shard_map/vmap(sgjp,sgjn->gjpn)/dot_general | solution.py:54
  22.6 4.4 %collective-permute-start.3 = (f32[1,32,64,128]{3,2,1,0:T(8,128)}, f32[1,32,64,128]{3,2,1,0:T(8,128)}, u32[]{:S(2)}, u32[]{:S(2)}) collective-permute-start(f32[1,32,64,128]{3,2,1,0:T(8,128)} %fusion.18), channel_id=1, source_target_pairs={{0,4},{4,8},{8,12},{12,16},{16,20},{20,24},{24,28},{1,5},{5,9},{9,... | collective-permute-start | bytes 3145736 | tf_op jit(solution)/shard_map/ppermute | solution.py:14
  27.0 0.0 all-gather.5.cloned.1.call-update
  27.0 0.0 all-gather.3.cloned.1.call-start
  27.1 34.6 %collective-permute-done.3 = f32[1,32,64,128]{3,2,1,0:T(8,128)} collective-permute-done((f32[1,32,64,128]{3,2,1,0:T(8,128)}, f32[1,32,64,128]{3,2,1,0:T(8,128)}, u32[]{:S(2)}, u32[]{:S(2)}) %collective-permute-start.3) | collective-permute-done | bytes 1048608 | tf_op jit(solution)/shard_map/ppermute | solution.py:14
  61.7 1.7 multiply_add_fusion.1
  63.4 0.0 copy-start.5
  63.4 3.6 %collective-permute-start.4 = (f32[1,32,64,128]{3,2,1,0:T(8,128)S(1)}, f32[1,32,64,128]{3,2,1,0:T(8,128)S(1)}, u32[]{:S(2)}, u32[]{:S(2)}) collective-permute-start(f32[1,32,64,128]{3,2,1,0:T(8,128)S(1)} %multiply_add_fusion.1), channel_id=1, source_target_pairs={{0,8},{4,12},{8,16},{12,20},{16,24},{20,28},{1,9},{5,13},{9,17},{1... | collective-permute-start | bytes 3145736 | tf_op jit(solution)/shard_map/ppermute | solution.py:14
  67.1 4.4 %collective-permute-start.1 = (f32[1,32]{1,0:T(1,128)S(1)}, f32[1,32]{1,0:T(1,128)S(1)}, u32[]{:S(2)}, u32[]{:S(2)}) collective-permute-start(f32[1,32]{1,0:T(1,128)S(1)} %bitcast.74), channel_id=1, source_target_pairs={{0,4},{4,8},{8,12},{12,16},{16,20},{20,24},{24,28},{1,5},{5,9},{9,... | collective-permute-start | bytes 392 | tf_op jit(solution)/shard_map/ppermute | solution.py:14
  71.5 1.2 collective-permute-done.1
  72.8 12.7 %collective-permute-done.4 = f32[1,32,64,128]{3,2,1,0:T(8,128)S(1)} collective-permute-done((f32[1,32,64,128]{3,2,1,0:T(8,128)S(1)}, f32[1,32,64,128]{3,2,1,0:T(8,128)S(1)}, u32[]{:S(2)}, u32[]{:S(2)}) %collective-permute-start.4) | collective-permute-done | bytes 1048608 | tf_op jit(solution)/shard_map/ppermute | solution.py:14
  85.5 0.2 multiply_add_fusion
  85.7 7.7 %collective-permute-start.5 = (f32[1,32,64,128]{3,2,1,0:T(8,128)S(1)}, f32[1,32,64,128]{3,2,1,0:T(8,128)S(1)}, u32[]{:S(2)}, u32[]{:S(2)}) collective-permute-start(f32[1,32,64,128]{3,2,1,0:T(8,128)S(1)} %multiply_add_fusion), channel_id=1, source_target_pairs={{0,16},{4,20},{8,24},{12,28},{1,17},{5,21},{9,25},{13,29},{2,18},{... | collective-permute-start | bytes 3145736 | tf_op jit(solution)/shard_map/ppermute | solution.py:14
  93.4 2.0 collective-permute-start.2
  95.4 15.1 %collective-permute-done.2 = f32[1,32]{1,0:T(1,128)S(1)} collective-permute-done((f32[1,32]{1,0:T(1,128)S(1)}, f32[1,32]{1,0:T(1,128)S(1)}, u32[]{:S(2)}, u32[]{:S(2)}) %collective-permute-start.2) | collective-permute-done | bytes 160 | tf_op jit(solution)/shard_map/ppermute | solution.py:14
  110.5 0.2 fusion.24
  110.7 0.0 copy-start.10
  110.7 2.1 fusion
  112.9 3.3 %fusion.14 = f32[256,1,32,64]{0,3,2,1:T(8,128)} fusion(f32[32,64,256]{2,1,0:T(8,128)S(1)} %fusion, f32[256,1,32,64]{0,3,2,1:T(8,128)S(1)} %bitcast.63, f32[32]{0:T(128)S(1)} %copy-done.10, f32[256,32]{0,1:T(8,128)S(1)} %bitcast.70, f32[1,32,64,128]{3,2,1,0:T(8,128)} %collective-permute-done.3, f32[1,32,64,128]{3,2,1,0:T(8,128)S(1)} %collective-permute-done.4, ...), kind=kOutput, calls=%fused_computation.24 | convolution fusion | flops 137625600 | bytes 9537024 | tf_op jit(solution)/shard_map/while/body/eval_jaxpr/tgn,gjpn->tgjp/dot_general | solution.py:59
  116.1 2.0 copy.32
  118.2 0.8 multiply_reduce_fusion
  118.9 1.9 multiply_convert_fusion.5
  120.9 0.0 all-gather.3.cloned.1.call-update
  120.9 0.0 reduce-scatter.2.cloned.1.call-start
  120.9 0.0 all-gather.5.cloned.1.call-done
  121.0 102.9 %all-gather.3.cloned.1.call-done = bf16[1024,2048]{1,0:T(8,128)(2,1)} async-done(((bf16[256,2048]{1,0:T(8,128)(2,1)}), bf16[1024,2048]{1,0:T(8,128)(2,1)}) %all-gather.3.cloned.1.call-update) | async-done | bytes 4194320 | tf_op jit(solution)/shard_map/all_gather | solution.py:168
  223.8 9.9 %fusion.33 = f32[1024,1024]{1,0:T(8,128)} fusion(bf16[1024,2048]{1,0:T(8,128)(2,1)} %all-gather.3.cloned.1.call-done, bf16[2048,1024]{1,0:T(8,128)(2,1)} %all-gather.5.cloned.1.call-done), kind=kOutput, calls=%fused_computation.79 | convolution fusion | flops 4294967296 | bytes 12582912 | tf_op jit(solution)/shard_map/dot_general | solution.py:170
  233.8 0.0 reduce-scatter.2.cloned.1.call-update
  233.8 42.1 %reduce-scatter.2.cloned.1.call-done = f32[256,1024]{1,0:T(8,128)} async-done(((f32[1024,1024]{1,0:T(8,128)}), f32[256,1024]{1,0:T(8,128)}) %reduce-scatter.2.cloned.1.call-update) | async-done | bytes 1048592 | tf_op jit(solution)/shard_map/reduce_scatter | solution.py:171
  275.9 1.3 convert_element_type.67
  277.2 5.4 %collective-permute-start.6 = (bf16[256,1024]{1,0:T(8,128)(2,1)S(1)}, bf16[256,1024]{1,0:T(8,128)(2,1)S(1)}, u32[]{:S(2)}, u32[]{:S(2)}) collective-permute-start(bf16[256,1024]{1,0:T(8,128)(2,1)S(1)} %convert_element_type.67), channel_id=1, source_target_pairs={{0,0},{1,8},{2,16},{3,24},{8,1},{9,9},{10,17},{11,25},{16,2},{17,1... | collective-permute-start | bytes 1572872 | tf_op jit(solution)/shard_map/ppermute | solution.py:173
  282.6 24.0 %collective-permute-done.6 = bf16[256,1024]{1,0:T(8,128)(2,1)S(1)} collective-permute-done((bf16[256,1024]{1,0:T(8,128)(2,1)S(1)}, bf16[256,1024]{1,0:T(8,128)(2,1)S(1)}, u32[]{:S(2)}, u32[]{:S(2)}) %collective-permute-start.6) | collective-permute-done | bytes 524320 | tf_op jit(solution)/shard_map/ppermute | solution.py:173
  306.6 0.8 copy.49
  (43 shorter events, 0.3 us)
Async XLA Ops:
  6.5 5.0 %copy-start = (f32[256,32]{0,1:T(8,128)S(1)}, f32[256,32]{0,1:T(8,128)}, u32[]{:S(2)}) copy-start(f32[256,32]{0,1:T(8,128)} %param.20) | copy-start | bytes 98308
  6.5 1.4 copy-start.3
  6.5 1.5 copy-start.4
  6.5 7.4 %copy-start.6 = (f32[4,2048]{1,0:T(4,128)S(1)}, f32[4,2048]{1,0:T(4,128)}, u32[]{:S(2)}) copy-start(f32[4,2048]{1,0:T(4,128)} %param.16) | copy-start | bytes 98308
  6.5 7.4 %copy-start.8 = (f32[4,128]{1,0:T(4,128)S(1)}, f32[4,128]{1,0:T(4,128)}, u32[]{:S(2)}) copy-start(f32[4,128]{1,0:T(4,128)} %param.17) | copy-start | bytes 6148
  6.5 7.4 %copy-start.9 = (f32[4,128]{1,0:T(4,128)S(1)}, f32[4,128]{1,0:T(4,128)}, u32[]{:S(2)}) copy-start(f32[4,128]{1,0:T(4,128)} %param.18) | copy-start | bytes 6148
  6.6 114.4 %all-gather.5.cloned.1.call-start = ((), (), s32[]{:S(2)}) async-start(), calls=%async_computation.2 | async-start | bytes 6291456 | tf_op jit(solution)/shard_map/all_gather | solution.py:169
  8.1 6.1 %collective-permute-start = (bf16[3,2304]{1,0:T(4,128)(2,1)S(1)}, bf16[3,2304]{1,0:T(4,128)(2,1)S(1)}, u32[]{:S(2)}, u32[]{:S(2)}) collective-permute-start(bf16[3,2304]{1,0:T(4,128)(2,1)S(1)} %slice.83), channel_id=1, source_target_pairs={{0,4},{4,8},{8,12},{12,16},{16,20},{20,24},{24,28},{1,5},{5,9},{9,... | collective-permute-start | bytes 41480 | tf_op jit(solution)/shard_map/ppermute | solution.py:14
  22.6 39.1 %collective-permute-start.3 = (f32[1,32,64,128]{3,2,1,0:T(8,128)}, f32[1,32,64,128]{3,2,1,0:T(8,128)}, u32[]{:S(2)}, u32[]{:S(2)}) collective-permute-start(f32[1,32,64,128]{3,2,1,0:T(8,128)} %fusion.18), channel_id=1, source_target_pairs={{0,4},{4,8},{8,12},{12,16},{16,20},{20,24},{24,28},{1,5},{5,9},{9,... | collective-permute-start | bytes 3145736 | tf_op jit(solution)/shard_map/ppermute | solution.py:14
  27.0 196.8 %all-gather.3.cloned.1.call-start = ((), (), s32[]{:S(2)}) async-start(), calls=%async_computation.1 | async-start | bytes 5242880 | tf_op jit(solution)/shard_map/all_gather | solution.py:168
  63.4 32.0 %copy-start.2 = (f32[1,256,1,32]{1,2,3,0:T(1,128)S(1)}, f32[1,256,1,32]{1,2,3,0:T(1,128)}, u32[]{:S(2)}) copy-start(f32[1,256,1,32]{1,2,3,0:T(1,128)} %get-tuple-element.39) | copy-start | bytes 98308
  63.4 47.3 %copy-start.5 = (f32[256,32]{0,1:T(8,128)S(1)}, f32[256,32]{0,1:T(8,128)}, u32[]{:S(2)}) copy-start(f32[256,32]{0,1:T(8,128)} %param.19) | copy-start | bytes 98308
  63.4 22.0 %collective-permute-start.4 = (f32[1,32,64,128]{3,2,1,0:T(8,128)S(1)}, f32[1,32,64,128]{3,2,1,0:T(8,128)S(1)}, u32[]{:S(2)}, u32[]{:S(2)}) collective-permute-start(f32[1,32,64,128]{3,2,1,0:T(8,128)S(1)} %multiply_add_fusion.1), channel_id=1, source_target_pairs={{0,8},{4,12},{8,16},{12,20},{16,24},{20,28},{1,9},{5,13},{9,17},{1... | collective-permute-start | bytes 3145736 | tf_op jit(solution)/shard_map/ppermute | solution.py:14
  67.1 5.7 %collective-permute-start.1 = (f32[1,32]{1,0:T(1,128)S(1)}, f32[1,32]{1,0:T(1,128)S(1)}, u32[]{:S(2)}, u32[]{:S(2)}) collective-permute-start(f32[1,32]{1,0:T(1,128)S(1)} %bitcast.74), channel_id=1, source_target_pairs={{0,4},{4,8},{8,12},{12,16},{16,20},{20,24},{24,28},{1,5},{5,9},{9,... | collective-permute-start | bytes 392 | tf_op jit(solution)/shard_map/ppermute | solution.py:14
  85.7 27.2 %collective-permute-start.5 = (f32[1,32,64,128]{3,2,1,0:T(8,128)S(1)}, f32[1,32,64,128]{3,2,1,0:T(8,128)S(1)}, u32[]{:S(2)}, u32[]{:S(2)}) collective-permute-start(f32[1,32,64,128]{3,2,1,0:T(8,128)S(1)} %multiply_add_fusion), channel_id=1, source_target_pairs={{0,16},{4,20},{8,24},{12,28},{1,17},{5,21},{9,25},{13,29},{2,18},{... | collective-permute-start | bytes 3145736 | tf_op jit(solution)/shard_map/ppermute | solution.py:14
  93.4 17.1 %collective-permute-start.2 = (f32[1,32]{1,0:T(1,128)S(1)}, f32[1,32]{1,0:T(1,128)S(1)}, u32[]{:S(2)}, u32[]{:S(2)}) collective-permute-start(f32[1,32]{1,0:T(1,128)S(1)} %bitcast_multiply_fusion.1), channel_id=1, source_target_pairs={{0,8},{4,12},{8,16},{12,20},{16,24},{20,28},{1,9},{5,13},{9,17},{1... | collective-permute-start | bytes 392 | tf_op jit(solution)/shard_map/ppermute | solution.py:14
  110.7 2.1 copy-start.10
  116.1 2.0 copy-start.1
  118.2 0.8 copy-start.7
  120.9 155.0 %reduce-scatter.2.cloned.1.call-start = ((), (), s32[]{:S(2)}) async-start(), calls=%async_computation.3 | async-start | bytes 5242880 | tf_op jit(solution)/shard_map/reduce_scatter | solution.py:171
  277.2 29.4 %collective-permute-start.6 = (bf16[256,1024]{1,0:T(8,128)(2,1)S(1)}, bf16[256,1024]{1,0:T(8,128)(2,1)S(1)}, u32[]{:S(2)}, u32[]{:S(2)}) collective-permute-start(bf16[256,1024]{1,0:T(8,128)(2,1)S(1)} %convert_element_type.67), channel_id=1, source_target_pairs={{0,0},{1,8},{2,16},{3,24},{8,1},{9,9},{10,17},{11,25},{16,2},{17,1... | collective-permute-start | bytes 1572872 | tf_op jit(solution)/shard_map/ppermute | solution.py:173
Sparse Core Ops, SparseCore 0:
  27.2 66.2 all-gather.4
  121.0 102.7 all-gather.2
  233.9 41.9 reduce-scatter.1

commit v3 on v2

--- a/solution.py
+++ b/solution.py
@@ -165,18 +165,43 @@
         return lax.psum_scatter(partial_out, "tp", scatter_dimension=1, tiled=True).astype(
             jnp.bfloat16
         )
-    rows_all = lax.all_gather(hidden, outer_axis, axis=0, tiled=True)
+    outer_at = lax.axis_index(outer_axis)
+    tp_at = lax.axis_index("tp")
+    arrived = [hidden] + [
+        lax.ppermute(hidden, outer_axis, [(s, (s + d) % tp_count) for s in range(tp_count)])
+        for d in range(1, tp_count)
+    ]
     cols_all = lax.all_gather(out_weight, inner_axis, axis=1, tiled=True)
-    partial_out = jnp.dot(rows_all, cols_all, preferred_element_type=jnp.float32)
-    reduced = lax.psum_scatter(partial_out, "tp", scatter_dimension=0, tiled=True)
+    by_source = jnp.stack(
+        [jnp.dot(rows, cols_all, preferred_element_type=jnp.float32) for rows in arrived]
+    )
+
+    def for_target(target):
+        return lax.dynamic_index_in_dim(
+            by_source, (outer_at - target + tp_count) % tp_count, 0, keepdims=False
+        )
+
+    held = {m: for_target(tp_at ^ m) for m in range(tp_count)}
+    bit = 1
+    while bit < tp_count:
+        going = sorted(m for m in held if m & bit)
+        got = lax.ppermute(
+            jnp.stack([held[m] for m in going]),
+            "tp",
+            [(s, s ^ bit) for s in range(tp_count)],
+        )
+        held = {m: held[m] for m in held if not m & bit}
+        for index, m in enumerate(going):
+            held[m ^ bit] = held[m ^ bit] + got[index]
+        bit *= 2
     swap = [(o * tp_count + t, t * tp_count + o) for o in range(tp_count) for t in range(tp_count)]
-    return lax.ppermute(reduced.astype(jnp.bfloat16), (outer_axis, "tp"), swap)
+    return lax.ppermute(held[0].astype(jnp.bfloat16), (outer_axis, "tp"), swap)
 
 
 def solution(mesh):
     ctx_count = mesh.shape["ctx"]
     tp_count = mesh.shape["tp"]
-    if ctx_count % tp_count == 0:
+    if ctx_count % tp_count == 0 and tp_count & (tp_count - 1) == 0:
         inner = ctx_count // tp_count
         grid = mesh.devices.reshape(tp_count, inner, tp_count)
         mesh = jax.sharding.Mesh(grid, ("outer", "inner", "tp"))

time: 314 us -> 302 us (0.962)
  waiting for transfers between devices: 233 us -> 192 us
  starting transfers between devices: 31.1 us -> 54.9 us
  other arithmetic: 10.8 us -> 14.6 us
  matrix products: 18.7 us -> 15.4 us
    ppermute x1 -> x6, waiting for transfers between devices: 24 us -> 136 us  [the longest x3 83 us: on_device(): lax.ppermute(hidden, outer_axis, [(s, (s + d) % tp_count) for s in range(...]
    all_gather x1 -> x0, waiting for transfers between devices: 103 us -> none  [on_device(): rows_all = lax.all_gather(hidden, outer_axis, axis=0, tiled=True)]
    reduce_scatter x1 -> x0, waiting for transfers between devices: 42.1 us -> none  [on_device(): lax.psum_scatter(partial_out, 'tp', scatter_dimension=0, tiled=True)]
    ppermute x1 -> x6, starting transfers between devices: 5.42 us -> 30.1 us  [the longest x3 27.3 us: on_device(): lax.ppermute(hidden, outer_axis, [(s, (s + d) % tp_count) for s in range(...]
    ppermute x6, waiting for transfers between devices: 63.6 us -> 56.6 us  [shifted(): lax.ppermute(value, axis, [(source, source + steps) for source in range(f...]
    dot_general x1 -> x4, matrix products: 9.93 us -> 7.62 us  [on_device(): jnp.dot(rows, cols_all, preferred_element_type=jnp.float32)]
  transfers between devices with their start and end apart: 10 -> 13, of which waited for: 7 -> 9; matrix products, arithmetic and copies ran while one was open for 5% -> 7% of each run, Pallas kernels for 0% -> 0%
where the time goes in v3:
time: 302 us; the launch traced here: 301 us
  waiting for transfers between devices  192 us (64%)
  starting transfers between devices  54.9 us (18%)
  matrix products  15.4 us (5%)
  other arithmetic  14.6 us (5%)
  between operations  13.9 us (5%)
  local copies, waits for them, and re-layouts  10.1 us (3%)
    ppermute x3, waiting for transfers between devices, on_device(): lax.ppermute(hidden, outer_axis, [(s, (s + d) % tp_count) for s in range(...  83 us
    ppermute x6, waiting for transfers between devices, shifted(): lax.ppermute(value, axis, [(source, source + steps) for source in range(f...  56.6 us
    ppermute x2, waiting for transfers between devices, on_device(): lax.ppermute(jnp.stack([held[m] for m in going]), 'tp', [(s, s ^ bit) for...  28.9 us
    ppermute x3, starting transfers between devices, on_device(): lax.ppermute(hidden, outer_axis, [(s, (s + d) % tp_count) for s in range(...  27.3 us
    ppermute x6, starting transfers between devices, shifted(): lax.ppermute(value, axis, [(source, source + steps) for source in range(f...  24.7 us
    ppermute x1, waiting for transfers between devices, on_device(): return lax.ppermute(held[0].astype(jnp.bfloat16), (outer_axis, 'tp'), swap)  23.8 us
    dot_general x4, matrix products, on_device(): jnp.dot(rows, cols_all, preferred_element_type=jnp.float32)  7.62 us
  transfers between devices with their start and end apart: 13, of which 9 were waited for; matrix products, arithmetic and copies ran while one was open for 7% of the time, Pallas kernels for 0%

profile of v3, /device:TPU:2, one launch (start us, length us, event | category | flops | bytes accessed | tf_op | source)
XLA Modules:
  0.0 301.1 jit_solution(13952639538319998849)
XLA Ops:
  6.6 1.4 constant_dynamic-update-slice_fusion.5
  8.1 3.4 %collective-permute-start = (bf16[3,2304]{1,0:T(4,128)(2,1)S(1)}, bf16[3,2304]{1,0:T(4,128)(2,1)S(1)}, u32[]{:S(2)}, u32[]{:S(2)}) collective-permute-start(bf16[3,2304]{1,0:T(4,128)(2,1)S(1)} %slice.91), channel_id=1, source_target_pairs={{0,4},{4,8},{8,12},{12,16},{16,20},{20,24},{24,28},{1,5},{5,9},{9,... | collective-permute-start | bytes 41480 | tf_op jit(solution)/shard_map/ppermute | solution.py:14
  11.5 0.6 reduce-window.6
  12.5 0.7 fusion.34
  13.2 0.5 exponential_reduce_fusion
  14.3 1.5 multiply_convert_fusion.3
  15.8 1.6 slice_convert_fusion
  17.4 1.9 copy.27
  19.4 2.2 fusion.18
  21.6 3.5 %collective-permute-start.3 = (f32[1,32,64,128]{3,2,1,0:T(8,128)S(1)}, f32[1,32,64,128]{3,2,1,0:T(8,128)S(1)}, u32[]{:S(2)}, u32[]{:S(2)}) collective-permute-start(f32[1,32,64,128]{3,2,1,0:T(8,128)S(1)} %fusion.18), channel_id=1, source_target_pairs={{0,4},{4,8},{8,12},{12,16},{16,20},{20,24},{24,28},{1,5},{5,9},{9,... | collective-permute-start | bytes 3145736 | tf_op jit(solution)/shard_map/ppermute | solution.py:14
  25.1 22.1 %collective-permute-done.3 = f32[1,32,64,128]{3,2,1,0:T(8,128)S(1)} collective-permute-done((f32[1,32,64,128]{3,2,1,0:T(8,128)S(1)}, f32[1,32,64,128]{3,2,1,0:T(8,128)S(1)}, u32[]{:S(2)}, u32[]{:S(2)}) %collective-permute-start.3) | collective-permute-done | bytes 1048608 | tf_op jit(solution)/shard_map/ppermute | solution.py:14
  47.1 1.0 copy-done.3
  48.1 1.2 multiply_add_fusion.1
  49.3 6.3 %collective-permute-start.4 = (f32[1,32,64,128]{3,2,1,0:T(8,128)}, f32[1,32,64,128]{3,2,1,0:T(8,128)}, u32[]{:S(2)}, u32[]{:S(2)}) collective-permute-start(f32[1,32,64,128]{3,2,1,0:T(8,128)} %multiply_add_fusion.1), channel_id=1, source_target_pairs={{0,8},{4,12},{8,16},{12,20},{16,24},{20,28},{1,9},{5,13},{9,17},{1... | collective-permute-start | bytes 3145736 | tf_op jit(solution)/shard_map/ppermute | solution.py:14
  55.7 2.5 collective-permute-start.1
  58.2 1.2 collective-permute-done.1
  59.5 16.3 %collective-permute-done.4 = f32[1,32,64,128]{3,2,1,0:T(8,128)} collective-permute-done((f32[1,32,64,128]{3,2,1,0:T(8,128)}, f32[1,32,64,128]{3,2,1,0:T(8,128)}, u32[]{:S(2)}, u32[]{:S(2)}) %collective-permute-start.4) | collective-permute-done | bytes 1048608 | tf_op jit(solution)/shard_map/ppermute | solution.py:14
  75.7 1.7 multiply_add_fusion
  77.5 5.9 %collective-permute-start.5 = (f32[1,32,64,128]{3,2,1,0:T(8,128)S(1)}, f32[1,32,64,128]{3,2,1,0:T(8,128)S(1)}, u32[]{:S(2)}, u32[]{:S(2)}) collective-permute-start(f32[1,32,64,128]{3,2,1,0:T(8,128)S(1)} %multiply_add_fusion), channel_id=1, source_target_pairs={{0,16},{4,20},{8,24},{12,28},{1,17},{5,21},{9,25},{13,29},{2,18},{... | collective-permute-start | bytes 3145736 | tf_op jit(solution)/shard_map/ppermute | solution.py:14
  83.4 3.1 %collective-permute-start.2 = (f32[1,32]{1,0:T(1,128)S(1)}, f32[1,32]{1,0:T(1,128)S(1)}, u32[]{:S(2)}, u32[]{:S(2)}) collective-permute-start(f32[1,32]{1,0:T(1,128)S(1)} %bitcast_multiply_fusion.1), channel_id=1, source_target_pairs={{0,8},{4,12},{8,16},{12,20},{16,24},{20,28},{1,9},{5,13},{9,17},{1... | collective-permute-start | bytes 392 | tf_op jit(solution)/shard_map/ppermute | solution.py:14
  86.5 17.1 %collective-permute-done.2 = f32[1,32]{1,0:T(1,128)S(1)} collective-permute-done((f32[1,32]{1,0:T(1,128)S(1)}, f32[1,32]{1,0:T(1,128)S(1)}, u32[]{:S(2)}, u32[]{:S(2)}) %collective-permute-start.2) | collective-permute-done | bytes 160 | tf_op jit(solution)/shard_map/ppermute | solution.py:14
  103.5 0.2 fusion.27
  103.8 2.1 fusion
  105.9 3.2 %fusion.14 = f32[256,1,32,64]{0,3,2,1:T(8,128)} fusion(f32[32,64,256]{2,1,0:T(8,128)S(1)} %fusion, f32[256,1,32,64]{0,3,2,1:T(8,128)S(1)} %bitcast.79, f32[32]{0:T(128)S(1)} %copy-done.13, f32[256,32]{0,1:T(8,128)S(1)} %bitcast.86, f32[1,32,64,128]{3,2,1,0:T(8,128)S(1)} %copy-done.4, f32[1,32,64,128]{3,2,1,0:T(8,128)} %collective-permute-done.4, ...), kind=kOutput, calls=%fused_computation.26 | convolution fusion | flops 137625600 | bytes 9537024 | tf_op jit(solution)/shard_map/while/body/eval_jaxpr/tgn,gjpn->tgjp/dot_general | solution.py:59
  109.2 2.0 copy.32
  111.2 0.8 multiply_reduce_fusion
  112.0 1.8 multiply_convert_fusion.5
  113.8 23.8 %collective-permute-start.8 = (bf16[256,2048]{1,0:T(8,128)(2,1)}, bf16[256,2048]{1,0:T(8,128)(2,1)S(1)}, u32[]{:S(2)}, u32[]{:S(2)}) collective-permute-start(bf16[256,2048]{1,0:T(8,128)(2,1)} %multiply_convert_fusion.5), channel_id=1, source_target_pairs={{0,24},{8,0},{16,8},{24,16},{1,25},{9,1},{17,9},{25,17},{2,26},{10... | collective-permute-start | bytes 3145736 | tf_op jit(solution)/shard_map/ppermute | solution.py:171
  137.6 1.5 collective-permute-start.7
  139.1 2.0 collective-permute-start.6
  141.1 3.9 %convolution_bitcast_fusion.3 = f32[1,256,1024]{2,1,0:T(8,128)S(1)} fusion(bf16[256,2048]{1,0:T(8,128)(2,1)} %multiply_convert_fusion.5, bf16[2048,1024]{1,0:T(8,128)(2,1)} %all-gather.2.cloned.1.call-done), kind=kOutput, calls=%fused_computation.37 | convolution fusion | flops 1073741824 | bytes 6291456 | tf_op jit(solution)/shard_map/dot_general | solution.py:176
  145.0 16.5 %collective-permute-done.8 = bf16[256,2048]{1,0:T(8,128)(2,1)S(1)} collective-permute-done((bf16[256,2048]{1,0:T(8,128)(2,1)}, bf16[256,2048]{1,0:T(8,128)(2,1)S(1)}, u32[]{:S(2)}, u32[]{:S(2)}) %collective-permute-start.8) | collective-permute-done | bytes 1048608 | tf_op jit(solution)/shard_map/ppermute | solution.py:171
  161.5 1.2 convolution_bitcast_fusion
  162.8 66.4 %collective-permute-done.7 = bf16[256,2048]{1,0:T(8,128)(2,1)S(1)} collective-permute-done((bf16[256,2048]{1,0:T(8,128)(2,1)}, bf16[256,2048]{1,0:T(8,128)(2,1)S(1)}, u32[]{:S(2)}, u32[]{:S(2)}) %collective-permute-start.7) | collective-permute-done | bytes 1048608 | tf_op jit(solution)/shard_map/ppermute | solution.py:171
  229.2 1.2 convolution_bitcast_fusion.1
  230.5 1.2 convolution_bitcast_fusion.2
  231.7 0.6 pad_maximum_fusion
  232.3 0.2 constant_dynamic-slice_fusion.1
  232.6 1.7 copy-done.1
  234.2 0.2 pad_maximum_fusion.1
  234.6 4.2 %collective-permute-done.9 = f32[2,256,1024]{2,1,0:T(8,128)} collective-permute-done((f32[2,256,1024]{2,1,0:T(8,128)S(1)}, f32[2,256,1024]{2,1,0:T(8,128)}, u32[]{:S(2)}, u32[]{:S(2)}) %collective-permute-start.9) | collective-permute-done | bytes 2097184 | tf_op jit(solution)/shard_map/ppermute | solution.py:188
  238.8 1.7 slice_add_fusion
  240.5 0.6 collective-permute-start.10
  241.1 24.6 %collective-permute-done.10 = f32[1,256,1024]{2,1,0:T(8,128)S(1)} collective-permute-done((f32[1,256,1024]{2,1,0:T(8,128)S(1)}, f32[1,256,1024]{2,1,0:T(8,128)S(1)}, u32[]{:S(2)}, u32[]{:S(2)}) %collective-permute-start.10) | collective-permute-done | bytes 1048608 | tf_op jit(solution)/shard_map/ppermute | solution.py:188
  265.8 1.8 fusion.23
  267.5 2.2 collective-permute-start.11
  269.7 23.8 %collective-permute-done.11 = bf16[256,1024]{1,0:T(8,128)(2,1)S(1)} collective-permute-done((bf16[256,1024]{1,0:T(8,128)(2,1)S(1)}, bf16[256,1024]{1,0:T(8,128)(2,1)S(1)}, u32[]{:S(2)}, u32[]{:S(2)}) %collective-permute-start.11) | collective-permute-done | bytes 524320 | tf_op jit(solution)/shard_map/ppermute | solution.py:198
  293.5 0.8 copy.49
  (62 shorter events, 1.2 us)
Async XLA Ops:
  6.5 5.0 %copy-start = (f32[256,32]{0,1:T(8,128)S(1)}, f32[256,32]{0,1:T(8,128)}, u32[]{:S(2)}) copy-start(f32[256,32]{0,1:T(8,128)} %param.20) | copy-start | bytes 98308
  6.5 1.4 copy-start.6
  6.5 1.5 copy-start.7
  6.5 7.4 %copy-start.9 = (f32[4,2048]{1,0:T(4,128)S(1)}, f32[4,2048]{1,0:T(4,128)}, u32[]{:S(2)}) copy-start(f32[4,2048]{1,0:T(4,128)} %param.16) | copy-start | bytes 98308
  6.5 7.4 %copy-start.11 = (f32[4,128]{1,0:T(4,128)S(1)}, f32[4,128]{1,0:T(4,128)}, u32[]{:S(2)}) copy-start(f32[4,128]{1,0:T(4,128)} %param.17) | copy-start | bytes 6148
  6.5 7.4 %copy-start.12 = (f32[4,128]{1,0:T(4,128)S(1)}, f32[4,128]{1,0:T(4,128)}, u32[]{:S(2)}) copy-start(f32[4,128]{1,0:T(4,128)} %param.18) | copy-start | bytes 6148
  6.6 134.5 %all-gather.2.cloned.1.call-start = ((), (), s32[]{:S(2)}) async-start(), calls=%async_computation | async-start | bytes 6291456 | tf_op jit(solution)/shard_map/all_gather | solution.py:174
  8.1 6.1 %collective-permute-start = (bf16[3,2304]{1,0:T(4,128)(2,1)S(1)}, bf16[3,2304]{1,0:T(4,128)(2,1)S(1)}, u32[]{:S(2)}, u32[]{:S(2)}) collective-permute-start(bf16[3,2304]{1,0:T(4,128)(2,1)S(1)} %slice.91), channel_id=1, source_target_pairs={{0,4},{4,8},{8,12},{12,16},{16,20},{20,24},{24,28},{1,5},{5,9},{9,... | collective-permute-start | bytes 41480 | tf_op jit(solution)/shard_map/ppermute | solution.py:14
  21.6 25.6 %collective-permute-start.3 = (f32[1,32,64,128]{3,2,1,0:T(8,128)S(1)}, f32[1,32,64,128]{3,2,1,0:T(8,128)S(1)}, u32[]{:S(2)}, u32[]{:S(2)}) collective-permute-start(f32[1,32,64,128]{3,2,1,0:T(8,128)S(1)} %fusion.18), channel_id=1, source_target_pairs={{0,4},{4,8},{8,12},{12,16},{16,20},{20,24},{24,28},{1,5},{5,9},{9,... | collective-permute-start | bytes 3145736 | tf_op jit(solution)/shard_map/ppermute | solution.py:14
  47.1 1.0 copy-start.3
  49.3 26.5 %collective-permute-start.4 = (f32[1,32,64,128]{3,2,1,0:T(8,128)}, f32[1,32,64,128]{3,2,1,0:T(8,128)}, u32[]{:S(2)}, u32[]{:S(2)}) collective-permute-start(f32[1,32,64,128]{3,2,1,0:T(8,128)} %multiply_add_fusion.1), channel_id=1, source_target_pairs={{0,8},{4,12},{8,16},{12,20},{16,24},{20,28},{1,9},{5,13},{9,17},{1... | collective-permute-start | bytes 3145736 | tf_op jit(solution)/shard_map/ppermute | solution.py:14
  55.6 30.8 %copy-start.5 = (f32[1,256,1,32]{1,2,3,0:T(1,128)S(1)}, f32[1,256,1,32]{1,2,3,0:T(1,128)}, u32[]{:S(2)}) copy-start(f32[1,256,1,32]{1,2,3,0:T(1,128)} %get-tuple-element.39) | copy-start | bytes 98308
  55.6 48.1 %copy-start.8 = (f32[256,32]{0,1:T(8,128)S(1)}, f32[256,32]{0,1:T(8,128)}, u32[]{:S(2)}) copy-start(f32[256,32]{0,1:T(8,128)} %param.19) | copy-start | bytes 98308
  55.7 3.8 %collective-permute-start.1 = (f32[1,32]{1,0:T(1,128)S(1)}, f32[1,32]{1,0:T(1,128)S(1)}, u32[]{:S(2)}, u32[]{:S(2)}) collective-permute-start(f32[1,32]{1,0:T(1,128)S(1)} %bitcast.90), channel_id=1, source_target_pairs={{0,4},{4,8},{8,12},{12,16},{16,20},{20,24},{24,28},{1,5},{5,9},{9,... | collective-permute-start | bytes 392 | tf_op jit(solution)/shard_map/ppermute | solution.py:14
  77.5 28.4 %collective-permute-start.5 = (f32[1,32,64,128]{3,2,1,0:T(8,128)S(1)}, f32[1,32,64,128]{3,2,1,0:T(8,128)S(1)}, u32[]{:S(2)}, u32[]{:S(2)}) collective-permute-start(f32[1,32,64,128]{3,2,1,0:T(8,128)S(1)} %multiply_add_fusion), channel_id=1, source_target_pairs={{0,16},{4,20},{8,24},{12,28},{1,17},{5,21},{9,25},{13,29},{2,18},{... | collective-permute-start | bytes 3145736 | tf_op jit(solution)/shard_map/ppermute | solution.py:14
  83.4 20.2 %collective-permute-start.2 = (f32[1,32]{1,0:T(1,128)S(1)}, f32[1,32]{1,0:T(1,128)S(1)}, u32[]{:S(2)}, u32[]{:S(2)}) collective-permute-start(f32[1,32]{1,0:T(1,128)S(1)} %bitcast_multiply_fusion.1), channel_id=1, source_target_pairs={{0,8},{4,12},{8,16},{12,20},{16,24},{20,28},{1,9},{5,13},{9,17},{1... | collective-permute-start | bytes 392 | tf_op jit(solution)/shard_map/ppermute | solution.py:14
  103.7 2.2 copy-start.4
  103.8 2.2 copy-start.13
  109.2 2.0 copy-start.2
  111.2 0.8 copy-start.10
  113.8 47.7 %collective-permute-start.8 = (bf16[256,2048]{1,0:T(8,128)(2,1)}, bf16[256,2048]{1,0:T(8,128)(2,1)S(1)}, u32[]{:S(2)}, u32[]{:S(2)}) collective-permute-start(bf16[256,2048]{1,0:T(8,128)(2,1)} %multiply_convert_fusion.5), channel_id=1, source_target_pairs={{0,24},{8,0},{16,8},{24,16},{1,25},{9,1},{17,9},{25,17},{2,26},{10... | collective-permute-start | bytes 3145736 | tf_op jit(solution)/shard_map/ppermute | solution.py:171
  137.6 91.6 %collective-permute-start.7 = (bf16[256,2048]{1,0:T(8,128)(2,1)}, bf16[256,2048]{1,0:T(8,128)(2,1)S(1)}, u32[]{:S(2)}, u32[]{:S(2)}) collective-permute-start(bf16[256,2048]{1,0:T(8,128)(2,1)} %multiply_convert_fusion.5), channel_id=1, source_target_pairs={{0,16},{8,24},{16,0},{24,8},{1,17},{9,25},{17,1},{25,9},{2,18},{10... | collective-permute-start | bytes 3145736 | tf_op jit(solution)/shard_map/ppermute | solution.py:171
  139.1 91.4 %collective-permute-start.6 = (bf16[256,2048]{1,0:T(8,128)(2,1)}, bf16[256,2048]{1,0:T(8,128)(2,1)S(1)}, u32[]{:S(2)}, u32[]{:S(2)}) collective-permute-start(bf16[256,2048]{1,0:T(8,128)(2,1)} %multiply_convert_fusion.5), channel_id=1, source_target_pairs={{0,8},{8,16},{16,24},{24,0},{1,9},{9,17},{17,25},{25,1},{2,10},{10... | collective-permute-start | bytes 3145736 | tf_op jit(solution)/shard_map/ppermute | solution.py:171
  141.1 20.5 %copy-start.14 = (bf16[2048,1024]{1,0:T(8,128)(2,1)S(1)}, bf16[2048,1024]{1,0:T(8,128)(2,1)}, u32[]{:S(2)}) copy-start(bf16[2048,1024]{1,0:T(8,128)(2,1)} %all-gather.2.cloned.1.call-done) | copy-start | bytes 12582916
  232.3 1.9 copy-start.1
  234.5 4.4 %collective-permute-start.9 = (f32[2,256,1024]{2,1,0:T(8,128)S(1)}, f32[2,256,1024]{2,1,0:T(8,128)}, u32[]{:S(2)}, u32[]{:S(2)}) collective-permute-start(f32[2,256,1024]{2,1,0:T(8,128)S(1)} %pad_maximum_fusion.1), channel_id=1, source_target_pairs={{0,1},{1,0},{2,3},{3,2},{4,5},{5,4},{6,7},{7,6},{8,9},{9,8},{10,11... | collective-permute-start | bytes 6291464 | tf_op jit(solution)/shard_map/ppermute | solution.py:188
  240.5 25.3 %collective-permute-start.10 = (f32[1,256,1024]{2,1,0:T(8,128)S(1)}, f32[1,256,1024]{2,1,0:T(8,128)S(1)}, u32[]{:S(2)}, u32[]{:S(2)}) collective-permute-start(f32[1,256,1024]{2,1,0:T(8,128)S(1)} %slice_add_fusion), channel_id=1, source_target_pairs={{0,2},{1,3},{2,0},{3,1},{4,6},{5,7},{6,4},{7,5},{8,10},{9,11},{10,... | collective-permute-start | bytes 3145736 | tf_op jit(solution)/shard_map/ppermute | solution.py:188
  267.5 25.9 %collective-permute-start.11 = (bf16[256,1024]{1,0:T(8,128)(2,1)S(1)}, bf16[256,1024]{1,0:T(8,128)(2,1)S(1)}, u32[]{:S(2)}, u32[]{:S(2)}) collective-permute-start(bf16[256,1024]{1,0:T(8,128)(2,1)S(1)} %fusion.23), channel_id=1, source_target_pairs={{0,0},{1,8},{2,16},{3,24},{8,1},{9,9},{10,17},{11,25},{16,2},{17,1... | collective-permute-start | bytes 1572872 | tf_op jit(solution)/shard_map/ppermute | solution.py:198
Sparse Core Ops, SparseCore 0:
  55.7 54.9 all-gather.1

commit v4 on v3

--- a/solution.py
+++ b/solution.py
@@ -167,8 +167,18 @@
         )
     outer_at = lax.axis_index(outer_axis)
     tp_at = lax.axis_index("tp")
+    from_left, from_right = {}, {}
+    going_right = going_left = hidden
+    for step in range(1, tp_count):
+        going_right = lax.ppermute(
+            going_right, outer_axis, [(s, s + 1) for s in range(step - 1, tp_count - 1)]
+        )
+        going_left = lax.ppermute(
+            going_left, outer_axis, [(s, s - 1) for s in range(1, tp_count - step + 1)]
+        )
+        from_left[step], from_right[step] = going_right, going_left
     arrived = [hidden] + [
-        lax.ppermute(hidden, outer_axis, [(s, (s + d) % tp_count) for s in range(tp_count)])
+        jnp.where(outer_at >= d, from_left[d], from_right[tp_count - d])
         for d in range(1, tp_count)
     ]
     cols_all = lax.all_gather(out_weight, inner_axis, axis=1, tiled=True)

time: 302 us -> 286 us (0.947)
  waiting for transfers between devices: 192 us -> 170 us
  starting transfers between devices: 54.9 us -> 59.5 us
    ppermute x3 -> x6, waiting for transfers between devices: 83 us -> 60.8 us  [the longest x3 60.8 us: on_device(): lax.ppermute(going_left, outer_axis, [(s, s - 1) for s in range(1, tp_cou...]
    ppermute x3 -> x6, starting transfers between devices: 27.3 us -> 32.2 us  [the longest x3 28.4 us: on_device(): lax.ppermute(going_right, outer_axis, [(s, s + 1) for s in range(step - 1...]
  transfers between devices with their start and end apart: 13 -> 16, of which waited for: 9 -> 10; matrix products, arithmetic and copies ran while one was open for 7% -> 8% of each run, Pallas kernels for 0% -> 0%
where the time goes in v4:
time: 286 us
  waiting for transfers between devices  170 us (59%)
  starting transfers between devices  59.5 us (21%)
  matrix products  18 us (6%)
  between operations  14.1 us (5%)
  other arithmetic  13.6 us (5%)
  local copies, waits for them, and re-layouts  10.1 us (4%)
    ppermute x3, waiting for transfers between devices, on_device(): lax.ppermute(going_left, outer_axis, [(s, s - 1) for s in range(1, tp_cou...  60.8 us
    ppermute x6, waiting for transfers between devices, shifted(): lax.ppermute(value, axis, [(source, source + steps) for source in range(f...  56.6 us
    ppermute x2, waiting for transfers between devices, on_device(): lax.ppermute(jnp.stack([held[m] for m in going]), 'tp', [(s, s ^ bit) for...  29 us
    ppermute x3, starting transfers between devices, on_device(): lax.ppermute(going_right, outer_axis, [(s, s + 1) for s in range(step - 1...  28.4 us
    ppermute x6, starting transfers between devices, shifted(): lax.ppermute(value, axis, [(source, source + steps) for source in range(f...  24.7 us
    ppermute x1, waiting for transfers between devices, on_device(): return lax.ppermute(held[0].astype(jnp.bfloat16), (outer_axis, 'tp'), swap)  24.1 us
    dot_general x4, matrix products, on_device(): jnp.dot(rows, cols_all, preferred_element_type=jnp.float32)  10.3 us
  transfers between devices with their start and end apart: 16, of which 10 were waited for; matrix products, arithmetic and copies ran while one was open for 8% of the time, Pallas kernels for 0%

profile of v4, /device:TPU:2, one launch (start us, length us, event | category | flops | bytes accessed | tf_op | source)
XLA Modules:
  0.0 285.7 jit_solution(856110234903117647)
XLA Ops:
  6.6 1.4 constant_dynamic-update-slice_fusion.5
  8.1 3.4 %collective-permute-start = (bf16[3,2304]{1,0:T(4,128)(2,1)S(1)}, bf16[3,2304]{1,0:T(4,128)(2,1)S(1)}, u32[]{:S(2)}, u32[]{:S(2)}) collective-permute-start(bf16[3,2304]{1,0:T(4,128)(2,1)S(1)} %slice.91), channel_id=1, source_target_pairs={{0,4},{4,8},{8,12},{12,16},{16,20},{20,24},{24,28},{1,5},{5,9},{9,... | collective-permute-start | bytes 41480 | tf_op jit(solution)/shard_map/ppermute | solution.py:14
  11.5 0.6 reduce-window.6
  12.5 0.7 fusion.40
  13.2 0.5 exponential_reduce_fusion
  14.3 1.5 multiply_convert_fusion.3
  15.8 1.6 slice_convert_fusion
  17.4 1.9 copy.27
  19.4 2.2 fusion.18
  21.6 3.5 %collective-permute-start.3 = (f32[1,32,64,128]{3,2,1,0:T(8,128)S(1)}, f32[1,32,64,128]{3,2,1,0:T(8,128)S(1)}, u32[]{:S(2)}, u32[]{:S(2)}) collective-permute-start(f32[1,32,64,128]{3,2,1,0:T(8,128)S(1)} %fusion.18), channel_id=1, source_target_pairs={{0,4},{4,8},{8,12},{12,16},{16,20},{20,24},{24,28},{1,5},{5,9},{9,... | collective-permute-start | bytes 3145736 | tf_op jit(solution)/shard_map/ppermute | solution.py:14
  25.1 22.1 %collective-permute-done.3 = f32[1,32,64,128]{3,2,1,0:T(8,128)S(1)} collective-permute-done((f32[1,32,64,128]{3,2,1,0:T(8,128)S(1)}, f32[1,32,64,128]{3,2,1,0:T(8,128)S(1)}, u32[]{:S(2)}, u32[]{:S(2)}) %collective-permute-start.3) | collective-permute-done | bytes 1048608 | tf_op jit(solution)/shard_map/ppermute | solution.py:14
  47.1 1.0 copy-done.3
  48.1 1.2 multiply_add_fusion.1
  49.2 6.3 %collective-permute-start.4 = (f32[1,32,64,128]{3,2,1,0:T(8,128)}, f32[1,32,64,128]{3,2,1,0:T(8,128)}, u32[]{:S(2)}, u32[]{:S(2)}) collective-permute-start(f32[1,32,64,128]{3,2,1,0:T(8,128)} %multiply_add_fusion.1), channel_id=1, source_target_pairs={{0,8},{4,12},{8,16},{12,20},{16,24},{20,28},{1,9},{5,13},{9,17},{1... | collective-permute-start | bytes 3145736 | tf_op jit(solution)/shard_map/ppermute | solution.py:14
  55.6 2.5 collective-permute-start.1
  58.2 1.2 collective-permute-done.1
  59.4 16.3 %collective-permute-done.4 = f32[1,32,64,128]{3,2,1,0:T(8,128)} collective-permute-done((f32[1,32,64,128]{3,2,1,0:T(8,128)}, f32[1,32,64,128]{3,2,1,0:T(8,128)}, u32[]{:S(2)}, u32[]{:S(2)}) %collective-permute-start.4) | collective-permute-done | bytes 1048608 | tf_op jit(solution)/shard_map/ppermute | solution.py:14
  75.7 1.7 multiply_add_fusion
  77.4 5.9 %collective-permute-start.5 = (f32[1,32,64,128]{3,2,1,0:T(8,128)S(1)}, f32[1,32,64,128]{3,2,1,0:T(8,128)S(1)}, u32[]{:S(2)}, u32[]{:S(2)}) collective-permute-start(f32[1,32,64,128]{3,2,1,0:T(8,128)S(1)} %multiply_add_fusion), channel_id=1, source_target_pairs={{0,16},{4,20},{8,24},{12,28},{1,17},{5,21},{9,25},{13,29},{2,18},{... | collective-permute-start | bytes 3145736 | tf_op jit(solution)/shard_map/ppermute | solution.py:14
  83.4 3.1 %collective-permute-start.2 = (f32[1,32]{1,0:T(1,128)S(1)}, f32[1,32]{1,0:T(1,128)S(1)}, u32[]{:S(2)}, u32[]{:S(2)}) collective-permute-start(f32[1,32]{1,0:T(1,128)S(1)} %bitcast_multiply_fusion.1), channel_id=1, source_target_pairs={{0,8},{4,12},{8,16},{12,20},{16,24},{20,28},{1,9},{5,13},{9,17},{1... | collective-permute-start | bytes 392 | tf_op jit(solution)/shard_map/ppermute | solution.py:14
  86.5 17.1 %collective-permute-done.2 = f32[1,32]{1,0:T(1,128)S(1)} collective-permute-done((f32[1,32]{1,0:T(1,128)S(1)}, f32[1,32]{1,0:T(1,128)S(1)}, u32[]{:S(2)}, u32[]{:S(2)}) %collective-permute-start.2) | collective-permute-done | bytes 160 | tf_op jit(solution)/shard_map/ppermute | solution.py:14
  103.7 2.1 fusion
  105.9 3.2 %fusion.14 = f32[256,1,32,64]{0,3,2,1:T(8,128)} fusion(f32[32,64,256]{2,1,0:T(8,128)S(1)} %fusion, f32[256,1,32,64]{0,3,2,1:T(8,128)S(1)} %bitcast.76, f32[32]{0:T(128)S(1)} %copy-done.14, f32[256,32]{0,1:T(8,128)S(1)} %bitcast.83, f32[1,32,64,128]{3,2,1,0:T(8,128)S(1)} %copy-done.4, f32[1,32,64,128]{3,2,1,0:T(8,128)} %collective-permute-done.4, ...), kind=kOutput, calls=%fused_computation.26 | convolution fusion | flops 137625600 | bytes 9537024 | tf_op jit(solution)/shard_map/while/body/eval_jaxpr/tgn,gjpn->tgjp/dot_general | solution.py:59
  109.1 2.0 copy.32
  111.1 0.8 multiply_reduce_fusion
  111.9 0.8 multiply_convert_fusion.5
  112.8 1.3 collective-permute-start.7
  114.1 26.0 %collective-permute-start.6 = (bf16[256,2048]{1,0:T(8,128)(2,1)S(1)}, bf16[256,2048]{1,0:T(8,128)(2,1)S(1)}, u32[]{:S(2)}, u32[]{:S(2)}) collective-permute-start(bf16[256,2048]{1,0:T(8,128)(2,1)S(1)} %multiply_convert_fusion.5), channel_id=1, source_target_pairs={{0,8},{8,16},{16,24},{1,9},{9,17},{17,25},{2,10},{10,18},{18,26},{... | collective-permute-start | bytes 3145736 | tf_op jit(solution)/shard_map/ppermute | solution.py:173
  140.1 20.8 %collective-permute-done.7 = bf16[256,2048]{1,0:T(8,128)(2,1)S(1)} collective-permute-done((bf16[256,2048]{1,0:T(8,128)(2,1)S(1)}, bf16[256,2048]{1,0:T(8,128)(2,1)S(1)}, u32[]{:S(2)}, u32[]{:S(2)}) %collective-permute-start.7) | collective-permute-done | bytes 1048608 | tf_op jit(solution)/shard_map/ppermute | solution.py:176
  160.9 1.3 collective-permute-start.8
  162.2 0.7 collective-permute-start.10
  162.9 24.1 %collective-permute-done.8 = bf16[256,2048]{1,0:T(8,128)(2,1)} collective-permute-done((bf16[256,2048]{1,0:T(8,128)(2,1)S(1)}, bf16[256,2048]{1,0:T(8,128)(2,1)}, u32[]{:S(2)}, u32[]{:S(2)}) %collective-permute-start.8) | collective-permute-done | bytes 1048608 | tf_op jit(solution)/shard_map/ppermute | solution.py:176
  187.0 1.3 collective-permute-start.9
  188.4 1.6 collective-permute-start.11
  190.0 3.9 %convolution_bitcast_fusion.3 = f32[1,256,1024]{2,1,0:T(8,128)S(1)} fusion(bf16[256,2048]{1,0:T(8,128)(2,1)} %copy-done.5, bf16[2048,1024]{1,0:T(8,128)(2,1)} %all-gather.2.cloned.1.call-done), kind=kOutput, calls=%fused_computation.37 | convolution fusion | flops 1073741824 | bytes 6291456 | tf_op jit(solution)/shard_map/dot_general | solution.py:186
  193.9 2.5 convolution_bitcast_fusion.1
  196.5 15.9 %collective-permute-done.9 = bf16[256,2048]{1,0:T(8,128)(2,1)} collective-permute-done((bf16[256,2048]{1,0:T(8,128)(2,1)}, bf16[256,2048]{1,0:T(8,128)(2,1)}, u32[]{:S(2)}, u32[]{:S(2)}) %collective-permute-start.9) | collective-permute-done | bytes 1048608 | tf_op jit(solution)/shard_map/ppermute | solution.py:176
  212.3 2.5 convolution_bitcast_fusion.2
  214.9 1.3 convolution_bitcast_fusion
  216.2 0.6 pad_maximum_fusion
  217.1 1.7 copy-done.1
  219.1 4.2 %collective-permute-done.12 = f32[2,256,1024]{2,1,0:T(8,128)} collective-permute-done((f32[2,256,1024]{2,1,0:T(8,128)S(1)}, f32[2,256,1024]{2,1,0:T(8,128)}, u32[]{:S(2)}, u32[]{:S(2)}) %collective-permute-start.12) | collective-permute-done | bytes 2097184 | tf_op jit(solution)/shard_map/ppermute | solution.py:198
  223.4 1.7 slice_add_fusion
  225.6 24.7 %collective-permute-done.13 = f32[1,256,1024]{2,1,0:T(8,128)S(1)} collective-permute-done((f32[1,256,1024]{2,1,0:T(8,128)S(1)}, f32[1,256,1024]{2,1,0:T(8,128)S(1)}, u32[]{:S(2)}, u32[]{:S(2)}) %collective-permute-start.13) | collective-permute-done | bytes 1048608 | tf_op jit(solution)/shard_map/ppermute | solution.py:198
  250.3 1.8 fusion.29
  252.1 1.9 collective-permute-start.14
  254.0 24.1 %collective-permute-done.14 = bf16[256,1024]{1,0:T(8,128)(2,1)S(1)} collective-permute-done((bf16[256,1024]{1,0:T(8,128)(2,1)S(1)}, bf16[256,1024]{1,0:T(8,128)(2,1)S(1)}, u32[]{:S(2)}, u32[]{:S(2)}) %collective-permute-start.14) | collective-permute-done | bytes 524320 | tf_op jit(solution)/shard_map/ppermute | solution.py:208
  278.1 0.8 copy.49
  (70 shorter events, 2.4 us)
Async XLA Ops:
  6.5 5.0 %copy-start = (f32[256,32]{0,1:T(8,128)S(1)}, f32[256,32]{0,1:T(8,128)}, u32[]{:S(2)}) copy-start(f32[256,32]{0,1:T(8,128)} %param.20) | copy-start | bytes 98308
  6.5 1.4 copy-start.7
  6.5 1.5 copy-start.8
  6.5 7.4 %copy-start.10 = (f32[4,2048]{1,0:T(4,128)S(1)}, f32[4,2048]{1,0:T(4,128)}, u32[]{:S(2)}) copy-start(f32[4,2048]{1,0:T(4,128)} %param.16) | copy-start | bytes 98308
  6.5 7.4 %copy-start.12 = (f32[4,128]{1,0:T(4,128)S(1)}, f32[4,128]{1,0:T(4,128)}, u32[]{:S(2)}) copy-start(f32[4,128]{1,0:T(4,128)} %param.17) | copy-start | bytes 6148
  6.5 7.4 %copy-start.13 = (f32[4,128]{1,0:T(4,128)S(1)}, f32[4,128]{1,0:T(4,128)}, u32[]{:S(2)}) copy-start(f32[4,128]{1,0:T(4,128)} %param.18) | copy-start | bytes 6148
  6.6 183.4 %all-gather.2.cloned.1.call-start = ((), (), s32[]{:S(2)}) async-start(), calls=%async_computation | async-start | bytes 6291456 | tf_op jit(solution)/shard_map/all_gather | solution.py:184
  8.1 6.1 %collective-permute-start = (bf16[3,2304]{1,0:T(4,128)(2,1)S(1)}, bf16[3,2304]{1,0:T(4,128)(2,1)S(1)}, u32[]{:S(2)}, u32[]{:S(2)}) collective-permute-start(bf16[3,2304]{1,0:T(4,128)(2,1)S(1)} %slice.91), channel_id=1, source_target_pairs={{0,4},{4,8},{8,12},{12,16},{16,20},{20,24},{24,28},{1,5},{5,9},{9,... | collective-permute-start | bytes 41480 | tf_op jit(solution)/shard_map/ppermute | solution.py:14
  21.6 25.6 %collective-permute-start.3 = (f32[1,32,64,128]{3,2,1,0:T(8,128)S(1)}, f32[1,32,64,128]{3,2,1,0:T(8,128)S(1)}, u32[]{:S(2)}, u32[]{:S(2)}) collective-permute-start(f32[1,32,64,128]{3,2,1,0:T(8,128)S(1)} %fusion.18), channel_id=1, source_target_pairs={{0,4},{4,8},{8,12},{12,16},{16,20},{20,24},{24,28},{1,5},{5,9},{9,... | collective-permute-start | bytes 3145736 | tf_op jit(solution)/shard_map/ppermute | solution.py:14
  47.1 1.0 copy-start.3
  49.2 26.5 %collective-permute-start.4 = (f32[1,32,64,128]{3,2,1,0:T(8,128)}, f32[1,32,64,128]{3,2,1,0:T(8,128)}, u32[]{:S(2)}, u32[]{:S(2)}) collective-permute-start(f32[1,32,64,128]{3,2,1,0:T(8,128)} %multiply_add_fusion.1), channel_id=1, source_target_pairs={{0,8},{4,12},{8,16},{12,20},{16,24},{20,28},{1,9},{5,13},{9,17},{1... | collective-permute-start | bytes 3145736 | tf_op jit(solution)/shard_map/ppermute | solution.py:14
  55.6 3.8 %collective-permute-start.1 = (f32[1,32]{1,0:T(1,128)S(1)}, f32[1,32]{1,0:T(1,128)S(1)}, u32[]{:S(2)}, u32[]{:S(2)}) collective-permute-start(f32[1,32]{1,0:T(1,128)S(1)} %bitcast.87), channel_id=1, source_target_pairs={{0,4},{4,8},{8,12},{12,16},{16,20},{20,24},{24,28},{1,5},{5,9},{9,... | collective-permute-start | bytes 392 | tf_op jit(solution)/shard_map/ppermute | solution.py:14
  58.1 28.3 %copy-start.6 = (f32[1,256,1,32]{1,2,3,0:T(1,128)S(1)}, f32[1,256,1,32]{1,2,3,0:T(1,128)}, u32[]{:S(2)}) copy-start(f32[1,256,1,32]{1,2,3,0:T(1,128)} %get-tuple-element.39) | copy-start | bytes 98308
  58.1 45.6 %copy-start.9 = (f32[256,32]{0,1:T(8,128)S(1)}, f32[256,32]{0,1:T(8,128)}, u32[]{:S(2)}) copy-start(f32[256,32]{0,1:T(8,128)} %param.19) | copy-start | bytes 98308
  77.4 28.4 %collective-permute-start.5 = (f32[1,32,64,128]{3,2,1,0:T(8,128)S(1)}, f32[1,32,64,128]{3,2,1,0:T(8,128)S(1)}, u32[]{:S(2)}, u32[]{:S(2)}) collective-permute-start(f32[1,32,64,128]{3,2,1,0:T(8,128)S(1)} %multiply_add_fusion), channel_id=1, source_target_pairs={{0,16},{4,20},{8,24},{12,28},{1,17},{5,21},{9,25},{13,29},{2,18},{... | collective-permute-start | bytes 3145736 | tf_op jit(solution)/shard_map/ppermute | solution.py:14
  83.4 20.2 %collective-permute-start.2 = (f32[1,32]{1,0:T(1,128)S(1)}, f32[1,32]{1,0:T(1,128)S(1)}, u32[]{:S(2)}, u32[]{:S(2)}) collective-permute-start(f32[1,32]{1,0:T(1,128)S(1)} %bitcast_multiply_fusion.1), channel_id=1, source_target_pairs={{0,8},{4,12},{8,16},{12,20},{16,24},{20,28},{1,9},{5,13},{9,17},{1... | collective-permute-start | bytes 392 | tf_op jit(solution)/shard_map/ppermute | solution.py:14
  103.7 2.1 copy-start.4
  103.7 2.1 copy-start.14
  109.1 2.0 copy-start.2
  111.1 0.8 copy-start.11
  112.7 1.3 copy-start.5
  112.8 48.1 %collective-permute-start.7 = (bf16[256,2048]{1,0:T(8,128)(2,1)S(1)}, bf16[256,2048]{1,0:T(8,128)(2,1)S(1)}, u32[]{:S(2)}, u32[]{:S(2)}) collective-permute-start(bf16[256,2048]{1,0:T(8,128)(2,1)S(1)} %multiply_convert_fusion.5), channel_id=1, source_target_pairs={{8,0},{16,8},{24,16},{9,1},{17,9},{25,17},{10,2},{18,10},{26,18},{... | collective-permute-start | bytes 3145736 | tf_op jit(solution)/shard_map/ppermute | solution.py:176
  114.1 48.1 %collective-permute-start.6 = (bf16[256,2048]{1,0:T(8,128)(2,1)S(1)}, bf16[256,2048]{1,0:T(8,128)(2,1)S(1)}, u32[]{:S(2)}, u32[]{:S(2)}) collective-permute-start(bf16[256,2048]{1,0:T(8,128)(2,1)S(1)} %multiply_convert_fusion.5), channel_id=1, source_target_pairs={{0,8},{8,16},{16,24},{1,9},{9,17},{17,25},{2,10},{10,18},{18,26},{... | collective-permute-start | bytes 3145736 | tf_op jit(solution)/shard_map/ppermute | solution.py:173
  160.9 26.1 %collective-permute-start.8 = (bf16[256,2048]{1,0:T(8,128)(2,1)S(1)}, bf16[256,2048]{1,0:T(8,128)(2,1)}, u32[]{:S(2)}, u32[]{:S(2)}) collective-permute-start(bf16[256,2048]{1,0:T(8,128)(2,1)S(1)} %collective-permute-done.7), channel_id=1, source_target_pairs={{8,0},{16,8},{9,1},{17,9},{10,2},{18,10},{11,3},{19,11},{12,4},{20... | collective-permute-start | bytes 3145736 | tf_op jit(solution)/shard_map/ppermute | solution.py:176
  162.2 26.2 %collective-permute-start.10 = (bf16[256,2048]{1,0:T(8,128)(2,1)S(1)}, bf16[256,2048]{1,0:T(8,128)(2,1)S(1)}, u32[]{:S(2)}, u32[]{:S(2)}) collective-permute-start(bf16[256,2048]{1,0:T(8,128)(2,1)S(1)} %collective-permute-done.6), channel_id=1, source_target_pairs={{8,16},{16,24},{9,17},{17,25},{10,18},{18,26},{11,19},{19,27},{12,... | collective-permute-start | bytes 3145736 | tf_op jit(solution)/shard_map/ppermute | solution.py:173
  187.0 25.3 %collective-permute-start.9 = (bf16[256,2048]{1,0:T(8,128)(2,1)}, bf16[256,2048]{1,0:T(8,128)(2,1)}, u32[]{:S(2)}, u32[]{:S(2)}) collective-permute-start(bf16[256,2048]{1,0:T(8,128)(2,1)} %collective-permute-done.8), channel_id=1, source_target_pairs={{8,0},{9,1},{10,2},{11,3},{12,4},{13,5},{14,6},{15,7}} | collective-permute-start | bytes 3145736 | tf_op jit(solution)/shard_map/ppermute | solution.py:176
  188.4 26.5 %collective-permute-start.11 = (bf16[256,2048]{1,0:T(8,128)(2,1)S(1)}, bf16[256,2048]{1,0:T(8,128)(2,1)}, u32[]{:S(2)}, u32[]{:S(2)}) collective-permute-start(bf16[256,2048]{1,0:T(8,128)(2,1)S(1)} %collective-permute-done.10), channel_id=1, source_target_pairs={{16,24},{17,25},{18,26},{19,27},{20,28},{21,29},{22,30},{23,31}} | collective-permute-start | bytes 3145736 | tf_op jit(solution)/shard_map/ppermute | solution.py:173
  190.0 3.9 %copy-start.15 = (bf16[2048,1024]{1,0:T(8,128)(2,1)S(1)}, bf16[2048,1024]{1,0:T(8,128)(2,1)}, u32[]{:S(2)}) copy-start(bf16[2048,1024]{1,0:T(8,128)(2,1)} %all-gather.2.cloned.1.call-done) | copy-start | bytes 12582916
  216.8 2.0 copy-start.1
  219.0 4.4 %collective-permute-start.12 = (f32[2,256,1024]{2,1,0:T(8,128)S(1)}, f32[2,256,1024]{2,1,0:T(8,128)}, u32[]{:S(2)}, u32[]{:S(2)}) collective-permute-start(f32[2,256,1024]{2,1,0:T(8,128)S(1)} %pad_maximum_fusion.1), channel_id=1, source_target_pairs={{0,1},{1,0},{2,3},{3,2},{4,5},{5,4},{6,7},{7,6},{8,9},{9,8},{10,11... | collective-permute-start | bytes 6291464 | tf_op jit(solution)/shard_map/ppermute | solution.py:198
  225.0 25.3 %collective-permute-start.13 = (f32[1,256,1024]{2,1,0:T(8,128)S(1)}, f32[1,256,1024]{2,1,0:T(8,128)S(1)}, u32[]{:S(2)}, u32[]{:S(2)}) collective-permute-start(f32[1,256,1024]{2,1,0:T(8,128)S(1)} %slice_add_fusion), channel_id=1, source_target_pairs={{0,2},{1,3},{2,0},{3,1},{4,6},{5,7},{6,4},{7,5},{8,10},{9,11},{10,... | collective-permute-start | bytes 3145736 | tf_op jit(solution)/shard_map/ppermute | solution.py:198
  252.1 26.0 %collective-permute-start.14 = (bf16[256,1024]{1,0:T(8,128)(2,1)S(1)}, bf16[256,1024]{1,0:T(8,128)(2,1)S(1)}, u32[]{:S(2)}, u32[]{:S(2)}) collective-permute-start(bf16[256,1024]{1,0:T(8,128)(2,1)S(1)} %fusion.29), channel_id=1, source_target_pairs={{0,0},{1,8},{2,16},{3,24},{8,1},{9,9},{10,17},{11,25},{16,2},{17,1... | collective-permute-start | bytes 1572872 | tf_op jit(solution)/shard_map/ppermute | solution.py:208
Sparse Core Ops, SparseCore 0:
  58.2 55.8 all-gather.1

commit v5 on v4

--- a/solution.py
+++ b/solution.py
@@ -63,24 +63,32 @@
 def combine(first_part, second_part):
     decay_first, state_first = first_part
     decay_second, state_second = second_part
-    return (decay_first * decay_second, decay_second[..., None, None] * state_first + state_second)
+    return (
+        decay_first * decay_second,
+        decay_second[..., None, None] * state_first.astype(jnp.float32) + state_second,
+    )
+
+
+def on_link(part):
+    decay, state = part
+    return (decay, state.astype(jnp.bfloat16))
 
 
 def prefix_states(dev_decay, dev_state, axis, count):
     own = (dev_decay, dev_state)
     if count == 1:
         return jnp.zeros_like(dev_state)
-    got = shifted(own, axis, 1, count)
+    got = shifted(on_link(own), axis, 1, count)
     before = got
     upto = combine(got, own)
     step = 2
     while step < count:
-        got = shifted(upto, axis, step, count)
+        got = shifted(on_link(upto), axis, step, count)
         before = combine(got, before)
         if step * 2 < count:
             upto = combine(got, upto)
         step *= 2
-    return before[1]
+    return before[1].astype(jnp.float32)
 
 
 def on_device(
@@ -195,14 +203,15 @@
     bit = 1
     while bit < tp_count:
         going = sorted(m for m in held if m & bit)
+        sent = jnp.stack([held[m] for m in going])
         got = lax.ppermute(
-            jnp.stack([held[m] for m in going]),
+            sent if bit == 1 else sent.astype(jnp.bfloat16),
             "tp",
             [(s, s ^ bit) for s in range(tp_count)],
         )
         held = {m: held[m] for m in held if not m & bit}
         for index, m in enumerate(going):
-            held[m ^ bit] = held[m ^ bit] + got[index]
+            held[m ^ bit] = held[m ^ bit] + got[index].astype(jnp.float32)
         bit *= 2
     swap = [(o * tp_count + t, t * tp_count + o) for o in range(tp_count) for t in range(tp_count)]
     return lax.ppermute(held[0].astype(jnp.bfloat16), (outer_axis, "tp"), swap)

time: 286 us -> 229 us (0.80)
  waiting for transfers between devices: 170 us -> 125 us
  starting transfers between devices: 59.5 us -> 47.8 us
    ppermute x6, waiting for transfers between devices: 56.6 us -> 22.6 us  [shifted(): lax.ppermute(value, axis, [(source, source + steps) for source in range(f...]
    ppermute x3, starting transfers between devices: 28.4 us -> 16.7 us  [on_device(): lax.ppermute(going_right, outer_axis, [(s, s + 1) for s in range(step - 1...]
    ppermute x2, waiting for transfers between devices: 29 us -> 17.8 us  [on_device(): lax.ppermute(sent if bit == 1 else sent.astype(jnp.bfloat16), 'tp', [(s,...]
    add x3 -> x0, other arithmetic: 4.55 us -> none  [the longest x2 2.87 us: combine(): decay_second[..., None, None] * state_first + state_second]
    convert_element_type x0 -> x4, other arithmetic: none -> 4.09 us  [the longest x3 2.74 us: on_link(): return (decay, state.astype(jnp.bfloat16))]
  transfers between devices with their start and end apart: 16 -> 16, of which waited for: 10 -> 10; matrix products, arithmetic and copies ran while one was open for 8% -> 10% of each run, Pallas kernels for 0% -> 0%
where the time goes in v5:
time: 229 us; the launch traced here: 228 us
  waiting for transfers between devices  125 us (55%)
  starting transfers between devices  47.8 us (21%)
  matrix products  18 us (8%)
  between operations  14 us (6%)
  other arithmetic  13.6 us (6%)
  local copies, waits for them, and re-layouts  9.89 us (4%)
    ppermute x3, waiting for transfers between devices, on_device(): lax.ppermute(going_left, outer_axis, [(s, s - 1) for s in range(1, tp_cou...  60.7 us
    ppermute x6, starting transfers between devices, shifted(): lax.ppermute(value, axis, [(source, source + steps) for source in range(f...  24.7 us
    ppermute x1, waiting for transfers between devices, on_device(): return lax.ppermute(held[0].astype(jnp.bfloat16), (outer_axis, 'tp'), swap)  24.1 us
    ppermute x6, waiting for transfers between devices, shifted(): lax.ppermute(value, axis, [(source, source + steps) for source in range(f...  22.6 us
    ppermute x2, waiting for transfers between devices, on_device(): lax.ppermute(sent if bit == 1 else sent.astype(jnp.bfloat16), 'tp', [(s,...  17.8 us
    ppermute x3, starting transfers between devices, on_device(): lax.ppermute(going_right, outer_axis, [(s, s + 1) for s in range(step - 1...  16.7 us
    dot_general x4, matrix products, on_device(): jnp.dot(rows, cols_all, preferred_element_type=jnp.float32)  10.3 us
    unnamed x40, local copies, waits for them, and re-layouts  4.74 us
  transfers between devices with their start and end apart: 16, of which 10 were waited for; matrix products, arithmetic and copies ran while one was open for 10% of the time, Pallas kernels for 0%

profile of v5, /device:TPU:2, one launch (start us, length us, event | category | flops | bytes accessed | tf_op | source)
XLA Modules:
  0.0 228.5 jit_solution(2922772994784332035)
XLA Ops:
  6.6 1.4 constant_dynamic-update-slice_fusion.5
  8.1 3.4 %collective-permute-start = (bf16[3,2304]{1,0:T(4,128)(2,1)S(1)}, bf16[3,2304]{1,0:T(4,128)(2,1)S(1)}, u32[]{:S(2)}, u32[]{:S(2)}) collective-permute-start(bf16[3,2304]{1,0:T(4,128)(2,1)S(1)} %slice.91), channel_id=1, source_target_pairs={{0,4},{4,8},{8,12},{12,16},{16,20},{20,24},{24,28},{1,5},{5,9},{9,... | collective-permute-start | bytes 41480 | tf_op jit(solution)/shard_map/ppermute | solution.py:14
  11.5 0.6 reduce-window.6
  13.7 1.5 multiply_convert_fusion.3
  15.2 1.7 slice_convert_fusion
  16.9 1.9 copy.27
  18.9 1.4 fusion.17
  20.4 3.6 %collective-permute-start.3 = (bf16[1,32,64,128]{3,2,1,0:T(8,128)(2,1)S(1)}, bf16[1,32,64,128]{3,2,1,0:T(8,128)(2,1)S(1)}, u32[]{:S(2)}, u32[]{:S(2)}) collective-permute-start(bf16[1,32,64,128]{3,2,1,0:T(8,128)(2,1)S(1)} %convert_bitcast_fusion), channel_id=1, source_target_pairs={{0,4},{4,8},{8,12},{12,16},{16,20},{20,24},{24,28},{1,5},{5,9},{9,... | collective-permute-start | bytes 1572872 | tf_op jit(solution)/shard_map/ppermute | solution.py:14
  24.0 10.7 %collective-permute-done.3 = bf16[1,32,64,128]{3,2,1,0:T(8,128)(2,1)S(1)} collective-permute-done((bf16[1,32,64,128]{3,2,1,0:T(8,128)(2,1)S(1)}, bf16[1,32,64,128]{3,2,1,0:T(8,128)(2,1)S(1)}, u32[]{:S(2)}, u32[]{:S(2)}) %collective-permute-start.3) | collective-permute-done | bytes 524320 | tf_op jit(solution)/shard_map/ppermute | solution.py:14
  34.7 0.8 copy-done.3
  35.5 1.0 fusion.32
  36.6 6.3 %collective-permute-start.4 = (bf16[1,32,64,128]{3,2,1,0:T(8,128)(2,1)}, bf16[1,32,64,128]{3,2,1,0:T(8,128)(2,1)}, u32[]{:S(2)}, u32[]{:S(2)}) collective-permute-start(bf16[1,32,64,128]{3,2,1,0:T(8,128)(2,1)} %fusion.32), channel_id=1, source_target_pairs={{0,8},{4,12},{8,16},{12,20},{16,24},{20,28},{1,9},{5,13},{9,17},{1... | collective-permute-start | bytes 1572872 | tf_op jit(solution)/shard_map/ppermute | solution.py:14
  42.9 2.3 %collective-permute-start.1 = (f32[1,32]{1,0:T(1,128)S(1)}, f32[1,32]{1,0:T(1,128)S(1)}, u32[]{:S(2)}, u32[]{:S(2)}) collective-permute-start(f32[1,32]{1,0:T(1,128)S(1)} %bitcast.94), channel_id=1, source_target_pairs={{0,4},{4,8},{8,12},{12,16},{16,20},{20,24},{24,28},{1,5},{5,9},{9,... | collective-permute-start | bytes 392 | tf_op jit(solution)/shard_map/ppermute | solution.py:14
  45.3 1.2 collective-permute-done.1
  46.5 5.0 %collective-permute-done.4 = bf16[1,32,64,128]{3,2,1,0:T(8,128)(2,1)} collective-permute-done((bf16[1,32,64,128]{3,2,1,0:T(8,128)(2,1)}, bf16[1,32,64,128]{3,2,1,0:T(8,128)(2,1)}, u32[]{:S(2)}, u32[]{:S(2)}) %collective-permute-start.4) | collective-permute-done | bytes 524320 | tf_op jit(solution)/shard_map/ppermute | solution.py:14
  51.5 1.6 fusion.22
  53.2 6.0 %collective-permute-start.5 = (bf16[1,32,64,128]{3,2,1,0:T(8,128)(2,1)S(1)}, bf16[1,32,64,128]{3,2,1,0:T(8,128)(2,1)S(1)}, u32[]{:S(2)}, u32[]{:S(2)}) collective-permute-start(bf16[1,32,64,128]{3,2,1,0:T(8,128)(2,1)S(1)} %fusion.22), channel_id=1, source_target_pairs={{0,16},{4,20},{8,24},{12,28},{1,17},{5,21},{9,25},{13,29},{2,18},{... | collective-permute-start | bytes 1572872 | tf_op jit(solution)/shard_map/ppermute | solution.py:14
  59.2 2.9 %collective-permute-start.2 = (f32[1,32]{1,0:T(1,128)S(1)}, f32[1,32]{1,0:T(1,128)S(1)}, u32[]{:S(2)}, u32[]{:S(2)}) collective-permute-start(f32[1,32]{1,0:T(1,128)S(1)} %bitcast_multiply_fusion.1), channel_id=1, source_target_pairs={{0,8},{4,12},{8,16},{12,20},{16,24},{20,28},{1,9},{5,13},{9,17},{1... | collective-permute-start | bytes 392 | tf_op jit(solution)/shard_map/ppermute | solution.py:14
  62.2 5.7 %collective-permute-done.2 = f32[1,32]{1,0:T(1,128)S(1)} collective-permute-done((f32[1,32]{1,0:T(1,128)S(1)}, f32[1,32]{1,0:T(1,128)S(1)}, u32[]{:S(2)}, u32[]{:S(2)}) %collective-permute-start.2) | collective-permute-done | bytes 160 | tf_op jit(solution)/shard_map/ppermute | solution.py:14
  67.9 1.1 fusion.40
  69.0 1.5 fusion.35
  70.5 3.7 %fusion.14 = f32[256,1,32,64]{0,3,2,1:T(8,128)} fusion(f32[32,64,256]{2,1,0:T(8,128)S(1)} %fusion.35, f32[256,1,32,64]{0,3,2,1:T(8,128)S(1)} %bitcast.82, f32[32,256]{1,0:T(8,128)S(1)} %bitcast.90, f32[256,256]{1,0:T(8,128)S(1)} %fusion.40, pred[256,256]{1,0:T(8,128)(4,1)S(1)} %iota_compare_fusion.1, f32[32]{0:T(128)S(1)} %copy-done.15, ...), kind=kOutput, calls=%fused_computation.26 | convolution fusion | flops 279969792 | bytes 8814720 | tf_op jit(solution)/shard_map/while/body/eval_jaxpr/gjts,sgjp->tgjp/dot_general | solution.py:46
  74.3 2.0 copy.32
  76.3 0.8 multiply_reduce_fusion
  77.1 0.8 multiply_convert_fusion.5
  77.9 1.3 collective-permute-start.7
  79.2 14.3 %collective-permute-start.6 = (bf16[256,2048]{1,0:T(8,128)(2,1)S(1)}, bf16[256,2048]{1,0:T(8,128)(2,1)S(1)}, u32[]{:S(2)}, u32[]{:S(2)}) collective-permute-start(bf16[256,2048]{1,0:T(8,128)(2,1)S(1)} %multiply_convert_fusion.5), channel_id=1, source_target_pairs={{0,8},{8,16},{16,24},{1,9},{9,17},{17,25},{2,10},{10,18},{18,26},{... | collective-permute-start | bytes 3145736 | tf_op jit(solution)/shard_map/ppermute | solution.py:181
  93.5 20.4 %collective-permute-done.7 = bf16[256,2048]{1,0:T(8,128)(2,1)S(1)} collective-permute-done((bf16[256,2048]{1,0:T(8,128)(2,1)S(1)}, bf16[256,2048]{1,0:T(8,128)(2,1)S(1)}, u32[]{:S(2)}, u32[]{:S(2)}) %collective-permute-start.7) | collective-permute-done | bytes 1048608 | tf_op jit(solution)/shard_map/ppermute | solution.py:184
  113.9 1.3 collective-permute-start.8
  115.2 0.7 collective-permute-start.10
  116.0 24.5 %collective-permute-done.8 = bf16[256,2048]{1,0:T(8,128)(2,1)} collective-permute-done((bf16[256,2048]{1,0:T(8,128)(2,1)S(1)}, bf16[256,2048]{1,0:T(8,128)(2,1)}, u32[]{:S(2)}, u32[]{:S(2)}) %collective-permute-start.8) | collective-permute-done | bytes 1048608 | tf_op jit(solution)/shard_map/ppermute | solution.py:184
  140.4 1.3 collective-permute-start.9
  141.8 1.6 collective-permute-start.11
  143.4 3.9 %convolution_bitcast_fusion.3 = f32[1,256,1024]{2,1,0:T(8,128)S(1)} fusion(bf16[256,2048]{1,0:T(8,128)(2,1)} %copy-done.6, bf16[2048,1024]{1,0:T(8,128)(2,1)} %all-gather.2.cloned.1.call-done), kind=kOutput, calls=%fused_computation.36 | convolution fusion | flops 1073741824 | bytes 6291456 | tf_op jit(solution)/shard_map/dot_general | solution.py:194
  147.3 2.5 %convolution_bitcast_fusion.1 = f32[1,256,1024]{2,1,0:T(8,128)S(1)} fusion(bf16[2048,1024]{1,0:T(8,128)(2,1)S(1)} %copy-done.14, bf16[256,2048]{1,0:T(8,128)(2,1)S(1)} %collective-permute-done.10, bf16[256,2048]{1,0:T(8,128)(2,1)} %collective-permute-done.8, pred[]{:T(512)S(6)} %ge.33), kind=kOutput, calls=%fused_computation.34 | convolution fusion | flops 1074266112 | bytes 7340033 | tf_op jit(solution)/shard_map/dot_general | solution.py:194
  149.9 15.8 %collective-permute-done.9 = bf16[256,2048]{1,0:T(8,128)(2,1)} collective-permute-done((bf16[256,2048]{1,0:T(8,128)(2,1)}, bf16[256,2048]{1,0:T(8,128)(2,1)}, u32[]{:S(2)}, u32[]{:S(2)}) %collective-permute-start.9) | collective-permute-done | bytes 1048608 | tf_op jit(solution)/shard_map/ppermute | solution.py:184
  165.7 2.5 %convolution_bitcast_fusion.2 = f32[1,256,1024]{2,1,0:T(8,128)S(1)} fusion(bf16[2048,1024]{1,0:T(8,128)(2,1)S(1)} %copy-done.14, bf16[256,2048]{1,0:T(8,128)(2,1)S(1)} %collective-permute-done.6, bf16[256,2048]{1,0:T(8,128)(2,1)} %collective-permute-done.9, pred[]{:T(512)S(6)} %ge.32), kind=kOutput, calls=%fused_computation.35 | convolution fusion | flops 1074266112 | bytes 7340033 | tf_op jit(solution)/shard_map/dot_general | solution.py:194
  168.3 1.3 convolution_bitcast_fusion
  170.4 1.7 copy-done.1
  172.1 1.5 pad_maximum_fusion.1
  173.6 4.4 %collective-permute-done.12 = f32[2,256,1024]{2,1,0:T(8,128)S(1)} collective-permute-done((f32[2,256,1024]{2,1,0:T(8,128)}, f32[2,256,1024]{2,1,0:T(8,128)S(1)}, u32[]{:S(2)}, u32[]{:S(2)}) %collective-permute-start.12) | collective-permute-done | bytes 2097184 | tf_op jit(solution)/shard_map/ppermute | solution.py:207
  178.0 1.4 fusion.23
  179.3 0.6 collective-permute-start.13
  179.9 13.4 %collective-permute-done.13 = bf16[1,256,1024]{2,1,0:T(8,128)(2,1)S(1)} collective-permute-done((bf16[1,256,1024]{2,1,0:T(8,128)(2,1)S(1)}, bf16[1,256,1024]{2,1,0:T(8,128)(2,1)S(1)}, u32[]{:S(2)}, u32[]{:S(2)}) %collective-permute-start.13) | collective-permute-done | bytes 524320 | tf_op jit(solution)/shard_map/ppermute | solution.py:207
  193.3 1.5 fusion.33
  194.8 1.9 collective-permute-start.14
  196.7 24.1 %collective-permute-done.14 = bf16[256,1024]{1,0:T(8,128)(2,1)S(1)} collective-permute-done((bf16[256,1024]{1,0:T(8,128)(2,1)S(1)}, bf16[256,1024]{1,0:T(8,128)(2,1)S(1)}, u32[]{:S(2)}, u32[]{:S(2)}) %collective-permute-start.14) | collective-permute-done | bytes 524320 | tf_op jit(solution)/shard_map/ppermute | solution.py:217
  220.8 0.8 copy.49
  (71 shorter events, 2.7 us)
Async XLA Ops:
  6.5 5.0 %copy-start = (f32[256,32]{0,1:T(8,128)S(1)}, f32[256,32]{0,1:T(8,128)}, u32[]{:S(2)}) copy-start(f32[256,32]{0,1:T(8,128)} %param.20) | copy-start | bytes 98308
  6.5 1.4 copy-start.7
  6.5 1.5 copy-start.8
  6.5 6.7 %copy-start.10 = (f32[4,2048]{1,0:T(4,128)S(1)}, f32[4,2048]{1,0:T(4,128)}, u32[]{:S(2)}) copy-start(f32[4,2048]{1,0:T(4,128)} %param.16) | copy-start | bytes 98308
  6.5 6.8 %copy-start.12 = (f32[4,128]{1,0:T(4,128)S(1)}, f32[4,128]{1,0:T(4,128)}, u32[]{:S(2)}) copy-start(f32[4,128]{1,0:T(4,128)} %param.17) | copy-start | bytes 6148
  6.5 6.8 %copy-start.13 = (f32[4,128]{1,0:T(4,128)S(1)}, f32[4,128]{1,0:T(4,128)}, u32[]{:S(2)}) copy-start(f32[4,128]{1,0:T(4,128)} %param.18) | copy-start | bytes 6148
  6.6 136.8 %all-gather.2.cloned.1.call-start = ((), (), s32[]{:S(2)}) async-start(), calls=%async_computation | async-start | bytes 6291456 | tf_op jit(solution)/shard_map/all_gather | solution.py:192
  8.1 5.5 %collective-permute-start = (bf16[3,2304]{1,0:T(4,128)(2,1)S(1)}, bf16[3,2304]{1,0:T(4,128)(2,1)S(1)}, u32[]{:S(2)}, u32[]{:S(2)}) collective-permute-start(bf16[3,2304]{1,0:T(4,128)(2,1)S(1)} %slice.91), channel_id=1, source_target_pairs={{0,4},{4,8},{8,12},{12,16},{16,20},{20,24},{24,28},{1,5},{5,9},{9,... | collective-permute-start | bytes 41480 | tf_op jit(solution)/shard_map/ppermute | solution.py:14
  15.2 1.7 copy-start.2
  16.9 1.9 copy-start.9
  20.4 14.3 %collective-permute-start.3 = (bf16[1,32,64,128]{3,2,1,0:T(8,128)(2,1)S(1)}, bf16[1,32,64,128]{3,2,1,0:T(8,128)(2,1)S(1)}, u32[]{:S(2)}, u32[]{:S(2)}) collective-permute-start(bf16[1,32,64,128]{3,2,1,0:T(8,128)(2,1)S(1)} %convert_bitcast_fusion), channel_id=1, source_target_pairs={{0,4},{4,8},{8,12},{12,16},{16,20},{20,24},{24,28},{1,5},{5,9},{9,... | collective-permute-start | bytes 1572872 | tf_op jit(solution)/shard_map/ppermute | solution.py:14
  34.7 0.8 copy-start.3
  36.6 15.0 %collective-permute-start.4 = (bf16[1,32,64,128]{3,2,1,0:T(8,128)(2,1)}, bf16[1,32,64,128]{3,2,1,0:T(8,128)(2,1)}, u32[]{:S(2)}, u32[]{:S(2)}) collective-permute-start(bf16[1,32,64,128]{3,2,1,0:T(8,128)(2,1)} %fusion.32), channel_id=1, source_target_pairs={{0,8},{4,12},{8,16},{12,20},{16,24},{20,28},{1,9},{5,13},{9,17},{1... | collective-permute-start | bytes 1572872 | tf_op jit(solution)/shard_map/ppermute | solution.py:14
  42.9 3.6 %collective-permute-start.1 = (f32[1,32]{1,0:T(1,128)S(1)}, f32[1,32]{1,0:T(1,128)S(1)}, u32[]{:S(2)}, u32[]{:S(2)}) collective-permute-start(f32[1,32]{1,0:T(1,128)S(1)} %bitcast.94), channel_id=1, source_target_pairs={{0,4},{4,8},{8,12},{12,16},{16,20},{20,24},{24,28},{1,5},{5,9},{9,... | collective-permute-start | bytes 392 | tf_op jit(solution)/shard_map/ppermute | solution.py:14
  45.3 23.7 %copy-start.4 = (bf16[1,32,64,128]{3,2,1,0:T(8,128)(2,1)S(1)}, bf16[1,32,64,128]{3,2,1,0:T(8,128)(2,1)}, u32[]{:S(2)}) copy-start(bf16[1,32,64,128]{3,2,1,0:T(8,128)(2,1)} %copy-done.3) | copy-start | bytes 1572868
  53.2 15.8 %collective-permute-start.5 = (bf16[1,32,64,128]{3,2,1,0:T(8,128)(2,1)S(1)}, bf16[1,32,64,128]{3,2,1,0:T(8,128)(2,1)S(1)}, u32[]{:S(2)}, u32[]{:S(2)}) collective-permute-start(bf16[1,32,64,128]{3,2,1,0:T(8,128)(2,1)S(1)} %fusion.22), channel_id=1, source_target_pairs={{0,16},{4,20},{8,24},{12,28},{1,17},{5,21},{9,25},{13,29},{2,18},{... | collective-permute-start | bytes 1572872 | tf_op jit(solution)/shard_map/ppermute | solution.py:14
  59.2 8.7 %collective-permute-start.2 = (f32[1,32]{1,0:T(1,128)S(1)}, f32[1,32]{1,0:T(1,128)S(1)}, u32[]{:S(2)}, u32[]{:S(2)}) collective-permute-start(f32[1,32]{1,0:T(1,128)S(1)} %bitcast_multiply_fusion.1), channel_id=1, source_target_pairs={{0,8},{4,12},{8,16},{12,20},{16,24},{20,28},{1,9},{5,13},{9,17},{1... | collective-permute-start | bytes 392 | tf_op jit(solution)/shard_map/ppermute | solution.py:14
  62.2 8.4 %copy-start.15 = (f32[32]{0:T(128)S(1)}, f32[32]{0:T(128)}, u32[]{:S(2)}) copy-start(f32[32]{0:T(128)} %param.21) | copy-start | bytes 388
  74.3 2.0 copy-start.5
  76.3 0.8 copy-start.11
  77.9 1.3 copy-start.6
  77.9 36.0 %collective-permute-start.7 = (bf16[256,2048]{1,0:T(8,128)(2,1)S(1)}, bf16[256,2048]{1,0:T(8,128)(2,1)S(1)}, u32[]{:S(2)}, u32[]{:S(2)}) collective-permute-start(bf16[256,2048]{1,0:T(8,128)(2,1)S(1)} %multiply_convert_fusion.5), channel_id=1, source_target_pairs={{8,0},{16,8},{24,16},{9,1},{17,9},{25,17},{10,2},{18,10},{26,18},{... | collective-permute-start | bytes 3145736 | tf_op jit(solution)/shard_map/ppermute | solution.py:184
  79.2 36.0 %collective-permute-start.6 = (bf16[256,2048]{1,0:T(8,128)(2,1)S(1)}, bf16[256,2048]{1,0:T(8,128)(2,1)S(1)}, u32[]{:S(2)}, u32[]{:S(2)}) collective-permute-start(bf16[256,2048]{1,0:T(8,128)(2,1)S(1)} %multiply_convert_fusion.5), channel_id=1, source_target_pairs={{0,8},{8,16},{16,24},{1,9},{9,17},{17,25},{2,10},{10,18},{18,26},{... | collective-permute-start | bytes 3145736 | tf_op jit(solution)/shard_map/ppermute | solution.py:181
  113.9 26.5 %collective-permute-start.8 = (bf16[256,2048]{1,0:T(8,128)(2,1)S(1)}, bf16[256,2048]{1,0:T(8,128)(2,1)}, u32[]{:S(2)}, u32[]{:S(2)}) collective-permute-start(bf16[256,2048]{1,0:T(8,128)(2,1)S(1)} %collective-permute-done.7), channel_id=1, source_target_pairs={{8,0},{16,8},{9,1},{17,9},{10,2},{18,10},{11,3},{19,11},{12,4},{20... | collective-permute-start | bytes 3145736 | tf_op jit(solution)/shard_map/ppermute | solution.py:184
  115.2 26.5 %collective-permute-start.10 = (bf16[256,2048]{1,0:T(8,128)(2,1)S(1)}, bf16[256,2048]{1,0:T(8,128)(2,1)S(1)}, u32[]{:S(2)}, u32[]{:S(2)}) collective-permute-start(bf16[256,2048]{1,0:T(8,128)(2,1)S(1)} %collective-permute-done.6), channel_id=1, source_target_pairs={{8,16},{16,24},{9,17},{17,25},{10,18},{18,26},{11,19},{19,27},{12,... | collective-permute-start | bytes 3145736 | tf_op jit(solution)/shard_map/ppermute | solution.py:181
  140.4 25.3 %collective-permute-start.9 = (bf16[256,2048]{1,0:T(8,128)(2,1)}, bf16[256,2048]{1,0:T(8,128)(2,1)}, u32[]{:S(2)}, u32[]{:S(2)}) collective-permute-start(bf16[256,2048]{1,0:T(8,128)(2,1)} %collective-permute-done.8), channel_id=1, source_target_pairs={{8,0},{9,1},{10,2},{11,3},{12,4},{13,5},{14,6},{15,7}} | collective-permute-start | bytes 3145736 | tf_op jit(solution)/shard_map/ppermute | solution.py:184
  141.8 26.5 %collective-permute-start.11 = (bf16[256,2048]{1,0:T(8,128)(2,1)S(1)}, bf16[256,2048]{1,0:T(8,128)(2,1)}, u32[]{:S(2)}, u32[]{:S(2)}) collective-permute-start(bf16[256,2048]{1,0:T(8,128)(2,1)S(1)} %collective-permute-done.10), channel_id=1, source_target_pairs={{16,24},{17,25},{18,26},{19,27},{20,28},{21,29},{22,30},{23,31}} | collective-permute-start | bytes 3145736 | tf_op jit(solution)/shard_map/ppermute | solution.py:181
  143.4 3.9 %copy-start.14 = (bf16[2048,1024]{1,0:T(8,128)(2,1)S(1)}, bf16[2048,1024]{1,0:T(8,128)(2,1)}, u32[]{:S(2)}) copy-start(bf16[2048,1024]{1,0:T(8,128)(2,1)} %all-gather.2.cloned.1.call-done) | copy-start | bytes 12582916
  170.2 2.0 copy-start.1
  173.6 4.4 %collective-permute-start.12 = (f32[2,256,1024]{2,1,0:T(8,128)}, f32[2,256,1024]{2,1,0:T(8,128)S(1)}, u32[]{:S(2)}, u32[]{:S(2)}) collective-permute-start(f32[2,256,1024]{2,1,0:T(8,128)} %pad_maximum_fusion.1), channel_id=1, source_target_pairs={{0,1},{1,0},{2,3},{3,2},{4,5},{5,4},{6,7},{7,6},{8,9},{9,8},{10,11... | collective-permute-start | bytes 6291464 | tf_op jit(solution)/shard_map/ppermute | solution.py:207
  179.3 14.0 %collective-permute-start.13 = (bf16[1,256,1024]{2,1,0:T(8,128)(2,1)S(1)}, bf16[1,256,1024]{2,1,0:T(8,128)(2,1)S(1)}, u32[]{:S(2)}, u32[]{:S(2)}) collective-permute-start(bf16[1,256,1024]{2,1,0:T(8,128)(2,1)S(1)} %fusion.23), channel_id=1, source_target_pairs={{0,2},{1,3},{2,0},{3,1},{4,6},{5,7},{6,4},{7,5},{8,10},{9,11},{10,... | collective-permute-start | bytes 1572872 | tf_op jit(solution)/shard_map/ppermute | solution.py:207
  194.8 26.0 %collective-permute-start.14 = (bf16[256,1024]{1,0:T(8,128)(2,1)S(1)}, bf16[256,1024]{1,0:T(8,128)(2,1)S(1)}, u32[]{:S(2)}, u32[]{:S(2)}) collective-permute-start(bf16[256,1024]{1,0:T(8,128)(2,1)S(1)} %fusion.33), channel_id=1, source_target_pairs={{0,0},{1,8},{2,16},{3,24},{8,1},{9,9},{10,17},{11,25},{16,2},{17,1... | collective-permute-start | bytes 1572872 | tf_op jit(solution)/shard_map/ppermute | solution.py:217
Sparse Core Ops, SparseCore 0:
  45.4 56.1 all-gather.1

commit v6 on v5

--- a/solution.py
+++ b/solution.py
@@ -175,20 +175,12 @@
         )
     outer_at = lax.axis_index(outer_axis)
     tp_at = lax.axis_index("tp")
-    from_left, from_right = {}, {}
-    going_right = going_left = hidden
-    for step in range(1, tp_count):
-        going_right = lax.ppermute(
-            going_right, outer_axis, [(s, s + 1) for s in range(step - 1, tp_count - 1)]
-        )
-        going_left = lax.ppermute(
-            going_left, outer_axis, [(s, s - 1) for s in range(1, tp_count - step + 1)]
-        )
-        from_left[step], from_right[step] = going_right, going_left
-    arrived = [hidden] + [
-        jnp.where(outer_at >= d, from_left[d], from_right[tp_count - d])
-        for d in range(1, tp_count)
-    ]
+    half = tok_rows // 2
+    across_y = lax.ppermute(hidden, outer_axis, [(s, s ^ 1) for s in range(tp_count)])
+    across_z = lax.ppermute(hidden, outer_axis, [(s, s ^ 2) for s in range(tp_count)])
+    first_half = lax.ppermute(across_y[:half], outer_axis, [(s, s ^ 2) for s in range(tp_count)])
+    second_half = lax.ppermute(across_z[half:], outer_axis, [(s, s ^ 1) for s in range(tp_count)])
+    arrived = [hidden, across_y, across_z, jnp.concatenate([first_half, second_half], axis=0)]
     cols_all = lax.all_gather(out_weight, inner_axis, axis=1, tiled=True)
     by_source = jnp.stack(
         [jnp.dot(rows, cols_all, preferred_element_type=jnp.float32) for rows in arrived]
@@ -196,7 +188,7 @@
 
     def for_target(target):
         return lax.dynamic_index_in_dim(
-            by_source, (outer_at - target + tp_count) % tp_count, 0, keepdims=False
+            by_source, outer_at ^ target, 0, keepdims=False
         )
 
     held = {m: for_target(tp_at ^ m) for m in range(tp_count)}
@@ -213,18 +205,33 @@
         for index, m in enumerate(going):
             held[m ^ bit] = held[m ^ bit] + got[index].astype(jnp.float32)
         bit *= 2
-    swap = [(o * tp_count + t, t * tp_count + o) for o in range(tp_count) for t in range(tp_count)]
-    return lax.ppermute(held[0].astype(jnp.bfloat16), (outer_axis, "tp"), swap)
+    inner_count = ctx_count // tp_count
+    width = out_weight.shape[1]
+    final = held[0].astype(jnp.bfloat16)
+    placed = [[] for _ in range(inner_count)]
+    for piece in range(inner_count):
+        for source in range(tp_count):
+            column = piece * tp_count + source
+            pairs = [
+                (source * tp_count + t, t * tp_count + column // inner_count)
+                for t in range(tp_count)
+            ]
+            placed[column % inner_count].append(
+                lax.ppermute(
+                    final[:, piece * width : (piece + 1) * width], (outer_axis, "tp"), pairs
+                )
+            )
+    return jnp.concatenate([sum(parts[1:], parts[0]) for parts in placed], axis=1)
 
 
 def solution(mesh):
     ctx_count = mesh.shape["ctx"]
     tp_count = mesh.shape["tp"]
-    if ctx_count % tp_count == 0 and tp_count & (tp_count - 1) == 0:
+    if ctx_count % tp_count == 0 and tp_count == 4:
         inner = ctx_count // tp_count
-        grid = mesh.devices.reshape(tp_count, inner, tp_count)
-        mesh = jax.sharding.Mesh(grid, ("outer", "inner", "tp"))
-        ctx_axes = ("outer", "inner")
+        grid = mesh.devices.reshape(inner, tp_count, tp_count)
+        mesh = jax.sharding.Mesh(grid, ("inner", "outer", "tp"))
+        ctx_axes = ("inner", "outer")
         layout = (ctx_axes, ctx_count, "outer", "inner", tp_count)
     else:
         ctx_axes = "ctx"

time: 229 us -> 267 us (1.17)
  the two profiles are of different devices: /device:TPU:2 before, /device:TPU:22 now
where the time goes in v6:
time: 267 us
  waiting for transfers between devices  170 us (64%)
  starting transfers between devices  40.2 us (15%)
  matrix products  17.6 us (7%)
  other arithmetic  15.6 us (6%)
  between operations  14 us (5%)
  local copies, waits for them, and re-layouts  9.21 us (3%)
    ppermute x6, waiting for transfers between devices, shifted(): lax.ppermute(value, axis, [(source, source + steps) for source in range(f...  95.8 us
    ppermute x1, waiting for transfers between devices, on_device(): lax.ppermute(hidden, outer_axis, [(s, s ^ 1) for s in range(tp_count)])  23 us
    ppermute x8, starting transfers between devices, on_device(): lax.ppermute(final[:, piece * width:(piece + 1) * width], (outer_axis, 't...  19.4 us
    ppermute x1, waiting for transfers between devices, on_device(): lax.ppermute(hidden, outer_axis, [(s, s ^ 2) for s in range(tp_count)])  19.2 us
    ppermute x2, waiting for transfers between devices, on_device(): lax.ppermute(sent if bit == 1 else sent.astype(jnp.bfloat16), 'tp', [(s,...  17.8 us
    ppermute x6, starting transfers between devices, shifted(): lax.ppermute(value, axis, [(source, source + steps) for source in range(f...  17.2 us
    dot_general x4, matrix products, on_device(): jnp.dot(rows, cols_all, preferred_element_type=jnp.float32)  9.86 us
    ppermute x8, waiting for transfers between devices, on_device(): lax.ppermute(final[:, piece * width:(piece + 1) * width], (outer_axis, 't...  8.69 us
  transfers between devices with their start and end apart: 21, of which 12 were waited for; matrix products, arithmetic and copies ran while one was open for 8% of the time, Pallas kernels for 0%

profile of v6, /device:TPU:22, one launch (start us, length us, event | category | flops | bytes accessed | tf_op | source)
XLA Modules:
  0.0 266.7 jit_solution(8215098430910462018)
XLA Ops:
  6.6 1.4 constant_dynamic-update-slice_fusion.5
  8.1 3.4 %collective-permute-start = (bf16[3,2304]{1,0:T(4,128)(2,1)S(1)}, bf16[3,2304]{1,0:T(4,128)(2,1)S(1)}, u32[]{:S(2)}, u32[]{:S(2)}) collective-permute-start(bf16[3,2304]{1,0:T(4,128)(2,1)S(1)} %slice.113), channel_id=1, source_target_pairs={{0,4},{4,8},{8,12},{12,16},{16,20},{20,24},{24,28},{1,5},{5,9},{9,... | collective-permute-start | bytes 41480 | tf_op jit(solution)/shard_map/ppermute | solution.py:14
  13.9 1.5 multiply_convert_fusion.3
  15.4 1.7 slice_convert_fusion
  17.1 1.9 copy.27
  19.1 1.4 fusion.17
  20.6 4.3 %collective-permute-start.3 = (bf16[1,32,64,128]{3,2,1,0:T(8,128)(2,1)S(1)}, bf16[1,32,64,128]{3,2,1,0:T(8,128)(2,1)S(1)}, u32[]{:S(2)}, u32[]{:S(2)}) collective-permute-start(bf16[1,32,64,128]{3,2,1,0:T(8,128)(2,1)S(1)} %convert_bitcast_fusion), channel_id=1, source_target_pairs={{0,4},{4,8},{8,12},{12,16},{16,20},{20,24},{24,28},{1,5},{5,9},{9,... | collective-permute-start | bytes 1572872 | tf_op jit(solution)/shard_map/ppermute | solution.py:14
  24.9 10.8 %collective-permute-done.3 = bf16[1,32,64,128]{3,2,1,0:T(8,128)(2,1)S(1)} collective-permute-done((bf16[1,32,64,128]{3,2,1,0:T(8,128)(2,1)S(1)}, bf16[1,32,64,128]{3,2,1,0:T(8,128)(2,1)S(1)}, u32[]{:S(2)}, u32[]{:S(2)}) %collective-permute-start.3) | collective-permute-done | bytes 524320 | tf_op jit(solution)/shard_map/ppermute | solution.py:14
  35.7 0.8 copy-done.3
  36.5 1.0 fusion.29
  37.5 2.8 %collective-permute-start.4 = (bf16[1,32,64,128]{3,2,1,0:T(8,128)(2,1)}, bf16[1,32,64,128]{3,2,1,0:T(8,128)(2,1)}, u32[]{:S(2)}, u32[]{:S(2)}) collective-permute-start(bf16[1,32,64,128]{3,2,1,0:T(8,128)(2,1)} %fusion.29), channel_id=1, source_target_pairs={{0,8},{4,12},{8,16},{12,20},{16,24},{20,28},{1,9},{5,13},{9,17},{1... | collective-permute-start | bytes 1572872 | tf_op jit(solution)/shard_map/ppermute | solution.py:14
  40.3 3.0 %collective-permute-start.1 = (f32[1,32]{1,0:T(1,128)S(1)}, f32[1,32]{1,0:T(1,128)S(1)}, u32[]{:S(2)}, u32[]{:S(2)}) collective-permute-start(f32[1,32]{1,0:T(1,128)S(1)} %bitcast.96), channel_id=1, source_target_pairs={{0,4},{4,8},{8,12},{12,16},{16,20},{20,24},{24,28},{1,5},{5,9},{9,... | collective-permute-start | bytes 392 | tf_op jit(solution)/shard_map/ppermute | solution.py:14
  43.4 6.5 %collective-permute-done.1 = f32[1,32]{1,0:T(1,128)S(1)} collective-permute-done((f32[1,32]{1,0:T(1,128)S(1)}, f32[1,32]{1,0:T(1,128)S(1)}, u32[]{:S(2)}, u32[]{:S(2)}) %collective-permute-start.1) | collective-permute-done | bytes 160 | tf_op jit(solution)/shard_map/ppermute | solution.py:14
  49.9 2.2 collective-permute-done.4
  52.1 1.7 fusion.22
  53.7 1.3 collective-permute-start.5
  55.1 2.4 collective-permute-start.2
  57.5 76.2 %collective-permute-done.2 = f32[1,32]{1,0:T(1,128)S(1)} collective-permute-done((f32[1,32]{1,0:T(1,128)S(1)}, f32[1,32]{1,0:T(1,128)S(1)}, u32[]{:S(2)}, u32[]{:S(2)}) %collective-permute-start.2) | collective-permute-done | bytes 160 | tf_op jit(solution)/shard_map/ppermute | solution.py:14
  133.7 1.1 fusion.37
  134.7 1.5 fusion.32
  136.3 3.7 %fusion.14 = f32[256,1,32,64]{0,3,2,1:T(8,128)} fusion(f32[32,64,256]{2,1,0:T(8,128)S(1)} %fusion.32, f32[256,1,32,64]{0,3,2,1:T(8,128)S(1)} %bitcast.84, f32[32,256]{1,0:T(8,128)S(1)} %bitcast.92, f32[256,256]{1,0:T(8,128)S(1)} %fusion.37, pred[256,256]{1,0:T(8,128)(4,1)S(1)} %iota_compare_fusion.1, f32[32]{0:T(128)S(1)} %copy-done.14, ...), kind=kOutput, calls=%fused_computation.26 | convolution fusion | flops 279969792 | bytes 8814720 | tf_op jit(solution)/shard_map/while/body/eval_jaxpr/gjts,sgjp->tgjp/dot_general | solution.py:46
  140.0 2.0 copy.32
  142.1 0.8 multiply_reduce_fusion
  142.9 1.8 multiply_convert_fusion.5
  144.7 0.8 collective-permute-start.6
  145.8 23.0 %collective-permute-done.6 = bf16[256,2048]{1,0:T(8,128)(2,1)S(1)} collective-permute-done((bf16[256,2048]{1,0:T(8,128)(2,1)}, bf16[256,2048]{1,0:T(8,128)(2,1)S(1)}, u32[]{:S(2)}, u32[]{:S(2)}) %collective-permute-start.6) | collective-permute-done | bytes 1048608 | tf_op jit(solution)/shard_map/ppermute | solution.py:179
  168.9 0.8 collective-permute-start.8
  169.7 19.2 %collective-permute-done.7 = bf16[256,2048]{1,0:T(8,128)(2,1)S(1)} collective-permute-done((bf16[256,2048]{1,0:T(8,128)(2,1)}, bf16[256,2048]{1,0:T(8,128)(2,1)S(1)}, u32[]{:S(2)}, u32[]{:S(2)}) %collective-permute-start.7) | collective-permute-done | bytes 1048608 | tf_op jit(solution)/shard_map/ppermute | solution.py:180
  189.0 0.9 collective-permute-start.9
  189.9 3.6 %convolution_bitcast_fusion.1 = f32[1,256,1024]{2,1,0:T(8,128)S(1)} fusion(bf16[256,2048]{1,0:T(8,128)(2,1)S(1)} %collective-permute-done.7, bf16[2048,1024]{1,0:T(8,128)(2,1)} %all-gather.2.cloned.1.call-done), kind=kOutput, calls=%fused_computation.34 | convolution fusion | flops 1073741824 | bytes 6291456 | tf_op jit(solution)/shard_map/dot_general | solution.py:186
  193.5 1.3 convolution_bitcast_fusion.2
  194.8 2.5 convolution_bitcast_fusion.3
  197.3 2.6 collective-permute-done.8
  200.0 2.9 %collective-permute-done.9 = bf16[128,2048]{1,0:T(8,128)(2,1)} collective-permute-done((bf16[128,2048]{1,0:T(8,128)(2,1)S(1)}, bf16[128,2048]{1,0:T(8,128)(2,1)}, u32[]{:S(2)}, u32[]{:S(2)}) %collective-permute-start.9) | collective-permute-done | bytes 524320 | tf_op jit(solution)/shard_map/ppermute | solution.py:182
  202.9 2.5 convolution_bitcast_fusion
  206.2 1.7 copy-done.1
  207.9 1.5 pad_maximum_fusion.1
  209.4 4.4 %collective-permute-done.10 = f32[2,256,1024]{2,1,0:T(8,128)S(1)} collective-permute-done((f32[2,256,1024]{2,1,0:T(8,128)}, f32[2,256,1024]{2,1,0:T(8,128)S(1)}, u32[]{:S(2)}, u32[]{:S(2)}) %collective-permute-start.10) | collective-permute-done | bytes 2097184 | tf_op jit(solution)/shard_map/ppermute | solution.py:199
  213.8 1.4 fusion.23
  215.7 13.4 %collective-permute-done.11 = bf16[1,256,1024]{2,1,0:T(8,128)(2,1)S(1)} collective-permute-done((bf16[1,256,1024]{2,1,0:T(8,128)(2,1)S(1)}, bf16[1,256,1024]{2,1,0:T(8,128)(2,1)S(1)}, u32[]{:S(2)}, u32[]{:S(2)}) %collective-permute-start.11) | collective-permute-done | bytes 524320 | tf_op jit(solution)/shard_map/ppermute | solution.py:199
  229.2 1.5 fusion.30
  232.1 1.3 collective-permute-start.14
  234.0 10.3 %collective-permute-start.16 = (bf16[256,512]{1,0:T(8,128)(2,1)S(1)}, bf16[256,512]{1,0:T(8,128)(2,1)S(1)}, u32[]{:S(2)}, u32[]{:S(2)}) collective-permute-start(bf16[256,512]{1,0:T(8,128)(2,1)S(1)} %get-tuple-element.52), channel_id=1, source_target_pairs={{4,0},{5,4},{6,8},{7,12},{20,16},{21,20},{22,24},{23,28}} | collective-permute-start | bytes 786440 | tf_op jit(solution)/shard_map/ppermute | solution.py:220
  244.4 0.7 collective-permute-start.17
  245.1 4.4 %collective-permute-start.18 = (bf16[256,512]{1,0:T(8,128)(2,1)S(1)}, bf16[256,512]{1,0:T(8,128)(2,1)S(1)}, u32[]{:S(2)}, u32[]{:S(2)}) collective-permute-start(bf16[256,512]{1,0:T(8,128)(2,1)S(1)} %get-tuple-element.54), channel_id=1, source_target_pairs={{4,2},{5,6},{6,10},{7,14},{20,18},{21,22},{22,26},{23,30}} | collective-permute-start | bytes 786440 | tf_op jit(solution)/shard_map/ppermute | solution.py:220
  249.5 0.7 collective-permute-start.19
  250.3 8.7 %collective-permute-done.18 = bf16[256,512]{1,0:T(8,128)(2,1)S(1)} collective-permute-done((bf16[256,512]{1,0:T(8,128)(2,1)S(1)}, bf16[256,512]{1,0:T(8,128)(2,1)S(1)}, u32[]{:S(2)}, u32[]{:S(2)}) %collective-permute-start.18) | collective-permute-done | bytes 262176 | tf_op jit(solution)/shard_map/ppermute | solution.py:220
  259.0 0.9 pad_maximum_fusion.2
  (84 shorter events, 6.6 us)
Async XLA Ops:
  6.5 5.0 %copy-start = (f32[256,32]{0,1:T(8,128)S(1)}, f32[256,32]{0,1:T(8,128)}, u32[]{:S(2)}) copy-start(f32[256,32]{0,1:T(8,128)} %param.20) | copy-start | bytes 98308
  6.5 1.4 copy-start.6
  6.5 1.5 copy-start.7
  6.5 6.8 %copy-start.9 = (f32[4,2048]{1,0:T(4,128)S(1)}, f32[4,2048]{1,0:T(4,128)}, u32[]{:S(2)}) copy-start(f32[4,2048]{1,0:T(4,128)} %param.16) | copy-start | bytes 98308
  6.5 6.8 %copy-start.11 = (f32[4,128]{1,0:T(4,128)S(1)}, f32[4,128]{1,0:T(4,128)}, u32[]{:S(2)}) copy-start(f32[4,128]{1,0:T(4,128)} %param.17) | copy-start | bytes 6148
  6.5 6.8 %copy-start.12 = (f32[4,128]{1,0:T(4,128)S(1)}, f32[4,128]{1,0:T(4,128)}, u32[]{:S(2)}) copy-start(f32[4,128]{1,0:T(4,128)} %param.18) | copy-start | bytes 6148
  6.6 183.4 %all-gather.2.cloned.1.call-start = ((), (), s32[]{:S(2)}) async-start(), calls=%async_computation | async-start | bytes 6291456 | tf_op jit(solution)/shard_map/all_gather | solution.py:184
  8.1 5.7 %collective-permute-start = (bf16[3,2304]{1,0:T(4,128)(2,1)S(1)}, bf16[3,2304]{1,0:T(4,128)(2,1)S(1)}, u32[]{:S(2)}, u32[]{:S(2)}) collective-permute-start(bf16[3,2304]{1,0:T(4,128)(2,1)S(1)} %slice.113), channel_id=1, source_target_pairs={{0,4},{4,8},{8,12},{12,16},{16,20},{20,24},{24,28},{1,5},{5,9},{9,... | collective-permute-start | bytes 41480 | tf_op jit(solution)/shard_map/ppermute | solution.py:14
  15.4 1.7 copy-start.2
  17.1 1.9 copy-start.8
  20.6 15.1 %collective-permute-start.3 = (bf16[1,32,64,128]{3,2,1,0:T(8,128)(2,1)S(1)}, bf16[1,32,64,128]{3,2,1,0:T(8,128)(2,1)S(1)}, u32[]{:S(2)}, u32[]{:S(2)}) collective-permute-start(bf16[1,32,64,128]{3,2,1,0:T(8,128)(2,1)S(1)} %convert_bitcast_fusion), channel_id=1, source_target_pairs={{0,4},{4,8},{8,12},{12,16},{16,20},{20,24},{24,28},{1,5},{5,9},{9,... | collective-permute-start | bytes 1572872 | tf_op jit(solution)/shard_map/ppermute | solution.py:14
  35.7 0.8 copy-start.3
  37.5 14.6 %collective-permute-start.4 = (bf16[1,32,64,128]{3,2,1,0:T(8,128)(2,1)}, bf16[1,32,64,128]{3,2,1,0:T(8,128)(2,1)}, u32[]{:S(2)}, u32[]{:S(2)}) collective-permute-start(bf16[1,32,64,128]{3,2,1,0:T(8,128)(2,1)} %fusion.29), channel_id=1, source_target_pairs={{0,8},{4,12},{8,16},{12,20},{16,24},{20,28},{1,9},{5,13},{9,17},{1... | collective-permute-start | bytes 1572872 | tf_op jit(solution)/shard_map/ppermute | solution.py:14
  40.3 9.6 %collective-permute-start.1 = (f32[1,32]{1,0:T(1,128)S(1)}, f32[1,32]{1,0:T(1,128)S(1)}, u32[]{:S(2)}, u32[]{:S(2)}) collective-permute-start(f32[1,32]{1,0:T(1,128)S(1)} %bitcast.96), channel_id=1, source_target_pairs={{0,4},{4,8},{8,12},{12,16},{16,20},{20,24},{24,28},{1,5},{5,9},{9,... | collective-permute-start | bytes 392 | tf_op jit(solution)/shard_map/ppermute | solution.py:14
  43.3 91.4 %copy-start.4 = (bf16[1,32,64,128]{3,2,1,0:T(8,128)(2,1)S(1)}, bf16[1,32,64,128]{3,2,1,0:T(8,128)(2,1)}, u32[]{:S(2)}) copy-start(bf16[1,32,64,128]{3,2,1,0:T(8,128)(2,1)} %copy-done.3) | copy-start | bytes 1572868
  53.7 81.0 %collective-permute-start.5 = (bf16[1,32,64,128]{3,2,1,0:T(8,128)(2,1)S(1)}, bf16[1,32,64,128]{3,2,1,0:T(8,128)(2,1)S(1)}, u32[]{:S(2)}, u32[]{:S(2)}) collective-permute-start(bf16[1,32,64,128]{3,2,1,0:T(8,128)(2,1)S(1)} %fusion.22), channel_id=1, source_target_pairs={{0,16},{4,20},{8,24},{12,28},{1,17},{5,21},{9,25},{13,29},{2,18},{... | collective-permute-start | bytes 1572872 | tf_op jit(solution)/shard_map/ppermute | solution.py:14
  55.1 78.6 %collective-permute-start.2 = (f32[1,32]{1,0:T(1,128)S(1)}, f32[1,32]{1,0:T(1,128)S(1)}, u32[]{:S(2)}, u32[]{:S(2)}) collective-permute-start(f32[1,32]{1,0:T(1,128)S(1)} %bitcast_multiply_fusion.1), channel_id=1, source_target_pairs={{0,8},{4,12},{8,16},{12,20},{16,24},{20,28},{1,9},{5,13},{9,17},{1... | collective-permute-start | bytes 392 | tf_op jit(solution)/shard_map/ppermute | solution.py:14
  57.5 78.8 %copy-start.14 = (f32[32]{0:T(128)S(1)}, f32[32]{0:T(128)}, u32[]{:S(2)}) copy-start(f32[32]{0:T(128)} %param.21) | copy-start | bytes 388
  140.0 2.0 copy-start.5
  142.1 0.8 copy-start.10
  144.7 24.1 %collective-permute-start.6 = (bf16[256,2048]{1,0:T(8,128)(2,1)}, bf16[256,2048]{1,0:T(8,128)(2,1)S(1)}, u32[]{:S(2)}, u32[]{:S(2)}) collective-permute-start(bf16[256,2048]{1,0:T(8,128)(2,1)} %multiply_convert_fusion.5), channel_id=1, source_target_pairs={{0,4},{4,0},{8,12},{12,8},{1,5},{5,1},{9,13},{13,9},{2,6},{6,2},{1... | collective-permute-start | bytes 3145736 | tf_op jit(solution)/shard_map/ppermute | solution.py:179
  145.5 43.5 %collective-permute-start.7 = (bf16[256,2048]{1,0:T(8,128)(2,1)}, bf16[256,2048]{1,0:T(8,128)(2,1)S(1)}, u32[]{:S(2)}, u32[]{:S(2)}) collective-permute-start(bf16[256,2048]{1,0:T(8,128)(2,1)} %multiply_convert_fusion.5), channel_id=1, source_target_pairs={{0,8},{4,12},{8,0},{12,4},{1,9},{5,13},{9,1},{13,5},{2,10},{6,14},... | collective-permute-start | bytes 3145736 | tf_op jit(solution)/shard_map/ppermute | solution.py:180
  168.9 31.1 %collective-permute-start.8 = (bf16[128,2048]{1,0:T(8,128)(2,1)S(1)}, bf16[128,2048]{1,0:T(8,128)(2,1)}, u32[]{:S(2)}, u32[]{:S(2)}) collective-permute-start(bf16[128,2048]{1,0:T(8,128)(2,1)S(1)} %slice.122), channel_id=1, source_target_pairs={{0,8},{4,12},{8,0},{12,4},{1,9},{5,13},{9,1},{13,5},{2,10},{6,14},... | collective-permute-start | bytes 1572872 | tf_op jit(solution)/shard_map/ppermute | solution.py:181
  189.0 13.9 %collective-permute-start.9 = (bf16[128,2048]{1,0:T(8,128)(2,1)S(1)}, bf16[128,2048]{1,0:T(8,128)(2,1)}, u32[]{:S(2)}, u32[]{:S(2)}) collective-permute-start(bf16[128,2048]{1,0:T(8,128)(2,1)S(1)} %slice.123), channel_id=1, source_target_pairs={{0,4},{4,0},{8,12},{12,8},{1,5},{5,1},{9,13},{13,9},{2,6},{6,2},{1... | collective-permute-start | bytes 1572872 | tf_op jit(solution)/shard_map/ppermute | solution.py:182
  189.9 3.6 %copy-start.13 = (bf16[2048,1024]{1,0:T(8,128)(2,1)S(1)}, bf16[2048,1024]{1,0:T(8,128)(2,1)}, u32[]{:S(2)}) copy-start(bf16[2048,1024]{1,0:T(8,128)(2,1)} %all-gather.2.cloned.1.call-done) | copy-start | bytes 12582916
  206.0 2.0 copy-start.1
  209.4 4.4 %collective-permute-start.10 = (f32[2,256,1024]{2,1,0:T(8,128)}, f32[2,256,1024]{2,1,0:T(8,128)S(1)}, u32[]{:S(2)}, u32[]{:S(2)}) collective-permute-start(f32[2,256,1024]{2,1,0:T(8,128)} %pad_maximum_fusion.1), channel_id=1, source_target_pairs={{0,1},{1,0},{2,3},{3,2},{4,5},{5,4},{6,7},{7,6},{8,9},{9,8},{10,11... | collective-permute-start | bytes 6291464 | tf_op jit(solution)/shard_map/ppermute | solution.py:199
  215.1 14.0 %collective-permute-start.11 = (bf16[1,256,1024]{2,1,0:T(8,128)(2,1)S(1)}, bf16[1,256,1024]{2,1,0:T(8,128)(2,1)S(1)}, u32[]{:S(2)}, u32[]{:S(2)}) collective-permute-start(bf16[1,256,1024]{2,1,0:T(8,128)(2,1)S(1)} %fusion.23), channel_id=1, source_target_pairs={{0,2},{1,3},{2,0},{3,1},{4,6},{5,7},{6,4},{7,5},{8,10},{9,11},{10,... | collective-permute-start | bytes 1572872 | tf_op jit(solution)/shard_map/ppermute | solution.py:199
  230.7 13.7 %collective-permute-start.12 = (bf16[256,512]{1,0:T(8,128)(2,1)S(1)}, bf16[256,512]{1,0:T(8,128)(2,1)S(1)}, u32[]{:S(2)}, u32[]{:S(2)}) collective-permute-start(bf16[256,512]{1,0:T(8,128)(2,1)S(1)} %get-tuple-element.52), channel_id=1, source_target_pairs={{0,0},{1,4},{2,8},{3,12},{16,16},{17,20},{18,24},{19,28}} | collective-permute-start | bytes 786440 | tf_op jit(solution)/shard_map/ppermute | solution.py:220
  231.4 13.7 %collective-permute-start.13 = (bf16[256,512]{1,0:T(8,128)(2,1)S(1)}, bf16[256,512]{1,0:T(8,128)(2,1)S(1)}, u32[]{:S(2)}, u32[]{:S(2)}) collective-permute-start(bf16[256,512]{1,0:T(8,128)(2,1)S(1)} %get-tuple-element.52), channel_id=1, source_target_pairs={{8,1},{9,5},{10,9},{11,13},{24,17},{25,21},{26,25},{27,29}} | collective-permute-start | bytes 786440 | tf_op jit(solution)/shard_map/ppermute | solution.py:220
  232.1 17.4 %collective-permute-start.14 = (bf16[256,512]{1,0:T(8,128)(2,1)S(1)}, bf16[256,512]{1,0:T(8,128)(2,1)S(1)}, u32[]{:S(2)}, u32[]{:S(2)}) collective-permute-start(bf16[256,512]{1,0:T(8,128)(2,1)S(1)} %get-tuple-element.54), channel_id=1, source_target_pairs={{0,2},{1,6},{2,10},{3,14},{16,18},{17,22},{18,26},{19,30}} | collective-permute-start | bytes 786440 | tf_op jit(solution)/shard_map/ppermute | solution.py:220
  233.4 16.8 %collective-permute-start.15 = (bf16[256,512]{1,0:T(8,128)(2,1)S(1)}, bf16[256,512]{1,0:T(8,128)(2,1)S(1)}, u32[]{:S(2)}, u32[]{:S(2)}) collective-permute-start(bf16[256,512]{1,0:T(8,128)(2,1)S(1)} %get-tuple-element.54), channel_id=1, source_target_pairs={{8,3},{9,7},{10,11},{11,15},{24,19},{25,23},{26,27},{27,31}} | collective-permute-start | bytes 786440 | tf_op jit(solution)/shard_map/ppermute | solution.py:220
  234.0 16.2 %collective-permute-start.16 = (bf16[256,512]{1,0:T(8,128)(2,1)S(1)}, bf16[256,512]{1,0:T(8,128)(2,1)S(1)}, u32[]{:S(2)}, u32[]{:S(2)}) collective-permute-start(bf16[256,512]{1,0:T(8,128)(2,1)S(1)} %get-tuple-element.52), channel_id=1, source_target_pairs={{4,0},{5,4},{6,8},{7,12},{20,16},{21,20},{22,24},{23,28}} | collective-permute-start | bytes 786440 | tf_op jit(solution)/shard_map/ppermute | solution.py:220
  244.4 5.9 %collective-permute-start.17 = (bf16[256,512]{1,0:T(8,128)(2,1)S(1)}, bf16[256,512]{1,0:T(8,128)(2,1)S(1)}, u32[]{:S(2)}, u32[]{:S(2)}) collective-permute-start(bf16[256,512]{1,0:T(8,128)(2,1)S(1)} %get-tuple-element.52), channel_id=1, source_target_pairs={{12,1},{13,5},{14,9},{15,13},{28,17},{29,21},{30,25},{31,29}} | collective-permute-start | bytes 786440 | tf_op jit(solution)/shard_map/ppermute | solution.py:220
  245.1 13.9 %collective-permute-start.18 = (bf16[256,512]{1,0:T(8,128)(2,1)S(1)}, bf16[256,512]{1,0:T(8,128)(2,1)S(1)}, u32[]{:S(2)}, u32[]{:S(2)}) collective-permute-start(bf16[256,512]{1,0:T(8,128)(2,1)S(1)} %get-tuple-element.54), channel_id=1, source_target_pairs={{4,2},{5,6},{6,10},{7,14},{20,18},{21,22},{22,26},{23,30}} | collective-permute-start | bytes 786440 | tf_op jit(solution)/shard_map/ppermute | solution.py:220
  249.5 9.5 %collective-permute-start.19 = (bf16[256,512]{1,0:T(8,128)(2,1)S(1)}, bf16[256,512]{1,0:T(8,128)(2,1)S(1)}, u32[]{:S(2)}, u32[]{:S(2)}) collective-permute-start(bf16[256,512]{1,0:T(8,128)(2,1)S(1)} %get-tuple-element.54), channel_id=1, source_target_pairs={{12,3},{13,7},{14,11},{15,15},{28,19},{29,23},{30,27},{31,31}} | collective-permute-start | bytes 786440 | tf_op jit(solution)/shard_map/ppermute | solution.py:220
Sparse Core Ops, SparseCore 0:
  43.5 100.7 all-gather.1

commit v7 on v5

--- a/solution.py
+++ b/solution.py
@@ -175,6 +175,27 @@
         )
     outer_at = lax.axis_index(outer_axis)
     tp_at = lax.axis_index("tp")
+    inner_count = ctx_count // tp_count
+    inner_at = lax.axis_index(inner_axis)
+    shifted_cols = jnp.stack(
+        [out_weight]
+        + [
+            lax.ppermute(
+                out_weight, inner_axis, [(s, (s + d) % inner_count) for s in range(inner_count)]
+            )
+            for d in range(1, inner_count)
+        ]
+    )
+    cols_all = jnp.concatenate(
+        [
+            lax.dynamic_index_in_dim(
+                shifted_cols, (inner_at - place + inner_count) % inner_count, 0, keepdims=False
+            )
+            for place in range(inner_count)
+        ],
+        axis=1,
+    )
+    cols_all, hidden = lax.optimization_barrier((cols_all, hidden))
     from_left, from_right = {}, {}
     going_right = going_left = hidden
     for step in range(1, tp_count):
@@ -189,7 +210,6 @@
         jnp.where(outer_at >= d, from_left[d], from_right[tp_count - d])
         for d in range(1, tp_count)
     ]
-    cols_all = lax.all_gather(out_weight, inner_axis, axis=1, tiled=True)
     by_source = jnp.stack(
         [jnp.dot(rows, cols_all, preferred_element_type=jnp.float32) for rows in arrived]
     )

time: 229 us -> 223 us (0.974)
  between operations: 14 us -> 0.67 us
  waiting for transfers between devices: 125 us -> 133 us
  starting transfers between devices: 47.8 us -> 39.9 us
  other arithmetic: 13.6 us -> 19.9 us
    ppermute x0 -> x1, waiting for transfers between devices: none -> 12 us  [on_device(): lax.ppermute(out_weight, inner_axis, [(s, (s + d) % inner_count) for s in...]
    ppermute x3, starting transfers between devices: 16.7 us -> 6.38 us  [on_device(): lax.ppermute(going_right, outer_axis, [(s, s + 1) for s in range(step - 1...]
    squeeze x0 -> x1, other arithmetic: none -> 3.07 us  [on_device(): lax.dynamic_index_in_dim(shifted_cols, (inner_at - place + inner_count) %...]
    concatenate x0 -> x1, other arithmetic: none -> 2.6 us  [on_device(): jnp.concatenate([lax.dynamic_index_in_dim(shifted_cols, (inner_at - place...]
    unnamed x40 -> x38, local copies, waits for them, and re-layouts: 4.74 us -> 4.7 us
  transfers between devices with their start and end apart: 16 -> 16, of which waited for: 10 -> 10; matrix products, arithmetic and copies ran while one was open for 10% -> 11% of each run, Pallas kernels for 0% -> 0%
where the time goes in v7:
time: 223 us; the launch traced here: 222 us
  waiting for transfers between devices  133 us (60%)
  starting transfers between devices  39.9 us (18%)
  other arithmetic  19.9 us (9%)
  matrix products  18.2 us (8%)
  local copies, waits for them, and re-layouts  9.85 us (4%)
    ppermute x3, waiting for transfers between devices, on_device(): lax.ppermute(going_left, outer_axis, [(s, s - 1) for s in range(1, tp_cou...  59 us
    ppermute x6, starting transfers between devices, shifted(): lax.ppermute(value, axis, [(source, source + steps) for source in range(f...  24.7 us
    ppermute x1, waiting for transfers between devices, on_device(): return lax.ppermute(held[0].astype(jnp.bfloat16), (outer_axis, 'tp'), swap)  23.6 us
    ppermute x6, waiting for transfers between devices, shifted(): lax.ppermute(value, axis, [(source, source + steps) for source in range(f...  21.1 us
    ppermute x2, waiting for transfers between devices, on_device(): lax.ppermute(sent if bit == 1 else sent.astype(jnp.bfloat16), 'tp', [(s,...  17.7 us
    ppermute x1, waiting for transfers between devices, on_device(): lax.ppermute(out_weight, inner_axis, [(s, (s + d) % inner_count) for s in...  12 us
    dot_general x4, matrix products, on_device(): jnp.dot(rows, cols_all, preferred_element_type=jnp.float32)  10.3 us
    ppermute x3, starting transfers between devices, on_device(): lax.ppermute(going_right, outer_axis, [(s, s + 1) for s in range(step - 1...  6.38 us
  transfers between devices with their start and end apart: 16, of which 10 were waited for; matrix products, arithmetic and copies ran while one was open for 11% of the time, Pallas kernels for 0%

profile of v7, /device:TPU:2, one launch (start us, length us, event | category | flops | bytes accessed | tf_op | source)
XLA Modules:
  0.0 222.0 jit_solution(14617140969940367331)
XLA Ops:
  0.0 1.3 constant_dynamic-update-slice_fusion.5
  1.5 3.4 %collective-permute-start.1 = (bf16[3,2304]{1,0:T(4,128)(2,1)S(1)}, bf16[3,2304]{1,0:T(4,128)(2,1)S(1)}, u32[]{:S(2)}, u32[]{:S(2)}) collective-permute-start(bf16[3,2304]{1,0:T(4,128)(2,1)S(1)} %slice.91), channel_id=1, source_target_pairs={{0,4},{4,8},{8,12},{12,16},{16,20},{20,24},{24,28},{1,5},{5,9},{9,... | collective-permute-start | bytes 41480 | tf_op jit(solution)/shard_map/ppermute | solution.py:14
  7.1 1.5 multiply_convert_fusion.3
  8.7 1.7 slice_convert_fusion
  10.4 1.9 copy.27
  12.3 1.4 fusion.21
  13.8 3.6 %collective-permute-start.4 = (bf16[1,32,64,128]{3,2,1,0:T(8,128)(2,1)S(1)}, bf16[1,32,64,128]{3,2,1,0:T(8,128)(2,1)S(1)}, u32[]{:S(2)}, u32[]{:S(2)}) collective-permute-start(bf16[1,32,64,128]{3,2,1,0:T(8,128)(2,1)S(1)} %convert_bitcast_fusion), channel_id=1, source_target_pairs={{0,4},{4,8},{8,12},{12,16},{16,20},{20,24},{24,28},{1,5},{5,9},{9,... | collective-permute-start | bytes 1572872 | tf_op jit(solution)/shard_map/ppermute | solution.py:14
  17.5 10.7 %collective-permute-done.4 = bf16[1,32,64,128]{3,2,1,0:T(8,128)(2,1)S(1)} collective-permute-done((bf16[1,32,64,128]{3,2,1,0:T(8,128)(2,1)S(1)}, bf16[1,32,64,128]{3,2,1,0:T(8,128)(2,1)S(1)}, u32[]{:S(2)}, u32[]{:S(2)}) %collective-permute-start.4) | collective-permute-done | bytes 524320 | tf_op jit(solution)/shard_map/ppermute | solution.py:14
  28.2 0.8 copy-done.3
  29.0 1.0 fusion.36
  30.0 6.3 %collective-permute-start.5 = (bf16[1,32,64,128]{3,2,1,0:T(8,128)(2,1)}, bf16[1,32,64,128]{3,2,1,0:T(8,128)(2,1)}, u32[]{:S(2)}, u32[]{:S(2)}) collective-permute-start(bf16[1,32,64,128]{3,2,1,0:T(8,128)(2,1)} %fusion.36), channel_id=1, source_target_pairs={{0,8},{4,12},{8,16},{12,20},{16,24},{20,28},{1,9},{5,13},{9,17},{1... | collective-permute-start | bytes 1572872 | tf_op jit(solution)/shard_map/ppermute | solution.py:14
  36.3 2.3 %collective-permute-start.2 = (f32[1,32]{1,0:T(1,128)S(1)}, f32[1,32]{1,0:T(1,128)S(1)}, u32[]{:S(2)}, u32[]{:S(2)}) collective-permute-start(f32[1,32]{1,0:T(1,128)S(1)} %bitcast.100), channel_id=1, source_target_pairs={{0,4},{4,8},{8,12},{12,16},{16,20},{20,24},{24,28},{1,5},{5,9},{9,... | collective-permute-start | bytes 392 | tf_op jit(solution)/shard_map/ppermute | solution.py:14
  38.6 1.9 collective-permute-start
  40.6 4.4 %collective-permute-done.5 = bf16[1,32,64,128]{3,2,1,0:T(8,128)(2,1)} collective-permute-done((bf16[1,32,64,128]{3,2,1,0:T(8,128)(2,1)}, bf16[1,32,64,128]{3,2,1,0:T(8,128)(2,1)}, u32[]{:S(2)}, u32[]{:S(2)}) %collective-permute-start.5) | collective-permute-done | bytes 524320 | tf_op jit(solution)/shard_map/ppermute | solution.py:14
  45.0 2.3 %fusion.26 = bf16[1,32,64,128]{3,2,1,0:T(8,128)(2,1)} fusion(bf16[1,32,64,128]{3,2,1,0:T(8,128)(2,1)} %collective-permute-done.5, f32[32,64,128]{2,1,0:T(8,128)S(1)} %fusion.21, bf16[1,32,64,128]{3,2,1,0:T(8,128)(2,1)} %copy-done.3, f32[32]{0:T(128)S(1)} %get-tuple-element.66, f32[32]{0:T(128)S(1)} %bitcast.99), kind=kLoop, calls=%fused_computation.54 | loop fusion | flops 1835008 | bytes 2621696 | tf_op jit(solution)/shard_map/convert_element_type | solution.py:74
  47.3 6.1 %collective-permute-start.6 = (bf16[1,32,64,128]{3,2,1,0:T(8,128)(2,1)}, bf16[1,32,64,128]{3,2,1,0:T(8,128)(2,1)S(1)}, u32[]{:S(2)}, u32[]{:S(2)}) collective-permute-start(bf16[1,32,64,128]{3,2,1,0:T(8,128)(2,1)} %fusion.26), channel_id=1, source_target_pairs={{0,16},{4,20},{8,24},{12,28},{1,17},{5,21},{9,25},{13,29},{2,18},{... | collective-permute-start | bytes 1572872 | tf_op jit(solution)/shard_map/ppermute | solution.py:14
  53.4 3.0 %collective-permute-start.3 = (f32[1,32]{1,0:T(1,128)S(1)}, f32[1,32]{1,0:T(1,128)S(1)}, u32[]{:S(2)}, u32[]{:S(2)}) collective-permute-start(f32[1,32]{1,0:T(1,128)S(1)} %bitcast_multiply_fusion.1), channel_id=1, source_target_pairs={{0,8},{4,12},{8,16},{12,20},{16,24},{20,28},{1,9},{5,13},{9,17},{1... | collective-permute-start | bytes 392 | tf_op jit(solution)/shard_map/ppermute | solution.py:14
  56.4 6.0 %collective-permute-done.3 = f32[1,32]{1,0:T(1,128)S(1)} collective-permute-done((f32[1,32]{1,0:T(1,128)S(1)}, f32[1,32]{1,0:T(1,128)S(1)}, u32[]{:S(2)}, u32[]{:S(2)}) %collective-permute-start.3) | collective-permute-done | bytes 160 | tf_op jit(solution)/shard_map/ppermute | solution.py:14
  62.4 1.1 fusion.44
  63.5 1.7 fusion.39
  65.2 3.7 %fusion.18 = f32[256,1,32,64]{0,3,2,1:T(8,128)} fusion(f32[32,64,256]{2,1,0:T(8,128)S(1)} %fusion.39, f32[256,1,32,64]{0,3,2,1:T(8,128)S(1)} %bitcast.88, f32[32,256]{1,0:T(8,128)S(1)} %bitcast.96, f32[256,256]{1,0:T(8,128)S(1)} %fusion.44, pred[256,256]{1,0:T(8,128)(4,1)S(1)} %iota_compare_fusion.1, f32[32]{0:T(128)S(1)} %copy-done.14, ...), kind=kOutput, calls=%fused_computation.35 | convolution fusion | flops 279969792 | bytes 8814720 | tf_op jit(solution)/shard_map/while/body/eval_jaxpr/gjts,sgjp->tgjp/dot_general | solution.py:46
  68.9 2.0 copy.32
  70.9 0.8 multiply_reduce_fusion
  71.7 0.8 multiply_convert_fusion.5
  72.5 12.0 %collective-permute-done = bf16[2048,512]{1,0:T(8,128)(2,1)} collective-permute-done((bf16[2048,512]{1,0:T(8,128)(2,1)}, bf16[2048,512]{1,0:T(8,128)(2,1)}, u32[]{:S(2)}, u32[]{:S(2)}) %collective-permute-start) | collective-permute-done | bytes 2097184 | tf_op jit(solution)/shard_map/ppermute | solution.py:183
  84.5 3.1 %fusion.16 = (bf16[2048,512]{1,0:T(8,128)(2,1)S(1)}, bf16[2048,512]{1,0:T(8,128)(2,1)S(1)}) fusion(s32[]{:T(128)S(6)} %select_n.76, bf16[1,2048,512]{2,1,0:T(8,128)(2,1)} %bitcast, bf16[1,2048,512]{2,1,0:T(8,128)(2,1)} %bitcast.1, s32[]{:T(128)S(6)} %select_n.78), kind=kLoop, calls=%fused_computation.31 | loop fusion | flops 2097152 | bytes 8388616 | tf_op jit(solution)/shard_map/jit(dynamic_index_in_dim)/squeeze | solution.py:191
  87.6 2.6 %pad_maximum_fusion = bf16[2048,1024]{1,0:T(8,128)(2,1)} fusion(bf16[2048,512]{1,0:T(8,128)(2,1)S(1)} %get-tuple-element.59, bf16[2048,512]{1,0:T(8,128)(2,1)S(1)} %get-tuple-element.58), kind=kLoop, calls=%fused_computation.6 | loop fusion | flops 8388608 | bytes 8388608 | tf_op jit(solution)/shard_map/concatenate | solution.py:189
  90.2 1.3 collective-permute-start.8
  91.5 4.6 %collective-permute-start.7 = (bf16[256,2048]{1,0:T(8,128)(2,1)S(1)}, bf16[256,2048]{1,0:T(8,128)(2,1)S(1)}, u32[]{:S(2)}, u32[]{:S(2)}) collective-permute-start(bf16[256,2048]{1,0:T(8,128)(2,1)S(1)} %multiply_convert_fusion.5), channel_id=1, source_target_pairs={{0,8},{8,16},{16,24},{1,9},{9,17},{17,25},{2,10},{10,18},{18,26},{... | collective-permute-start | bytes 3145736 | tf_op jit(solution)/shard_map/ppermute | solution.py:202
  96.1 18.7 %collective-permute-done.8 = bf16[256,2048]{1,0:T(8,128)(2,1)S(1)} collective-permute-done((bf16[256,2048]{1,0:T(8,128)(2,1)S(1)}, bf16[256,2048]{1,0:T(8,128)(2,1)S(1)}, u32[]{:S(2)}, u32[]{:S(2)}) %collective-permute-start.8) | collective-permute-done | bytes 1048608 | tf_op jit(solution)/shard_map/ppermute | solution.py:205
  114.8 1.3 collective-permute-start.9
  116.9 24.1 %collective-permute-done.9 = bf16[256,2048]{1,0:T(8,128)(2,1)} collective-permute-done((bf16[256,2048]{1,0:T(8,128)(2,1)S(1)}, bf16[256,2048]{1,0:T(8,128)(2,1)}, u32[]{:S(2)}, u32[]{:S(2)}) %collective-permute-start.9) | collective-permute-done | bytes 1048608 | tf_op jit(solution)/shard_map/ppermute | solution.py:205
  141.0 1.3 collective-permute-start.10
  142.4 1.0 collective-permute-start.12
  143.4 3.9 %convolution_bitcast_fusion.3 = f32[1,256,1024]{2,1,0:T(8,128)S(1)} fusion(bf16[256,2048]{1,0:T(8,128)(2,1)} %copy-done.6, bf16[2048,1024]{1,0:T(8,128)(2,1)} %pad_maximum_fusion), kind=kOutput, calls=%fused_computation.45 | convolution fusion | flops 1073741824 | bytes 6291456 | tf_op jit(solution)/shard_map/dot_general | solution.py:214
  147.4 2.5 %convolution_bitcast_fusion.1 = f32[1,256,1024]{2,1,0:T(8,128)S(1)} fusion(bf16[2048,1024]{1,0:T(8,128)(2,1)S(1)} %copy-done.5, bf16[256,2048]{1,0:T(8,128)(2,1)S(1)} %collective-permute-done.11, bf16[256,2048]{1,0:T(8,128)(2,1)} %collective-permute-done.9, pred[]{:T(512)S(6)} %ge.33), kind=kOutput, calls=%fused_computation.43 | convolution fusion | flops 1074266112 | bytes 7340033 | tf_op jit(solution)/shard_map/dot_general | solution.py:214
  149.9 16.1 %collective-permute-done.10 = bf16[256,2048]{1,0:T(8,128)(2,1)} collective-permute-done((bf16[256,2048]{1,0:T(8,128)(2,1)}, bf16[256,2048]{1,0:T(8,128)(2,1)}, u32[]{:S(2)}, u32[]{:S(2)}) %collective-permute-start.10) | collective-permute-done | bytes 1048608 | tf_op jit(solution)/shard_map/ppermute | solution.py:205
  166.1 2.5 %convolution_bitcast_fusion.2 = f32[1,256,1024]{2,1,0:T(8,128)S(1)} fusion(bf16[2048,1024]{1,0:T(8,128)(2,1)S(1)} %copy-done.5, bf16[256,2048]{1,0:T(8,128)(2,1)S(1)} %collective-permute-done.7, bf16[256,2048]{1,0:T(8,128)(2,1)} %collective-permute-done.10, pred[]{:T(512)S(6)} %ge.32), kind=kOutput, calls=%fused_computation.44 | convolution fusion | flops 1074266112 | bytes 7340033 | tf_op jit(solution)/shard_map/dot_general | solution.py:214
  168.6 1.3 convolution_bitcast_fusion
  170.8 1.7 copy-done.1
  172.5 1.5 pad_maximum_fusion.2
  173.9 4.4 %collective-permute-done.13 = f32[2,256,1024]{2,1,0:T(8,128)S(1)} collective-permute-done((f32[2,256,1024]{2,1,0:T(8,128)}, f32[2,256,1024]{2,1,0:T(8,128)S(1)}, u32[]{:S(2)}, u32[]{:S(2)}) %collective-permute-start.13) | collective-permute-done | bytes 2097184 | tf_op jit(solution)/shard_map/ppermute | solution.py:227
  178.3 1.4 fusion.27
  180.3 13.4 %collective-permute-done.14 = bf16[1,256,1024]{2,1,0:T(8,128)(2,1)S(1)} collective-permute-done((bf16[1,256,1024]{2,1,0:T(8,128)(2,1)S(1)}, bf16[1,256,1024]{2,1,0:T(8,128)(2,1)S(1)}, u32[]{:S(2)}, u32[]{:S(2)}) %collective-permute-start.14) | collective-permute-done | bytes 524320 | tf_op jit(solution)/shard_map/ppermute | solution.py:227
  193.7 1.5 fusion.37
  195.2 2.4 %collective-permute-start.15 = (bf16[256,1024]{1,0:T(8,128)(2,1)S(1)}, bf16[256,1024]{1,0:T(8,128)(2,1)S(1)}, u32[]{:S(2)}, u32[]{:S(2)}) collective-permute-start(bf16[256,1024]{1,0:T(8,128)(2,1)S(1)} %fusion.37), channel_id=1, source_target_pairs={{0,0},{1,8},{2,16},{3,24},{8,1},{9,9},{10,17},{11,25},{16,2},{17,1... | collective-permute-start | bytes 1572872 | tf_op jit(solution)/shard_map/ppermute | solution.py:237
  197.6 23.6 %collective-permute-done.15 = bf16[256,1024]{1,0:T(8,128)(2,1)S(1)} collective-permute-done((bf16[256,1024]{1,0:T(8,128)(2,1)S(1)}, bf16[256,1024]{1,0:T(8,128)(2,1)S(1)}, u32[]{:S(2)}, u32[]{:S(2)}) %collective-permute-start.15) | collective-permute-done | bytes 524320 | tf_op jit(solution)/shard_map/ppermute | solution.py:237
  221.2 0.8 copy.49
  (70 shorter events, 4.6 us)
Async XLA Ops:
  0.0 4.9 %copy-start = (f32[256,32]{0,1:T(8,128)S(1)}, f32[256,32]{0,1:T(8,128)}, u32[]{:S(2)}) copy-start(f32[256,32]{0,1:T(8,128)} %param.20) | copy-start | bytes 98308
  0.0 1.4 copy-start.7
  0.0 1.4 copy-start.8
  0.0 6.7 %copy-start.10 = (f32[4,2048]{1,0:T(4,128)S(1)}, f32[4,2048]{1,0:T(4,128)}, u32[]{:S(2)}) copy-start(f32[4,2048]{1,0:T(4,128)} %param.16) | copy-start | bytes 98308
  0.0 6.7 %copy-start.12 = (f32[4,128]{1,0:T(4,128)S(1)}, f32[4,128]{1,0:T(4,128)}, u32[]{:S(2)}) copy-start(f32[4,128]{1,0:T(4,128)} %param.17) | copy-start | bytes 6148
  0.0 6.7 %copy-start.13 = (f32[4,128]{1,0:T(4,128)S(1)}, f32[4,128]{1,0:T(4,128)}, u32[]{:S(2)}) copy-start(f32[4,128]{1,0:T(4,128)} %param.18) | copy-start | bytes 6148
  1.5 5.5 %collective-permute-start.1 = (bf16[3,2304]{1,0:T(4,128)(2,1)S(1)}, bf16[3,2304]{1,0:T(4,128)(2,1)S(1)}, u32[]{:S(2)}, u32[]{:S(2)}) collective-permute-start(bf16[3,2304]{1,0:T(4,128)(2,1)S(1)} %slice.91), channel_id=1, source_target_pairs={{0,4},{4,8},{8,12},{12,16},{16,20},{20,24},{24,28},{1,5},{5,9},{9,... | collective-permute-start | bytes 41480 | tf_op jit(solution)/shard_map/ppermute | solution.py:14
  8.6 1.7 copy-start.2
  10.4 1.9 copy-start.9
  13.8 14.3 %collective-permute-start.4 = (bf16[1,32,64,128]{3,2,1,0:T(8,128)(2,1)S(1)}, bf16[1,32,64,128]{3,2,1,0:T(8,128)(2,1)S(1)}, u32[]{:S(2)}, u32[]{:S(2)}) collective-permute-start(bf16[1,32,64,128]{3,2,1,0:T(8,128)(2,1)S(1)} %convert_bitcast_fusion), channel_id=1, source_target_pairs={{0,4},{4,8},{8,12},{12,16},{16,20},{20,24},{24,28},{1,5},{5,9},{9,... | collective-permute-start | bytes 1572872 | tf_op jit(solution)/shard_map/ppermute | solution.py:14
  28.2 0.8 copy-start.3
  30.0 15.0 %collective-permute-start.5 = (bf16[1,32,64,128]{3,2,1,0:T(8,128)(2,1)}, bf16[1,32,64,128]{3,2,1,0:T(8,128)(2,1)}, u32[]{:S(2)}, u32[]{:S(2)}) collective-permute-start(bf16[1,32,64,128]{3,2,1,0:T(8,128)(2,1)} %fusion.36), channel_id=1, source_target_pairs={{0,8},{4,12},{8,16},{12,20},{16,24},{20,28},{1,9},{5,13},{9,17},{1... | collective-permute-start | bytes 1572872 | tf_op jit(solution)/shard_map/ppermute | solution.py:14
  36.3 4.3 %collective-permute-start.2 = (f32[1,32]{1,0:T(1,128)S(1)}, f32[1,32]{1,0:T(1,128)S(1)}, u32[]{:S(2)}, u32[]{:S(2)}) collective-permute-start(f32[1,32]{1,0:T(1,128)S(1)} %bitcast.100), channel_id=1, source_target_pairs={{0,4},{4,8},{8,12},{12,16},{16,20},{20,24},{24,28},{1,5},{5,9},{9,... | collective-permute-start | bytes 392 | tf_op jit(solution)/shard_map/ppermute | solution.py:14
  38.6 45.9 %collective-permute-start = (bf16[2048,512]{1,0:T(8,128)(2,1)}, bf16[2048,512]{1,0:T(8,128)(2,1)}, u32[]{:S(2)}, u32[]{:S(2)}) collective-permute-start(bf16[2048,512]{1,0:T(8,128)(2,1)} %param.23), channel_id=1, source_target_pairs={{0,4},{4,0},{1,5},{5,1},{2,6},{6,2},{3,7},{7,3},{8,12},{12,8},{9,1... | collective-permute-start | bytes 6291464 | tf_op jit(solution)/shard_map/ppermute | solution.py:183
  47.3 17.9 %copy-start.14 = (f32[32]{0:T(128)S(1)}, f32[32]{0:T(128)}, u32[]{:S(2)}) copy-start(f32[32]{0:T(128)} %param.21) | copy-start | bytes 388
  47.3 16.2 %collective-permute-start.6 = (bf16[1,32,64,128]{3,2,1,0:T(8,128)(2,1)}, bf16[1,32,64,128]{3,2,1,0:T(8,128)(2,1)S(1)}, u32[]{:S(2)}, u32[]{:S(2)}) collective-permute-start(bf16[1,32,64,128]{3,2,1,0:T(8,128)(2,1)} %fusion.26), channel_id=1, source_target_pairs={{0,16},{4,20},{8,24},{12,28},{1,17},{5,21},{9,25},{13,29},{2,18},{... | collective-permute-start | bytes 1572872 | tf_op jit(solution)/shard_map/ppermute | solution.py:14
  53.4 9.0 %collective-permute-start.3 = (f32[1,32]{1,0:T(1,128)S(1)}, f32[1,32]{1,0:T(1,128)S(1)}, u32[]{:S(2)}, u32[]{:S(2)}) collective-permute-start(f32[1,32]{1,0:T(1,128)S(1)} %bitcast_multiply_fusion.1), channel_id=1, source_target_pairs={{0,8},{4,12},{8,16},{12,20},{16,24},{20,28},{1,9},{5,13},{9,17},{1... | collective-permute-start | bytes 392 | tf_op jit(solution)/shard_map/ppermute | solution.py:14
  68.9 2.0 copy-start.4
  70.9 0.8 copy-start.11
  72.5 19.0 %copy-start.6 = (bf16[256,2048]{1,0:T(8,128)(2,1)}, bf16[256,2048]{1,0:T(8,128)(2,1)S(1)}, u32[]{:S(2)}) copy-start(bf16[256,2048]{1,0:T(8,128)(2,1)S(1)} %multiply_convert_fusion.5) | copy-start | bytes 3145732
  90.2 24.6 %collective-permute-start.8 = (bf16[256,2048]{1,0:T(8,128)(2,1)S(1)}, bf16[256,2048]{1,0:T(8,128)(2,1)S(1)}, u32[]{:S(2)}, u32[]{:S(2)}) collective-permute-start(bf16[256,2048]{1,0:T(8,128)(2,1)S(1)} %multiply_convert_fusion.5), channel_id=1, source_target_pairs={{8,0},{16,8},{24,16},{9,1},{17,9},{25,17},{10,2},{18,10},{26,18},{... | collective-permute-start | bytes 3145736 | tf_op jit(solution)/shard_map/ppermute | solution.py:205
  91.5 24.6 %collective-permute-start.7 = (bf16[256,2048]{1,0:T(8,128)(2,1)S(1)}, bf16[256,2048]{1,0:T(8,128)(2,1)S(1)}, u32[]{:S(2)}, u32[]{:S(2)}) collective-permute-start(bf16[256,2048]{1,0:T(8,128)(2,1)S(1)} %multiply_convert_fusion.5), channel_id=1, source_target_pairs={{0,8},{8,16},{16,24},{1,9},{9,17},{17,25},{2,10},{10,18},{18,26},{... | collective-permute-start | bytes 3145736 | tf_op jit(solution)/shard_map/ppermute | solution.py:202
  114.8 26.2 %collective-permute-start.9 = (bf16[256,2048]{1,0:T(8,128)(2,1)S(1)}, bf16[256,2048]{1,0:T(8,128)(2,1)}, u32[]{:S(2)}, u32[]{:S(2)}) collective-permute-start(bf16[256,2048]{1,0:T(8,128)(2,1)S(1)} %collective-permute-done.8), channel_id=1, source_target_pairs={{8,0},{16,8},{9,1},{17,9},{10,2},{18,10},{11,3},{19,11},{12,4},{20... | collective-permute-start | bytes 3145736 | tf_op jit(solution)/shard_map/ppermute | solution.py:205
  116.1 26.2 %collective-permute-start.11 = (bf16[256,2048]{1,0:T(8,128)(2,1)S(1)}, bf16[256,2048]{1,0:T(8,128)(2,1)S(1)}, u32[]{:S(2)}, u32[]{:S(2)}) collective-permute-start(bf16[256,2048]{1,0:T(8,128)(2,1)S(1)} %collective-permute-done.7), channel_id=1, source_target_pairs={{8,16},{16,24},{9,17},{17,25},{10,18},{18,26},{11,19},{19,27},{12,... | collective-permute-start | bytes 3145736 | tf_op jit(solution)/shard_map/ppermute | solution.py:202
  141.0 25.1 %collective-permute-start.10 = (bf16[256,2048]{1,0:T(8,128)(2,1)}, bf16[256,2048]{1,0:T(8,128)(2,1)}, u32[]{:S(2)}, u32[]{:S(2)}) collective-permute-start(bf16[256,2048]{1,0:T(8,128)(2,1)} %collective-permute-done.9), channel_id=1, source_target_pairs={{8,0},{9,1},{10,2},{11,3},{12,4},{13,5},{14,6},{15,7}} | collective-permute-start | bytes 3145736 | tf_op jit(solution)/shard_map/ppermute | solution.py:205
  142.4 5.0 %copy-start.5 = (bf16[2048,1024]{1,0:T(8,128)(2,1)S(1)}, bf16[2048,1024]{1,0:T(8,128)(2,1)}, u32[]{:S(2)}) copy-start(bf16[2048,1024]{1,0:T(8,128)(2,1)} %pad_maximum_fusion) | copy-start | bytes 12582916
  142.4 26.2 %collective-permute-start.12 = (bf16[256,2048]{1,0:T(8,128)(2,1)S(1)}, bf16[256,2048]{1,0:T(8,128)(2,1)S(1)}, u32[]{:S(2)}, u32[]{:S(2)}) collective-permute-start(bf16[256,2048]{1,0:T(8,128)(2,1)S(1)} %collective-permute-done.11), channel_id=1, source_target_pairs={{16,24},{17,25},{18,26},{19,27},{20,28},{21,29},{22,30},{23,31}} | collective-permute-start | bytes 3145736 | tf_op jit(solution)/shard_map/ppermute | solution.py:202
  170.5 1.9 copy-start.1
  173.9 4.4 %collective-permute-start.13 = (f32[2,256,1024]{2,1,0:T(8,128)}, f32[2,256,1024]{2,1,0:T(8,128)S(1)}, u32[]{:S(2)}, u32[]{:S(2)}) collective-permute-start(f32[2,256,1024]{2,1,0:T(8,128)} %pad_maximum_fusion.2), channel_id=1, source_target_pairs={{0,1},{1,0},{2,3},{3,2},{4,5},{5,4},{6,7},{7,6},{8,9},{9,8},{10,11... | collective-permute-start | bytes 6291464 | tf_op jit(solution)/shard_map/ppermute | solution.py:227
  179.6 14.0 %collective-permute-start.14 = (bf16[1,256,1024]{2,1,0:T(8,128)(2,1)S(1)}, bf16[1,256,1024]{2,1,0:T(8,128)(2,1)S(1)}, u32[]{:S(2)}, u32[]{:S(2)}) collective-permute-start(bf16[1,256,1024]{2,1,0:T(8,128)(2,1)S(1)} %fusion.27), channel_id=1, source_target_pairs={{0,2},{1,3},{2,0},{3,1},{4,6},{5,7},{6,4},{7,5},{8,10},{9,11},{10,... | collective-permute-start | bytes 1572872 | tf_op jit(solution)/shard_map/ppermute | solution.py:227
  195.2 26.0 %collective-permute-start.15 = (bf16[256,1024]{1,0:T(8,128)(2,1)S(1)}, bf16[256,1024]{1,0:T(8,128)(2,1)S(1)}, u32[]{:S(2)}, u32[]{:S(2)}) collective-permute-start(bf16[256,1024]{1,0:T(8,128)(2,1)S(1)} %fusion.37), channel_id=1, source_target_pairs={{0,0},{1,8},{2,16},{3,24},{8,1},{9,9},{10,17},{11,25},{16,2},{17,1... | collective-permute-start | bytes 1572872 | tf_op jit(solution)/shard_map/ppermute | solution.py:237

commit v8 on v5

--- a/solution.py
+++ b/solution.py
@@ -149,6 +149,15 @@
     )
     dev_decay = jnp.prod(blk_decay, axis=0)
     incoming = prefix_states(dev_decay, dev_state, ctx_axes, ctx_count)
+    if outer_axis is not None:
+        inner_count = ctx_count // tp_count
+        weight_pieces = [out_weight] + [
+            lax.ppermute(
+                out_weight, inner_axis, [(s, (s + d) % inner_count) for s in range(inner_count)]
+            )
+            for d in range(1, inner_count)
+        ]
+        weight_pieces, incoming = lax.optimization_barrier((weight_pieces, incoming))
 
     def advance(state_carry, block_in):
         scaled_k, b_k, c_k, cum_k, decay_k, state_k = block_in
@@ -175,6 +184,8 @@
         )
     outer_at = lax.axis_index(outer_axis)
     tp_at = lax.axis_index("tp")
+    inner_count = ctx_count // tp_count
+    inner_at = lax.axis_index(inner_axis)
     from_left, from_right = {}, {}
     going_right = going_left = hidden
     for step in range(1, tp_count):
@@ -189,9 +200,17 @@
         jnp.where(outer_at >= d, from_left[d], from_right[tp_count - d])
         for d in range(1, tp_count)
     ]
-    cols_all = lax.all_gather(out_weight, inner_axis, axis=1, tiled=True)
     by_source = jnp.stack(
-        [jnp.dot(rows, cols_all, preferred_element_type=jnp.float32) for rows in arrived]
+        [
+            jnp.concatenate(
+                [
+                    jnp.dot(rows, piece, preferred_element_type=jnp.float32)
+                    for piece in weight_pieces
+                ],
+                axis=1,
+            )
+            for rows in arrived
+        ]
     )
 
     def for_target(target):
@@ -214,7 +233,19 @@
             held[m ^ bit] = held[m ^ bit] + got[index].astype(jnp.float32)
         bit *= 2
     swap = [(o * tp_count + t, t * tp_count + o) for o in range(tp_count) for t in range(tp_count)]
-    return lax.ppermute(held[0].astype(jnp.bfloat16), (outer_axis, "tp"), swap)
+    rotated = lax.ppermute(held[0].astype(jnp.bfloat16), (outer_axis, "tp"), swap)
+    width = out_weight.shape[1]
+    pieces = jnp.stack([rotated[:, d * width : (d + 1) * width] for d in range(inner_count)])
+    inner_at = lax.axis_index(inner_axis)
+    return jnp.concatenate(
+        [
+            lax.dynamic_index_in_dim(
+                pieces, (inner_at - place + inner_count) % inner_count, 0, keepdims=False
+            )
+            for place in range(inner_count)
+        ],
+        axis=1,
+    )
 
 
 def solution(mesh):

time: 229 us -> 245 us (1.070)
  waiting for transfers between devices: 125 us -> 151 us
  between operations: 14 us -> 0.74 us
    ppermute x6, waiting for transfers between devices: 22.6 us -> 53.4 us  [shifted(): lax.ppermute(value, axis, [(source, source + steps) for source in range(f...]
    ppermute x3, waiting for transfers between devices: 60.7 us -> 54.8 us  [on_device(): lax.ppermute(going_left, outer_axis, [(s, s - 1) for s in range(1, tp_cou...]
    ppermute x1 -> x2, starting transfers between devices: 1.92 us -> 6.04 us  [the longest x1 4.04 us: on_device(): lax.ppermute(held[0].astype(jnp.bfloat16), (outer_axis, 'tp'), swap)]
    ppermute x6, starting transfers between devices: 24.7 us -> 21.6 us  [shifted(): lax.ppermute(value, axis, [(source, source + steps) for source in range(f...]
    dot_general x4 -> x8, matrix products: 10.3 us -> 12.5 us  [on_device(): jnp.dot(rows, piece, preferred_element_type=jnp.float32)]
    ppermute x1 -> x2, waiting for transfers between devices: 24.1 us -> 25.4 us  [the longest x1 25.4 us: on_device(): lax.ppermute(held[0].astype(jnp.bfloat16), (outer_axis, 'tp'), swap)]
  transfers between devices with their start and end apart: 16 -> 16, of which waited for: 10 -> 9; matrix products, arithmetic and copies ran while one was open for 10% -> 5% of each run, Pallas kernels for 0% -> 0%
where the time goes in v8:
time: 245 us; the launch traced here: 243 us
  waiting for transfers between devices  151 us (62%)
  starting transfers between devices  49.2 us (20%)
  matrix products  19.1 us (8%)
  other arithmetic  13.7 us (6%)
  local copies, waits for them, and re-layouts  9.22 us (4%)
    ppermute x3, waiting for transfers between devices, on_device(): lax.ppermute(going_left, outer_axis, [(s, s - 1) for s in range(1, tp_cou...  54.8 us
    ppermute x6, waiting for transfers between devices, shifted(): lax.ppermute(value, axis, [(source, source + steps) for source in range(f...  53.4 us
    ppermute x1, waiting for transfers between devices, on_device(): lax.ppermute(held[0].astype(jnp.bfloat16), (outer_axis, 'tp'), swap)  25.4 us
    ppermute x6, starting transfers between devices, shifted(): lax.ppermute(value, axis, [(source, source + steps) for source in range(f...  21.6 us
    ppermute x2, waiting for transfers between devices, on_device(): lax.ppermute(sent if bit == 1 else sent.astype(jnp.bfloat16), 'tp', [(s,...  17.9 us
    ppermute x3, starting transfers between devices, on_device(): lax.ppermute(going_right, outer_axis, [(s, s + 1) for s in range(step - 1...  16.9 us
    dot_general x8, matrix products, on_device(): jnp.dot(rows, piece, preferred_element_type=jnp.float32)  12.5 us
  transfers between devices with their start and end apart: 16, of which 9 were waited for; matrix products, arithmetic and copies ran while one was open for 5% of the time, Pallas kernels for 0%

profile of v8, /device:TPU:2, one launch (start us, length us, event | category | flops | bytes accessed | tf_op | source)
XLA Modules:
  0.0 243.4 jit_solution(17689548409164645241)
XLA Ops:
  0.0 1.3 constant_dynamic-update-slice_fusion.5
  1.5 3.4 %collective-permute-start = (bf16[3,2304]{1,0:T(4,128)(2,1)S(1)}, bf16[3,2304]{1,0:T(4,128)(2,1)S(1)}, u32[]{:S(2)}, u32[]{:S(2)}) collective-permute-start(bf16[3,2304]{1,0:T(4,128)(2,1)S(1)} %slice.99), channel_id=1, source_target_pairs={{0,4},{4,8},{8,12},{12,16},{16,20},{20,24},{24,28},{1,5},{5,9},{9,... | collective-permute-start | bytes 41480 | tf_op jit(solution)/shard_map/ppermute | solution.py:14
  4.9 0.6 reduce-window.6
  5.9 0.7 fusion.48
  7.7 1.5 multiply_convert_fusion.3
  9.3 1.6 slice_convert_fusion
  10.8 1.9 copy.27
  12.8 2.3 fusion.17
  15.2 3.5 %collective-permute-start.4 = (bf16[1,32,64,128]{3,2,1,0:T(8,128)(2,1)S(1)}, bf16[1,32,64,128]{3,2,1,0:T(8,128)(2,1)S(1)}, u32[]{:S(2)}, u32[]{:S(2)}) collective-permute-start(bf16[1,32,64,128]{3,2,1,0:T(8,128)(2,1)S(1)} %convert_bitcast_fusion), channel_id=1, source_target_pairs={{0,4},{4,8},{8,12},{12,16},{16,20},{20,24},{24,28},{1,5},{5,9},{9,... | collective-permute-start | bytes 1572872 | tf_op jit(solution)/shard_map/ppermute | solution.py:14
  18.7 2.0 collective-permute-start.1
  20.7 10.3 %collective-permute-done.4 = bf16[1,32,64,128]{3,2,1,0:T(8,128)(2,1)S(1)} collective-permute-done((bf16[1,32,64,128]{3,2,1,0:T(8,128)(2,1)S(1)}, bf16[1,32,64,128]{3,2,1,0:T(8,128)(2,1)S(1)}, u32[]{:S(2)}, u32[]{:S(2)}) %collective-permute-start.4) | collective-permute-done | bytes 524320 | tf_op jit(solution)/shard_map/ppermute | solution.py:14
  31.2 4.1 %collective-permute-start.5 = (bf16[1,32,64,128]{3,2,1,0:T(8,128)(2,1)S(1)}, bf16[1,32,64,128]{3,2,1,0:T(8,128)(2,1)S(1)}, u32[]{:S(2)}, u32[]{:S(2)}) collective-permute-start(bf16[1,32,64,128]{3,2,1,0:T(8,128)(2,1)S(1)} %fusion.25), channel_id=1, source_target_pairs={{0,8},{4,12},{8,16},{12,20},{16,24},{20,28},{1,9},{5,13},{9,17},{1... | collective-permute-start | bytes 1572872 | tf_op jit(solution)/shard_map/ppermute | solution.py:14
  35.2 3.8 %collective-permute-start.2 = (f32[1,32]{1,0:T(1,128)S(1)}, f32[1,32]{1,0:T(1,128)S(1)}, u32[]{:S(2)}, u32[]{:S(2)}) collective-permute-start(f32[1,32]{1,0:T(1,128)S(1)} %bitcast.106), channel_id=1, source_target_pairs={{0,4},{4,8},{8,12},{12,16},{16,20},{20,24},{24,28},{1,5},{5,9},{9,... | collective-permute-start | bytes 392 | tf_op jit(solution)/shard_map/ppermute | solution.py:14
  39.1 35.4 %collective-permute-done.2 = f32[1,32]{1,0:T(1,128)S(1)} collective-permute-done((f32[1,32]{1,0:T(1,128)S(1)}, f32[1,32]{1,0:T(1,128)S(1)}, u32[]{:S(2)}, u32[]{:S(2)}) %collective-permute-start.2) | collective-permute-done | bytes 160 | tf_op jit(solution)/shard_map/ppermute | solution.py:14
  74.9 4.5 %collective-permute-start.6 = (bf16[1,32,64,128]{3,2,1,0:T(8,128)(2,1)S(1)}, bf16[1,32,64,128]{3,2,1,0:T(8,128)(2,1)S(1)}, u32[]{:S(2)}, u32[]{:S(2)}) collective-permute-start(bf16[1,32,64,128]{3,2,1,0:T(8,128)(2,1)S(1)} %fusion.21), channel_id=1, source_target_pairs={{0,16},{4,20},{8,24},{12,28},{1,17},{5,21},{9,25},{13,29},{2,18},{... | collective-permute-start | bytes 1572872 | tf_op jit(solution)/shard_map/ppermute | solution.py:14
  79.4 2.3 collective-permute-start.3
  81.7 7.8 %collective-permute-done.3 = f32[1,32]{1,0:T(1,128)S(1)} collective-permute-done((f32[1,32]{1,0:T(1,128)S(1)}, f32[1,32]{1,0:T(1,128)S(1)}, u32[]{:S(2)}, u32[]{:S(2)}) %collective-permute-start.3) | collective-permute-done | bytes 160 | tf_op jit(solution)/shard_map/ppermute | solution.py:14
  90.5 0.9 copy-done.15
  91.4 3.7 %fusion.14 = f32[256,1,32,64]{0,3,2,1:T(8,128)} fusion(f32[32,64,256]{2,1,0:T(8,128)S(1)} %fusion.27, f32[256,1,32,64]{0,3,2,1:T(8,128)S(1)} %bitcast.95, f32[32,256]{1,0:T(8,128)S(1)} %bitcast.103, f32[256,256]{1,0:T(8,128)S(1)} %fusion.41, pred[256,256]{1,0:T(8,128)(4,1)S(1)} %iota_compare_fusion.1, f32[32]{0:T(128)S(1)} %copy-done.17, ...), kind=kOutput, calls=%fused_computation.26 | convolution fusion | flops 279969792 | bytes 8814720 | tf_op jit(solution)/shard_map/while/body/eval_jaxpr/gjts,sgjp->tgjp/dot_general | solution.py:46
  95.1 2.0 copy.32
  97.2 0.8 multiply_reduce_fusion
  97.9 0.8 multiply_convert_fusion.5
  98.8 1.6 collective-permute-start.8
  100.4 14.3 %collective-permute-start.7 = (bf16[256,2048]{1,0:T(8,128)(2,1)S(1)}, bf16[256,2048]{1,0:T(8,128)(2,1)}, u32[]{:S(2)}, u32[]{:S(2)}) collective-permute-start(bf16[256,2048]{1,0:T(8,128)(2,1)S(1)} %multiply_convert_fusion.5), channel_id=1, source_target_pairs={{0,8},{8,16},{16,24},{1,9},{9,17},{17,25},{2,10},{10,18},{18,26},{... | collective-permute-start | bytes 3145736 | tf_op jit(solution)/shard_map/ppermute | solution.py:192
  114.7 18.6 %collective-permute-done.8 = bf16[256,2048]{1,0:T(8,128)(2,1)} collective-permute-done((bf16[256,2048]{1,0:T(8,128)(2,1)S(1)}, bf16[256,2048]{1,0:T(8,128)(2,1)}, u32[]{:S(2)}, u32[]{:S(2)}) %collective-permute-start.8) | collective-permute-done | bytes 1048608 | tf_op jit(solution)/shard_map/ppermute | solution.py:195
  133.3 1.3 collective-permute-start.9
  134.6 1.7 collective-permute-start.11
  136.2 2.6 %fusion.50 = f32[256,512]{1,0:T(8,128)S(1)} fusion(bf16[256,2048]{1,0:T(8,128)(2,1)} %copy-done.3, bf16[2048,512]{1,0:T(8,128)(2,1)} %param.23), kind=kOutput, calls=%fused_computation.119 | convolution fusion | flops 536870912 | bytes 3670016 | tf_op jit(solution)/shard_map/dot_general | solution.py:207
  138.9 19.3 %collective-permute-done.9 = bf16[256,2048]{1,0:T(8,128)(2,1)} collective-permute-done((bf16[256,2048]{1,0:T(8,128)(2,1)}, bf16[256,2048]{1,0:T(8,128)(2,1)}, u32[]{:S(2)}, u32[]{:S(2)}) %collective-permute-start.9) | collective-permute-done | bytes 1048608 | tf_op jit(solution)/shard_map/ppermute | solution.py:195
  158.2 1.3 collective-permute-start.10
  159.5 0.7 fusion.51
  160.3 0.9 collective-permute-start.12
  161.3 1.9 fusion.33
  163.2 1.9 fusion.32
  165.3 16.8 %collective-permute-done.10 = bf16[256,2048]{1,0:T(8,128)(2,1)S(1)} collective-permute-done((bf16[256,2048]{1,0:T(8,128)(2,1)}, bf16[256,2048]{1,0:T(8,128)(2,1)S(1)}, u32[]{:S(2)}, u32[]{:S(2)}) %collective-permute-start.10) | collective-permute-done | bytes 1048608 | tf_op jit(solution)/shard_map/ppermute | solution.py:195
  182.1 0.7 fusion.31
  182.8 0.7 fusion.30
  183.6 1.9 fusion.35
  185.5 1.9 fusion.34
  188.4 1.7 copy-done.1
  190.1 1.5 pad_maximum_fusion.1
  191.6 4.4 %collective-permute-done.13 = f32[2,256,1024]{2,1,0:T(8,128)S(1)} collective-permute-done((f32[2,256,1024]{2,1,0:T(8,128)}, f32[2,256,1024]{2,1,0:T(8,128)S(1)}, u32[]{:S(2)}, u32[]{:S(2)}) %collective-permute-start.13) | collective-permute-done | bytes 2097184 | tf_op jit(solution)/shard_map/ppermute | solution.py:226
  196.0 1.4 fusion.22
  197.8 13.5 %collective-permute-done.14 = bf16[1,256,1024]{2,1,0:T(8,128)(2,1)S(1)} collective-permute-done((bf16[1,256,1024]{2,1,0:T(8,128)(2,1)S(1)}, bf16[1,256,1024]{2,1,0:T(8,128)(2,1)S(1)}, u32[]{:S(2)}, u32[]{:S(2)}) %collective-permute-start.14) | collective-permute-done | bytes 524320 | tf_op jit(solution)/shard_map/ppermute | solution.py:226
  211.3 1.5 fusion.26
  212.8 4.0 %collective-permute-start.15 = (bf16[256,1024]{1,0:T(8,128)(2,1)S(1)}, bf16[256,1024]{1,0:T(8,128)(2,1)S(1)}, u32[]{:S(2)}, u32[]{:S(2)}) collective-permute-start(bf16[256,1024]{1,0:T(8,128)(2,1)S(1)} %fusion.26), channel_id=1, source_target_pairs={{0,0},{1,8},{2,16},{3,24},{8,1},{9,9},{10,17},{11,25},{16,2},{17,1... | collective-permute-start | bytes 1572872 | tf_op jit(solution)/shard_map/ppermute | solution.py:236
  216.9 25.4 %collective-permute-done.15 = bf16[256,1024]{1,0:T(8,128)(2,1)S(1)} collective-permute-done((bf16[256,1024]{1,0:T(8,128)(2,1)S(1)}, bf16[256,1024]{1,0:T(8,128)(2,1)S(1)}, u32[]{:S(2)}, u32[]{:S(2)}) %collective-permute-start.15) | collective-permute-done | bytes 524320 | tf_op jit(solution)/shard_map/ppermute | solution.py:236
  242.6 0.9 pad_maximum_fusion.2
  (85 shorter events, 5.1 us)
Async XLA Ops:
  0.0 4.9 %copy-start = (f32[256,32]{0,1:T(8,128)S(1)}, f32[256,32]{0,1:T(8,128)}, u32[]{:S(2)}) copy-start(f32[256,32]{0,1:T(8,128)} %param.20) | copy-start | bytes 98308
  0.0 1.4 copy-start.6
  0.0 1.4 copy-start.7
  0.0 7.3 %copy-start.9 = (f32[4,2048]{1,0:T(4,128)S(1)}, f32[4,2048]{1,0:T(4,128)}, u32[]{:S(2)}) copy-start(f32[4,2048]{1,0:T(4,128)} %param.16) | copy-start | bytes 98308
  0.0 7.3 %copy-start.11 = (f32[4,128]{1,0:T(4,128)S(1)}, f32[4,128]{1,0:T(4,128)}, u32[]{:S(2)}) copy-start(f32[4,128]{1,0:T(4,128)} %param.17) | copy-start | bytes 6148
  0.0 7.3 %copy-start.12 = (f32[4,128]{1,0:T(4,128)S(1)}, f32[4,128]{1,0:T(4,128)}, u32[]{:S(2)}) copy-start(f32[4,128]{1,0:T(4,128)} %param.18) | copy-start | bytes 6148
  1.5 6.1 %collective-permute-start = (bf16[3,2304]{1,0:T(4,128)(2,1)S(1)}, bf16[3,2304]{1,0:T(4,128)(2,1)S(1)}, u32[]{:S(2)}, u32[]{:S(2)}) collective-permute-start(bf16[3,2304]{1,0:T(4,128)(2,1)S(1)} %slice.99), channel_id=1, source_target_pairs={{0,4},{4,8},{8,12},{12,16},{16,20},{20,24},{24,28},{1,5},{5,9},{9,... | collective-permute-start | bytes 41480 | tf_op jit(solution)/shard_map/ppermute | solution.py:14
  12.8 5.9 %copy-start.13 = (bf16[2048,512]{1,0:T(8,128)(2,1)S(1)}, bf16[2048,512]{1,0:T(8,128)(2,1)}, u32[]{:S(2)}) copy-start(bf16[2048,512]{1,0:T(8,128)(2,1)} %param.23) | copy-start | bytes 6291460
  15.2 15.7 %collective-permute-start.4 = (bf16[1,32,64,128]{3,2,1,0:T(8,128)(2,1)S(1)}, bf16[1,32,64,128]{3,2,1,0:T(8,128)(2,1)S(1)}, u32[]{:S(2)}, u32[]{:S(2)}) collective-permute-start(bf16[1,32,64,128]{3,2,1,0:T(8,128)(2,1)S(1)} %convert_bitcast_fusion), channel_id=1, source_target_pairs={{0,4},{4,8},{8,12},{12,16},{16,20},{20,24},{24,28},{1,5},{5,9},{9,... | collective-permute-start | bytes 1572872 | tf_op jit(solution)/shard_map/ppermute | solution.py:14
  18.7 71.4 %collective-permute-start.1 = (bf16[2048,512]{1,0:T(8,128)(2,1)S(1)}, bf16[2048,512]{1,0:T(8,128)(2,1)S(1)}, u32[]{:S(2)}, u32[]{:S(2)}) collective-permute-start(bf16[2048,512]{1,0:T(8,128)(2,1)S(1)} %copy-done.13), channel_id=1, source_target_pairs={{0,4},{4,0},{1,5},{5,1},{2,6},{6,2},{3,7},{7,3},{8,12},{12,8},{9,1... | collective-permute-start | bytes 6291464 | tf_op jit(solution)/shard_map/ppermute | solution.py:155
  31.0 50.7 %copy-start.5 = (f32[1,256,1,32]{1,2,3,0:T(1,128)S(1)}, f32[1,256,1,32]{1,2,3,0:T(1,128)}, u32[]{:S(2)}) copy-start(f32[1,256,1,32]{1,2,3,0:T(1,128)} %get-tuple-element.56) | copy-start | bytes 98308
  31.2 43.4 %collective-permute-start.5 = (bf16[1,32,64,128]{3,2,1,0:T(8,128)(2,1)S(1)}, bf16[1,32,64,128]{3,2,1,0:T(8,128)(2,1)S(1)}, u32[]{:S(2)}, u32[]{:S(2)}) collective-permute-start(bf16[1,32,64,128]{3,2,1,0:T(8,128)(2,1)S(1)} %fusion.25), channel_id=1, source_target_pairs={{0,8},{4,12},{8,16},{12,20},{16,24},{20,28},{1,9},{5,13},{9,17},{1... | collective-permute-start | bytes 1572872 | tf_op jit(solution)/shard_map/ppermute | solution.py:14
  35.2 39.3 %collective-permute-start.2 = (f32[1,32]{1,0:T(1,128)S(1)}, f32[1,32]{1,0:T(1,128)S(1)}, u32[]{:S(2)}, u32[]{:S(2)}) collective-permute-start(f32[1,32]{1,0:T(1,128)S(1)} %bitcast.106), channel_id=1, source_target_pairs={{0,4},{4,8},{8,12},{12,16},{16,20},{20,24},{24,28},{1,5},{5,9},{9,... | collective-permute-start | bytes 392 | tf_op jit(solution)/shard_map/ppermute | solution.py:14
  74.9 14.8 %collective-permute-start.6 = (bf16[1,32,64,128]{3,2,1,0:T(8,128)(2,1)S(1)}, bf16[1,32,64,128]{3,2,1,0:T(8,128)(2,1)S(1)}, u32[]{:S(2)}, u32[]{:S(2)}) collective-permute-start(bf16[1,32,64,128]{3,2,1,0:T(8,128)(2,1)S(1)} %fusion.21), channel_id=1, source_target_pairs={{0,16},{4,20},{8,24},{12,28},{1,17},{5,21},{9,25},{13,29},{2,18},{... | collective-permute-start | bytes 1572872 | tf_op jit(solution)/shard_map/ppermute | solution.py:14
  79.4 10.1 %collective-permute-start.3 = (f32[1,32]{1,0:T(1,128)S(1)}, f32[1,32]{1,0:T(1,128)S(1)}, u32[]{:S(2)}, u32[]{:S(2)}) collective-permute-start(f32[1,32]{1,0:T(1,128)S(1)} %bitcast_multiply_fusion.1), channel_id=1, source_target_pairs={{0,8},{4,12},{8,16},{12,20},{16,24},{20,28},{1,9},{5,13},{9,17},{1... | collective-permute-start | bytes 392 | tf_op jit(solution)/shard_map/ppermute | solution.py:14
  89.7 1.7 copy-start.8
  89.7 1.7 copy-start.17
  90.1 1.3 copy-start.15
  95.1 2.0 copy-start.2
  97.2 0.8 copy-start.10
  98.8 1.6 copy-start.3
  98.8 60.8 %copy-start.16 = (bf16[2048,512]{1,0:T(8,128)(2,1)S(1)}, bf16[2048,512]{1,0:T(8,128)(2,1)}, u32[]{:S(2)}) copy-start(bf16[2048,512]{1,0:T(8,128)(2,1)} %copy-done.15) | copy-start | bytes 6291460
  98.8 34.5 %collective-permute-start.8 = (bf16[256,2048]{1,0:T(8,128)(2,1)S(1)}, bf16[256,2048]{1,0:T(8,128)(2,1)}, u32[]{:S(2)}, u32[]{:S(2)}) collective-permute-start(bf16[256,2048]{1,0:T(8,128)(2,1)S(1)} %multiply_convert_fusion.5), channel_id=1, source_target_pairs={{8,0},{16,8},{24,16},{9,1},{17,9},{25,17},{10,2},{18,10},{26,18},{... | collective-permute-start | bytes 3145736 | tf_op jit(solution)/shard_map/ppermute | solution.py:195
  100.4 34.2 %collective-permute-start.7 = (bf16[256,2048]{1,0:T(8,128)(2,1)S(1)}, bf16[256,2048]{1,0:T(8,128)(2,1)}, u32[]{:S(2)}, u32[]{:S(2)}) collective-permute-start(bf16[256,2048]{1,0:T(8,128)(2,1)S(1)} %multiply_convert_fusion.5), channel_id=1, source_target_pairs={{0,8},{8,16},{16,24},{1,9},{9,17},{17,25},{2,10},{10,18},{18,26},{... | collective-permute-start | bytes 3145736 | tf_op jit(solution)/shard_map/ppermute | solution.py:192
  114.7 44.9 %copy-start.4 = (bf16[256,2048]{1,0:T(8,128)(2,1)S(1)}, bf16[256,2048]{1,0:T(8,128)(2,1)}, u32[]{:S(2)}) copy-start(bf16[256,2048]{1,0:T(8,128)(2,1)} %copy-done.3) | copy-start | bytes 3145732
  133.3 24.9 %collective-permute-start.9 = (bf16[256,2048]{1,0:T(8,128)(2,1)}, bf16[256,2048]{1,0:T(8,128)(2,1)}, u32[]{:S(2)}, u32[]{:S(2)}) collective-permute-start(bf16[256,2048]{1,0:T(8,128)(2,1)} %collective-permute-done.8), channel_id=1, source_target_pairs={{8,0},{16,8},{9,1},{17,9},{10,2},{18,10},{11,3},{19,11},{12,4},{20... | collective-permute-start | bytes 3145736 | tf_op jit(solution)/shard_map/ppermute | solution.py:195
  134.6 25.8 %collective-permute-start.11 = (bf16[256,2048]{1,0:T(8,128)(2,1)}, bf16[256,2048]{1,0:T(8,128)(2,1)}, u32[]{:S(2)}, u32[]{:S(2)}) collective-permute-start(bf16[256,2048]{1,0:T(8,128)(2,1)} %collective-permute-done.7), channel_id=1, source_target_pairs={{8,16},{16,24},{9,17},{17,25},{10,18},{18,26},{11,19},{19,27},{12,... | collective-permute-start | bytes 3145736 | tf_op jit(solution)/shard_map/ppermute | solution.py:192
  138.9 22.4 %copy-start.14 = (bf16[2048,512]{1,0:T(8,128)(2,1)S(1)}, bf16[2048,512]{1,0:T(8,128)(2,1)}, u32[]{:S(2)}) copy-start(bf16[2048,512]{1,0:T(8,128)(2,1)} %param.23) | copy-start | bytes 6291460
  158.2 23.8 %collective-permute-start.10 = (bf16[256,2048]{1,0:T(8,128)(2,1)}, bf16[256,2048]{1,0:T(8,128)(2,1)S(1)}, u32[]{:S(2)}, u32[]{:S(2)}) collective-permute-start(bf16[256,2048]{1,0:T(8,128)(2,1)} %collective-permute-done.9), channel_id=1, source_target_pairs={{8,0},{9,1},{10,2},{11,3},{12,4},{13,5},{14,6},{15,7}} | collective-permute-start | bytes 3145736 | tf_op jit(solution)/shard_map/ppermute | solution.py:195
  160.3 23.2 %collective-permute-start.12 = (bf16[256,2048]{1,0:T(8,128)(2,1)}, bf16[256,2048]{1,0:T(8,128)(2,1)S(1)}, u32[]{:S(2)}, u32[]{:S(2)}) collective-permute-start(bf16[256,2048]{1,0:T(8,128)(2,1)} %collective-permute-done.11), channel_id=1, source_target_pairs={{16,24},{17,25},{18,26},{19,27},{20,28},{21,29},{22,30},{23,31}} | collective-permute-start | bytes 3145736 | tf_op jit(solution)/shard_map/ppermute | solution.py:192
  188.2 2.0 copy-start.1
  191.6 4.4 %collective-permute-start.13 = (f32[2,256,1024]{2,1,0:T(8,128)}, f32[2,256,1024]{2,1,0:T(8,128)S(1)}, u32[]{:S(2)}, u32[]{:S(2)}) collective-permute-start(f32[2,256,1024]{2,1,0:T(8,128)} %pad_maximum_fusion.1), channel_id=1, source_target_pairs={{0,1},{1,0},{2,3},{3,2},{4,5},{5,4},{6,7},{7,6},{8,9},{9,8},{10,11... | collective-permute-start | bytes 6291464 | tf_op jit(solution)/shard_map/ppermute | solution.py:226
  197.3 14.0 %collective-permute-start.14 = (bf16[1,256,1024]{2,1,0:T(8,128)(2,1)S(1)}, bf16[1,256,1024]{2,1,0:T(8,128)(2,1)S(1)}, u32[]{:S(2)}, u32[]{:S(2)}) collective-permute-start(bf16[1,256,1024]{2,1,0:T(8,128)(2,1)S(1)} %fusion.22), channel_id=1, source_target_pairs={{0,2},{1,3},{2,0},{3,1},{4,6},{5,7},{6,4},{7,5},{8,10},{9,11},{10,... | collective-permute-start | bytes 1572872 | tf_op jit(solution)/shard_map/ppermute | solution.py:226
  212.8 29.5 %collective-permute-start.15 = (bf16[256,1024]{1,0:T(8,128)(2,1)S(1)}, bf16[256,1024]{1,0:T(8,128)(2,1)S(1)}, u32[]{:S(2)}, u32[]{:S(2)}) collective-permute-start(bf16[256,1024]{1,0:T(8,128)(2,1)S(1)} %fusion.26), channel_id=1, source_target_pairs={{0,0},{1,8},{2,16},{3,24},{8,1},{9,9},{10,17},{11,25},{16,2},{17,1... | collective-permute-start | bytes 1572872 | tf_op jit(solution)/shard_map/ppermute | solution.py:236

commit v9 on v8

--- a/solution.py
+++ b/solution.py
@@ -149,15 +149,6 @@
     )
     dev_decay = jnp.prod(blk_decay, axis=0)
     incoming = prefix_states(dev_decay, dev_state, ctx_axes, ctx_count)
-    if outer_axis is not None:
-        inner_count = ctx_count // tp_count
-        weight_pieces = [out_weight] + [
-            lax.ppermute(
-                out_weight, inner_axis, [(s, (s + d) % inner_count) for s in range(inner_count)]
-            )
-            for d in range(1, inner_count)
-        ]
-        weight_pieces, incoming = lax.optimization_barrier((weight_pieces, incoming))
 
     def advance(state_carry, block_in):
         scaled_k, b_k, c_k, cum_k, decay_k, state_k = block_in
@@ -185,7 +176,13 @@
     outer_at = lax.axis_index(outer_axis)
     tp_at = lax.axis_index("tp")
     inner_count = ctx_count // tp_count
-    inner_at = lax.axis_index(inner_axis)
+    weight_pieces = [out_weight] + [
+        lax.ppermute(
+            out_weight, inner_axis, [(s, (s + d) % inner_count) for s in range(inner_count)]
+        )
+        for d in range(1, inner_count)
+    ]
+    weight_pieces, hidden = lax.optimization_barrier((weight_pieces, hidden))
     from_left, from_right = {}, {}
     going_right = going_left = hidden
     for step in range(1, tp_count):

time: 245 us -> 217 us (0.89)
  waiting for transfers between devices: 151 us -> 129 us
  starting transfers between devices: 49.2 us -> 39.7 us
  matrix products: 19.1 us -> 25.9 us
    ppermute x6, waiting for transfers between devices: 53.4 us -> 21.2 us  [shifted(): lax.ppermute(value, axis, [(source, source + steps) for source in range(f...]
    ppermute x1, waiting for transfers between devices: 0.01 us -> 15.9 us  [on_device(): lax.ppermute(out_weight, inner_axis, [(s, (s + d) % inner_count) for s in...]
    ppermute x3, starting transfers between devices: 16.9 us -> 7.18 us  [on_device(): lax.ppermute(going_right, outer_axis, [(s, s + 1) for s in range(step - 1...]
    dot_general x8, matrix products: 12.5 us -> 19.3 us  [on_device(): jnp.dot(rows, piece, preferred_element_type=jnp.float32)]
    ppermute x3, waiting for transfers between devices: 54.8 us -> 48.4 us  [on_device(): lax.ppermute(going_left, outer_axis, [(s, s - 1) for s in range(1, tp_cou...]
  transfers between devices with their start and end apart: 16 -> 16, of which waited for: 9 -> 10; matrix products, arithmetic and copies ran while one was open for 5% -> 12% of each run, Pallas kernels for 0% -> 0%
where the time goes in v9:
time: 217 us
  waiting for transfers between devices  129 us (59%)
  starting transfers between devices  39.7 us (18%)
  matrix products  25.9 us (12%)
  other arithmetic  13.4 us (6%)
  local copies, waits for them, and re-layouts  8.3 us (4%)
    ppermute x3, waiting for transfers between devices, on_device(): lax.ppermute(going_left, outer_axis, [(s, s - 1) for s in range(1, tp_cou...  48.4 us
    ppermute x1, waiting for transfers between devices, on_device(): lax.ppermute(held[0].astype(jnp.bfloat16), (outer_axis, 'tp'), swap)  25.2 us
    ppermute x6, starting transfers between devices, shifted(): lax.ppermute(value, axis, [(source, source + steps) for source in range(f...  23.7 us
    ppermute x6, waiting for transfers between devices, shifted(): lax.ppermute(value, axis, [(source, source + steps) for source in range(f...  21.2 us
    dot_general x8, matrix products, on_device(): jnp.dot(rows, piece, preferred_element_type=jnp.float32)  19.3 us
    ppermute x2, waiting for transfers between devices, on_device(): lax.ppermute(sent if bit == 1 else sent.astype(jnp.bfloat16), 'tp', [(s,...  17.8 us
    ppermute x1, waiting for transfers between devices, on_device(): lax.ppermute(out_weight, inner_axis, [(s, (s + d) % inner_count) for s in...  15.9 us
    ppermute x3, starting transfers between devices, on_device(): lax.ppermute(going_right, outer_axis, [(s, s + 1) for s in range(step - 1...  7.18 us
  transfers between devices with their start and end apart: 16, of which 10 were waited for; matrix products, arithmetic and copies ran while one was open for 12% of the time, Pallas kernels for 0%

profile of v9, /device:TPU:2, one launch (start us, length us, event | category | flops | bytes accessed | tf_op | source)
XLA Modules:
  0.0 216.6 jit_solution(16485904984259221864)
XLA Ops:
  0.0 1.3 constant_dynamic-update-slice_fusion.5
  1.5 3.4 %collective-permute-start.1 = (bf16[3,2304]{1,0:T(4,128)(2,1)S(1)}, bf16[3,2304]{1,0:T(4,128)(2,1)S(1)}, u32[]{:S(2)}, u32[]{:S(2)}) collective-permute-start(bf16[3,2304]{1,0:T(4,128)(2,1)S(1)} %slice.99), channel_id=1, source_target_pairs={{0,4},{4,8},{8,12},{12,16},{16,20},{20,24},{24,28},{1,5},{5,9},{9,... | collective-permute-start | bytes 41480 | tf_op jit(solution)/shard_map/ppermute | solution.py:14
  5.9 0.7 fusion.51
  7.7 1.5 multiply_convert_fusion.3
  9.3 1.6 slice_convert_fusion
  10.9 1.9 copy.27
  12.8 2.2 %fusion.17 = f32[32,64,128]{2,1,0:T(8,128)S(1)} fusion(f32[256,32]{0,1:T(8,128)S(1)} %bitcast.101, f32[256,128]{1,0:T(8,128)S(1)} %slice_convert_fusion.1, f32[32]{0:T(128)S(1)} %get-tuple-element.71, f32[256,32,64]{0,2,1:T(8,128)S(1)} %bitcast.93, f32[256,32]{0,1:T(8,128)} %param.19), kind=kOutput, calls=%fused_computation.32 | convolution fusion | flops 137625600 | bytes 3342464 | tf_op jit(solution)/shard_map/vmap(sgjp,sgjn->gjpn)/dot_general | solution.py:54
  15.1 3.5 %collective-permute-start.4 = (bf16[1,32,64,128]{3,2,1,0:T(8,128)(2,1)S(1)}, bf16[1,32,64,128]{3,2,1,0:T(8,128)(2,1)S(1)}, u32[]{:S(2)}, u32[]{:S(2)}) collective-permute-start(bf16[1,32,64,128]{3,2,1,0:T(8,128)(2,1)S(1)} %convert_bitcast_fusion), channel_id=1, source_target_pairs={{0,4},{4,8},{8,12},{12,16},{16,20},{20,24},{24,28},{1,5},{5,9},{9,... | collective-permute-start | bytes 1572872 | tf_op jit(solution)/shard_map/ppermute | solution.py:14
  18.5 10.9 %collective-permute-done.4 = bf16[1,32,64,128]{3,2,1,0:T(8,128)(2,1)S(1)} collective-permute-done((bf16[1,32,64,128]{3,2,1,0:T(8,128)(2,1)S(1)}, bf16[1,32,64,128]{3,2,1,0:T(8,128)(2,1)S(1)}, u32[]{:S(2)}, u32[]{:S(2)}) %collective-permute-start.4) | collective-permute-done | bytes 524320 | tf_op jit(solution)/shard_map/ppermute | solution.py:14
  29.6 5.4 %collective-permute-start.5 = (bf16[1,32,64,128]{3,2,1,0:T(8,128)(2,1)S(1)}, bf16[1,32,64,128]{3,2,1,0:T(8,128)(2,1)S(1)}, u32[]{:S(2)}, u32[]{:S(2)}) collective-permute-start(bf16[1,32,64,128]{3,2,1,0:T(8,128)(2,1)S(1)} %fusion.26), channel_id=1, source_target_pairs={{0,8},{4,12},{8,16},{12,20},{16,24},{20,28},{1,9},{5,13},{9,17},{1... | collective-permute-start | bytes 1572872 | tf_op jit(solution)/shard_map/ppermute | solution.py:14
  35.0 2.5 %collective-permute-start.2 = (f32[1,32]{1,0:T(1,128)S(1)}, f32[1,32]{1,0:T(1,128)S(1)}, u32[]{:S(2)}, u32[]{:S(2)}) collective-permute-start(f32[1,32]{1,0:T(1,128)S(1)} %bitcast.107), channel_id=1, source_target_pairs={{0,4},{4,8},{8,12},{12,16},{16,20},{20,24},{24,28},{1,5},{5,9},{9,... | collective-permute-start | bytes 392 | tf_op jit(solution)/shard_map/ppermute | solution.py:14
  37.5 2.5 %collective-permute-start = (bf16[2048,512]{1,0:T(8,128)(2,1)}, bf16[2048,512]{1,0:T(8,128)(2,1)}, u32[]{:S(2)}, u32[]{:S(2)}) collective-permute-start(bf16[2048,512]{1,0:T(8,128)(2,1)} %param.23), channel_id=1, source_target_pairs={{0,4},{4,0},{1,5},{5,1},{2,6},{6,2},{3,7},{7,3},{8,12},{12,8},{9,1... | collective-permute-start | bytes 6291464 | tf_op jit(solution)/shard_map/ppermute | solution.py:180
  40.0 4.5 %collective-permute-done.5 = bf16[1,32,64,128]{3,2,1,0:T(8,128)(2,1)S(1)} collective-permute-done((bf16[1,32,64,128]{3,2,1,0:T(8,128)(2,1)S(1)}, bf16[1,32,64,128]{3,2,1,0:T(8,128)(2,1)S(1)}, u32[]{:S(2)}, u32[]{:S(2)}) %collective-permute-start.5) | collective-permute-done | bytes 524320 | tf_op jit(solution)/shard_map/ppermute | solution.py:14
  44.9 6.0 %collective-permute-start.6 = (bf16[1,32,64,128]{3,2,1,0:T(8,128)(2,1)S(1)}, bf16[1,32,64,128]{3,2,1,0:T(8,128)(2,1)S(1)}, u32[]{:S(2)}, u32[]{:S(2)}) collective-permute-start(bf16[1,32,64,128]{3,2,1,0:T(8,128)(2,1)S(1)} %fusion.22), channel_id=1, source_target_pairs={{0,16},{4,20},{8,24},{12,28},{1,17},{5,21},{9,25},{13,29},{2,18},{... | collective-permute-start | bytes 1572872 | tf_op jit(solution)/shard_map/ppermute | solution.py:14
  50.9 3.0 %collective-permute-start.3 = (f32[1,32]{1,0:T(1,128)S(1)}, f32[1,32]{1,0:T(1,128)S(1)}, u32[]{:S(2)}, u32[]{:S(2)}) collective-permute-start(f32[1,32]{1,0:T(1,128)S(1)} %bitcast_multiply_fusion.1), channel_id=1, source_target_pairs={{0,8},{4,12},{8,16},{12,20},{16,24},{20,28},{1,9},{5,13},{9,17},{1... | collective-permute-start | bytes 392 | tf_op jit(solution)/shard_map/ppermute | solution.py:14
  53.9 5.9 %collective-permute-done.3 = f32[1,32]{1,0:T(1,128)S(1)} collective-permute-done((f32[1,32]{1,0:T(1,128)S(1)}, f32[1,32]{1,0:T(1,128)S(1)}, u32[]{:S(2)}, u32[]{:S(2)}) %collective-permute-start.3) | collective-permute-done | bytes 160 | tf_op jit(solution)/shard_map/ppermute | solution.py:14
  60.5 3.7 %fusion.14 = f32[256,1,32,64]{0,3,2,1:T(8,128)} fusion(f32[32,64,256]{2,1,0:T(8,128)S(1)} %fusion.29, f32[256,1,32,64]{0,3,2,1:T(8,128)S(1)} %bitcast.95, f32[32,256]{1,0:T(8,128)S(1)} %bitcast.103, f32[256,256]{1,0:T(8,128)S(1)} %fusion.44, pred[256,256]{1,0:T(8,128)(4,1)S(1)} %iota_compare_fusion.1, f32[32]{0:T(128)S(1)} %copy-done.13, ...), kind=kOutput, calls=%fused_computation.26 | convolution fusion | flops 279969792 | bytes 8814720 | tf_op jit(solution)/shard_map/while/body/eval_jaxpr/gjts,sgjp->tgjp/dot_general | solution.py:46
  64.2 2.0 copy.32
  66.2 0.8 multiply_reduce_fusion
  67.0 0.8 multiply_convert_fusion.5
  67.8 15.9 %collective-permute-done = bf16[2048,512]{1,0:T(8,128)(2,1)} collective-permute-done((bf16[2048,512]{1,0:T(8,128)(2,1)}, bf16[2048,512]{1,0:T(8,128)(2,1)}, u32[]{:S(2)}, u32[]{:S(2)}) %collective-permute-start) | collective-permute-done | bytes 2097184 | tf_op jit(solution)/shard_map/ppermute | solution.py:180
  83.8 1.3 collective-permute-start.8
  85.1 4.6 %collective-permute-start.7 = (bf16[256,2048]{1,0:T(8,128)(2,1)S(1)}, bf16[256,2048]{1,0:T(8,128)(2,1)S(1)}, u32[]{:S(2)}, u32[]{:S(2)}) collective-permute-start(bf16[256,2048]{1,0:T(8,128)(2,1)S(1)} %multiply_convert_fusion.5), channel_id=1, source_target_pairs={{0,8},{8,16},{16,24},{1,9},{9,17},{17,25},{2,10},{10,18},{18,26},{... | collective-permute-start | bytes 3145736 | tf_op jit(solution)/shard_map/ppermute | solution.py:189
  89.7 18.1 %collective-permute-done.8 = bf16[256,2048]{1,0:T(8,128)(2,1)S(1)} collective-permute-done((bf16[256,2048]{1,0:T(8,128)(2,1)S(1)}, bf16[256,2048]{1,0:T(8,128)(2,1)S(1)}, u32[]{:S(2)}, u32[]{:S(2)}) %collective-permute-start.8) | collective-permute-done | bytes 1048608 | tf_op jit(solution)/shard_map/ppermute | solution.py:192
  107.9 1.3 collective-permute-start.9
  109.2 1.7 collective-permute-start.11
  110.8 2.6 %fusion.53 = f32[256,512]{1,0:T(8,128)S(1)} fusion(bf16[256,2048]{1,0:T(8,128)(2,1)} %copy-done.3, bf16[2048,512]{1,0:T(8,128)(2,1)} %param.23), kind=kOutput, calls=%fused_computation.121 | convolution fusion | flops 536870912 | bytes 3670016 | tf_op jit(solution)/shard_map/dot_general | solution.py:204
  113.4 17.7 %collective-permute-done.9 = bf16[256,2048]{1,0:T(8,128)(2,1)} collective-permute-done((bf16[256,2048]{1,0:T(8,128)(2,1)S(1)}, bf16[256,2048]{1,0:T(8,128)(2,1)}, u32[]{:S(2)}, u32[]{:S(2)}) %collective-permute-start.9) | collective-permute-done | bytes 1048608 | tf_op jit(solution)/shard_map/ppermute | solution.py:192
  131.2 1.3 collective-permute-start.10
  132.5 2.3 %fusion.54 = f32[256,512]{1,0:T(8,128)S(1)} fusion(bf16[256,2048]{1,0:T(8,128)(2,1)S(1)} %copy-done.4, bf16[2048,512]{1,0:T(8,128)(2,1)} %collective-permute-done), kind=kOutput, calls=%fused_computation.122 | convolution fusion | flops 536870912 | bytes 3670016 | tf_op jit(solution)/shard_map/dot_general | solution.py:204
  134.9 0.9 collective-permute-start.12
  135.8 2.6 %fusion.36 = f32[256,512]{1,0:T(8,128)S(1)} fusion(bf16[2048,512]{1,0:T(8,128)(2,1)} %param.23, bf16[256,2048]{1,0:T(8,128)(2,1)} %collective-permute-done.11, bf16[256,2048]{1,0:T(8,128)(2,1)} %collective-permute-done.9, pred[]{:T(512)S(6)} %ge.33), kind=kOutput, calls=%fused_computation.70 | convolution fusion | flops 537395200 | bytes 4718593 | tf_op jit(solution)/shard_map/dot_general | solution.py:204
  138.4 2.6 %fusion.35 = f32[256,512]{1,0:T(8,128)S(1)} fusion(bf16[2048,512]{1,0:T(8,128)(2,1)} %collective-permute-done, bf16[256,2048]{1,0:T(8,128)(2,1)} %collective-permute-done.11, bf16[256,2048]{1,0:T(8,128)(2,1)} %collective-permute-done.9, pred[]{:T(512)S(6)} %ge.33), kind=kOutput, calls=%fused_computation.69 | convolution fusion | flops 537395200 | bytes 4718593 | tf_op jit(solution)/shard_map/dot_general | solution.py:204
  141.2 12.6 %collective-permute-done.10 = bf16[256,2048]{1,0:T(8,128)(2,1)S(1)} collective-permute-done((bf16[256,2048]{1,0:T(8,128)(2,1)}, bf16[256,2048]{1,0:T(8,128)(2,1)S(1)}, u32[]{:S(2)}, u32[]{:S(2)}) %collective-permute-start.10) | collective-permute-done | bytes 1048608 | tf_op jit(solution)/shard_map/ppermute | solution.py:192
  153.7 2.3 %fusion.34 = f32[256,512]{1,0:T(8,128)S(1)} fusion(bf16[2048,512]{1,0:T(8,128)(2,1)} %param.23, bf16[256,2048]{1,0:T(8,128)(2,1)S(1)} %collective-permute-done.7, bf16[256,2048]{1,0:T(8,128)(2,1)S(1)} %collective-permute-done.10, pred[]{:T(512)S(6)} %ge.32), kind=kOutput, calls=%fused_computation.68 | convolution fusion | flops 537395200 | bytes 4718593 | tf_op jit(solution)/shard_map/dot_general | solution.py:204
  156.0 2.3 %fusion.33 = f32[256,512]{1,0:T(8,128)S(1)} fusion(bf16[2048,512]{1,0:T(8,128)(2,1)} %collective-permute-done, bf16[256,2048]{1,0:T(8,128)(2,1)S(1)} %collective-permute-done.7, bf16[256,2048]{1,0:T(8,128)(2,1)S(1)} %collective-permute-done.10, pred[]{:T(512)S(6)} %ge.32), kind=kOutput, calls=%fused_computation.67 | convolution fusion | flops 537395200 | bytes 4718593 | tf_op jit(solution)/shard_map/dot_general | solution.py:204
  158.4 2.3 %fusion.38 = f32[256,512]{1,0:T(8,128)S(1)} fusion(bf16[2048,512]{1,0:T(8,128)(2,1)} %param.23, bf16[256,2048]{1,0:T(8,128)(2,1)S(1)} %collective-permute-done.12, bf16[256,2048]{1,0:T(8,128)(2,1)S(1)} %collective-permute-done.8, pred[]{:T(512)S(6)} %ge.34), kind=kOutput, calls=%fused_computation.72 | convolution fusion | flops 537395200 | bytes 4718593 | tf_op jit(solution)/shard_map/dot_general | solution.py:204
  160.7 2.3 %fusion.37 = f32[256,512]{1,0:T(8,128)S(1)} fusion(bf16[2048,512]{1,0:T(8,128)(2,1)} %collective-permute-done, bf16[256,2048]{1,0:T(8,128)(2,1)S(1)} %collective-permute-done.12, bf16[256,2048]{1,0:T(8,128)(2,1)S(1)} %collective-permute-done.8, pred[]{:T(512)S(6)} %ge.34), kind=kOutput, calls=%fused_computation.71 | convolution fusion | flops 537395200 | bytes 4718593 | tf_op jit(solution)/shard_map/dot_general | solution.py:204
  164.0 1.7 copy-done.1
  165.6 1.5 pad_maximum_fusion.1
  167.1 4.4 %collective-permute-done.13 = f32[2,256,1024]{2,1,0:T(8,128)S(1)} collective-permute-done((f32[2,256,1024]{2,1,0:T(8,128)}, f32[2,256,1024]{2,1,0:T(8,128)S(1)}, u32[]{:S(2)}, u32[]{:S(2)}) %collective-permute-start.13) | collective-permute-done | bytes 2097184 | tf_op jit(solution)/shard_map/ppermute | solution.py:223
  171.5 1.4 fusion.23
  172.8 0.6 collective-permute-start.14
  173.5 13.4 %collective-permute-done.14 = bf16[1,256,1024]{2,1,0:T(8,128)(2,1)S(1)} collective-permute-done((bf16[1,256,1024]{2,1,0:T(8,128)(2,1)S(1)}, bf16[1,256,1024]{2,1,0:T(8,128)(2,1)S(1)}, u32[]{:S(2)}, u32[]{:S(2)}) %collective-permute-start.14) | collective-permute-done | bytes 524320 | tf_op jit(solution)/shard_map/ppermute | solution.py:223
  186.9 1.5 fusion.27
  188.3 1.9 collective-permute-start.15
  190.3 25.2 %collective-permute-done.15 = bf16[256,1024]{1,0:T(8,128)(2,1)S(1)} collective-permute-done((bf16[256,1024]{1,0:T(8,128)(2,1)S(1)}, bf16[256,1024]{1,0:T(8,128)(2,1)S(1)}, u32[]{:S(2)}, u32[]{:S(2)}) %collective-permute-start.15) | collective-permute-done | bytes 524320 | tf_op jit(solution)/shard_map/ppermute | solution.py:233
  215.7 0.9 pad_maximum_fusion.2
  (76 shorter events, 4.9 us)
Async XLA Ops:
  0.0 4.9 %copy-start = (f32[256,32]{0,1:T(8,128)S(1)}, f32[256,32]{0,1:T(8,128)}, u32[]{:S(2)}) copy-start(f32[256,32]{0,1:T(8,128)} %param.20) | copy-start | bytes 98308
  0.0 1.4 copy-start.6
  0.0 1.4 copy-start.7
  0.0 7.3 %copy-start.9 = (f32[4,2048]{1,0:T(4,128)S(1)}, f32[4,2048]{1,0:T(4,128)}, u32[]{:S(2)}) copy-start(f32[4,2048]{1,0:T(4,128)} %param.16) | copy-start | bytes 98308
  0.0 7.3 %copy-start.11 = (f32[4,128]{1,0:T(4,128)S(1)}, f32[4,128]{1,0:T(4,128)}, u32[]{:S(2)}) copy-start(f32[4,128]{1,0:T(4,128)} %param.17) | copy-start | bytes 6148
  0.0 7.3 %copy-start.12 = (f32[4,128]{1,0:T(4,128)S(1)}, f32[4,128]{1,0:T(4,128)}, u32[]{:S(2)}) copy-start(f32[4,128]{1,0:T(4,128)} %param.18) | copy-start | bytes 6148
  1.5 6.1 %collective-permute-start.1 = (bf16[3,2304]{1,0:T(4,128)(2,1)S(1)}, bf16[3,2304]{1,0:T(4,128)(2,1)S(1)}, u32[]{:S(2)}, u32[]{:S(2)}) collective-permute-start(bf16[3,2304]{1,0:T(4,128)(2,1)S(1)} %slice.99), channel_id=1, source_target_pairs={{0,4},{4,8},{8,12},{12,16},{16,20},{20,24},{24,28},{1,5},{5,9},{9,... | collective-permute-start | bytes 41480 | tf_op jit(solution)/shard_map/ppermute | solution.py:14
  15.1 14.3 %collective-permute-start.4 = (bf16[1,32,64,128]{3,2,1,0:T(8,128)(2,1)S(1)}, bf16[1,32,64,128]{3,2,1,0:T(8,128)(2,1)S(1)}, u32[]{:S(2)}, u32[]{:S(2)}) collective-permute-start(bf16[1,32,64,128]{3,2,1,0:T(8,128)(2,1)S(1)} %convert_bitcast_fusion), channel_id=1, source_target_pairs={{0,4},{4,8},{8,12},{12,16},{16,20},{20,24},{24,28},{1,5},{5,9},{9,... | collective-permute-start | bytes 1572872 | tf_op jit(solution)/shard_map/ppermute | solution.py:14
  29.4 24.4 %copy-start.5 = (f32[1,256,1,32]{1,2,3,0:T(1,128)S(1)}, f32[1,256,1,32]{1,2,3,0:T(1,128)}, u32[]{:S(2)}) copy-start(f32[1,256,1,32]{1,2,3,0:T(1,128)} %get-tuple-element.56) | copy-start | bytes 98308
  29.6 14.9 %collective-permute-start.5 = (bf16[1,32,64,128]{3,2,1,0:T(8,128)(2,1)S(1)}, bf16[1,32,64,128]{3,2,1,0:T(8,128)(2,1)S(1)}, u32[]{:S(2)}, u32[]{:S(2)}) collective-permute-start(bf16[1,32,64,128]{3,2,1,0:T(8,128)(2,1)S(1)} %fusion.26), channel_id=1, source_target_pairs={{0,8},{4,12},{8,16},{12,20},{16,24},{20,28},{1,9},{5,13},{9,17},{1... | collective-permute-start | bytes 1572872 | tf_op jit(solution)/shard_map/ppermute | solution.py:14
  35.0 5.0 %collective-permute-start.2 = (f32[1,32]{1,0:T(1,128)S(1)}, f32[1,32]{1,0:T(1,128)S(1)}, u32[]{:S(2)}, u32[]{:S(2)}) collective-permute-start(f32[1,32]{1,0:T(1,128)S(1)} %bitcast.107), channel_id=1, source_target_pairs={{0,4},{4,8},{8,12},{12,16},{16,20},{20,24},{24,28},{1,5},{5,9},{9,... | collective-permute-start | bytes 392 | tf_op jit(solution)/shard_map/ppermute | solution.py:14
  37.5 46.3 %collective-permute-start = (bf16[2048,512]{1,0:T(8,128)(2,1)}, bf16[2048,512]{1,0:T(8,128)(2,1)}, u32[]{:S(2)}, u32[]{:S(2)}) collective-permute-start(bf16[2048,512]{1,0:T(8,128)(2,1)} %param.23), channel_id=1, source_target_pairs={{0,4},{4,0},{1,5},{5,1},{2,6},{6,2},{3,7},{7,3},{8,12},{12,8},{9,1... | collective-permute-start | bytes 6291464 | tf_op jit(solution)/shard_map/ppermute | solution.py:180
  44.9 15.1 %collective-permute-start.6 = (bf16[1,32,64,128]{3,2,1,0:T(8,128)(2,1)S(1)}, bf16[1,32,64,128]{3,2,1,0:T(8,128)(2,1)S(1)}, u32[]{:S(2)}, u32[]{:S(2)}) collective-permute-start(bf16[1,32,64,128]{3,2,1,0:T(8,128)(2,1)S(1)} %fusion.22), channel_id=1, source_target_pairs={{0,16},{4,20},{8,24},{12,28},{1,17},{5,21},{9,25},{13,29},{2,18},{... | collective-permute-start | bytes 1572872 | tf_op jit(solution)/shard_map/ppermute | solution.py:14
  50.9 8.9 %collective-permute-start.3 = (f32[1,32]{1,0:T(1,128)S(1)}, f32[1,32]{1,0:T(1,128)S(1)}, u32[]{:S(2)}, u32[]{:S(2)}) collective-permute-start(f32[1,32]{1,0:T(1,128)S(1)} %bitcast_multiply_fusion.1), channel_id=1, source_target_pairs={{0,8},{4,12},{8,16},{12,20},{16,24},{20,28},{1,9},{5,13},{9,17},{1... | collective-permute-start | bytes 392 | tf_op jit(solution)/shard_map/ppermute | solution.py:14
  53.9 6.6 %copy-start.8 = (f32[256,32]{0,1:T(8,128)S(1)}, f32[256,32]{0,1:T(8,128)}, u32[]{:S(2)}) copy-start(f32[256,32]{0,1:T(8,128)} %param.19) | copy-start | bytes 98308
  53.9 6.6 %copy-start.13 = (f32[32]{0:T(128)S(1)}, f32[32]{0:T(128)}, u32[]{:S(2)}) copy-start(f32[32]{0:T(128)} %param.21) | copy-start | bytes 388
  64.2 2.0 copy-start.2
  66.2 0.8 copy-start.10
  67.8 17.2 %copy-start.3 = (bf16[256,2048]{1,0:T(8,128)(2,1)}, bf16[256,2048]{1,0:T(8,128)(2,1)S(1)}, u32[]{:S(2)}) copy-start(bf16[256,2048]{1,0:T(8,128)(2,1)S(1)} %multiply_convert_fusion.5) | copy-start | bytes 3145732
  83.8 24.1 %collective-permute-start.8 = (bf16[256,2048]{1,0:T(8,128)(2,1)S(1)}, bf16[256,2048]{1,0:T(8,128)(2,1)S(1)}, u32[]{:S(2)}, u32[]{:S(2)}) collective-permute-start(bf16[256,2048]{1,0:T(8,128)(2,1)S(1)} %multiply_convert_fusion.5), channel_id=1, source_target_pairs={{8,0},{16,8},{24,16},{9,1},{17,9},{25,17},{10,2},{18,10},{26,18},{... | collective-permute-start | bytes 3145736 | tf_op jit(solution)/shard_map/ppermute | solution.py:192
  85.1 24.1 %collective-permute-start.7 = (bf16[256,2048]{1,0:T(8,128)(2,1)S(1)}, bf16[256,2048]{1,0:T(8,128)(2,1)S(1)}, u32[]{:S(2)}, u32[]{:S(2)}) collective-permute-start(bf16[256,2048]{1,0:T(8,128)(2,1)S(1)} %multiply_convert_fusion.5), channel_id=1, source_target_pairs={{0,8},{8,16},{16,24},{1,9},{9,17},{17,25},{2,10},{10,18},{18,26},{... | collective-permute-start | bytes 3145736 | tf_op jit(solution)/shard_map/ppermute | solution.py:189
  89.7 42.7 %copy-start.4 = (bf16[256,2048]{1,0:T(8,128)(2,1)S(1)}, bf16[256,2048]{1,0:T(8,128)(2,1)}, u32[]{:S(2)}) copy-start(bf16[256,2048]{1,0:T(8,128)(2,1)} %copy-done.3) | copy-start | bytes 3145732
  107.9 23.3 %collective-permute-start.9 = (bf16[256,2048]{1,0:T(8,128)(2,1)S(1)}, bf16[256,2048]{1,0:T(8,128)(2,1)}, u32[]{:S(2)}, u32[]{:S(2)}) collective-permute-start(bf16[256,2048]{1,0:T(8,128)(2,1)S(1)} %collective-permute-done.8), channel_id=1, source_target_pairs={{8,0},{16,8},{9,1},{17,9},{10,2},{18,10},{11,3},{19,11},{12,4},{20... | collective-permute-start | bytes 3145736 | tf_op jit(solution)/shard_map/ppermute | solution.py:192
  109.2 25.7 %collective-permute-start.11 = (bf16[256,2048]{1,0:T(8,128)(2,1)S(1)}, bf16[256,2048]{1,0:T(8,128)(2,1)}, u32[]{:S(2)}, u32[]{:S(2)}) collective-permute-start(bf16[256,2048]{1,0:T(8,128)(2,1)S(1)} %collective-permute-done.7), channel_id=1, source_target_pairs={{8,16},{16,24},{9,17},{17,25},{10,18},{18,26},{11,19},{19,27},{12,... | collective-permute-start | bytes 3145736 | tf_op jit(solution)/shard_map/ppermute | solution.py:189
  131.2 22.6 %collective-permute-start.10 = (bf16[256,2048]{1,0:T(8,128)(2,1)}, bf16[256,2048]{1,0:T(8,128)(2,1)S(1)}, u32[]{:S(2)}, u32[]{:S(2)}) collective-permute-start(bf16[256,2048]{1,0:T(8,128)(2,1)} %collective-permute-done.9), channel_id=1, source_target_pairs={{8,0},{9,1},{10,2},{11,3},{12,4},{13,5},{14,6},{15,7}} | collective-permute-start | bytes 3145736 | tf_op jit(solution)/shard_map/ppermute | solution.py:192
  134.9 23.6 %collective-permute-start.12 = (bf16[256,2048]{1,0:T(8,128)(2,1)}, bf16[256,2048]{1,0:T(8,128)(2,1)S(1)}, u32[]{:S(2)}, u32[]{:S(2)}) collective-permute-start(bf16[256,2048]{1,0:T(8,128)(2,1)} %collective-permute-done.11), channel_id=1, source_target_pairs={{16,24},{17,25},{18,26},{19,27},{20,28},{21,29},{22,30},{23,31}} | collective-permute-start | bytes 3145736 | tf_op jit(solution)/shard_map/ppermute | solution.py:189
  163.7 1.9 copy-start.1
  167.1 4.4 %collective-permute-start.13 = (f32[2,256,1024]{2,1,0:T(8,128)}, f32[2,256,1024]{2,1,0:T(8,128)S(1)}, u32[]{:S(2)}, u32[]{:S(2)}) collective-permute-start(f32[2,256,1024]{2,1,0:T(8,128)} %pad_maximum_fusion.1), channel_id=1, source_target_pairs={{0,1},{1,0},{2,3},{3,2},{4,5},{5,4},{6,7},{7,6},{8,9},{9,8},{10,11... | collective-permute-start | bytes 6291464 | tf_op jit(solution)/shard_map/ppermute | solution.py:223
  172.8 14.0 %collective-permute-start.14 = (bf16[1,256,1024]{2,1,0:T(8,128)(2,1)S(1)}, bf16[1,256,1024]{2,1,0:T(8,128)(2,1)S(1)}, u32[]{:S(2)}, u32[]{:S(2)}) collective-permute-start(bf16[1,256,1024]{2,1,0:T(8,128)(2,1)S(1)} %fusion.23), channel_id=1, source_target_pairs={{0,2},{1,3},{2,0},{3,1},{4,6},{5,7},{6,4},{7,5},{8,10},{9,11},{10,... | collective-permute-start | bytes 1572872 | tf_op jit(solution)/shard_map/ppermute | solution.py:223
  188.3 27.1 %collective-permute-start.15 = (bf16[256,1024]{1,0:T(8,128)(2,1)S(1)}, bf16[256,1024]{1,0:T(8,128)(2,1)S(1)}, u32[]{:S(2)}, u32[]{:S(2)}) collective-permute-start(bf16[256,1024]{1,0:T(8,128)(2,1)S(1)} %fusion.27), channel_id=1, source_target_pairs={{0,0},{1,8},{2,16},{3,24},{8,1},{9,9},{10,17},{11,25},{16,2},{17,1... | collective-permute-start | bytes 1572872 | tf_op jit(solution)/shard_map/ppermute | solution.py:233

commit v10 on v9

--- a/solution.py
+++ b/solution.py
@@ -182,7 +182,6 @@
         )
         for d in range(1, inner_count)
     ]
-    weight_pieces, hidden = lax.optimization_barrier((weight_pieces, hidden))
     from_left, from_right = {}, {}
     going_right = going_left = hidden
     for step in range(1, tp_count):
@@ -192,6 +191,10 @@
         going_left = lax.ppermute(
             going_left, outer_axis, [(s, s - 1) for s in range(1, tp_count - step + 1)]
         )
+        if step == 1:
+            weight_pieces, going_right, going_left = lax.optimization_barrier(
+                (weight_pieces, going_right, going_left)
+            )
         from_left[step], from_right[step] = going_right, going_left
     arrived = [hidden] + [
         jnp.where(outer_at >= d, from_left[d], from_right[tp_count - d])

time: 217 us -> 224 us (1.032)
  starting transfers between devices: 39.7 us -> 49.2 us
  waiting for transfers between devices: 129 us -> 125 us
    ppermute x3, waiting for transfers between devices: 0.01 us -> 20.3 us  [on_device(): lax.ppermute(going_right, outer_axis, [(s, s + 1) for s in range(step - 1...]
    ppermute x1, waiting for transfers between devices: 15.9 us -> 0.42 us  [on_device(): lax.ppermute(out_weight, inner_axis, [(s, (s + d) % inner_count) for s in...]
    ppermute x3, starting transfers between devices: 7.18 us -> 16.8 us  [on_device(): lax.ppermute(going_right, outer_axis, [(s, s + 1) for s in range(step - 1...]
    ppermute x3, waiting for transfers between devices: 48.4 us -> 40.4 us  [on_device(): lax.ppermute(going_left, outer_axis, [(s, s - 1) for s in range(1, tp_cou...]
  transfers between devices with their start and end apart: 16 -> 16, of which waited for: 10 -> 11; matrix products, arithmetic and copies ran while one was open for 12% -> 12% of each run, Pallas kernels for 0% -> 0%
where the time goes in v10:
time: 224 us; the launch traced here: 223 us
  waiting for transfers between devices  125 us (56%)
  starting transfers between devices  49.2 us (22%)
  matrix products  25.9 us (12%)
  other arithmetic  13.4 us (6%)
  local copies, waits for them, and re-layouts  8.3 us (4%)
    ppermute x3, waiting for transfers between devices, on_device(): lax.ppermute(going_left, outer_axis, [(s, s - 1) for s in range(1, tp_cou...  40.4 us
    ppermute x1, waiting for transfers between devices, on_device(): lax.ppermute(held[0].astype(jnp.bfloat16), (outer_axis, 'tp'), swap)  25.2 us
    ppermute x6, starting transfers between devices, shifted(): lax.ppermute(value, axis, [(source, source + steps) for source in range(f...  23.7 us
    ppermute x6, waiting for transfers between devices, shifted(): lax.ppermute(value, axis, [(source, source + steps) for source in range(f...  21.2 us
    ppermute x3, waiting for transfers between devices, on_device(): lax.ppermute(going_right, outer_axis, [(s, s + 1) for s in range(step - 1...  20.3 us
    dot_general x8, matrix products, on_device(): jnp.dot(rows, piece, preferred_element_type=jnp.float32)  19.3 us
    ppermute x2, waiting for transfers between devices, on_device(): lax.ppermute(sent if bit == 1 else sent.astype(jnp.bfloat16), 'tp', [(s,...  17.9 us
    ppermute x3, starting transfers between devices, on_device(): lax.ppermute(going_right, outer_axis, [(s, s + 1) for s in range(step - 1...  16.8 us
  transfers between devices with their start and end apart: 16, of which 11 were waited for; matrix products, arithmetic and copies ran while one was open for 12% of the time, Pallas kernels for 0%

profile of v10, /device:TPU:2, one launch (start us, length us, event | category | flops | bytes accessed | tf_op | source)
XLA Modules:
  0.0 222.9 jit_solution(18238336580735983808)
XLA Ops:
  0.0 1.3 constant_dynamic-update-slice_fusion.5
  1.5 3.4 %collective-permute-start = (bf16[3,2304]{1,0:T(4,128)(2,1)S(1)}, bf16[3,2304]{1,0:T(4,128)(2,1)S(1)}, u32[]{:S(2)}, u32[]{:S(2)}) collective-permute-start(bf16[3,2304]{1,0:T(4,128)(2,1)S(1)} %slice.99), channel_id=1, source_target_pairs={{0,4},{4,8},{8,12},{12,16},{16,20},{20,24},{24,28},{1,5},{5,9},{9,... | collective-permute-start | bytes 41480 | tf_op jit(solution)/shard_map/ppermute | solution.py:14
  4.9 0.6 reduce-window.6
  5.9 0.7 fusion.51
  7.7 1.5 multiply_convert_fusion.3
  9.3 1.6 slice_convert_fusion
  10.9 1.9 copy.27
  12.8 2.2 fusion.17
  15.1 3.5 %collective-permute-start.3 = (bf16[1,32,64,128]{3,2,1,0:T(8,128)(2,1)S(1)}, bf16[1,32,64,128]{3,2,1,0:T(8,128)(2,1)S(1)}, u32[]{:S(2)}, u32[]{:S(2)}) collective-permute-start(bf16[1,32,64,128]{3,2,1,0:T(8,128)(2,1)S(1)} %convert_bitcast_fusion), channel_id=1, source_target_pairs={{0,4},{4,8},{8,12},{12,16},{16,20},{20,24},{24,28},{1,5},{5,9},{9,... | collective-permute-start | bytes 1572872 | tf_op jit(solution)/shard_map/ppermute | solution.py:14
  18.5 10.9 %collective-permute-done.3 = bf16[1,32,64,128]{3,2,1,0:T(8,128)(2,1)S(1)} collective-permute-done((bf16[1,32,64,128]{3,2,1,0:T(8,128)(2,1)S(1)}, bf16[1,32,64,128]{3,2,1,0:T(8,128)(2,1)S(1)}, u32[]{:S(2)}, u32[]{:S(2)}) %collective-permute-start.3) | collective-permute-done | bytes 524320 | tf_op jit(solution)/shard_map/ppermute | solution.py:14
  29.6 5.4 %collective-permute-start.4 = (bf16[1,32,64,128]{3,2,1,0:T(8,128)(2,1)S(1)}, bf16[1,32,64,128]{3,2,1,0:T(8,128)(2,1)S(1)}, u32[]{:S(2)}, u32[]{:S(2)}) collective-permute-start(bf16[1,32,64,128]{3,2,1,0:T(8,128)(2,1)S(1)} %fusion.26), channel_id=1, source_target_pairs={{0,8},{4,12},{8,16},{12,20},{16,24},{20,28},{1,9},{5,13},{9,17},{1... | collective-permute-start | bytes 1572872 | tf_op jit(solution)/shard_map/ppermute | solution.py:14
  35.0 2.5 %collective-permute-start.1 = (f32[1,32]{1,0:T(1,128)S(1)}, f32[1,32]{1,0:T(1,128)S(1)}, u32[]{:S(2)}, u32[]{:S(2)}) collective-permute-start(f32[1,32]{1,0:T(1,128)S(1)} %bitcast.107), channel_id=1, source_target_pairs={{0,4},{4,8},{8,12},{12,16},{16,20},{20,24},{24,28},{1,5},{5,9},{9,... | collective-permute-start | bytes 392 | tf_op jit(solution)/shard_map/ppermute | solution.py:14
  37.5 2.5 %collective-permute-start.6 = (bf16[2048,512]{1,0:T(8,128)(2,1)}, bf16[2048,512]{1,0:T(8,128)(2,1)}, u32[]{:S(2)}, u32[]{:S(2)}) collective-permute-start(bf16[2048,512]{1,0:T(8,128)(2,1)} %param.23), channel_id=1, source_target_pairs={{0,4},{4,0},{1,5},{5,1},{2,6},{6,2},{3,7},{7,3},{8,12},{12,8},{9,1... | collective-permute-start | bytes 6291464 | tf_op jit(solution)/shard_map/ppermute | solution.py:180
  40.0 4.5 %collective-permute-done.4 = bf16[1,32,64,128]{3,2,1,0:T(8,128)(2,1)S(1)} collective-permute-done((bf16[1,32,64,128]{3,2,1,0:T(8,128)(2,1)S(1)}, bf16[1,32,64,128]{3,2,1,0:T(8,128)(2,1)S(1)}, u32[]{:S(2)}, u32[]{:S(2)}) %collective-permute-start.4) | collective-permute-done | bytes 524320 | tf_op jit(solution)/shard_map/ppermute | solution.py:14
  44.9 6.0 %collective-permute-start.5 = (bf16[1,32,64,128]{3,2,1,0:T(8,128)(2,1)S(1)}, bf16[1,32,64,128]{3,2,1,0:T(8,128)(2,1)S(1)}, u32[]{:S(2)}, u32[]{:S(2)}) collective-permute-start(bf16[1,32,64,128]{3,2,1,0:T(8,128)(2,1)S(1)} %fusion.22), channel_id=1, source_target_pairs={{0,16},{4,20},{8,24},{12,28},{1,17},{5,21},{9,25},{13,29},{2,18},{... | collective-permute-start | bytes 1572872 | tf_op jit(solution)/shard_map/ppermute | solution.py:14
  50.9 3.0 %collective-permute-start.2 = (f32[1,32]{1,0:T(1,128)S(1)}, f32[1,32]{1,0:T(1,128)S(1)}, u32[]{:S(2)}, u32[]{:S(2)}) collective-permute-start(f32[1,32]{1,0:T(1,128)S(1)} %bitcast_multiply_fusion.1), channel_id=1, source_target_pairs={{0,8},{4,12},{8,16},{12,20},{16,24},{20,28},{1,9},{5,13},{9,17},{1... | collective-permute-start | bytes 392 | tf_op jit(solution)/shard_map/ppermute | solution.py:14
  53.9 5.9 %collective-permute-done.2 = f32[1,32]{1,0:T(1,128)S(1)} collective-permute-done((f32[1,32]{1,0:T(1,128)S(1)}, f32[1,32]{1,0:T(1,128)S(1)}, u32[]{:S(2)}, u32[]{:S(2)}) %collective-permute-start.2) | collective-permute-done | bytes 160 | tf_op jit(solution)/shard_map/ppermute | solution.py:14
  60.5 3.7 %fusion.14 = f32[256,1,32,64]{0,3,2,1:T(8,128)} fusion(f32[32,64,256]{2,1,0:T(8,128)S(1)} %fusion.29, f32[256,1,32,64]{0,3,2,1:T(8,128)S(1)} %bitcast.95, f32[32,256]{1,0:T(8,128)S(1)} %bitcast.103, f32[256,256]{1,0:T(8,128)S(1)} %fusion.44, pred[256,256]{1,0:T(8,128)(4,1)S(1)} %iota_compare_fusion.1, f32[32]{0:T(128)S(1)} %copy-done.13, ...), kind=kOutput, calls=%fused_computation.26 | convolution fusion | flops 279969792 | bytes 8814720 | tf_op jit(solution)/shard_map/while/body/eval_jaxpr/gjts,sgjp->tgjp/dot_general | solution.py:46
  64.2 2.0 copy.32
  66.2 0.8 multiply_reduce_fusion
  67.0 0.8 multiply_convert_fusion.5
  67.8 14.2 %collective-permute-start.7 = (bf16[256,2048]{1,0:T(8,128)(2,1)S(1)}, bf16[256,2048]{1,0:T(8,128)(2,1)S(1)}, u32[]{:S(2)}, u32[]{:S(2)}) collective-permute-start(bf16[256,2048]{1,0:T(8,128)(2,1)S(1)} %multiply_convert_fusion.5), channel_id=1, source_target_pairs={{0,8},{8,16},{16,24},{1,9},{9,17},{17,25},{2,10},{10,18},{18,26},{... | collective-permute-start | bytes 3145736 | tf_op jit(solution)/shard_map/ppermute | solution.py:188
  82.1 1.3 collective-permute-start.8
  83.8 20.3 %collective-permute-done.7 = bf16[256,2048]{1,0:T(8,128)(2,1)S(1)} collective-permute-done((bf16[256,2048]{1,0:T(8,128)(2,1)S(1)}, bf16[256,2048]{1,0:T(8,128)(2,1)S(1)}, u32[]{:S(2)}, u32[]{:S(2)}) %collective-permute-start.7) | collective-permute-done | bytes 1048608 | tf_op jit(solution)/shard_map/ppermute | solution.py:188
  104.1 4.9 %collective-permute-done.8 = bf16[256,2048]{1,0:T(8,128)(2,1)S(1)} collective-permute-done((bf16[256,2048]{1,0:T(8,128)(2,1)S(1)}, bf16[256,2048]{1,0:T(8,128)(2,1)S(1)}, u32[]{:S(2)}, u32[]{:S(2)}) %collective-permute-start.8) | collective-permute-done | bytes 1048608 | tf_op jit(solution)/shard_map/ppermute | solution.py:191
  109.1 1.3 collective-permute-start.9
  110.4 1.7 collective-permute-start.11
  112.0 2.6 %fusion.53 = f32[256,512]{1,0:T(8,128)S(1)} fusion(bf16[256,2048]{1,0:T(8,128)(2,1)} %copy-done.3, bf16[2048,512]{1,0:T(8,128)(2,1)} %param.23), kind=kOutput, calls=%fused_computation.121 | convolution fusion | flops 536870912 | bytes 3670016 | tf_op jit(solution)/shard_map/dot_general | solution.py:207
  114.6 20.3 %collective-permute-done.9 = bf16[256,2048]{1,0:T(8,128)(2,1)} collective-permute-done((bf16[256,2048]{1,0:T(8,128)(2,1)S(1)}, bf16[256,2048]{1,0:T(8,128)(2,1)}, u32[]{:S(2)}, u32[]{:S(2)}) %collective-permute-start.9) | collective-permute-done | bytes 1048608 | tf_op jit(solution)/shard_map/ppermute | solution.py:191
  135.0 1.3 collective-permute-start.10
  136.3 2.3 %fusion.54 = f32[256,512]{1,0:T(8,128)S(1)} fusion(bf16[256,2048]{1,0:T(8,128)(2,1)S(1)} %copy-done.4, bf16[2048,512]{1,0:T(8,128)(2,1)} %collective-permute-done.6), kind=kOutput, calls=%fused_computation.122 | convolution fusion | flops 536870912 | bytes 3670016 | tf_op jit(solution)/shard_map/dot_general | solution.py:207
  138.6 0.9 collective-permute-start.12
  139.6 2.6 %fusion.36 = f32[256,512]{1,0:T(8,128)S(1)} fusion(bf16[2048,512]{1,0:T(8,128)(2,1)} %param.23, bf16[256,2048]{1,0:T(8,128)(2,1)} %collective-permute-done.11, bf16[256,2048]{1,0:T(8,128)(2,1)} %collective-permute-done.9, pred[]{:T(512)S(6)} %ge.33), kind=kOutput, calls=%fused_computation.70 | convolution fusion | flops 537395200 | bytes 4718593 | tf_op jit(solution)/shard_map/dot_general | solution.py:207
  142.2 2.6 %fusion.35 = f32[256,512]{1,0:T(8,128)S(1)} fusion(bf16[2048,512]{1,0:T(8,128)(2,1)} %collective-permute-done.6, bf16[256,2048]{1,0:T(8,128)(2,1)} %collective-permute-done.11, bf16[256,2048]{1,0:T(8,128)(2,1)} %collective-permute-done.9, pred[]{:T(512)S(6)} %ge.33), kind=kOutput, calls=%fused_computation.69 | convolution fusion | flops 537395200 | bytes 4718593 | tf_op jit(solution)/shard_map/dot_general | solution.py:207
  144.9 15.1 %collective-permute-done.10 = bf16[256,2048]{1,0:T(8,128)(2,1)S(1)} collective-permute-done((bf16[256,2048]{1,0:T(8,128)(2,1)}, bf16[256,2048]{1,0:T(8,128)(2,1)S(1)}, u32[]{:S(2)}, u32[]{:S(2)}) %collective-permute-start.10) | collective-permute-done | bytes 1048608 | tf_op jit(solution)/shard_map/ppermute | solution.py:191
  160.1 2.3 %fusion.34 = f32[256,512]{1,0:T(8,128)S(1)} fusion(bf16[2048,512]{1,0:T(8,128)(2,1)} %param.23, bf16[256,2048]{1,0:T(8,128)(2,1)S(1)} %collective-permute-done.7, bf16[256,2048]{1,0:T(8,128)(2,1)S(1)} %collective-permute-done.10, pred[]{:T(512)S(6)} %ge.32), kind=kOutput, calls=%fused_computation.68 | convolution fusion | flops 537395200 | bytes 4718593 | tf_op jit(solution)/shard_map/dot_general | solution.py:207
  162.4 2.3 %fusion.33 = f32[256,512]{1,0:T(8,128)S(1)} fusion(bf16[2048,512]{1,0:T(8,128)(2,1)} %collective-permute-done.6, bf16[256,2048]{1,0:T(8,128)(2,1)S(1)} %collective-permute-done.7, bf16[256,2048]{1,0:T(8,128)(2,1)S(1)} %collective-permute-done.10, pred[]{:T(512)S(6)} %ge.32), kind=kOutput, calls=%fused_computation.67 | convolution fusion | flops 537395200 | bytes 4718593 | tf_op jit(solution)/shard_map/dot_general | solution.py:207
  164.8 2.3 %fusion.38 = f32[256,512]{1,0:T(8,128)S(1)} fusion(bf16[2048,512]{1,0:T(8,128)(2,1)} %param.23, bf16[256,2048]{1,0:T(8,128)(2,1)S(1)} %collective-permute-done.12, bf16[256,2048]{1,0:T(8,128)(2,1)S(1)} %collective-permute-done.8, pred[]{:T(512)S(6)} %ge.34), kind=kOutput, calls=%fused_computation.72 | convolution fusion | flops 537395200 | bytes 4718593 | tf_op jit(solution)/shard_map/dot_general | solution.py:207
  167.1 2.3 %fusion.37 = f32[256,512]{1,0:T(8,128)S(1)} fusion(bf16[2048,512]{1,0:T(8,128)(2,1)} %collective-permute-done.6, bf16[256,2048]{1,0:T(8,128)(2,1)S(1)} %collective-permute-done.12, bf16[256,2048]{1,0:T(8,128)(2,1)S(1)} %collective-permute-done.8, pred[]{:T(512)S(6)} %ge.34), kind=kOutput, calls=%fused_computation.71 | convolution fusion | flops 537395200 | bytes 4718593 | tf_op jit(solution)/shard_map/dot_general | solution.py:207
  170.3 1.7 copy-done.1
  172.0 1.5 pad_maximum_fusion.1
  173.5 4.4 %collective-permute-done.13 = f32[2,256,1024]{2,1,0:T(8,128)S(1)} collective-permute-done((f32[2,256,1024]{2,1,0:T(8,128)}, f32[2,256,1024]{2,1,0:T(8,128)S(1)}, u32[]{:S(2)}, u32[]{:S(2)}) %collective-permute-start.13) | collective-permute-done | bytes 2097184 | tf_op jit(solution)/shard_map/ppermute | solution.py:226
  177.8 1.4 fusion.23
  179.7 13.5 %collective-permute-done.14 = bf16[1,256,1024]{2,1,0:T(8,128)(2,1)S(1)} collective-permute-done((bf16[1,256,1024]{2,1,0:T(8,128)(2,1)S(1)}, bf16[1,256,1024]{2,1,0:T(8,128)(2,1)S(1)}, u32[]{:S(2)}, u32[]{:S(2)}) %collective-permute-start.14) | collective-permute-done | bytes 524320 | tf_op jit(solution)/shard_map/ppermute | solution.py:226
  193.2 1.5 fusion.27
  194.7 1.9 collective-permute-start.15
  196.7 25.2 %collective-permute-done.15 = bf16[256,1024]{1,0:T(8,128)(2,1)S(1)} collective-permute-done((bf16[256,1024]{1,0:T(8,128)(2,1)S(1)}, bf16[256,1024]{1,0:T(8,128)(2,1)S(1)}, u32[]{:S(2)}, u32[]{:S(2)}) %collective-permute-start.15) | collective-permute-done | bytes 524320 | tf_op jit(solution)/shard_map/ppermute | solution.py:236
  222.1 0.9 pad_maximum_fusion.2
  (76 shorter events, 5.3 us)
Async XLA Ops:
  0.0 4.9 %copy-start = (f32[256,32]{0,1:T(8,128)S(1)}, f32[256,32]{0,1:T(8,128)}, u32[]{:S(2)}) copy-start(f32[256,32]{0,1:T(8,128)} %param.20) | copy-start | bytes 98308
  0.0 1.4 copy-start.6
  0.0 1.4 copy-start.7
  0.0 7.3 %copy-start.9 = (f32[4,2048]{1,0:T(4,128)S(1)}, f32[4,2048]{1,0:T(4,128)}, u32[]{:S(2)}) copy-start(f32[4,2048]{1,0:T(4,128)} %param.16) | copy-start | bytes 98308
  0.0 7.3 %copy-start.11 = (f32[4,128]{1,0:T(4,128)S(1)}, f32[4,128]{1,0:T(4,128)}, u32[]{:S(2)}) copy-start(f32[4,128]{1,0:T(4,128)} %param.17) | copy-start | bytes 6148
  0.0 7.3 %copy-start.12 = (f32[4,128]{1,0:T(4,128)S(1)}, f32[4,128]{1,0:T(4,128)}, u32[]{:S(2)}) copy-start(f32[4,128]{1,0:T(4,128)} %param.18) | copy-start | bytes 6148
  1.5 6.1 %collective-permute-start = (bf16[3,2304]{1,0:T(4,128)(2,1)S(1)}, bf16[3,2304]{1,0:T(4,128)(2,1)S(1)}, u32[]{:S(2)}, u32[]{:S(2)}) collective-permute-start(bf16[3,2304]{1,0:T(4,128)(2,1)S(1)} %slice.99), channel_id=1, source_target_pairs={{0,4},{4,8},{8,12},{12,16},{16,20},{20,24},{24,28},{1,5},{5,9},{9,... | collective-permute-start | bytes 41480 | tf_op jit(solution)/shard_map/ppermute | solution.py:14
  15.1 14.3 %collective-permute-start.3 = (bf16[1,32,64,128]{3,2,1,0:T(8,128)(2,1)S(1)}, bf16[1,32,64,128]{3,2,1,0:T(8,128)(2,1)S(1)}, u32[]{:S(2)}, u32[]{:S(2)}) collective-permute-start(bf16[1,32,64,128]{3,2,1,0:T(8,128)(2,1)S(1)} %convert_bitcast_fusion), channel_id=1, source_target_pairs={{0,4},{4,8},{8,12},{12,16},{16,20},{20,24},{24,28},{1,5},{5,9},{9,... | collective-permute-start | bytes 1572872 | tf_op jit(solution)/shard_map/ppermute | solution.py:14
  29.4 24.4 %copy-start.5 = (f32[1,256,1,32]{1,2,3,0:T(1,128)S(1)}, f32[1,256,1,32]{1,2,3,0:T(1,128)}, u32[]{:S(2)}) copy-start(f32[1,256,1,32]{1,2,3,0:T(1,128)} %get-tuple-element.58) | copy-start | bytes 98308
  29.6 14.9 %collective-permute-start.4 = (bf16[1,32,64,128]{3,2,1,0:T(8,128)(2,1)S(1)}, bf16[1,32,64,128]{3,2,1,0:T(8,128)(2,1)S(1)}, u32[]{:S(2)}, u32[]{:S(2)}) collective-permute-start(bf16[1,32,64,128]{3,2,1,0:T(8,128)(2,1)S(1)} %fusion.26), channel_id=1, source_target_pairs={{0,8},{4,12},{8,16},{12,20},{16,24},{20,28},{1,9},{5,13},{9,17},{1... | collective-permute-start | bytes 1572872 | tf_op jit(solution)/shard_map/ppermute | solution.py:14
  35.0 5.0 %collective-permute-start.1 = (f32[1,32]{1,0:T(1,128)S(1)}, f32[1,32]{1,0:T(1,128)S(1)}, u32[]{:S(2)}, u32[]{:S(2)}) collective-permute-start(f32[1,32]{1,0:T(1,128)S(1)} %bitcast.107), channel_id=1, source_target_pairs={{0,4},{4,8},{8,12},{12,16},{16,20},{20,24},{24,28},{1,5},{5,9},{9,... | collective-permute-start | bytes 392 | tf_op jit(solution)/shard_map/ppermute | solution.py:14
  37.5 46.3 %collective-permute-start.6 = (bf16[2048,512]{1,0:T(8,128)(2,1)}, bf16[2048,512]{1,0:T(8,128)(2,1)}, u32[]{:S(2)}, u32[]{:S(2)}) collective-permute-start(bf16[2048,512]{1,0:T(8,128)(2,1)} %param.23), channel_id=1, source_target_pairs={{0,4},{4,0},{1,5},{5,1},{2,6},{6,2},{3,7},{7,3},{8,12},{12,8},{9,1... | collective-permute-start | bytes 6291464 | tf_op jit(solution)/shard_map/ppermute | solution.py:180
  44.9 15.1 %collective-permute-start.5 = (bf16[1,32,64,128]{3,2,1,0:T(8,128)(2,1)S(1)}, bf16[1,32,64,128]{3,2,1,0:T(8,128)(2,1)S(1)}, u32[]{:S(2)}, u32[]{:S(2)}) collective-permute-start(bf16[1,32,64,128]{3,2,1,0:T(8,128)(2,1)S(1)} %fusion.22), channel_id=1, source_target_pairs={{0,16},{4,20},{8,24},{12,28},{1,17},{5,21},{9,25},{13,29},{2,18},{... | collective-permute-start | bytes 1572872 | tf_op jit(solution)/shard_map/ppermute | solution.py:14
  50.9 8.9 %collective-permute-start.2 = (f32[1,32]{1,0:T(1,128)S(1)}, f32[1,32]{1,0:T(1,128)S(1)}, u32[]{:S(2)}, u32[]{:S(2)}) collective-permute-start(f32[1,32]{1,0:T(1,128)S(1)} %bitcast_multiply_fusion.1), channel_id=1, source_target_pairs={{0,8},{4,12},{8,16},{12,20},{16,24},{20,28},{1,9},{5,13},{9,17},{1... | collective-permute-start | bytes 392 | tf_op jit(solution)/shard_map/ppermute | solution.py:14
  53.9 6.6 %copy-start.8 = (f32[256,32]{0,1:T(8,128)S(1)}, f32[256,32]{0,1:T(8,128)}, u32[]{:S(2)}) copy-start(f32[256,32]{0,1:T(8,128)} %param.19) | copy-start | bytes 98308
  53.9 6.6 %copy-start.13 = (f32[32]{0:T(128)S(1)}, f32[32]{0:T(128)}, u32[]{:S(2)}) copy-start(f32[32]{0:T(128)} %param.21) | copy-start | bytes 388
  64.2 2.0 copy-start.2
  66.2 0.8 copy-start.10
  67.8 14.2 %copy-start.3 = (bf16[256,2048]{1,0:T(8,128)(2,1)}, bf16[256,2048]{1,0:T(8,128)(2,1)S(1)}, u32[]{:S(2)}) copy-start(bf16[256,2048]{1,0:T(8,128)(2,1)S(1)} %multiply_convert_fusion.5) | copy-start | bytes 3145732
  67.8 36.3 %collective-permute-start.7 = (bf16[256,2048]{1,0:T(8,128)(2,1)S(1)}, bf16[256,2048]{1,0:T(8,128)(2,1)S(1)}, u32[]{:S(2)}, u32[]{:S(2)}) collective-permute-start(bf16[256,2048]{1,0:T(8,128)(2,1)S(1)} %multiply_convert_fusion.5), channel_id=1, source_target_pairs={{0,8},{8,16},{16,24},{1,9},{9,17},{17,25},{2,10},{10,18},{18,26},{... | collective-permute-start | bytes 3145736 | tf_op jit(solution)/shard_map/ppermute | solution.py:188
  82.1 27.0 %collective-permute-start.8 = (bf16[256,2048]{1,0:T(8,128)(2,1)S(1)}, bf16[256,2048]{1,0:T(8,128)(2,1)S(1)}, u32[]{:S(2)}, u32[]{:S(2)}) collective-permute-start(bf16[256,2048]{1,0:T(8,128)(2,1)S(1)} %multiply_convert_fusion.5), channel_id=1, source_target_pairs={{8,0},{16,8},{24,16},{9,1},{17,9},{25,17},{10,2},{18,10},{26,18},{... | collective-permute-start | bytes 3145736 | tf_op jit(solution)/shard_map/ppermute | solution.py:191
  83.4 52.9 %copy-start.4 = (bf16[256,2048]{1,0:T(8,128)(2,1)S(1)}, bf16[256,2048]{1,0:T(8,128)(2,1)}, u32[]{:S(2)}) copy-start(bf16[256,2048]{1,0:T(8,128)(2,1)} %copy-done.3) | copy-start | bytes 3145732
  109.1 25.9 %collective-permute-start.9 = (bf16[256,2048]{1,0:T(8,128)(2,1)S(1)}, bf16[256,2048]{1,0:T(8,128)(2,1)}, u32[]{:S(2)}, u32[]{:S(2)}) collective-permute-start(bf16[256,2048]{1,0:T(8,128)(2,1)S(1)} %collective-permute-done.8), channel_id=1, source_target_pairs={{8,0},{16,8},{9,1},{17,9},{10,2},{18,10},{11,3},{19,11},{12,4},{20... | collective-permute-start | bytes 3145736 | tf_op jit(solution)/shard_map/ppermute | solution.py:191
  110.4 28.3 %collective-permute-start.11 = (bf16[256,2048]{1,0:T(8,128)(2,1)S(1)}, bf16[256,2048]{1,0:T(8,128)(2,1)}, u32[]{:S(2)}, u32[]{:S(2)}) collective-permute-start(bf16[256,2048]{1,0:T(8,128)(2,1)S(1)} %collective-permute-done.7), channel_id=1, source_target_pairs={{8,16},{16,24},{9,17},{17,25},{10,18},{18,26},{11,19},{19,27},{12,... | collective-permute-start | bytes 3145736 | tf_op jit(solution)/shard_map/ppermute | solution.py:188
  135.0 25.1 %collective-permute-start.10 = (bf16[256,2048]{1,0:T(8,128)(2,1)}, bf16[256,2048]{1,0:T(8,128)(2,1)S(1)}, u32[]{:S(2)}, u32[]{:S(2)}) collective-permute-start(bf16[256,2048]{1,0:T(8,128)(2,1)} %collective-permute-done.9), channel_id=1, source_target_pairs={{8,0},{9,1},{10,2},{11,3},{12,4},{13,5},{14,6},{15,7}} | collective-permute-start | bytes 3145736 | tf_op jit(solution)/shard_map/ppermute | solution.py:191
  138.6 26.1 %collective-permute-start.12 = (bf16[256,2048]{1,0:T(8,128)(2,1)}, bf16[256,2048]{1,0:T(8,128)(2,1)S(1)}, u32[]{:S(2)}, u32[]{:S(2)}) collective-permute-start(bf16[256,2048]{1,0:T(8,128)(2,1)} %collective-permute-done.11), channel_id=1, source_target_pairs={{16,24},{17,25},{18,26},{19,27},{20,28},{21,29},{22,30},{23,31}} | collective-permute-start | bytes 3145736 | tf_op jit(solution)/shard_map/ppermute | solution.py:188
  170.1 1.9 copy-start.1
  173.5 4.4 %collective-permute-start.13 = (f32[2,256,1024]{2,1,0:T(8,128)}, f32[2,256,1024]{2,1,0:T(8,128)S(1)}, u32[]{:S(2)}, u32[]{:S(2)}) collective-permute-start(f32[2,256,1024]{2,1,0:T(8,128)} %pad_maximum_fusion.1), channel_id=1, source_target_pairs={{0,1},{1,0},{2,3},{3,2},{4,5},{5,4},{6,7},{7,6},{8,9},{9,8},{10,11... | collective-permute-start | bytes 6291464 | tf_op jit(solution)/shard_map/ppermute | solution.py:226
  179.2 14.0 %collective-permute-start.14 = (bf16[1,256,1024]{2,1,0:T(8,128)(2,1)S(1)}, bf16[1,256,1024]{2,1,0:T(8,128)(2,1)S(1)}, u32[]{:S(2)}, u32[]{:S(2)}) collective-permute-start(bf16[1,256,1024]{2,1,0:T(8,128)(2,1)S(1)} %fusion.23), channel_id=1, source_target_pairs={{0,2},{1,3},{2,0},{3,1},{4,6},{5,7},{6,4},{7,5},{8,10},{9,11},{10,... | collective-permute-start | bytes 1572872 | tf_op jit(solution)/shard_map/ppermute | solution.py:226
  194.7 27.1 %collective-permute-start.15 = (bf16[256,1024]{1,0:T(8,128)(2,1)S(1)}, bf16[256,1024]{1,0:T(8,128)(2,1)S(1)}, u32[]{:S(2)}, u32[]{:S(2)}) collective-permute-start(bf16[256,1024]{1,0:T(8,128)(2,1)S(1)} %fusion.27), channel_id=1, source_target_pairs={{0,0},{1,8},{2,16},{3,24},{8,1},{9,9},{10,17},{11,25},{16,2},{17,1... | collective-permute-start | bytes 1572872 | tf_op jit(solution)/shard_map/ppermute | solution.py:236

commit v11 on v9

--- a/solution.py
+++ b/solution.py
@@ -183,9 +183,15 @@
         for d in range(1, inner_count)
     ]
     weight_pieces, hidden = lax.optimization_barrier((weight_pieces, hidden))
+    def times_weight(rows):
+        return jnp.concatenate(
+            [jnp.dot(rows, piece, preferred_element_type=jnp.float32) for piece in weight_pieces],
+            axis=1,
+        )
+
     from_left, from_right = {}, {}
     going_right = going_left = hidden
-    for step in range(1, tp_count):
+    for step in range(1, tp_count - 1):
         going_right = lax.ppermute(
             going_right, outer_axis, [(s, s + 1) for s in range(step - 1, tp_count - 1)]
         )
@@ -193,20 +199,23 @@
             going_left, outer_axis, [(s, s - 1) for s in range(1, tp_count - step + 1)]
         )
         from_left[step], from_right[step] = going_right, going_left
-    arrived = [hidden] + [
-        jnp.where(outer_at >= d, from_left[d], from_right[tp_count - d])
-        for d in range(1, tp_count)
-    ]
+    far = lax.ppermute(
+        jnp.where(outer_at == tp_count - 2, going_right, going_left),
+        outer_axis,
+        [(tp_count - 2, tp_count - 1), (1, 0)],
+    )
+    far_part = times_weight(far)
     by_source = jnp.stack(
-        [
-            jnp.concatenate(
-                [
-                    jnp.dot(rows, piece, preferred_element_type=jnp.float32)
-                    for piece in weight_pieces
-                ],
-                axis=1,
+        [times_weight(hidden)]
+        + [
+            jnp.where(
+                outer_at >= d,
+                times_weight(from_left[d]) if d < tp_count - 1 else far_part,
+                times_weight(from_right[tp_count - d]) if d > 1 else far_part,
             )
-            for rows in arrived
+            if d != tp_count // 2
+            else times_weight(jnp.where(outer_at >= d, from_left[d], from_right[d]))
+            for d in range(1, tp_count)
         ]
     )
 
@@ -248,7 +257,7 @@
 def solution(mesh):
     ctx_count = mesh.shape["ctx"]
     tp_count = mesh.shape["tp"]
-    if ctx_count % tp_count == 0 and tp_count & (tp_count - 1) == 0:
+    if ctx_count % tp_count == 0 and tp_count == 4:
         inner = ctx_count // tp_count
         grid = mesh.devices.reshape(tp_count, inner, tp_count)
         mesh = jax.sharding.Mesh(grid, ("outer", "inner", "tp"))

time: 217 us -> 214 us (0.986)
  waiting for transfers between devices: 129 us -> 118 us
  matrix products: 25.9 us -> 30.4 us
    ppermute x3 -> x2, waiting for transfers between devices: 48.4 us -> 27.2 us  [on_device(): lax.ppermute(going_left, outer_axis, [(s, s - 1) for s in range(1, tp_cou...]
    ppermute x0 -> x1, waiting for transfers between devices: none -> 13.9 us  [on_device(): lax.ppermute(jnp.where(outer_at == tp_count - 2, going_right, going_left)...]
    dot_general x8 -> x10, matrix products: 19.3 us -> 23.8 us  [times_weight(): jnp.dot(rows, piece, preferred_element_type=jnp.float32)]
    ppermute x1, starting transfers between devices: 1.92 us -> 4.46 us  [on_device(): lax.ppermute(held[0].astype(jnp.bfloat16), (outer_axis, 'tp'), swap)]
    ppermute x1, waiting for transfers between devices: 25.2 us -> 22.7 us  [on_device(): lax.ppermute(held[0].astype(jnp.bfloat16), (outer_axis, 'tp'), swap)]
    ppermute x3 -> x2, starting transfers between devices: 7.18 us -> 5.34 us  [on_device(): lax.ppermute(going_right, outer_axis, [(s, s + 1) for s in range(step - 1...]
  transfers between devices with their start and end apart: 16 -> 15, of which waited for: 10 -> 10; matrix products, arithmetic and copies ran while one was open for 12% -> 15% of each run, Pallas kernels for 0% -> 0%
where the time goes in v11:
time: 214 us; the launch traced here: 212 us
  waiting for transfers between devices  118 us (55%)
  starting transfers between devices  40.6 us (19%)
  matrix products  30.4 us (14%)
  other arithmetic  14.6 us (7%)
  local copies, waits for them, and re-layouts  8.29 us (4%)
    ppermute x2, waiting for transfers between devices, on_device(): lax.ppermute(going_left, outer_axis, [(s, s - 1) for s in range(1, tp_cou...  27.2 us
    dot_general x10, matrix products, times_weight(): jnp.dot(rows, piece, preferred_element_type=jnp.float32)  23.8 us
    ppermute x6, starting transfers between devices, shifted(): lax.ppermute(value, axis, [(source, source + steps) for source in range(f...  23.7 us
    ppermute x1, waiting for transfers between devices, on_device(): lax.ppermute(held[0].astype(jnp.bfloat16), (outer_axis, 'tp'), swap)  22.7 us
    ppermute x6, waiting for transfers between devices, shifted(): lax.ppermute(value, axis, [(source, source + steps) for source in range(f...  21.2 us
    ppermute x2, waiting for transfers between devices, on_device(): lax.ppermute(sent if bit == 1 else sent.astype(jnp.bfloat16), 'tp', [(s,...  17.8 us
    ppermute x1, waiting for transfers between devices, on_device(): lax.ppermute(out_weight, inner_axis, [(s, (s + d) % inner_count) for s in...  14.9 us
    ppermute x1, waiting for transfers between devices, on_device(): lax.ppermute(jnp.where(outer_at == tp_count - 2, going_right, going_left)...  13.9 us
  transfers between devices with their start and end apart: 15, of which 10 were waited for; matrix products, arithmetic and copies ran while one was open for 15% of the time, Pallas kernels for 0%

profile of v11, /device:TPU:2, one launch (start us, length us, event | category | flops | bytes accessed | tf_op | source)
XLA Modules:
  0.0 212.5 jit_solution(17294021350640016020)
XLA Ops:
  0.0 1.3 constant_dynamic-update-slice_fusion.5
  1.5 3.4 %collective-permute-start.1 = (bf16[3,2304]{1,0:T(4,128)(2,1)S(1)}, bf16[3,2304]{1,0:T(4,128)(2,1)S(1)}, u32[]{:S(2)}, u32[]{:S(2)}) collective-permute-start(bf16[3,2304]{1,0:T(4,128)(2,1)S(1)} %slice.99), channel_id=1, source_target_pairs={{0,4},{4,8},{8,12},{12,16},{16,20},{20,24},{24,28},{1,5},{5,9},{9,... | collective-permute-start | bytes 41480 | tf_op jit(solution)/shard_map/ppermute | solution.py:14
  5.9 0.7 fusion.47
  7.7 1.5 multiply_convert_fusion.3
  9.3 1.6 slice_convert_fusion
  10.9 1.9 copy.27
  12.8 2.2 %fusion.17 = f32[32,64,128]{2,1,0:T(8,128)S(1)} fusion(f32[256,32]{0,1:T(8,128)S(1)} %bitcast.117, f32[256,128]{1,0:T(8,128)S(1)} %slice_convert_fusion.1, f32[32]{0:T(128)S(1)} %get-tuple-element.73, f32[256,32,64]{0,2,1:T(8,128)S(1)} %bitcast.109, f32[256,32]{0,1:T(8,128)} %param.19), kind=kOutput, calls=%fused_computation.32 | convolution fusion | flops 137625600 | bytes 3342464 | tf_op jit(solution)/shard_map/vmap(sgjp,sgjn->gjpn)/dot_general | solution.py:54
  15.1 3.5 %collective-permute-start.4 = (bf16[1,32,64,128]{3,2,1,0:T(8,128)(2,1)S(1)}, bf16[1,32,64,128]{3,2,1,0:T(8,128)(2,1)S(1)}, u32[]{:S(2)}, u32[]{:S(2)}) collective-permute-start(bf16[1,32,64,128]{3,2,1,0:T(8,128)(2,1)S(1)} %convert_bitcast_fusion), channel_id=1, source_target_pairs={{0,4},{4,8},{8,12},{12,16},{16,20},{20,24},{24,28},{1,5},{5,9},{9,... | collective-permute-start | bytes 1572872 | tf_op jit(solution)/shard_map/ppermute | solution.py:14
  18.5 10.9 %collective-permute-done.4 = bf16[1,32,64,128]{3,2,1,0:T(8,128)(2,1)S(1)} collective-permute-done((bf16[1,32,64,128]{3,2,1,0:T(8,128)(2,1)S(1)}, bf16[1,32,64,128]{3,2,1,0:T(8,128)(2,1)S(1)}, u32[]{:S(2)}, u32[]{:S(2)}) %collective-permute-start.4) | collective-permute-done | bytes 524320 | tf_op jit(solution)/shard_map/ppermute | solution.py:14
  29.6 5.4 %collective-permute-start.5 = (bf16[1,32,64,128]{3,2,1,0:T(8,128)(2,1)S(1)}, bf16[1,32,64,128]{3,2,1,0:T(8,128)(2,1)S(1)}, u32[]{:S(2)}, u32[]{:S(2)}) collective-permute-start(bf16[1,32,64,128]{3,2,1,0:T(8,128)(2,1)S(1)} %fusion.26), channel_id=1, source_target_pairs={{0,8},{4,12},{8,16},{12,20},{16,24},{20,28},{1,9},{5,13},{9,17},{1... | collective-permute-start | bytes 1572872 | tf_op jit(solution)/shard_map/ppermute | solution.py:14
  35.0 2.5 %collective-permute-start.2 = (f32[1,32]{1,0:T(1,128)S(1)}, f32[1,32]{1,0:T(1,128)S(1)}, u32[]{:S(2)}, u32[]{:S(2)}) collective-permute-start(f32[1,32]{1,0:T(1,128)S(1)} %bitcast.123), channel_id=1, source_target_pairs={{0,4},{4,8},{8,12},{12,16},{16,20},{20,24},{24,28},{1,5},{5,9},{9,... | collective-permute-start | bytes 392 | tf_op jit(solution)/shard_map/ppermute | solution.py:14
  37.5 2.5 %collective-permute-start = (bf16[2048,512]{1,0:T(8,128)(2,1)}, bf16[2048,512]{1,0:T(8,128)(2,1)}, u32[]{:S(2)}, u32[]{:S(2)}) collective-permute-start(bf16[2048,512]{1,0:T(8,128)(2,1)} %param.23), channel_id=1, source_target_pairs={{0,4},{4,0},{1,5},{5,1},{2,6},{6,2},{3,7},{7,3},{8,12},{12,8},{9,1... | collective-permute-start | bytes 6291464 | tf_op jit(solution)/shard_map/ppermute | solution.py:180
  40.0 4.5 %collective-permute-done.5 = bf16[1,32,64,128]{3,2,1,0:T(8,128)(2,1)S(1)} collective-permute-done((bf16[1,32,64,128]{3,2,1,0:T(8,128)(2,1)S(1)}, bf16[1,32,64,128]{3,2,1,0:T(8,128)(2,1)S(1)}, u32[]{:S(2)}, u32[]{:S(2)}) %collective-permute-start.5) | collective-permute-done | bytes 524320 | tf_op jit(solution)/shard_map/ppermute | solution.py:14
  44.9 6.0 %collective-permute-start.6 = (bf16[1,32,64,128]{3,2,1,0:T(8,128)(2,1)S(1)}, bf16[1,32,64,128]{3,2,1,0:T(8,128)(2,1)S(1)}, u32[]{:S(2)}, u32[]{:S(2)}) collective-permute-start(bf16[1,32,64,128]{3,2,1,0:T(8,128)(2,1)S(1)} %fusion.22), channel_id=1, source_target_pairs={{0,16},{4,20},{8,24},{12,28},{1,17},{5,21},{9,25},{13,29},{2,18},{... | collective-permute-start | bytes 1572872 | tf_op jit(solution)/shard_map/ppermute | solution.py:14
  50.9 3.0 %collective-permute-start.3 = (f32[1,32]{1,0:T(1,128)S(1)}, f32[1,32]{1,0:T(1,128)S(1)}, u32[]{:S(2)}, u32[]{:S(2)}) collective-permute-start(f32[1,32]{1,0:T(1,128)S(1)} %bitcast_multiply_fusion.1), channel_id=1, source_target_pairs={{0,8},{4,12},{8,16},{12,20},{16,24},{20,28},{1,9},{5,13},{9,17},{1... | collective-permute-start | bytes 392 | tf_op jit(solution)/shard_map/ppermute | solution.py:14
  53.9 5.9 %collective-permute-done.3 = f32[1,32]{1,0:T(1,128)S(1)} collective-permute-done((f32[1,32]{1,0:T(1,128)S(1)}, f32[1,32]{1,0:T(1,128)S(1)}, u32[]{:S(2)}, u32[]{:S(2)}) %collective-permute-start.3) | collective-permute-done | bytes 160 | tf_op jit(solution)/shard_map/ppermute | solution.py:14
  60.5 3.7 %fusion.14 = f32[256,1,32,64]{0,3,2,1:T(8,128)} fusion(f32[32,64,256]{2,1,0:T(8,128)S(1)} %fusion.29, f32[256,1,32,64]{0,3,2,1:T(8,128)S(1)} %bitcast.111, f32[32,256]{1,0:T(8,128)S(1)} %bitcast.119, f32[256,256]{1,0:T(8,128)S(1)} %fusion.40, pred[256,256]{1,0:T(8,128)(4,1)S(1)} %iota_compare_fusion.1, f32[32]{0:T(128)S(1)} %copy-done.11, ...), kind=kOutput, calls=%fused_computation.26 | convolution fusion | flops 279969792 | bytes 8814720 | tf_op jit(solution)/shard_map/while/body/eval_jaxpr/gjts,sgjp->tgjp/dot_general | solution.py:46
  64.2 2.0 copy.32
  66.2 0.8 multiply_reduce_fusion
  67.0 1.8 multiply_convert_fusion.5
  68.9 14.9 %collective-permute-done = bf16[2048,512]{1,0:T(8,128)(2,1)} collective-permute-done((bf16[2048,512]{1,0:T(8,128)(2,1)}, bf16[2048,512]{1,0:T(8,128)(2,1)}, u32[]{:S(2)}, u32[]{:S(2)}) %collective-permute-start) | collective-permute-done | bytes 2097184 | tf_op jit(solution)/shard_map/ppermute | solution.py:180
  83.8 1.3 collective-permute-start.9
  85.1 4.6 %collective-permute-start.7 = (bf16[256,2048]{1,0:T(8,128)(2,1)}, bf16[256,2048]{1,0:T(8,128)(2,1)S(1)}, u32[]{:S(2)}, u32[]{:S(2)}) collective-permute-start(bf16[256,2048]{1,0:T(8,128)(2,1)} %multiply_convert_fusion.5), channel_id=1, source_target_pairs={{0,8},{8,16},{16,24},{1,9},{9,17},{17,25},{2,10},{10,18},{18,26},{... | collective-permute-start | bytes 3145736 | tf_op jit(solution)/shard_map/ppermute | solution.py:195
  89.7 2.6 %fusion.49 = f32[256,512]{1,0:T(8,128)S(1)} fusion(bf16[256,2048]{1,0:T(8,128)(2,1)} %multiply_convert_fusion.5, bf16[2048,512]{1,0:T(8,128)(2,1)} %param.23), kind=kOutput, calls=%fused_computation.123 | convolution fusion | flops 536870912 | bytes 3670016 | tf_op jit(solution)/shard_map/dot_general | solution.py:188
  92.4 15.7 %collective-permute-done.9 = bf16[256,2048]{1,0:T(8,128)(2,1)S(1)} collective-permute-done((bf16[256,2048]{1,0:T(8,128)(2,1)}, bf16[256,2048]{1,0:T(8,128)(2,1)S(1)}, u32[]{:S(2)}, u32[]{:S(2)}) %collective-permute-start.9) | collective-permute-done | bytes 1048608 | tf_op jit(solution)/shard_map/ppermute | solution.py:198
  108.1 1.3 collective-permute-start.10
  109.4 0.7 collective-permute-start.8
  110.1 2.6 %fusion.50 = f32[256,512]{1,0:T(8,128)S(1)} fusion(bf16[256,2048]{1,0:T(8,128)(2,1)} %multiply_convert_fusion.5, bf16[2048,512]{1,0:T(8,128)(2,1)} %collective-permute-done), kind=kOutput, calls=%fused_computation.124 | convolution fusion | flops 536870912 | bytes 3670016 | tf_op jit(solution)/shard_map/dot_general | solution.py:188
  112.8 2.3 %convolution_bitcast_fusion.1 = f32[1,256,512]{2,1,0:T(8,128)S(1)} fusion(bf16[256,2048]{1,0:T(8,128)(2,1)S(1)} %collective-permute-done.9, bf16[2048,512]{1,0:T(8,128)(2,1)} %param.23), kind=kOutput, calls=%fused_computation.38 | convolution fusion | flops 536870912 | bytes 3670016 | tf_op jit(solution)/shard_map/dot_general | solution.py:188
  115.1 2.3 %convolution_bitcast_fusion = f32[1,256,512]{2,1,0:T(8,128)S(1)} fusion(bf16[256,2048]{1,0:T(8,128)(2,1)S(1)} %collective-permute-done.9, bf16[2048,512]{1,0:T(8,128)(2,1)} %collective-permute-done), kind=kOutput, calls=%fused_computation.37 | convolution fusion | flops 536870912 | bytes 3670016 | tf_op jit(solution)/shard_map/dot_general | solution.py:188
  117.4 2.3 %convolution_bitcast_fusion.5 = f32[1,256,512]{2,1,0:T(8,128)S(1)} fusion(bf16[256,2048]{1,0:T(8,128)(2,1)S(1)} %collective-permute-done.7, bf16[2048,512]{1,0:T(8,128)(2,1)} %param.23), kind=kOutput, calls=%fused_computation.42 | convolution fusion | flops 536870912 | bytes 3670016 | tf_op jit(solution)/shard_map/dot_general | solution.py:188
  119.7 11.6 %collective-permute-done.10 = bf16[256,2048]{1,0:T(8,128)(2,1)S(1)} collective-permute-done((bf16[256,2048]{1,0:T(8,128)(2,1)S(1)}, bf16[256,2048]{1,0:T(8,128)(2,1)S(1)}, u32[]{:S(2)}, u32[]{:S(2)}) %collective-permute-start.10) | collective-permute-done | bytes 1048608 | tf_op jit(solution)/shard_map/ppermute | solution.py:198
  131.4 1.5 collective-permute-start.11
  132.9 2.3 %convolution_bitcast_fusion.4 = f32[1,256,512]{2,1,0:T(8,128)S(1)} fusion(bf16[256,2048]{1,0:T(8,128)(2,1)S(1)} %collective-permute-done.7, bf16[2048,512]{1,0:T(8,128)(2,1)} %collective-permute-done), kind=kOutput, calls=%fused_computation.41 | convolution fusion | flops 536870912 | bytes 3670016 | tf_op jit(solution)/shard_map/dot_general | solution.py:188
  135.2 2.4 %fusion.34 = f32[256,512]{1,0:T(8,128)S(1)} fusion(bf16[2048,512]{1,0:T(8,128)(2,1)} %param.23, bf16[256,2048]{1,0:T(8,128)(2,1)S(1)} %collective-permute-done.8, bf16[256,2048]{1,0:T(8,128)(2,1)S(1)} %collective-permute-done.10, pred[]{:T(512)S(6)} %ge.33), kind=kOutput, calls=%fused_computation.74 | convolution fusion | flops 537395200 | bytes 4718593 | tf_op jit(solution)/shard_map/dot_general | solution.py:188
  137.6 2.4 %fusion.33 = f32[256,512]{1,0:T(8,128)S(1)} fusion(bf16[2048,512]{1,0:T(8,128)(2,1)} %collective-permute-done, bf16[256,2048]{1,0:T(8,128)(2,1)S(1)} %collective-permute-done.8, bf16[256,2048]{1,0:T(8,128)(2,1)S(1)} %collective-permute-done.10, pred[]{:T(512)S(6)} %ge.33), kind=kOutput, calls=%fused_computation.73 | convolution fusion | flops 537395200 | bytes 4718593 | tf_op jit(solution)/shard_map/dot_general | solution.py:188
  140.0 13.9 %collective-permute-done.11 = bf16[256,2048]{1,0:T(8,128)(2,1)S(1)} collective-permute-done((bf16[256,2048]{1,0:T(8,128)(2,1)S(1)}, bf16[256,2048]{1,0:T(8,128)(2,1)S(1)}, u32[]{:S(2)}, u32[]{:S(2)}) %collective-permute-start.11) | collective-permute-done | bytes 1048608 | tf_op jit(solution)/shard_map/ppermute | solution.py:202
  154.0 2.3 %convolution_bitcast_fusion.3 = f32[1,256,512]{2,1,0:T(8,128)S(1)} fusion(bf16[256,2048]{1,0:T(8,128)(2,1)S(1)} %collective-permute-done.11, bf16[2048,512]{1,0:T(8,128)(2,1)} %param.23), kind=kOutput, calls=%fused_computation.40 | convolution fusion | flops 536870912 | bytes 3670016 | tf_op jit(solution)/shard_map/dot_general | solution.py:188
  156.3 2.3 %convolution_bitcast_fusion.2 = f32[1,256,512]{2,1,0:T(8,128)S(1)} fusion(bf16[256,2048]{1,0:T(8,128)(2,1)S(1)} %collective-permute-done.11, bf16[2048,512]{1,0:T(8,128)(2,1)} %collective-permute-done), kind=kOutput, calls=%fused_computation.39 | convolution fusion | flops 536870912 | bytes 3670016 | tf_op jit(solution)/shard_map/dot_general | solution.py:188
  159.8 1.7 copy-done.1
  161.4 1.5 pad_maximum_fusion.1
  162.9 4.4 %collective-permute-done.12 = f32[2,256,1024]{2,1,0:T(8,128)S(1)} collective-permute-done((f32[2,256,1024]{2,1,0:T(8,128)}, f32[2,256,1024]{2,1,0:T(8,128)S(1)}, u32[]{:S(2)}, u32[]{:S(2)}) %collective-permute-start.12) | collective-permute-done | bytes 2097184 | tf_op jit(solution)/shard_map/ppermute | solution.py:232
  167.3 1.4 fusion.23
  169.2 13.4 %collective-permute-done.13 = bf16[1,256,1024]{2,1,0:T(8,128)(2,1)S(1)} collective-permute-done((bf16[1,256,1024]{2,1,0:T(8,128)(2,1)S(1)}, bf16[1,256,1024]{2,1,0:T(8,128)(2,1)S(1)}, u32[]{:S(2)}, u32[]{:S(2)}) %collective-permute-start.13) | collective-permute-done | bytes 524320 | tf_op jit(solution)/shard_map/ppermute | solution.py:232
  182.6 1.5 fusion.27
  184.1 4.5 %collective-permute-start.14 = (bf16[256,1024]{1,0:T(8,128)(2,1)S(1)}, bf16[256,1024]{1,0:T(8,128)(2,1)S(1)}, u32[]{:S(2)}, u32[]{:S(2)}) collective-permute-start(bf16[256,1024]{1,0:T(8,128)(2,1)S(1)} %fusion.27), channel_id=1, source_target_pairs={{0,0},{1,8},{2,16},{3,24},{8,1},{9,9},{10,17},{11,25},{16,2},{17,1... | collective-permute-start | bytes 1572872 | tf_op jit(solution)/shard_map/ppermute | solution.py:242
  188.6 22.7 %collective-permute-done.14 = bf16[256,1024]{1,0:T(8,128)(2,1)S(1)} collective-permute-done((bf16[256,1024]{1,0:T(8,128)(2,1)S(1)}, bf16[256,1024]{1,0:T(8,128)(2,1)S(1)}, u32[]{:S(2)}, u32[]{:S(2)}) %collective-permute-start.14) | collective-permute-done | bytes 524320 | tf_op jit(solution)/shard_map/ppermute | solution.py:242
  211.6 0.9 pad_maximum_fusion.3
  (72 shorter events, 5.7 us)
Async XLA Ops:
  0.0 4.9 %copy-start = (f32[256,32]{0,1:T(8,128)S(1)}, f32[256,32]{0,1:T(8,128)}, u32[]{:S(2)}) copy-start(f32[256,32]{0,1:T(8,128)} %param.20) | copy-start | bytes 98308
  0.0 1.4 copy-start.4
  0.0 1.4 copy-start.5
  0.0 7.3 %copy-start.7 = (f32[4,2048]{1,0:T(4,128)S(1)}, f32[4,2048]{1,0:T(4,128)}, u32[]{:S(2)}) copy-start(f32[4,2048]{1,0:T(4,128)} %param.16) | copy-start | bytes 98308
  0.0 7.3 %copy-start.9 = (f32[4,128]{1,0:T(4,128)S(1)}, f32[4,128]{1,0:T(4,128)}, u32[]{:S(2)}) copy-start(f32[4,128]{1,0:T(4,128)} %param.17) | copy-start | bytes 6148
  0.0 7.3 %copy-start.10 = (f32[4,128]{1,0:T(4,128)S(1)}, f32[4,128]{1,0:T(4,128)}, u32[]{:S(2)}) copy-start(f32[4,128]{1,0:T(4,128)} %param.18) | copy-start | bytes 6148
  1.5 6.1 %collective-permute-start.1 = (bf16[3,2304]{1,0:T(4,128)(2,1)S(1)}, bf16[3,2304]{1,0:T(4,128)(2,1)S(1)}, u32[]{:S(2)}, u32[]{:S(2)}) collective-permute-start(bf16[3,2304]{1,0:T(4,128)(2,1)S(1)} %slice.99), channel_id=1, source_target_pairs={{0,4},{4,8},{8,12},{12,16},{16,20},{20,24},{24,28},{1,5},{5,9},{9,... | collective-permute-start | bytes 41480 | tf_op jit(solution)/shard_map/ppermute | solution.py:14
  15.1 14.3 %collective-permute-start.4 = (bf16[1,32,64,128]{3,2,1,0:T(8,128)(2,1)S(1)}, bf16[1,32,64,128]{3,2,1,0:T(8,128)(2,1)S(1)}, u32[]{:S(2)}, u32[]{:S(2)}) collective-permute-start(bf16[1,32,64,128]{3,2,1,0:T(8,128)(2,1)S(1)} %convert_bitcast_fusion), channel_id=1, source_target_pairs={{0,4},{4,8},{8,12},{12,16},{16,20},{20,24},{24,28},{1,5},{5,9},{9,... | collective-permute-start | bytes 1572872 | tf_op jit(solution)/shard_map/ppermute | solution.py:14
  29.4 24.4 %copy-start.3 = (f32[1,256,1,32]{1,2,3,0:T(1,128)S(1)}, f32[1,256,1,32]{1,2,3,0:T(1,128)}, u32[]{:S(2)}) copy-start(f32[1,256,1,32]{1,2,3,0:T(1,128)} %get-tuple-element.56) | copy-start | bytes 98308
  29.6 14.9 %collective-permute-start.5 = (bf16[1,32,64,128]{3,2,1,0:T(8,128)(2,1)S(1)}, bf16[1,32,64,128]{3,2,1,0:T(8,128)(2,1)S(1)}, u32[]{:S(2)}, u32[]{:S(2)}) collective-permute-start(bf16[1,32,64,128]{3,2,1,0:T(8,128)(2,1)S(1)} %fusion.26), channel_id=1, source_target_pairs={{0,8},{4,12},{8,16},{12,20},{16,24},{20,28},{1,9},{5,13},{9,17},{1... | collective-permute-start | bytes 1572872 | tf_op jit(solution)/shard_map/ppermute | solution.py:14
  35.0 5.0 %collective-permute-start.2 = (f32[1,32]{1,0:T(1,128)S(1)}, f32[1,32]{1,0:T(1,128)S(1)}, u32[]{:S(2)}, u32[]{:S(2)}) collective-permute-start(f32[1,32]{1,0:T(1,128)S(1)} %bitcast.123), channel_id=1, source_target_pairs={{0,4},{4,8},{8,12},{12,16},{16,20},{20,24},{24,28},{1,5},{5,9},{9,... | collective-permute-start | bytes 392 | tf_op jit(solution)/shard_map/ppermute | solution.py:14
  37.5 46.3 %collective-permute-start = (bf16[2048,512]{1,0:T(8,128)(2,1)}, bf16[2048,512]{1,0:T(8,128)(2,1)}, u32[]{:S(2)}, u32[]{:S(2)}) collective-permute-start(bf16[2048,512]{1,0:T(8,128)(2,1)} %param.23), channel_id=1, source_target_pairs={{0,4},{4,0},{1,5},{5,1},{2,6},{6,2},{3,7},{7,3},{8,12},{12,8},{9,1... | collective-permute-start | bytes 6291464 | tf_op jit(solution)/shard_map/ppermute | solution.py:180
  44.9 15.1 %collective-permute-start.6 = (bf16[1,32,64,128]{3,2,1,0:T(8,128)(2,1)S(1)}, bf16[1,32,64,128]{3,2,1,0:T(8,128)(2,1)S(1)}, u32[]{:S(2)}, u32[]{:S(2)}) collective-permute-start(bf16[1,32,64,128]{3,2,1,0:T(8,128)(2,1)S(1)} %fusion.22), channel_id=1, source_target_pairs={{0,16},{4,20},{8,24},{12,28},{1,17},{5,21},{9,25},{13,29},{2,18},{... | collective-permute-start | bytes 1572872 | tf_op jit(solution)/shard_map/ppermute | solution.py:14
  50.9 8.9 %collective-permute-start.3 = (f32[1,32]{1,0:T(1,128)S(1)}, f32[1,32]{1,0:T(1,128)S(1)}, u32[]{:S(2)}, u32[]{:S(2)}) collective-permute-start(f32[1,32]{1,0:T(1,128)S(1)} %bitcast_multiply_fusion.1), channel_id=1, source_target_pairs={{0,8},{4,12},{8,16},{12,20},{16,24},{20,28},{1,9},{5,13},{9,17},{1... | collective-permute-start | bytes 392 | tf_op jit(solution)/shard_map/ppermute | solution.py:14
  53.9 6.6 %copy-start.6 = (f32[256,32]{0,1:T(8,128)S(1)}, f32[256,32]{0,1:T(8,128)}, u32[]{:S(2)}) copy-start(f32[256,32]{0,1:T(8,128)} %param.19) | copy-start | bytes 98308
  53.9 6.6 %copy-start.11 = (f32[32]{0:T(128)S(1)}, f32[32]{0:T(128)}, u32[]{:S(2)}) copy-start(f32[32]{0:T(128)} %param.21) | copy-start | bytes 388
  64.2 2.0 copy-start.2
  66.2 0.8 copy-start.8
  83.8 24.3 %collective-permute-start.9 = (bf16[256,2048]{1,0:T(8,128)(2,1)}, bf16[256,2048]{1,0:T(8,128)(2,1)S(1)}, u32[]{:S(2)}, u32[]{:S(2)}) collective-permute-start(bf16[256,2048]{1,0:T(8,128)(2,1)} %multiply_convert_fusion.5), channel_id=1, source_target_pairs={{8,0},{16,8},{24,16},{9,1},{17,9},{25,17},{10,2},{18,10},{26,18},{... | collective-permute-start | bytes 3145736 | tf_op jit(solution)/shard_map/ppermute | solution.py:198
  85.1 24.3 %collective-permute-start.7 = (bf16[256,2048]{1,0:T(8,128)(2,1)}, bf16[256,2048]{1,0:T(8,128)(2,1)S(1)}, u32[]{:S(2)}, u32[]{:S(2)}) collective-permute-start(bf16[256,2048]{1,0:T(8,128)(2,1)} %multiply_convert_fusion.5), channel_id=1, source_target_pairs={{0,8},{8,16},{16,24},{1,9},{9,17},{17,25},{2,10},{10,18},{18,26},{... | collective-permute-start | bytes 3145736 | tf_op jit(solution)/shard_map/ppermute | solution.py:195
  108.1 23.2 %collective-permute-start.10 = (bf16[256,2048]{1,0:T(8,128)(2,1)S(1)}, bf16[256,2048]{1,0:T(8,128)(2,1)S(1)}, u32[]{:S(2)}, u32[]{:S(2)}) collective-permute-start(bf16[256,2048]{1,0:T(8,128)(2,1)S(1)} %collective-permute-done.9), channel_id=1, source_target_pairs={{8,0},{16,8},{9,1},{17,9},{10,2},{18,10},{11,3},{19,11},{12,4},{20... | collective-permute-start | bytes 3145736 | tf_op jit(solution)/shard_map/ppermute | solution.py:198
  109.4 21.9 %collective-permute-start.8 = (bf16[256,2048]{1,0:T(8,128)(2,1)S(1)}, bf16[256,2048]{1,0:T(8,128)(2,1)S(1)}, u32[]{:S(2)}, u32[]{:S(2)}) collective-permute-start(bf16[256,2048]{1,0:T(8,128)(2,1)S(1)} %collective-permute-done.7), channel_id=1, source_target_pairs={{8,16},{16,24},{9,17},{17,25},{10,18},{18,26},{11,19},{19,27},{12,... | collective-permute-start | bytes 3145736 | tf_op jit(solution)/shard_map/ppermute | solution.py:195
  131.4 22.6 %collective-permute-start.11 = (bf16[256,2048]{1,0:T(8,128)(2,1)S(1)}, bf16[256,2048]{1,0:T(8,128)(2,1)S(1)}, u32[]{:S(2)}, u32[]{:S(2)}) collective-permute-start(bf16[256,2048]{1,0:T(8,128)(2,1)S(1)} %broadcast_select_fusion.1), channel_id=1, source_target_pairs={{16,24},{8,0},{17,25},{9,1},{18,26},{10,2},{19,27},{11,3},{20,28},... | collective-permute-start | bytes 3145736 | tf_op jit(solution)/shard_map/ppermute | solution.py:202
  159.5 1.9 copy-start.1
  162.9 4.4 %collective-permute-start.12 = (f32[2,256,1024]{2,1,0:T(8,128)}, f32[2,256,1024]{2,1,0:T(8,128)S(1)}, u32[]{:S(2)}, u32[]{:S(2)}) collective-permute-start(f32[2,256,1024]{2,1,0:T(8,128)} %pad_maximum_fusion.1), channel_id=1, source_target_pairs={{0,1},{1,0},{2,3},{3,2},{4,5},{5,4},{6,7},{7,6},{8,9},{9,8},{10,11... | collective-permute-start | bytes 6291464 | tf_op jit(solution)/shard_map/ppermute | solution.py:232
  168.6 14.0 %collective-permute-start.13 = (bf16[1,256,1024]{2,1,0:T(8,128)(2,1)S(1)}, bf16[1,256,1024]{2,1,0:T(8,128)(2,1)S(1)}, u32[]{:S(2)}, u32[]{:S(2)}) collective-permute-start(bf16[1,256,1024]{2,1,0:T(8,128)(2,1)S(1)} %fusion.23), channel_id=1, source_target_pairs={{0,2},{1,3},{2,0},{3,1},{4,6},{5,7},{6,4},{7,5},{8,10},{9,11},{10,... | collective-permute-start | bytes 1572872 | tf_op jit(solution)/shard_map/ppermute | solution.py:232
  184.1 27.2 %collective-permute-start.14 = (bf16[256,1024]{1,0:T(8,128)(2,1)S(1)}, bf16[256,1024]{1,0:T(8,128)(2,1)S(1)}, u32[]{:S(2)}, u32[]{:S(2)}) collective-permute-start(bf16[256,1024]{1,0:T(8,128)(2,1)S(1)} %fusion.27), channel_id=1, source_target_pairs={{0,0},{1,8},{2,16},{3,24},{8,1},{9,9},{10,17},{11,25},{16,2},{17,1... | collective-permute-start | bytes 1572872 | tf_op jit(solution)/shard_map/ppermute | solution.py:242

commit v12 on v11

--- a/solution.py
+++ b/solution.py
@@ -148,6 +148,18 @@
         fold_local, jnp.zeros(blk_states.shape[1:], jnp.float32), (blk_decay, blk_states)
     )
     dev_decay = jnp.prod(blk_decay, axis=0)
+    if outer_axis is not None:
+        inner_count = ctx_count // tp_count
+        split = out_weight.shape[1] // 2
+        early, late = [], []
+        for d in range(1, inner_count):
+            pairs = [(s, (s + d) % inner_count) for s in range(inner_count)]
+            early.append(lax.ppermute(out_weight[:, :split], inner_axis, pairs))
+            late.append(lax.ppermute(out_weight[:, split:], inner_axis, pairs))
+        early, dev_state = lax.optimization_barrier((early, dev_state))
+        weight_pieces = [out_weight]
+        for first, second in zip(early, late):
+            weight_pieces += [first, second]
     incoming = prefix_states(dev_decay, dev_state, ctx_axes, ctx_count)
 
     def advance(state_carry, block_in):
@@ -176,12 +188,6 @@
     outer_at = lax.axis_index(outer_axis)
     tp_at = lax.axis_index("tp")
     inner_count = ctx_count // tp_count
-    weight_pieces = [out_weight] + [
-        lax.ppermute(
-            out_weight, inner_axis, [(s, (s + d) % inner_count) for s in range(inner_count)]
-        )
-        for d in range(1, inner_count)
-    ]
     weight_pieces, hidden = lax.optimization_barrier((weight_pieces, hidden))
     def times_weight(rows):
         return jnp.concatenate(

time: 214 us -> 235 us (1.098)
  starting transfers between devices: 40.6 us -> 54.8 us
  waiting for transfers between devices: 118 us -> 127 us
  matrix products: 30.4 us -> 22.8 us
  local copies, waits for them, and re-layouts: 8.29 us -> 12.6 us
    ppermute x2, starting transfers between devices: 5.34 us -> 17.1 us  [on_device(): lax.ppermute(going_right, outer_axis, [(s, s + 1) for s in range(step - 1...]
    dot_general x10 -> x15, matrix products: 23.8 us -> 15.3 us  [times_weight(): jnp.dot(rows, piece, preferred_element_type=jnp.float32)]
    ppermute x1, waiting for transfers between devices: 13.9 us -> 21 us  [on_device(): lax.ppermute(jnp.where(outer_at == tp_count - 2, going_right, going_left)...]
    ppermute x2, waiting for transfers between devices: 27.2 us -> 33.8 us  [on_device(): lax.ppermute(going_left, outer_axis, [(s, s - 1) for s in range(1, tp_cou...]
    ppermute x1 -> x2, waiting for transfers between devices: 14.9 us -> 12.7 us  [the longest x1 12.7 us: on_device(): early.append(lax.ppermute(out_weight[:, :split], inner_axis, pairs))]
    unnamed x31 -> x43, local copies, waits for them, and re-layouts: 3.1 us -> 5.03 us
  transfers between devices with their start and end apart: 15 -> 16, of which waited for: 10 -> 10; matrix products, arithmetic and copies ran while one was open for 15% -> 16% of each run, Pallas kernels for 0% -> 0%
where the time goes in v12:
time: 235 us; the launch traced here: 233 us
  waiting for transfers between devices  127 us (54%)
  starting transfers between devices  54.8 us (23%)
  matrix products  22.8 us (10%)
  other arithmetic  15.7 us (7%)
  local copies, waits for them, and re-layouts  12.6 us (5%)
    ppermute x2, waiting for transfers between devices, on_device(): lax.ppermute(going_left, outer_axis, [(s, s - 1) for s in range(1, tp_cou...  33.8 us
    ppermute x6, starting transfers between devices, shifted(): lax.ppermute(value, axis, [(source, source + steps) for source in range(f...  23.8 us
    ppermute x1, waiting for transfers between devices, on_device(): lax.ppermute(held[0].astype(jnp.bfloat16), (outer_axis, 'tp'), swap)  22.6 us
    ppermute x1, waiting for transfers between devices, on_device(): lax.ppermute(jnp.where(outer_at == tp_count - 2, going_right, going_left)...  21 us
    ppermute x6, waiting for transfers between devices, shifted(): lax.ppermute(value, axis, [(source, source + steps) for source in range(f...  18.9 us
    ppermute x2, waiting for transfers between devices, on_device(): lax.ppermute(sent if bit == 1 else sent.astype(jnp.bfloat16), 'tp', [(s,...  17.8 us
    ppermute x2, starting transfers between devices, on_device(): lax.ppermute(going_right, outer_axis, [(s, s + 1) for s in range(step - 1...  17.1 us
    dot_general x15, matrix products, times_weight(): jnp.dot(rows, piece, preferred_element_type=jnp.float32)  15.3 us
  transfers between devices with their start and end apart: 16, of which 10 were waited for; matrix products, arithmetic and copies ran while one was open for 16% of the time, Pallas kernels for 0%

profile of v12, /device:TPU:2, one launch (start us, length us, event | category | flops | bytes accessed | tf_op | source)
XLA Modules:
  0.0 233.3 jit_solution(15381167813089684867)
XLA Ops:
  0.0 1.4 constant_dynamic-update-slice_fusion.5
  1.6 3.6 %collective-permute-start.1 = (bf16[3,2304]{1,0:T(4,128)(2,1)S(1)}, bf16[3,2304]{1,0:T(4,128)(2,1)S(1)}, u32[]{:S(2)}, u32[]{:S(2)}) collective-permute-start(bf16[3,2304]{1,0:T(4,128)(2,1)S(1)} %slice.109), channel_id=1, source_target_pairs={{0,4},{4,8},{8,12},{12,16},{16,20},{20,24},{24,28},{1,5},{5,9},{9,... | collective-permute-start | bytes 41480 | tf_op jit(solution)/shard_map/ppermute | solution.py:14
  5.2 1.5 fusion.47
  6.7 1.5 collective-permute-start
  10.4 1.5 multiply_convert_fusion.3
  11.9 1.0 copy-done.5
  12.9 1.6 slice_convert_fusion
  14.5 1.9 copy.50
  16.4 0.9 slice_convert_fusion.1
  17.4 1.4 fusion.18
  18.8 12.7 %collective-permute-done = bf16[2048,256]{1,0:T(8,128)(2,1)S(1)} collective-permute-done((bf16[2048,256]{1,0:T(8,128)(2,1)}, bf16[2048,256]{1,0:T(8,128)(2,1)S(1)}, u32[]{:S(2)}, u32[]{:S(2)}) %collective-permute-start) | collective-permute-done | bytes 1048608 | tf_op jit(solution)/shard_map/ppermute | solution.py:157
  31.6 3.5 %collective-permute-start.5 = (bf16[1,32,64,128]{3,2,1,0:T(8,128)(2,1)S(1)}, bf16[1,32,64,128]{3,2,1,0:T(8,128)(2,1)S(1)}, u32[]{:S(2)}, u32[]{:S(2)}) collective-permute-start(bf16[1,32,64,128]{3,2,1,0:T(8,128)(2,1)S(1)} %convert_element_type.96), channel_id=1, source_target_pairs={{0,4},{4,8},{8,12},{12,16},{16,20},{20,24},{24,28},{1,5},{5,9},{9,... | collective-permute-start | bytes 1572872 | tf_op jit(solution)/shard_map/ppermute | solution.py:14
  35.1 10.0 %collective-permute-done.5 = bf16[1,32,64,128]{3,2,1,0:T(8,128)(2,1)S(1)} collective-permute-done((bf16[1,32,64,128]{3,2,1,0:T(8,128)(2,1)S(1)}, bf16[1,32,64,128]{3,2,1,0:T(8,128)(2,1)S(1)}, u32[]{:S(2)}, u32[]{:S(2)}) %collective-permute-start.5) | collective-permute-done | bytes 524320 | tf_op jit(solution)/shard_map/ppermute | solution.py:14
  45.3 5.4 %collective-permute-start.6 = (bf16[1,32,64,128]{3,2,1,0:T(8,128)(2,1)S(1)}, bf16[1,32,64,128]{3,2,1,0:T(8,128)(2,1)S(1)}, u32[]{:S(2)}, u32[]{:S(2)}) collective-permute-start(bf16[1,32,64,128]{3,2,1,0:T(8,128)(2,1)S(1)} %fusion.27), channel_id=1, source_target_pairs={{0,8},{4,12},{8,16},{12,20},{16,24},{20,28},{1,9},{5,13},{9,17},{1... | collective-permute-start | bytes 1572872 | tf_op jit(solution)/shard_map/ppermute | solution.py:14
  50.6 2.5 %collective-permute-start.3 = (f32[1,32]{1,0:T(1,128)S(1)}, f32[1,32]{1,0:T(1,128)S(1)}, u32[]{:S(2)}, u32[]{:S(2)}) collective-permute-start(f32[1,32]{1,0:T(1,128)S(1)} %bitcast.135), channel_id=1, source_target_pairs={{0,4},{4,8},{8,12},{12,16},{16,20},{20,24},{24,28},{1,5},{5,9},{9,... | collective-permute-start | bytes 392 | tf_op jit(solution)/shard_map/ppermute | solution.py:14
  53.2 2.5 %collective-permute-start.2 = (bf16[2048,256]{1,0:T(8,128)(2,1)}, bf16[2048,256]{1,0:T(8,128)(2,1)S(1)}, u32[]{:S(2)}, u32[]{:S(2)}) collective-permute-start(bf16[2048,256]{1,0:T(8,128)(2,1)} %get-tuple-element.68), channel_id=1, source_target_pairs={{0,4},{4,0},{1,5},{5,1},{2,6},{6,2},{3,7},{7,3},{8,12},{12,8},{9,1... | collective-permute-start | bytes 3145736 | tf_op jit(solution)/shard_map/ppermute | solution.py:158
  55.7 4.1 %collective-permute-done.6 = bf16[1,32,64,128]{3,2,1,0:T(8,128)(2,1)S(1)} collective-permute-done((bf16[1,32,64,128]{3,2,1,0:T(8,128)(2,1)S(1)}, bf16[1,32,64,128]{3,2,1,0:T(8,128)(2,1)S(1)}, u32[]{:S(2)}, u32[]{:S(2)}) %collective-permute-start.6) | collective-permute-done | bytes 524320 | tf_op jit(solution)/shard_map/ppermute | solution.py:14
  60.1 5.5 %collective-permute-start.7 = (bf16[1,32,64,128]{3,2,1,0:T(8,128)(2,1)S(1)}, bf16[1,32,64,128]{3,2,1,0:T(8,128)(2,1)S(1)}, u32[]{:S(2)}, u32[]{:S(2)}) collective-permute-start(bf16[1,32,64,128]{3,2,1,0:T(8,128)(2,1)S(1)} %fusion.23), channel_id=1, source_target_pairs={{0,16},{4,20},{8,24},{12,28},{1,17},{5,21},{9,25},{13,29},{2,18},{... | collective-permute-start | bytes 1572872 | tf_op jit(solution)/shard_map/ppermute | solution.py:14
  65.7 3.4 %collective-permute-start.4 = (f32[1,32]{1,0:T(1,128)S(1)}, f32[1,32]{1,0:T(1,128)S(1)}, u32[]{:S(2)}, u32[]{:S(2)}) collective-permute-start(f32[1,32]{1,0:T(1,128)S(1)} %bitcast_multiply_fusion.1), channel_id=1, source_target_pairs={{0,8},{4,12},{8,16},{12,20},{16,24},{20,28},{1,9},{5,13},{9,17},{1... | collective-permute-start | bytes 392 | tf_op jit(solution)/shard_map/ppermute | solution.py:14
  69.1 4.8 %collective-permute-done.4 = f32[1,32]{1,0:T(1,128)S(1)} collective-permute-done((f32[1,32]{1,0:T(1,128)S(1)}, f32[1,32]{1,0:T(1,128)S(1)}, u32[]{:S(2)}, u32[]{:S(2)}) %collective-permute-start.4) | collective-permute-done | bytes 160 | tf_op jit(solution)/shard_map/ppermute | solution.py:14
  73.9 1.1 fusion.40
  75.0 1.3 fusion.30
  76.4 3.7 %fusion.14 = f32[256,1,32,64]{0,3,2,1:T(8,128)} fusion(f32[32,64,256]{2,1,0:T(8,128)S(1)} %fusion.30, f32[256,1,32,64]{0,3,2,1:T(8,128)S(1)} %bitcast.123, f32[32,256]{1,0:T(8,128)S(1)} %bitcast.131, f32[256,256]{1,0:T(8,128)S(1)} %fusion.40, pred[256,256]{1,0:T(8,128)(4,1)S(1)} %iota_compare_fusion.1, f32[32]{0:T(128)S(1)} %copy-done.17, ...), kind=kOutput, calls=%fused_computation.26 | convolution fusion | flops 279969792 | bytes 8814720 | tf_op jit(solution)/shard_map/while/body/eval_jaxpr/gjts,sgjp->tgjp/dot_general | solution.py:46
  80.1 3.0 %copy.52 = f32[256,2048]{1,0:T(8,128)} copy(f32[256,2048]{0,1:T(8,128)} %bitcast.124) | data formatting | bytes 4194304 | tf_op jit(solution)/shard_map/reshape | solution.py:175
  83.1 2.5 %multiply_reduce_fusion = f32[256]{0:T(256)S(1)} fusion(f32[256,2048]{1,0:T(8,128)} %copy.52, bf16[256,2048]{1,0:T(8,128)(2,1)S(1)} %copy-done.6), kind=kLoop, calls=%fused_computation.28 | loop fusion | flops 4194048 | bytes 3146752 | tf_op jit(solution)/shard_map/reduce_sum | solution.py:177
  86.5 1.3 collective-permute-start.10
  87.8 16.2 %collective-permute-start.8 = (bf16[256,2048]{1,0:T(8,128)(2,1)S(1)}, bf16[256,2048]{1,0:T(8,128)(2,1)}, u32[]{:S(2)}, u32[]{:S(2)}) collective-permute-start(bf16[256,2048]{1,0:T(8,128)(2,1)S(1)} %multiply_convert_fusion.5), channel_id=1, source_target_pairs={{0,8},{8,16},{16,24},{1,9},{9,17},{17,25},{2,10},{10,18},{18,26},{... | collective-permute-start | bytes 3145736 | tf_op jit(solution)/shard_map/ppermute | solution.py:201
  106.3 18.1 %collective-permute-done.10 = bf16[256,2048]{1,0:T(8,128)(2,1)} collective-permute-done((bf16[256,2048]{1,0:T(8,128)(2,1)S(1)}, bf16[256,2048]{1,0:T(8,128)(2,1)}, u32[]{:S(2)}, u32[]{:S(2)}) %collective-permute-start.10) | collective-permute-done | bytes 1048608 | tf_op jit(solution)/shard_map/ppermute | solution.py:204
  124.5 1.3 collective-permute-start.11
  125.8 0.9 collective-permute-start.9
  126.7 1.7 convolution_bitcast_fusion.4
  128.4 1.7 convolution_bitcast_fusion.3
  130.0 1.7 convolution_bitcast_fusion.8
  131.7 1.9 convolution_bitcast_fusion
  133.6 1.9 convolution_bitcast_fusion.2
  135.6 15.6 %collective-permute-done.11 = bf16[256,2048]{1,0:T(8,128)(2,1)S(1)} collective-permute-done((bf16[256,2048]{1,0:T(8,128)(2,1)}, bf16[256,2048]{1,0:T(8,128)(2,1)S(1)}, u32[]{:S(2)}, u32[]{:S(2)}) %collective-permute-start.11) | collective-permute-done | bytes 1048608 | tf_op jit(solution)/shard_map/ppermute | solution.py:204
  151.3 1.3 collective-permute-start.12
  152.6 1.7 convolution_bitcast_fusion.7
  156.0 21.0 %collective-permute-done.12 = bf16[256,2048]{1,0:T(8,128)(2,1)S(1)} collective-permute-done((bf16[256,2048]{1,0:T(8,128)(2,1)S(1)}, bf16[256,2048]{1,0:T(8,128)(2,1)S(1)}, u32[]{:S(2)}, u32[]{:S(2)}) %collective-permute-start.12) | collective-permute-done | bytes 1048608 | tf_op jit(solution)/shard_map/ppermute | solution.py:208
  179.7 1.7 copy-done.2
  181.5 1.5 pad_maximum_fusion.1
  183.0 4.4 %collective-permute-done.13 = f32[2,256,1024]{2,1,0:T(8,128)S(1)} collective-permute-done((f32[2,256,1024]{2,1,0:T(8,128)}, f32[2,256,1024]{2,1,0:T(8,128)S(1)}, u32[]{:S(2)}, u32[]{:S(2)}) %collective-permute-start.13) | collective-permute-done | bytes 2097184 | tf_op jit(solution)/shard_map/ppermute | solution.py:238
  187.4 1.4 fusion.24
  189.3 13.4 %collective-permute-done.14 = bf16[1,256,1024]{2,1,0:T(8,128)(2,1)S(1)} collective-permute-done((bf16[1,256,1024]{2,1,0:T(8,128)(2,1)S(1)}, bf16[1,256,1024]{2,1,0:T(8,128)(2,1)S(1)}, u32[]{:S(2)}, u32[]{:S(2)}) %collective-permute-start.14) | collective-permute-done | bytes 524320 | tf_op jit(solution)/shard_map/ppermute | solution.py:238
  202.8 1.5 fusion.28
  204.2 5.4 %collective-permute-start.15 = (bf16[256,1024]{1,0:T(8,128)(2,1)S(1)}, bf16[256,1024]{1,0:T(8,128)(2,1)S(1)}, u32[]{:S(2)}, u32[]{:S(2)}) collective-permute-start(bf16[256,1024]{1,0:T(8,128)(2,1)S(1)} %fusion.28), channel_id=1, source_target_pairs={{0,0},{1,8},{2,16},{3,24},{8,1},{9,9},{10,17},{11,25},{16,2},{17,1... | collective-permute-start | bytes 1572872 | tf_op jit(solution)/shard_map/ppermute | solution.py:248
  209.7 22.6 %collective-permute-done.15 = bf16[256,1024]{1,0:T(8,128)(2,1)S(1)} collective-permute-done((bf16[256,1024]{1,0:T(8,128)(2,1)S(1)}, bf16[256,1024]{1,0:T(8,128)(2,1)S(1)}, u32[]{:S(2)}, u32[]{:S(2)}) %collective-permute-start.15) | collective-permute-done | bytes 524320 | tf_op jit(solution)/shard_map/ppermute | solution.py:248
  232.5 0.9 pad_maximum_fusion.3
  (92 shorter events, 11.4 us)
Async XLA Ops:
  0.0 8.2 %copy-start = (f32[256,32]{0,1:T(8,128)S(1)}, f32[256,32]{0,1:T(8,128)}, u32[]{:S(2)}) copy-start(f32[256,32]{0,1:T(8,128)} %param.20) | copy-start | bytes 98308
  0.0 1.5 copy-start.10
  0.0 1.5 copy-start.11
  0.0 5.2 %copy-start.8 = (bf16[2048,512]{1,0:T(8,128)(2,1)S(1)}, bf16[2048,512]{1,0:T(8,128)(2,1)}, u32[]{:S(2)}) copy-start(bf16[2048,512]{1,0:T(8,128)(2,1)} %param.23) | copy-start | bytes 6291460
  1.6 8.4 %copy-start.13 = (f32[4,2048]{1,0:T(4,128)S(1)}, f32[4,2048]{1,0:T(4,128)}, u32[]{:S(2)}) copy-start(f32[4,2048]{1,0:T(4,128)} %param.16) | copy-start | bytes 98308
  1.6 8.4 %copy-start.15 = (f32[4,128]{1,0:T(4,128)S(1)}, f32[4,128]{1,0:T(4,128)}, u32[]{:S(2)}) copy-start(f32[4,128]{1,0:T(4,128)} %param.17) | copy-start | bytes 6148
  1.6 8.4 %copy-start.16 = (f32[4,128]{1,0:T(4,128)S(1)}, f32[4,128]{1,0:T(4,128)}, u32[]{:S(2)}) copy-start(f32[4,128]{1,0:T(4,128)} %param.18) | copy-start | bytes 6148
  1.6 8.6 %collective-permute-start.1 = (bf16[3,2304]{1,0:T(4,128)(2,1)S(1)}, bf16[3,2304]{1,0:T(4,128)(2,1)S(1)}, u32[]{:S(2)}, u32[]{:S(2)}) collective-permute-start(bf16[3,2304]{1,0:T(4,128)(2,1)S(1)} %slice.109), channel_id=1, source_target_pairs={{0,4},{4,8},{8,12},{12,16},{16,20},{20,24},{24,28},{1,5},{5,9},{9,... | collective-permute-start | bytes 41480 | tf_op jit(solution)/shard_map/ppermute | solution.py:14
  6.7 24.8 %collective-permute-start = (bf16[2048,256]{1,0:T(8,128)(2,1)}, bf16[2048,256]{1,0:T(8,128)(2,1)S(1)}, u32[]{:S(2)}, u32[]{:S(2)}) collective-permute-start(bf16[2048,256]{1,0:T(8,128)(2,1)} %get-tuple-element.69), channel_id=1, source_target_pairs={{0,4},{4,0},{1,5},{5,1},{2,6},{6,2},{3,7},{7,3},{8,12},{12,8},{9,1... | collective-permute-start | bytes 3145736 | tf_op jit(solution)/shard_map/ppermute | solution.py:157
  11.9 1.0 copy-start.5
  14.5 2.9 %copy-start.12 = (f32[256,32]{0,1:T(8,128)S(1)}, f32[256,32]{0,1:T(8,128)}, u32[]{:S(2)}) copy-start(f32[256,32]{0,1:T(8,128)} %param.19) | copy-start | bytes 98308
  16.4 15.1 %copy-start.3 = (f32[256,2048]{0,1:T(8,128)}, f32[256,2048]{0,1:T(8,128)S(1)}, u32[]{:S(2)}) copy-start(f32[256,2048]{0,1:T(8,128)S(1)} %copy.50) | copy-start | bytes 6291460
  31.6 13.5 %collective-permute-start.5 = (bf16[1,32,64,128]{3,2,1,0:T(8,128)(2,1)S(1)}, bf16[1,32,64,128]{3,2,1,0:T(8,128)(2,1)S(1)}, u32[]{:S(2)}, u32[]{:S(2)}) collective-permute-start(bf16[1,32,64,128]{3,2,1,0:T(8,128)(2,1)S(1)} %convert_element_type.96), channel_id=1, source_target_pairs={{0,4},{4,8},{8,12},{12,16},{16,20},{20,24},{24,28},{1,5},{5,9},{9,... | collective-permute-start | bytes 1572872 | tf_op jit(solution)/shard_map/ppermute | solution.py:14
  45.3 14.5 %collective-permute-start.6 = (bf16[1,32,64,128]{3,2,1,0:T(8,128)(2,1)S(1)}, bf16[1,32,64,128]{3,2,1,0:T(8,128)(2,1)S(1)}, u32[]{:S(2)}, u32[]{:S(2)}) collective-permute-start(bf16[1,32,64,128]{3,2,1,0:T(8,128)(2,1)S(1)} %fusion.27), channel_id=1, source_target_pairs={{0,8},{4,12},{8,16},{12,20},{16,24},{20,28},{1,9},{5,13},{9,17},{1... | collective-permute-start | bytes 1572872 | tf_op jit(solution)/shard_map/ppermute | solution.py:14
  50.6 5.0 %collective-permute-start.3 = (f32[1,32]{1,0:T(1,128)S(1)}, f32[1,32]{1,0:T(1,128)S(1)}, u32[]{:S(2)}, u32[]{:S(2)}) collective-permute-start(f32[1,32]{1,0:T(1,128)S(1)} %bitcast.135), channel_id=1, source_target_pairs={{0,4},{4,8},{8,12},{12,16},{16,20},{20,24},{24,28},{1,5},{5,9},{9,... | collective-permute-start | bytes 392 | tf_op jit(solution)/shard_map/ppermute | solution.py:14
  53.2 33.3 %collective-permute-start.2 = (bf16[2048,256]{1,0:T(8,128)(2,1)}, bf16[2048,256]{1,0:T(8,128)(2,1)S(1)}, u32[]{:S(2)}, u32[]{:S(2)}) collective-permute-start(bf16[2048,256]{1,0:T(8,128)(2,1)} %get-tuple-element.68), channel_id=1, source_target_pairs={{0,4},{4,0},{1,5},{5,1},{2,6},{6,2},{3,7},{7,3},{8,12},{12,8},{9,1... | collective-permute-start | bytes 3145736 | tf_op jit(solution)/shard_map/ppermute | solution.py:158
  60.1 14.9 %collective-permute-start.7 = (bf16[1,32,64,128]{3,2,1,0:T(8,128)(2,1)S(1)}, bf16[1,32,64,128]{3,2,1,0:T(8,128)(2,1)S(1)}, u32[]{:S(2)}, u32[]{:S(2)}) collective-permute-start(bf16[1,32,64,128]{3,2,1,0:T(8,128)(2,1)S(1)} %fusion.23), channel_id=1, source_target_pairs={{0,16},{4,20},{8,24},{12,28},{1,17},{5,21},{9,25},{13,29},{2,18},{... | collective-permute-start | bytes 1572872 | tf_op jit(solution)/shard_map/ppermute | solution.py:14
  65.7 8.3 %collective-permute-start.4 = (f32[1,32]{1,0:T(1,128)S(1)}, f32[1,32]{1,0:T(1,128)S(1)}, u32[]{:S(2)}, u32[]{:S(2)}) collective-permute-start(f32[1,32]{1,0:T(1,128)S(1)} %bitcast_multiply_fusion.1), channel_id=1, source_target_pairs={{0,8},{4,12},{8,16},{12,20},{16,24},{20,28},{1,9},{5,13},{9,17},{1... | collective-permute-start | bytes 392 | tf_op jit(solution)/shard_map/ppermute | solution.py:14
  69.1 7.3 %copy-start.4 = (f32[256,2048]{0,1:T(8,128)S(1)}, f32[256,2048]{0,1:T(8,128)}, u32[]{:S(2)}) copy-start(f32[256,2048]{0,1:T(8,128)} %copy-done.3) | copy-start | bytes 6291460
  69.1 7.3 %copy-start.17 = (f32[32]{0:T(128)S(1)}, f32[32]{0:T(128)}, u32[]{:S(2)}) copy-start(f32[32]{0:T(128)} %param.21) | copy-start | bytes 388
  80.1 3.0 %copy-start.6 = (bf16[256,2048]{1,0:T(8,128)(2,1)S(1)}, bf16[256,2048]{1,0:T(8,128)(2,1)}, u32[]{:S(2)}) copy-start(bf16[256,2048]{1,0:T(8,128)(2,1)} %param.15) | copy-start | bytes 3145732
  80.1 5.5 %copy-start.14 = (f32[2048]{0:T(1024)S(1)}, f32[2048]{0:T(1024)}, u32[]{:S(2)}) copy-start(f32[2048]{0:T(1024)} %param.22) | copy-start | bytes 24580
  83.1 2.5 %copy-start.1 = (f32[256,2048]{1,0:T(8,128)S(1)}, f32[256,2048]{1,0:T(8,128)}, u32[]{:S(2)}) copy-start(f32[256,2048]{1,0:T(8,128)} %copy.52) | copy-start | bytes 6291460
  83.1 2.5 %copy-start.7 = (bf16[256,2048]{1,0:T(8,128)(2,1)S(1)}, bf16[256,2048]{1,0:T(8,128)(2,1)}, u32[]{:S(2)}) copy-start(bf16[256,2048]{1,0:T(8,128)(2,1)} %param.15) | copy-start | bytes 3145732
  86.5 38.0 %collective-permute-start.10 = (bf16[256,2048]{1,0:T(8,128)(2,1)S(1)}, bf16[256,2048]{1,0:T(8,128)(2,1)}, u32[]{:S(2)}, u32[]{:S(2)}) collective-permute-start(bf16[256,2048]{1,0:T(8,128)(2,1)S(1)} %multiply_convert_fusion.5), channel_id=1, source_target_pairs={{8,0},{16,8},{24,16},{9,1},{17,9},{25,17},{10,2},{18,10},{26,18},{... | collective-permute-start | bytes 3145736 | tf_op jit(solution)/shard_map/ppermute | solution.py:204
  87.8 38.0 %collective-permute-start.8 = (bf16[256,2048]{1,0:T(8,128)(2,1)S(1)}, bf16[256,2048]{1,0:T(8,128)(2,1)}, u32[]{:S(2)}, u32[]{:S(2)}) collective-permute-start(bf16[256,2048]{1,0:T(8,128)(2,1)S(1)} %multiply_convert_fusion.5), channel_id=1, source_target_pairs={{0,8},{8,16},{16,24},{1,9},{9,17},{17,25},{2,10},{10,18},{18,26},{... | collective-permute-start | bytes 3145736 | tf_op jit(solution)/shard_map/ppermute | solution.py:201
  103.9 1.6 copy-start.9
  124.5 26.7 %collective-permute-start.11 = (bf16[256,2048]{1,0:T(8,128)(2,1)}, bf16[256,2048]{1,0:T(8,128)(2,1)S(1)}, u32[]{:S(2)}, u32[]{:S(2)}) collective-permute-start(bf16[256,2048]{1,0:T(8,128)(2,1)} %collective-permute-done.10), channel_id=1, source_target_pairs={{8,0},{16,8},{9,1},{17,9},{10,2},{18,10},{11,3},{19,11},{12,4},{20... | collective-permute-start | bytes 3145736 | tf_op jit(solution)/shard_map/ppermute | solution.py:204
  125.8 25.4 %collective-permute-start.9 = (bf16[256,2048]{1,0:T(8,128)(2,1)}, bf16[256,2048]{1,0:T(8,128)(2,1)S(1)}, u32[]{:S(2)}, u32[]{:S(2)}) collective-permute-start(bf16[256,2048]{1,0:T(8,128)(2,1)} %collective-permute-done.8), channel_id=1, source_target_pairs={{8,16},{16,24},{9,17},{17,25},{10,18},{18,26},{11,19},{19,27},{12,... | collective-permute-start | bytes 3145736 | tf_op jit(solution)/shard_map/ppermute | solution.py:201
  151.3 25.7 %collective-permute-start.12 = (bf16[256,2048]{1,0:T(8,128)(2,1)S(1)}, bf16[256,2048]{1,0:T(8,128)(2,1)S(1)}, u32[]{:S(2)}, u32[]{:S(2)}) collective-permute-start(bf16[256,2048]{1,0:T(8,128)(2,1)S(1)} %get-tuple-element.67), channel_id=1, source_target_pairs={{16,24},{8,0},{17,25},{9,1},{18,26},{10,2},{19,27},{11,3},{20,28},... | collective-permute-start | bytes 3145736 | tf_op jit(solution)/shard_map/ppermute | solution.py:208
  179.5 2.0 copy-start.2
  183.0 4.4 %collective-permute-start.13 = (f32[2,256,1024]{2,1,0:T(8,128)}, f32[2,256,1024]{2,1,0:T(8,128)S(1)}, u32[]{:S(2)}, u32[]{:S(2)}) collective-permute-start(f32[2,256,1024]{2,1,0:T(8,128)} %pad_maximum_fusion.1), channel_id=1, source_target_pairs={{0,1},{1,0},{2,3},{3,2},{4,5},{5,4},{6,7},{7,6},{8,9},{9,8},{10,11... | collective-permute-start | bytes 6291464 | tf_op jit(solution)/shard_map/ppermute | solution.py:238
  188.7 14.0 %collective-permute-start.14 = (bf16[1,256,1024]{2,1,0:T(8,128)(2,1)S(1)}, bf16[1,256,1024]{2,1,0:T(8,128)(2,1)S(1)}, u32[]{:S(2)}, u32[]{:S(2)}) collective-permute-start(bf16[1,256,1024]{2,1,0:T(8,128)(2,1)S(1)} %fusion.24), channel_id=1, source_target_pairs={{0,2},{1,3},{2,0},{3,1},{4,6},{5,7},{6,4},{7,5},{8,10},{9,11},{10,... | collective-permute-start | bytes 1572872 | tf_op jit(solution)/shard_map/ppermute | solution.py:238
  204.2 28.0 %collective-permute-start.15 = (bf16[256,1024]{1,0:T(8,128)(2,1)S(1)}, bf16[256,1024]{1,0:T(8,128)(2,1)S(1)}, u32[]{:S(2)}, u32[]{:S(2)}) collective-permute-start(bf16[256,1024]{1,0:T(8,128)(2,1)S(1)} %fusion.28), channel_id=1, source_target_pairs={{0,0},{1,8},{2,16},{3,24},{8,1},{9,9},{10,17},{11,25},{16,2},{17,1... | collective-permute-start | bytes 1572872 | tf_op jit(solution)/shard_map/ppermute | solution.py:248

commit v13 on v11

--- a/solution.py
+++ b/solution.py
@@ -78,16 +78,21 @@
     own = (dev_decay, dev_state)
     if count == 1:
         return jnp.zeros_like(dev_state)
-    got = shifted(on_link(own), axis, 1, count)
-    before = got
-    upto = combine(got, own)
-    step = 2
-    while step < count:
-        got = shifted(on_link(upto), axis, step, count)
-        before = combine(got, before)
-        if step * 2 < count:
-            upto = combine(got, upto)
-        step *= 2
+    radix = 4
+    before = (jnp.ones_like(dev_decay), jnp.zeros_like(dev_state))
+    upto = own
+    span = 1
+    while span < count:
+        got = [
+            shifted(on_link(upto), axis, d * span, count)
+            for d in range(1, radix)
+            if d * span < count
+        ]
+        for item in got:
+            before = combine(item, before)
+        span *= radix
+        if span < count:
+            upto = combine(before, own)
     return before[1].astype(jnp.float32)
 
 

time: 214 us -> 254 us (1.19)
  starting transfers between devices: 40.6 us -> 71.1 us
  waiting for transfers between devices: 118 us -> 128 us
    ppermute x6 -> x8, starting transfers between devices: 23.7 us -> 47.4 us  [shifted(): lax.ppermute(value, axis, [(source, source + steps) for source in range(f...]
    ppermute x2, waiting for transfers between devices: 0.01 us -> 17.6 us  [on_device(): lax.ppermute(going_right, outer_axis, [(s, s + 1) for s in range(step - 1...]
    ppermute x2, waiting for transfers between devices: 27.2 us -> 17 us  [on_device(): lax.ppermute(going_left, outer_axis, [(s, s - 1) for s in range(1, tp_cou...]
    ppermute x1, starting transfers between devices: 2.46 us -> 10.8 us  [on_device(): lax.ppermute(out_weight, inner_axis, [(s, (s + d) % inner_count) for s in...]
    ppermute x6 -> x8, waiting for transfers between devices: 21.2 us -> 15.9 us  [shifted(): lax.ppermute(value, axis, [(source, source + steps) for source in range(f...]
    ppermute x1, waiting for transfers between devices: 14.9 us -> 19.2 us  [on_device(): lax.ppermute(out_weight, inner_axis, [(s, (s + d) % inner_count) for s in...]
  transfers between devices with their start and end apart: 15 -> 17, of which waited for: 10 -> 10; matrix products, arithmetic and copies ran while one was open for 15% -> 12% of each run, Pallas kernels for 0% -> 0%
where the time goes in v13:
time: 254 us; the launch traced here: 253 us
  waiting for transfers between devices  128 us (50%)
  starting transfers between devices  71.1 us (28%)
  matrix products  30.4 us (12%)
  other arithmetic  14.6 us (6%)
  local copies, waits for them, and re-layouts  8.47 us (3%)
    ppermute x8, starting transfers between devices, shifted(): lax.ppermute(value, axis, [(source, source + steps) for source in range(f...  47.4 us
    ppermute x1, waiting for transfers between devices, on_device(): lax.ppermute(held[0].astype(jnp.bfloat16), (outer_axis, 'tp'), swap)  25.1 us
    dot_general x10, matrix products, times_weight(): jnp.dot(rows, piece, preferred_element_type=jnp.float32)  23.8 us
    ppermute x1, waiting for transfers between devices, on_device(): lax.ppermute(out_weight, inner_axis, [(s, (s + d) % inner_count) for s in...  19.2 us
    ppermute x2, waiting for transfers between devices, on_device(): lax.ppermute(sent if bit == 1 else sent.astype(jnp.bfloat16), 'tp', [(s,...  17.8 us
    ppermute x2, waiting for transfers between devices, on_device(): lax.ppermute(going_right, outer_axis, [(s, s + 1) for s in range(step - 1...  17.6 us
    ppermute x2, waiting for transfers between devices, on_device(): lax.ppermute(going_left, outer_axis, [(s, s - 1) for s in range(1, tp_cou...  17 us
    ppermute x8, waiting for transfers between devices, shifted(): lax.ppermute(value, axis, [(source, source + steps) for source in range(f...  15.9 us
  transfers between devices with their start and end apart: 17, of which 10 were waited for; matrix products, arithmetic and copies ran while one was open for 12% of the time, Pallas kernels for 0%

profile of v13, /device:TPU:2, one launch (start us, length us, event | category | flops | bytes accessed | tf_op | source)
XLA Modules:
  0.0 253.1 jit_solution(1949417120000064398)
XLA Ops:
  0.0 1.3 constant_dynamic-update-slice_fusion.5
  1.5 3.4 %collective-permute-start.1 = (bf16[3,2304]{1,0:T(4,128)(2,1)S(1)}, bf16[3,2304]{1,0:T(4,128)(2,1)S(1)}, u32[]{:S(2)}, u32[]{:S(2)}) collective-permute-start(bf16[3,2304]{1,0:T(4,128)(2,1)S(1)} %slice.99), channel_id=1, source_target_pairs={{0,4},{4,8},{8,12},{12,16},{16,20},{20,24},{24,28},{1,5},{5,9},{9,... | collective-permute-start | bytes 41480 | tf_op jit(solution)/shard_map/ppermute | solution.py:14
  7.7 1.5 multiply_convert_fusion.3
  9.3 1.6 slice_convert_fusion
  10.9 1.9 copy.27
  12.8 2.2 fusion.17
  15.1 4.5 %collective-permute-start.5 = (bf16[1,32,64,128]{3,2,1,0:T(8,128)(2,1)S(1)}, bf16[1,32,64,128]{3,2,1,0:T(8,128)(2,1)S(1)}, u32[]{:S(2)}, u32[]{:S(2)}) collective-permute-start(bf16[1,32,64,128]{3,2,1,0:T(8,128)(2,1)S(1)} %convert_bitcast_fusion), channel_id=1, source_target_pairs={{0,12},{4,16},{8,20},{12,24},{16,28},{1,13},{5,17},{9,21},{13,25},... | collective-permute-start | bytes 1572872 | tf_op jit(solution)/shard_map/ppermute | solution.py:14
  19.6 3.5 %collective-permute-start.6 = (bf16[1,32,64,128]{3,2,1,0:T(8,128)(2,1)S(1)}, bf16[1,32,64,128]{3,2,1,0:T(8,128)(2,1)S(1)}, u32[]{:S(2)}, u32[]{:S(2)}) collective-permute-start(bf16[1,32,64,128]{3,2,1,0:T(8,128)(2,1)S(1)} %convert_bitcast_fusion), channel_id=1, source_target_pairs={{0,8},{4,12},{8,16},{12,20},{16,24},{20,28},{1,9},{5,13},{9,17},{1... | collective-permute-start | bytes 1572872 | tf_op jit(solution)/shard_map/ppermute | solution.py:14
  23.1 3.9 %collective-permute-start.7 = (bf16[1,32,64,128]{3,2,1,0:T(8,128)(2,1)S(1)}, bf16[1,32,64,128]{3,2,1,0:T(8,128)(2,1)S(1)}, u32[]{:S(2)}, u32[]{:S(2)}) collective-permute-start(bf16[1,32,64,128]{3,2,1,0:T(8,128)(2,1)S(1)} %convert_bitcast_fusion), channel_id=1, source_target_pairs={{0,4},{4,8},{8,12},{12,16},{16,20},{20,24},{24,28},{1,5},{5,9},{9,... | collective-permute-start | bytes 1572872 | tf_op jit(solution)/shard_map/ppermute | solution.py:14
  27.0 2.5 collective-permute-start.4
  29.5 1.4 collective-permute-start.2
  30.9 6.0 %collective-permute-done.4 = f32[1,32]{1,0:T(1,128)S(1)} collective-permute-done((f32[1,32]{1,0:T(1,128)S(1)}, f32[1,32]{1,0:T(1,128)S(1)}, u32[]{:S(2)}, u32[]{:S(2)}) %collective-permute-start.4) | collective-permute-done | bytes 160 | tf_op jit(solution)/shard_map/ppermute | solution.py:14
  36.9 21.5 %collective-permute-start.3 = (f32[1,32]{1,0:T(1,128)S(1)}, f32[1,32]{1,0:T(1,128)S(1)}, u32[]{:S(2)}, u32[]{:S(2)}) collective-permute-start(f32[1,32]{1,0:T(1,128)S(1)} %bitcast.123), channel_id=1, source_target_pairs={{0,8},{4,12},{8,16},{12,20},{16,24},{20,28},{1,9},{5,13},{9,17},{1... | collective-permute-start | bytes 392 | tf_op jit(solution)/shard_map/ppermute | solution.py:14
  58.4 10.8 %collective-permute-start = (bf16[2048,512]{1,0:T(8,128)(2,1)}, bf16[2048,512]{1,0:T(8,128)(2,1)}, u32[]{:S(2)}, u32[]{:S(2)}) collective-permute-start(bf16[2048,512]{1,0:T(8,128)(2,1)} %param.23), channel_id=1, source_target_pairs={{0,4},{4,0},{1,5},{5,1},{2,6},{6,2},{3,7},{7,3},{8,12},{12,8},{9,1... | collective-permute-start | bytes 6291464 | tf_op jit(solution)/shard_map/ppermute | solution.py:185
  69.8 6.8 %collective-permute-start.8 = (bf16[1,32,64,128]{3,2,1,0:T(8,128)(2,1)S(1)}, bf16[1,32,64,128]{3,2,1,0:T(8,128)(2,1)S(1)}, u32[]{:S(2)}, u32[]{:S(2)}) collective-permute-start(bf16[1,32,64,128]{3,2,1,0:T(8,128)(2,1)S(1)} %fusion.21), channel_id=1, source_target_pairs={{0,16},{4,20},{8,24},{12,28},{1,17},{5,21},{9,25},{13,29},{2,18},{... | collective-permute-start | bytes 1572872 | tf_op jit(solution)/shard_map/ppermute | solution.py:14
  76.9 9.8 %collective-permute-done.8 = bf16[1,32,64,128]{3,2,1,0:T(8,128)(2,1)S(1)} collective-permute-done((bf16[1,32,64,128]{3,2,1,0:T(8,128)(2,1)S(1)}, bf16[1,32,64,128]{3,2,1,0:T(8,128)(2,1)S(1)}, u32[]{:S(2)}, u32[]{:S(2)}) %collective-permute-start.8) | collective-permute-done | bytes 524320 | tf_op jit(solution)/shard_map/ppermute | solution.py:14
  87.5 3.7 %fusion.14 = f32[256,1,32,64]{0,3,2,1:T(8,128)} fusion(f32[32,64,256]{2,1,0:T(8,128)S(1)} %fusion.23, f32[256,1,32,64]{0,3,2,1:T(8,128)S(1)} %bitcast.109, f32[32,256]{1,0:T(8,128)S(1)} %bitcast.117, f32[256,256]{1,0:T(8,128)S(1)} %fusion.36, pred[256,256]{1,0:T(8,128)(4,1)S(1)} %iota_compare_fusion.1, f32[32]{0:T(128)S(1)} %copy-done.11, ...), kind=kOutput, calls=%fused_computation.26 | convolution fusion | flops 279969792 | bytes 8814720 | tf_op jit(solution)/shard_map/while/body/eval_jaxpr/gjts,sgjp->tgjp/dot_general | solution.py:46
  91.2 2.0 copy.32
  93.2 0.8 multiply_reduce_fusion
  94.0 1.8 multiply_convert_fusion.5
  95.8 19.2 %collective-permute-done = bf16[2048,512]{1,0:T(8,128)(2,1)} collective-permute-done((bf16[2048,512]{1,0:T(8,128)(2,1)}, bf16[2048,512]{1,0:T(8,128)(2,1)}, u32[]{:S(2)}, u32[]{:S(2)}) %collective-permute-start) | collective-permute-done | bytes 2097184 | tf_op jit(solution)/shard_map/ppermute | solution.py:185
  115.0 5.6 %collective-permute-start.9 = (bf16[256,2048]{1,0:T(8,128)(2,1)}, bf16[256,2048]{1,0:T(8,128)(2,1)S(1)}, u32[]{:S(2)}, u32[]{:S(2)}) collective-permute-start(bf16[256,2048]{1,0:T(8,128)(2,1)} %multiply_convert_fusion.5), channel_id=1, source_target_pairs={{0,8},{8,16},{16,24},{1,9},{9,17},{17,25},{2,10},{10,18},{18,26},{... | collective-permute-start | bytes 3145736 | tf_op jit(solution)/shard_map/ppermute | solution.py:200
  120.6 1.3 collective-permute-start.11
  122.0 2.6 %fusion.45 = f32[256,512]{1,0:T(8,128)S(1)} fusion(bf16[256,2048]{1,0:T(8,128)(2,1)} %multiply_convert_fusion.5, bf16[2048,512]{1,0:T(8,128)(2,1)} %param.23), kind=kOutput, calls=%fused_computation.118 | convolution fusion | flops 536870912 | bytes 3670016 | tf_op jit(solution)/shard_map/dot_general | solution.py:193
  124.6 17.6 %collective-permute-done.9 = bf16[256,2048]{1,0:T(8,128)(2,1)S(1)} collective-permute-done((bf16[256,2048]{1,0:T(8,128)(2,1)}, bf16[256,2048]{1,0:T(8,128)(2,1)S(1)}, u32[]{:S(2)}, u32[]{:S(2)}) %collective-permute-start.9) | collective-permute-done | bytes 1048608 | tf_op jit(solution)/shard_map/ppermute | solution.py:200
  143.0 3.3 %collective-permute-done.11 = bf16[256,2048]{1,0:T(8,128)(2,1)S(1)} collective-permute-done((bf16[256,2048]{1,0:T(8,128)(2,1)}, bf16[256,2048]{1,0:T(8,128)(2,1)S(1)}, u32[]{:S(2)}, u32[]{:S(2)}) %collective-permute-start.11) | collective-permute-done | bytes 1048608 | tf_op jit(solution)/shard_map/ppermute | solution.py:203
  146.3 1.3 collective-permute-start.12
  147.6 2.6 %fusion.46 = f32[256,512]{1,0:T(8,128)S(1)} fusion(bf16[256,2048]{1,0:T(8,128)(2,1)} %multiply_convert_fusion.5, bf16[2048,512]{1,0:T(8,128)(2,1)} %collective-permute-done), kind=kOutput, calls=%fused_computation.119 | convolution fusion | flops 536870912 | bytes 3670016 | tf_op jit(solution)/shard_map/dot_general | solution.py:193
  150.3 2.3 convolution_bitcast_fusion.1
  152.6 2.3 convolution_bitcast_fusion
  154.9 2.3 convolution_bitcast_fusion.5
  157.2 13.7 %collective-permute-done.12 = bf16[256,2048]{1,0:T(8,128)(2,1)S(1)} collective-permute-done((bf16[256,2048]{1,0:T(8,128)(2,1)S(1)}, bf16[256,2048]{1,0:T(8,128)(2,1)S(1)}, u32[]{:S(2)}, u32[]{:S(2)}) %collective-permute-start.12) | collective-permute-done | bytes 1048608 | tf_op jit(solution)/shard_map/ppermute | solution.py:203
  171.0 1.5 collective-permute-start.13
  172.5 2.3 convolution_bitcast_fusion.4
  174.8 2.4 fusion.30
  177.2 2.4 fusion.29
  179.7 15.1 %collective-permute-done.13 = bf16[256,2048]{1,0:T(8,128)(2,1)S(1)} collective-permute-done((bf16[256,2048]{1,0:T(8,128)(2,1)S(1)}, bf16[256,2048]{1,0:T(8,128)(2,1)S(1)}, u32[]{:S(2)}, u32[]{:S(2)}) %collective-permute-start.13) | collective-permute-done | bytes 1048608 | tf_op jit(solution)/shard_map/ppermute | solution.py:207
  194.8 2.3 convolution_bitcast_fusion.3
  197.1 2.3 convolution_bitcast_fusion.2
  200.6 1.7 copy-done.1
  202.3 1.5 pad_maximum_fusion.1
  203.7 4.4 %collective-permute-done.14 = f32[2,256,1024]{2,1,0:T(8,128)S(1)} collective-permute-done((f32[2,256,1024]{2,1,0:T(8,128)}, f32[2,256,1024]{2,1,0:T(8,128)S(1)}, u32[]{:S(2)}, u32[]{:S(2)}) %collective-permute-start.14) | collective-permute-done | bytes 2097184 | tf_op jit(solution)/shard_map/ppermute | solution.py:237
  208.1 1.4 fusion.18
  210.0 13.4 %collective-permute-done.15 = bf16[1,256,1024]{2,1,0:T(8,128)(2,1)S(1)} collective-permute-done((bf16[1,256,1024]{2,1,0:T(8,128)(2,1)S(1)}, bf16[1,256,1024]{2,1,0:T(8,128)(2,1)S(1)}, u32[]{:S(2)}, u32[]{:S(2)}) %collective-permute-start.15) | collective-permute-done | bytes 524320 | tf_op jit(solution)/shard_map/ppermute | solution.py:237
  223.5 1.5 fusion.25
  225.0 1.9 collective-permute-start.16
  226.9 25.1 %collective-permute-done.16 = bf16[256,1024]{1,0:T(8,128)(2,1)S(1)} collective-permute-done((bf16[256,1024]{1,0:T(8,128)(2,1)S(1)}, bf16[256,1024]{1,0:T(8,128)(2,1)S(1)}, u32[]{:S(2)}, u32[]{:S(2)}) %collective-permute-start.16) | collective-permute-done | bytes 524320 | tf_op jit(solution)/shard_map/ppermute | solution.py:247
  252.2 0.9 pad_maximum_fusion.3
  (74 shorter events, 7.4 us)
Async XLA Ops:
  0.0 4.9 %copy-start = (f32[256,32]{0,1:T(8,128)S(1)}, f32[256,32]{0,1:T(8,128)}, u32[]{:S(2)}) copy-start(f32[256,32]{0,1:T(8,128)} %param.20) | copy-start | bytes 98308
  0.0 1.4 copy-start.4
  0.0 1.4 copy-start.5
  0.0 7.3 %copy-start.7 = (f32[4,2048]{1,0:T(4,128)S(1)}, f32[4,2048]{1,0:T(4,128)}, u32[]{:S(2)}) copy-start(f32[4,2048]{1,0:T(4,128)} %param.16) | copy-start | bytes 98308
  0.0 7.3 %copy-start.9 = (f32[4,128]{1,0:T(4,128)S(1)}, f32[4,128]{1,0:T(4,128)}, u32[]{:S(2)}) copy-start(f32[4,128]{1,0:T(4,128)} %param.17) | copy-start | bytes 6148
  0.0 7.3 %copy-start.10 = (f32[4,128]{1,0:T(4,128)S(1)}, f32[4,128]{1,0:T(4,128)}, u32[]{:S(2)}) copy-start(f32[4,128]{1,0:T(4,128)} %param.18) | copy-start | bytes 6148
  1.5 6.1 %collective-permute-start.1 = (bf16[3,2304]{1,0:T(4,128)(2,1)S(1)}, bf16[3,2304]{1,0:T(4,128)(2,1)S(1)}, u32[]{:S(2)}, u32[]{:S(2)}) collective-permute-start(bf16[3,2304]{1,0:T(4,128)(2,1)S(1)} %slice.99), channel_id=1, source_target_pairs={{0,4},{4,8},{8,12},{12,16},{16,20},{20,24},{24,28},{1,5},{5,9},{9,... | collective-permute-start | bytes 41480 | tf_op jit(solution)/shard_map/ppermute | solution.py:14
  12.8 18.0 %copy-start.3 = (f32[1,256,1,32]{1,2,3,0:T(1,128)S(1)}, f32[1,256,1,32]{1,2,3,0:T(1,128)}, u32[]{:S(2)}) copy-start(f32[1,256,1,32]{1,2,3,0:T(1,128)} %get-tuple-element.56) | copy-start | bytes 98308
  15.1 54.1 %collective-permute-start.5 = (bf16[1,32,64,128]{3,2,1,0:T(8,128)(2,1)S(1)}, bf16[1,32,64,128]{3,2,1,0:T(8,128)(2,1)S(1)}, u32[]{:S(2)}, u32[]{:S(2)}) collective-permute-start(bf16[1,32,64,128]{3,2,1,0:T(8,128)(2,1)S(1)} %convert_bitcast_fusion), channel_id=1, source_target_pairs={{0,12},{4,16},{8,20},{12,24},{16,28},{1,13},{5,17},{9,21},{13,25},... | collective-permute-start | bytes 1572872 | tf_op jit(solution)/shard_map/ppermute | solution.py:14
  19.6 49.6 %collective-permute-start.6 = (bf16[1,32,64,128]{3,2,1,0:T(8,128)(2,1)S(1)}, bf16[1,32,64,128]{3,2,1,0:T(8,128)(2,1)S(1)}, u32[]{:S(2)}, u32[]{:S(2)}) collective-permute-start(bf16[1,32,64,128]{3,2,1,0:T(8,128)(2,1)S(1)} %convert_bitcast_fusion), channel_id=1, source_target_pairs={{0,8},{4,12},{8,16},{12,20},{16,24},{20,28},{1,9},{5,13},{9,17},{1... | collective-permute-start | bytes 1572872 | tf_op jit(solution)/shard_map/ppermute | solution.py:14
  23.1 46.1 %collective-permute-start.7 = (bf16[1,32,64,128]{3,2,1,0:T(8,128)(2,1)S(1)}, bf16[1,32,64,128]{3,2,1,0:T(8,128)(2,1)S(1)}, u32[]{:S(2)}, u32[]{:S(2)}) collective-permute-start(bf16[1,32,64,128]{3,2,1,0:T(8,128)(2,1)S(1)} %convert_bitcast_fusion), channel_id=1, source_target_pairs={{0,4},{4,8},{8,12},{12,16},{16,20},{20,24},{24,28},{1,5},{5,9},{9,... | collective-permute-start | bytes 1572872 | tf_op jit(solution)/shard_map/ppermute | solution.py:14
  27.0 9.9 %collective-permute-start.4 = (f32[1,32]{1,0:T(1,128)S(1)}, f32[1,32]{1,0:T(1,128)S(1)}, u32[]{:S(2)}, u32[]{:S(2)}) collective-permute-start(f32[1,32]{1,0:T(1,128)S(1)} %bitcast.121), channel_id=1, source_target_pairs={{0,4},{4,8},{8,12},{12,16},{16,20},{20,24},{24,28},{1,5},{5,9},{9,... | collective-permute-start | bytes 392 | tf_op jit(solution)/shard_map/ppermute | solution.py:14
  29.5 28.9 %collective-permute-start.2 = (f32[1,32]{1,0:T(1,128)S(1)}, f32[1,32]{1,0:T(1,128)S(1)}, u32[]{:S(2)}, u32[]{:S(2)}) collective-permute-start(f32[1,32]{1,0:T(1,128)S(1)} %bitcast.122), channel_id=1, source_target_pairs={{0,12},{4,16},{8,20},{12,24},{16,28},{1,13},{5,17},{9,21},{13,25},... | collective-permute-start | bytes 392 | tf_op jit(solution)/shard_map/ppermute | solution.py:14
  36.9 32.3 %collective-permute-start.3 = (f32[1,32]{1,0:T(1,128)S(1)}, f32[1,32]{1,0:T(1,128)S(1)}, u32[]{:S(2)}, u32[]{:S(2)}) collective-permute-start(f32[1,32]{1,0:T(1,128)S(1)} %bitcast.123), channel_id=1, source_target_pairs={{0,8},{4,12},{8,16},{12,20},{16,24},{20,28},{1,9},{5,13},{9,17},{1... | collective-permute-start | bytes 392 | tf_op jit(solution)/shard_map/ppermute | solution.py:14
  58.4 56.7 %collective-permute-start = (bf16[2048,512]{1,0:T(8,128)(2,1)}, bf16[2048,512]{1,0:T(8,128)(2,1)}, u32[]{:S(2)}, u32[]{:S(2)}) collective-permute-start(bf16[2048,512]{1,0:T(8,128)(2,1)} %param.23), channel_id=1, source_target_pairs={{0,4},{4,0},{1,5},{5,1},{2,6},{6,2},{3,7},{7,3},{8,12},{12,8},{9,1... | collective-permute-start | bytes 6291464 | tf_op jit(solution)/shard_map/ppermute | solution.py:185
  69.8 16.9 %collective-permute-start.8 = (bf16[1,32,64,128]{3,2,1,0:T(8,128)(2,1)S(1)}, bf16[1,32,64,128]{3,2,1,0:T(8,128)(2,1)S(1)}, u32[]{:S(2)}, u32[]{:S(2)}) collective-permute-start(bf16[1,32,64,128]{3,2,1,0:T(8,128)(2,1)S(1)} %fusion.21), channel_id=1, source_target_pairs={{0,16},{4,20},{8,24},{12,28},{1,17},{5,21},{9,25},{13,29},{2,18},{... | collective-permute-start | bytes 1572872 | tf_op jit(solution)/shard_map/ppermute | solution.py:14
  86.7 0.8 copy-start.6
  86.7 0.8 copy-start.11
  91.2 2.0 copy-start.2
  93.2 0.8 copy-start.8
  115.0 27.2 %collective-permute-start.9 = (bf16[256,2048]{1,0:T(8,128)(2,1)}, bf16[256,2048]{1,0:T(8,128)(2,1)S(1)}, u32[]{:S(2)}, u32[]{:S(2)}) collective-permute-start(bf16[256,2048]{1,0:T(8,128)(2,1)} %multiply_convert_fusion.5), channel_id=1, source_target_pairs={{0,8},{8,16},{16,24},{1,9},{9,17},{17,25},{2,10},{10,18},{18,26},{... | collective-permute-start | bytes 3145736 | tf_op jit(solution)/shard_map/ppermute | solution.py:200
  120.6 25.7 %collective-permute-start.11 = (bf16[256,2048]{1,0:T(8,128)(2,1)}, bf16[256,2048]{1,0:T(8,128)(2,1)S(1)}, u32[]{:S(2)}, u32[]{:S(2)}) collective-permute-start(bf16[256,2048]{1,0:T(8,128)(2,1)} %multiply_convert_fusion.5), channel_id=1, source_target_pairs={{8,0},{16,8},{24,16},{9,1},{17,9},{25,17},{10,2},{18,10},{26,18},{... | collective-permute-start | bytes 3145736 | tf_op jit(solution)/shard_map/ppermute | solution.py:203
  142.2 15.0 %collective-permute-start.10 = (bf16[256,2048]{1,0:T(8,128)(2,1)S(1)}, bf16[256,2048]{1,0:T(8,128)(2,1)S(1)}, u32[]{:S(2)}, u32[]{:S(2)}) collective-permute-start(bf16[256,2048]{1,0:T(8,128)(2,1)S(1)} %collective-permute-done.9), channel_id=1, source_target_pairs={{8,16},{16,24},{9,17},{17,25},{10,18},{18,26},{11,19},{19,27},{12,... | collective-permute-start | bytes 3145736 | tf_op jit(solution)/shard_map/ppermute | solution.py:200
  146.3 24.6 %collective-permute-start.12 = (bf16[256,2048]{1,0:T(8,128)(2,1)S(1)}, bf16[256,2048]{1,0:T(8,128)(2,1)S(1)}, u32[]{:S(2)}, u32[]{:S(2)}) collective-permute-start(bf16[256,2048]{1,0:T(8,128)(2,1)S(1)} %collective-permute-done.11), channel_id=1, source_target_pairs={{8,0},{16,8},{9,1},{17,9},{10,2},{18,10},{11,3},{19,11},{12,4},{20... | collective-permute-start | bytes 3145736 | tf_op jit(solution)/shard_map/ppermute | solution.py:203
  171.0 23.8 %collective-permute-start.13 = (bf16[256,2048]{1,0:T(8,128)(2,1)S(1)}, bf16[256,2048]{1,0:T(8,128)(2,1)S(1)}, u32[]{:S(2)}, u32[]{:S(2)}) collective-permute-start(bf16[256,2048]{1,0:T(8,128)(2,1)S(1)} %broadcast_select_fusion.1), channel_id=1, source_target_pairs={{16,24},{8,0},{17,25},{9,1},{18,26},{10,2},{19,27},{11,3},{20,28},... | collective-permute-start | bytes 3145736 | tf_op jit(solution)/shard_map/ppermute | solution.py:207
  200.3 1.9 copy-start.1
  203.7 4.4 %collective-permute-start.14 = (f32[2,256,1024]{2,1,0:T(8,128)}, f32[2,256,1024]{2,1,0:T(8,128)S(1)}, u32[]{:S(2)}, u32[]{:S(2)}) collective-permute-start(f32[2,256,1024]{2,1,0:T(8,128)} %pad_maximum_fusion.1), channel_id=1, source_target_pairs={{0,1},{1,0},{2,3},{3,2},{4,5},{5,4},{6,7},{7,6},{8,9},{9,8},{10,11... | collective-permute-start | bytes 6291464 | tf_op jit(solution)/shard_map/ppermute | solution.py:237
  209.4 14.0 %collective-permute-start.15 = (bf16[1,256,1024]{2,1,0:T(8,128)(2,1)S(1)}, bf16[1,256,1024]{2,1,0:T(8,128)(2,1)S(1)}, u32[]{:S(2)}, u32[]{:S(2)}) collective-permute-start(bf16[1,256,1024]{2,1,0:T(8,128)(2,1)S(1)} %fusion.18), channel_id=1, source_target_pairs={{0,2},{1,3},{2,0},{3,1},{4,6},{5,7},{6,4},{7,5},{8,10},{9,11},{10,... | collective-permute-start | bytes 1572872 | tf_op jit(solution)/shard_map/ppermute | solution.py:237
  225.0 27.0 %collective-permute-start.16 = (bf16[256,1024]{1,0:T(8,128)(2,1)S(1)}, bf16[256,1024]{1,0:T(8,128)(2,1)S(1)}, u32[]{:S(2)}, u32[]{:S(2)}) collective-permute-start(bf16[256,1024]{1,0:T(8,128)(2,1)S(1)} %fusion.25), channel_id=1, source_target_pairs={{0,0},{1,8},{2,16},{3,24},{8,1},{9,9},{10,17},{11,25},{16,2},{17,1... | collective-permute-start | bytes 1572872 | tf_op jit(solution)/shard_map/ppermute | solution.py:247

commit v14 on v11

--- a/solution.py
+++ b/solution.py
@@ -75,20 +75,29 @@
 
 
 def prefix_states(dev_decay, dev_state, axis, count):
-    own = (dev_decay, dev_state)
     if count == 1:
         return jnp.zeros_like(dev_state)
-    got = shifted(on_link(own), axis, 1, count)
-    before = got
-    upto = combine(got, own)
+    got = shifted(dev_decay, axis, 1, count)
+    decay_before, decay_upto = got, got * dev_decay
+    scales = []
     step = 2
     while step < count:
-        got = shifted(on_link(upto), axis, step, count)
-        before = combine(got, before)
+        scales.append((decay_before, decay_upto))
+        got = shifted(decay_upto, axis, step, count)
+        decay_before, decay_upto = got * decay_before, got * decay_upto
+        step *= 2
+    scales, dev_state = lax.optimization_barrier((scales, dev_state))
+    got = shifted(dev_state.astype(jnp.bfloat16), axis, 1, count).astype(jnp.float32)
+    before = got
+    upto = dev_decay[..., None, None] * got + dev_state
+    step = 2
+    for scale_before, scale_upto in scales:
+        got = shifted(upto.astype(jnp.bfloat16), axis, step, count).astype(jnp.float32)
+        before = scale_before[..., None, None] * got + before
         if step * 2 < count:
-            upto = combine(got, upto)
+            upto = scale_upto[..., None, None] * got + upto
         step *= 2
-    return before[1].astype(jnp.float32)
+    return before
 
 
 def on_device(

time: 214 us -> 218 us (1.019)
    ppermute x6, waiting for transfers between devices: 21.2 us -> 24.8 us  [shifted(): lax.ppermute(value, axis, [(source, source + steps) for source in range(f...]
    ppermute x6, starting transfers between devices: 23.7 us -> 26.6 us  [shifted(): lax.ppermute(value, axis, [(source, source + steps) for source in range(f...]
    ppermute x1, starting transfers between devices: 2.46 us -> 0.07 us  [on_device(): lax.ppermute(out_weight, inner_axis, [(s, (s + d) % inner_count) for s in...]
  transfers between devices with their start and end apart: 15 -> 15, of which waited for: 10 -> 12; matrix products, arithmetic and copies ran while one was open for 15% -> 15% of each run, Pallas kernels for 0% -> 0%
where the time goes in v14:
time: 218 us; the launch traced here: 216 us
  waiting for transfers between devices  119 us (55%)
  starting transfers between devices  42.5 us (19%)
  matrix products  30.4 us (14%)
  other arithmetic  15.1 us (7%)
  local copies, waits for them, and re-layouts  8.3 us (4%)
    ppermute x6, starting transfers between devices, shifted(): lax.ppermute(value, axis, [(source, source + steps) for source in range(f...  26.6 us
    ppermute x2, waiting for transfers between devices, on_device(): lax.ppermute(going_left, outer_axis, [(s, s - 1) for s in range(1, tp_cou...  26 us
    ppermute x6, waiting for transfers between devices, shifted(): lax.ppermute(value, axis, [(source, source + steps) for source in range(f...  24.8 us
    dot_general x10, matrix products, times_weight(): jnp.dot(rows, piece, preferred_element_type=jnp.float32)  23.8 us
    ppermute x1, waiting for transfers between devices, on_device(): lax.ppermute(held[0].astype(jnp.bfloat16), (outer_axis, 'tp'), swap)  22.6 us
    ppermute x2, waiting for transfers between devices, on_device(): lax.ppermute(sent if bit == 1 else sent.astype(jnp.bfloat16), 'tp', [(s,...  17.8 us
    ppermute x1, waiting for transfers between devices, on_device(): lax.ppermute(out_weight, inner_axis, [(s, (s + d) % inner_count) for s in...  14.7 us
    ppermute x1, waiting for transfers between devices, on_device(): lax.ppermute(jnp.where(outer_at == tp_count - 2, going_right, going_left)...  13.4 us
  transfers between devices with their start and end apart: 15, of which 12 were waited for; matrix products, arithmetic and copies ran while one was open for 15% of the time, Pallas kernels for 0%

profile of v14, /device:TPU:2, one launch (start us, length us, event | category | flops | bytes accessed | tf_op | source)
XLA Modules:
  0.0 216.3 jit_solution(6371874748100010762)
XLA Ops:
  0.0 1.3 constant_dynamic-update-slice_fusion.5
  1.5 3.4 %collective-permute-start.1 = (bf16[3,2304]{1,0:T(4,128)(2,1)S(1)}, bf16[3,2304]{1,0:T(4,128)(2,1)S(1)}, u32[]{:S(2)}, u32[]{:S(2)}) collective-permute-start(bf16[3,2304]{1,0:T(4,128)(2,1)S(1)} %slice.99), channel_id=1, source_target_pairs={{0,4},{4,8},{8,12},{12,16},{16,20},{20,24},{24,28},{1,5},{5,9},{9,... | collective-permute-start | bytes 41480 | tf_op jit(solution)/shard_map/ppermute | solution.py:14
  5.9 0.7 fusion.48
  7.2 3.4 %collective-permute-start.2 = (f32[1,32]{1,0:T(1,128)S(1)}, f32[1,32]{1,0:T(1,128)S(1)}, u32[]{:S(2)}, u32[]{:S(2)}) collective-permute-start(f32[1,32]{1,0:T(1,128)S(1)} %bitcast.117), channel_id=1, source_target_pairs={{0,4},{4,8},{8,12},{12,16},{16,20},{20,24},{24,28},{1,5},{5,9},{9,... | collective-permute-start | bytes 392 | tf_op jit(solution)/shard_map/ppermute | solution.py:14
  11.9 5.1 %collective-permute-start.3 = (f32[1,32]{1,0:T(1,128)S(1)}, f32[1,32]{1,0:T(1,128)S(1)}, u32[]{:S(2)}, u32[]{:S(2)}) collective-permute-start(f32[1,32]{1,0:T(1,128)S(1)} %bitcast_multiply_fusion.1), channel_id=1, source_target_pairs={{0,8},{4,12},{8,16},{12,20},{16,24},{20,28},{1,9},{5,13},{9,17},{1... | collective-permute-start | bytes 392 | tf_op jit(solution)/shard_map/ppermute | solution.py:14
  17.2 1.1 collective-permute-done.3
  18.5 1.5 multiply_convert_fusion.3
  20.0 1.6 slice_convert_fusion
  21.6 1.9 copy.27
  23.5 2.2 %fusion.18 = f32[1,32,64,128]{3,2,1,0:T(8,128)S(1)} fusion(f32[256,32]{0,1:T(8,128)S(1)} %bitcast.110, f32[256,128]{1,0:T(8,128)S(1)} %slice_convert_fusion.1, f32[32]{0:T(128)} %get-tuple-element.81, f32[256,32,64]{0,2,1:T(8,128)S(1)} %bitcast.102, f32[256,32]{0,1:T(8,128)} %param.19), kind=kOutput, calls=%fused_computation.33 | convolution fusion | flops 137625600 | bytes 3342464 | tf_op jit(solution)/shard_map/vmap(sgjp,sgjn->gjpn)/dot_general | solution.py:54
  25.8 2.6 %collective-permute-start.4 = (bf16[1,32,64,128]{3,2,1,0:T(8,128)(2,1)S(1)}, bf16[1,32,64,128]{3,2,1,0:T(8,128)(2,1)S(1)}, u32[]{:S(2)}, u32[]{:S(2)}) collective-permute-start(bf16[1,32,64,128]{3,2,1,0:T(8,128)(2,1)S(1)} %convert_element_type.94), channel_id=1, source_target_pairs={{0,4},{4,8},{8,12},{12,16},{16,20},{20,24},{24,28},{1,5},{5,9},{9,... | collective-permute-start | bytes 1572872 | tf_op jit(solution)/shard_map/ppermute | solution.py:14
  28.4 8.8 %collective-permute-done.4 = bf16[1,32,64,128]{3,2,1,0:T(8,128)(2,1)S(1)} collective-permute-done((bf16[1,32,64,128]{3,2,1,0:T(8,128)(2,1)S(1)}, bf16[1,32,64,128]{3,2,1,0:T(8,128)(2,1)S(1)}, u32[]{:S(2)}, u32[]{:S(2)}) %collective-permute-start.4) | collective-permute-done | bytes 524320 | tf_op jit(solution)/shard_map/ppermute | solution.py:14
  37.5 6.7 %collective-permute-start.5 = (bf16[1,32,64,128]{3,2,1,0:T(8,128)(2,1)S(1)}, bf16[1,32,64,128]{3,2,1,0:T(8,128)(2,1)S(1)}, u32[]{:S(2)}, u32[]{:S(2)}) collective-permute-start(bf16[1,32,64,128]{3,2,1,0:T(8,128)(2,1)S(1)} %fusion.27), channel_id=1, source_target_pairs={{0,8},{4,12},{8,16},{12,20},{16,24},{20,28},{1,9},{5,13},{9,17},{1... | collective-permute-start | bytes 1572872 | tf_op jit(solution)/shard_map/ppermute | solution.py:14
  44.2 7.6 %collective-permute-done.5 = bf16[1,32,64,128]{3,2,1,0:T(8,128)(2,1)S(1)} collective-permute-done((bf16[1,32,64,128]{3,2,1,0:T(8,128)(2,1)S(1)}, bf16[1,32,64,128]{3,2,1,0:T(8,128)(2,1)S(1)}, u32[]{:S(2)}, u32[]{:S(2)}) %collective-permute-start.5) | collective-permute-done | bytes 524320 | tf_op jit(solution)/shard_map/ppermute | solution.py:14
  52.2 5.4 %collective-permute-start.6 = (bf16[1,32,64,128]{3,2,1,0:T(8,128)(2,1)S(1)}, bf16[1,32,64,128]{3,2,1,0:T(8,128)(2,1)S(1)}, u32[]{:S(2)}, u32[]{:S(2)}) collective-permute-start(bf16[1,32,64,128]{3,2,1,0:T(8,128)(2,1)S(1)} %fusion.23), channel_id=1, source_target_pairs={{0,16},{4,20},{8,24},{12,28},{1,17},{5,21},{9,25},{13,29},{2,18},{... | collective-permute-start | bytes 1572872 | tf_op jit(solution)/shard_map/ppermute | solution.py:14
  57.9 6.7 %collective-permute-done.6 = bf16[1,32,64,128]{3,2,1,0:T(8,128)(2,1)S(1)} collective-permute-done((bf16[1,32,64,128]{3,2,1,0:T(8,128)(2,1)S(1)}, bf16[1,32,64,128]{3,2,1,0:T(8,128)(2,1)S(1)}, u32[]{:S(2)}, u32[]{:S(2)}) %collective-permute-start.6) | collective-permute-done | bytes 524320 | tf_op jit(solution)/shard_map/ppermute | solution.py:14
  65.1 3.7 %fusion.14 = f32[256,1,32,64]{0,3,2,1:T(8,128)} fusion(f32[32,64,256]{2,1,0:T(8,128)S(1)} %fusion.30, f32[256,1,32,64]{0,3,2,1:T(8,128)S(1)} %bitcast.104, f32[32,256]{1,0:T(8,128)S(1)} %bitcast.112, f32[256,256]{1,0:T(8,128)S(1)} %fusion.41, pred[256,256]{1,0:T(8,128)(4,1)S(1)} %iota_compare_fusion.1, f32[32]{0:T(128)S(1)} %copy-done.11, ...), kind=kOutput, calls=%fused_computation.26 | convolution fusion | flops 279969792 | bytes 8814720 | tf_op jit(solution)/shard_map/while/body/eval_jaxpr/gjts,sgjp->tgjp/dot_general | solution.py:46
  68.8 2.0 copy.32
  70.9 0.8 multiply_reduce_fusion
  71.7 1.8 multiply_convert_fusion.5
  73.5 14.7 %collective-permute-done = bf16[2048,512]{1,0:T(8,128)(2,1)} collective-permute-done((bf16[2048,512]{1,0:T(8,128)(2,1)}, bf16[2048,512]{1,0:T(8,128)(2,1)}, u32[]{:S(2)}, u32[]{:S(2)}) %collective-permute-start) | collective-permute-done | bytes 2097184 | tf_op jit(solution)/shard_map/ppermute | solution.py:189
  88.2 1.3 collective-permute-start.9
  89.5 4.6 %collective-permute-start.7 = (bf16[256,2048]{1,0:T(8,128)(2,1)}, bf16[256,2048]{1,0:T(8,128)(2,1)S(1)}, u32[]{:S(2)}, u32[]{:S(2)}) collective-permute-start(bf16[256,2048]{1,0:T(8,128)(2,1)} %multiply_convert_fusion.5), channel_id=1, source_target_pairs={{0,8},{8,16},{16,24},{1,9},{9,17},{17,25},{2,10},{10,18},{18,26},{... | collective-permute-start | bytes 3145736 | tf_op jit(solution)/shard_map/ppermute | solution.py:204
  94.1 2.6 %fusion.50 = f32[256,512]{1,0:T(8,128)S(1)} fusion(bf16[256,2048]{1,0:T(8,128)(2,1)} %multiply_convert_fusion.5, bf16[2048,512]{1,0:T(8,128)(2,1)} %param.23), kind=kOutput, calls=%fused_computation.122 | convolution fusion | flops 536870912 | bytes 3670016 | tf_op jit(solution)/shard_map/dot_general | solution.py:197
  96.8 14.8 %collective-permute-done.9 = bf16[256,2048]{1,0:T(8,128)(2,1)S(1)} collective-permute-done((bf16[256,2048]{1,0:T(8,128)(2,1)}, bf16[256,2048]{1,0:T(8,128)(2,1)S(1)}, u32[]{:S(2)}, u32[]{:S(2)}) %collective-permute-start.9) | collective-permute-done | bytes 1048608 | tf_op jit(solution)/shard_map/ppermute | solution.py:207
  111.6 1.3 collective-permute-start.10
  112.9 0.7 collective-permute-start.8
  113.6 2.6 %fusion.51 = f32[256,512]{1,0:T(8,128)S(1)} fusion(bf16[256,2048]{1,0:T(8,128)(2,1)} %multiply_convert_fusion.5, bf16[2048,512]{1,0:T(8,128)(2,1)} %collective-permute-done), kind=kOutput, calls=%fused_computation.123 | convolution fusion | flops 536870912 | bytes 3670016 | tf_op jit(solution)/shard_map/dot_general | solution.py:197
  116.3 2.3 %convolution_bitcast_fusion.1 = f32[1,256,512]{2,1,0:T(8,128)S(1)} fusion(bf16[256,2048]{1,0:T(8,128)(2,1)S(1)} %collective-permute-done.9, bf16[2048,512]{1,0:T(8,128)(2,1)} %param.23), kind=kOutput, calls=%fused_computation.39 | convolution fusion | flops 536870912 | bytes 3670016 | tf_op jit(solution)/shard_map/dot_general | solution.py:197
  118.6 2.3 %convolution_bitcast_fusion = f32[1,256,512]{2,1,0:T(8,128)S(1)} fusion(bf16[256,2048]{1,0:T(8,128)(2,1)S(1)} %collective-permute-done.9, bf16[2048,512]{1,0:T(8,128)(2,1)} %collective-permute-done), kind=kOutput, calls=%fused_computation.38 | convolution fusion | flops 536870912 | bytes 3670016 | tf_op jit(solution)/shard_map/dot_general | solution.py:197
  120.9 2.3 %convolution_bitcast_fusion.5 = f32[1,256,512]{2,1,0:T(8,128)S(1)} fusion(bf16[256,2048]{1,0:T(8,128)(2,1)S(1)} %collective-permute-done.7, bf16[2048,512]{1,0:T(8,128)(2,1)} %param.23), kind=kOutput, calls=%fused_computation.43 | convolution fusion | flops 536870912 | bytes 3670016 | tf_op jit(solution)/shard_map/dot_general | solution.py:197
  123.2 11.2 %collective-permute-done.10 = bf16[256,2048]{1,0:T(8,128)(2,1)S(1)} collective-permute-done((bf16[256,2048]{1,0:T(8,128)(2,1)S(1)}, bf16[256,2048]{1,0:T(8,128)(2,1)S(1)}, u32[]{:S(2)}, u32[]{:S(2)}) %collective-permute-start.10) | collective-permute-done | bytes 1048608 | tf_op jit(solution)/shard_map/ppermute | solution.py:207
  134.6 1.5 collective-permute-start.11
  136.0 2.3 %convolution_bitcast_fusion.4 = f32[1,256,512]{2,1,0:T(8,128)S(1)} fusion(bf16[256,2048]{1,0:T(8,128)(2,1)S(1)} %collective-permute-done.7, bf16[2048,512]{1,0:T(8,128)(2,1)} %collective-permute-done), kind=kOutput, calls=%fused_computation.42 | convolution fusion | flops 536870912 | bytes 3670016 | tf_op jit(solution)/shard_map/dot_general | solution.py:197
  138.3 2.4 %fusion.35 = f32[256,512]{1,0:T(8,128)S(1)} fusion(bf16[2048,512]{1,0:T(8,128)(2,1)} %param.23, bf16[256,2048]{1,0:T(8,128)(2,1)S(1)} %collective-permute-done.8, bf16[256,2048]{1,0:T(8,128)(2,1)S(1)} %collective-permute-done.10, pred[]{:T(512)S(6)} %ge.33), kind=kOutput, calls=%fused_computation.74 | convolution fusion | flops 537395200 | bytes 4718593 | tf_op jit(solution)/shard_map/dot_general | solution.py:197
  140.7 2.4 %fusion.34 = f32[256,512]{1,0:T(8,128)S(1)} fusion(bf16[2048,512]{1,0:T(8,128)(2,1)} %collective-permute-done, bf16[256,2048]{1,0:T(8,128)(2,1)S(1)} %collective-permute-done.8, bf16[256,2048]{1,0:T(8,128)(2,1)S(1)} %collective-permute-done.10, pred[]{:T(512)S(6)} %ge.33), kind=kOutput, calls=%fused_computation.73 | convolution fusion | flops 537395200 | bytes 4718593 | tf_op jit(solution)/shard_map/dot_general | solution.py:197
  143.2 13.4 %collective-permute-done.11 = bf16[256,2048]{1,0:T(8,128)(2,1)S(1)} collective-permute-done((bf16[256,2048]{1,0:T(8,128)(2,1)S(1)}, bf16[256,2048]{1,0:T(8,128)(2,1)S(1)}, u32[]{:S(2)}, u32[]{:S(2)}) %collective-permute-start.11) | collective-permute-done | bytes 1048608 | tf_op jit(solution)/shard_map/ppermute | solution.py:211
  156.6 2.3 %convolution_bitcast_fusion.3 = f32[1,256,512]{2,1,0:T(8,128)S(1)} fusion(bf16[256,2048]{1,0:T(8,128)(2,1)S(1)} %collective-permute-done.11, bf16[2048,512]{1,0:T(8,128)(2,1)} %param.23), kind=kOutput, calls=%fused_computation.41 | convolution fusion | flops 536870912 | bytes 3670016 | tf_op jit(solution)/shard_map/dot_general | solution.py:197
  158.9 2.3 %convolution_bitcast_fusion.2 = f32[1,256,512]{2,1,0:T(8,128)S(1)} fusion(bf16[256,2048]{1,0:T(8,128)(2,1)S(1)} %collective-permute-done.11, bf16[2048,512]{1,0:T(8,128)(2,1)} %collective-permute-done), kind=kOutput, calls=%fused_computation.40 | convolution fusion | flops 536870912 | bytes 3670016 | tf_op jit(solution)/shard_map/dot_general | solution.py:197
  162.4 1.7 copy-done.1
  164.1 1.5 pad_maximum_fusion.1
  165.5 4.4 %collective-permute-done.12 = f32[2,256,1024]{2,1,0:T(8,128)S(1)} collective-permute-done((f32[2,256,1024]{2,1,0:T(8,128)}, f32[2,256,1024]{2,1,0:T(8,128)S(1)}, u32[]{:S(2)}, u32[]{:S(2)}) %collective-permute-start.12) | collective-permute-done | bytes 2097184 | tf_op jit(solution)/shard_map/ppermute | solution.py:241
  169.9 1.4 fusion.24
  171.8 13.4 %collective-permute-done.13 = bf16[1,256,1024]{2,1,0:T(8,128)(2,1)S(1)} collective-permute-done((bf16[1,256,1024]{2,1,0:T(8,128)(2,1)S(1)}, bf16[1,256,1024]{2,1,0:T(8,128)(2,1)S(1)}, u32[]{:S(2)}, u32[]{:S(2)}) %collective-permute-start.13) | collective-permute-done | bytes 524320 | tf_op jit(solution)/shard_map/ppermute | solution.py:241
  185.3 1.5 fusion.28
  186.8 5.8 %collective-permute-start.14 = (bf16[256,1024]{1,0:T(8,128)(2,1)S(1)}, bf16[256,1024]{1,0:T(8,128)(2,1)S(1)}, u32[]{:S(2)}, u32[]{:S(2)}) collective-permute-start(bf16[256,1024]{1,0:T(8,128)(2,1)S(1)} %fusion.28), channel_id=1, source_target_pairs={{0,0},{1,8},{2,16},{3,24},{8,1},{9,9},{10,17},{11,25},{16,2},{17,1... | collective-permute-start | bytes 1572872 | tf_op jit(solution)/shard_map/ppermute | solution.py:251
  192.6 22.6 %collective-permute-done.14 = bf16[256,1024]{1,0:T(8,128)(2,1)S(1)} collective-permute-done((bf16[256,1024]{1,0:T(8,128)(2,1)S(1)}, bf16[256,1024]{1,0:T(8,128)(2,1)S(1)}, u32[]{:S(2)}, u32[]{:S(2)}) %collective-permute-start.14) | collective-permute-done | bytes 524320 | tf_op jit(solution)/shard_map/ppermute | solution.py:251
  215.4 0.9 pad_maximum_fusion.3
  (72 shorter events, 6.9 us)
Async XLA Ops:
  0.0 4.9 %copy-start = (f32[256,32]{0,1:T(8,128)S(1)}, f32[256,32]{0,1:T(8,128)}, u32[]{:S(2)}) copy-start(f32[256,32]{0,1:T(8,128)} %param.20) | copy-start | bytes 98308
  0.0 1.4 copy-start.4
  0.0 1.4 copy-start.5
  0.0 11.2 %copy-start.7 = (f32[4,2048]{1,0:T(4,128)S(1)}, f32[4,2048]{1,0:T(4,128)}, u32[]{:S(2)}) copy-start(f32[4,2048]{1,0:T(4,128)} %param.16) | copy-start | bytes 98308
  0.0 11.2 %copy-start.9 = (f32[4,128]{1,0:T(4,128)S(1)}, f32[4,128]{1,0:T(4,128)}, u32[]{:S(2)}) copy-start(f32[4,128]{1,0:T(4,128)} %param.17) | copy-start | bytes 6148
  0.0 11.2 %copy-start.10 = (f32[4,128]{1,0:T(4,128)S(1)}, f32[4,128]{1,0:T(4,128)}, u32[]{:S(2)}) copy-start(f32[4,128]{1,0:T(4,128)} %param.18) | copy-start | bytes 6148
  1.5 16.8 %collective-permute-start.1 = (bf16[3,2304]{1,0:T(4,128)(2,1)S(1)}, bf16[3,2304]{1,0:T(4,128)(2,1)S(1)}, u32[]{:S(2)}, u32[]{:S(2)}) collective-permute-start(bf16[3,2304]{1,0:T(4,128)(2,1)S(1)} %slice.99), channel_id=1, source_target_pairs={{0,4},{4,8},{8,12},{12,16},{16,20},{20,24},{24,28},{1,5},{5,9},{9,... | collective-permute-start | bytes 41480 | tf_op jit(solution)/shard_map/ppermute | solution.py:14
  7.2 4.7 %collective-permute-start.2 = (f32[1,32]{1,0:T(1,128)S(1)}, f32[1,32]{1,0:T(1,128)S(1)}, u32[]{:S(2)}, u32[]{:S(2)}) collective-permute-start(f32[1,32]{1,0:T(1,128)S(1)} %bitcast.117), channel_id=1, source_target_pairs={{0,4},{4,8},{8,12},{12,16},{16,20},{20,24},{24,28},{1,5},{5,9},{9,... | collective-permute-start | bytes 392 | tf_op jit(solution)/shard_map/ppermute | solution.py:14
  11.9 6.4 %collective-permute-start.3 = (f32[1,32]{1,0:T(1,128)S(1)}, f32[1,32]{1,0:T(1,128)S(1)}, u32[]{:S(2)}, u32[]{:S(2)}) collective-permute-start(f32[1,32]{1,0:T(1,128)S(1)} %bitcast_multiply_fusion.1), channel_id=1, source_target_pairs={{0,8},{4,12},{8,16},{12,20},{16,24},{20,28},{1,9},{5,13},{9,17},{1... | collective-permute-start | bytes 392 | tf_op jit(solution)/shard_map/ppermute | solution.py:14
  25.7 18.5 %copy-start.3 = (f32[1,256,1,32]{1,2,3,0:T(1,128)S(1)}, f32[1,256,1,32]{1,2,3,0:T(1,128)}, u32[]{:S(2)}) copy-start(f32[1,256,1,32]{1,2,3,0:T(1,128)} %get-tuple-element.64) | copy-start | bytes 98308
  25.8 11.4 %collective-permute-start.4 = (bf16[1,32,64,128]{3,2,1,0:T(8,128)(2,1)S(1)}, bf16[1,32,64,128]{3,2,1,0:T(8,128)(2,1)S(1)}, u32[]{:S(2)}, u32[]{:S(2)}) collective-permute-start(bf16[1,32,64,128]{3,2,1,0:T(8,128)(2,1)S(1)} %convert_element_type.94), channel_id=1, source_target_pairs={{0,4},{4,8},{8,12},{12,16},{16,20},{20,24},{24,28},{1,5},{5,9},{9,... | collective-permute-start | bytes 1572872 | tf_op jit(solution)/shard_map/ppermute | solution.py:14
  37.5 14.4 %collective-permute-start.5 = (bf16[1,32,64,128]{3,2,1,0:T(8,128)(2,1)S(1)}, bf16[1,32,64,128]{3,2,1,0:T(8,128)(2,1)S(1)}, u32[]{:S(2)}, u32[]{:S(2)}) collective-permute-start(bf16[1,32,64,128]{3,2,1,0:T(8,128)(2,1)S(1)} %fusion.27), channel_id=1, source_target_pairs={{0,8},{4,12},{8,16},{12,20},{16,24},{20,28},{1,9},{5,13},{9,17},{1... | collective-permute-start | bytes 1572872 | tf_op jit(solution)/shard_map/ppermute | solution.py:14
  44.1 44.0 %collective-permute-start = (bf16[2048,512]{1,0:T(8,128)(2,1)}, bf16[2048,512]{1,0:T(8,128)(2,1)}, u32[]{:S(2)}, u32[]{:S(2)}) collective-permute-start(bf16[2048,512]{1,0:T(8,128)(2,1)} %param.23), channel_id=1, source_target_pairs={{0,4},{4,0},{1,5},{5,1},{2,6},{6,2},{3,7},{7,3},{8,12},{12,8},{9,1... | collective-permute-start | bytes 6291464 | tf_op jit(solution)/shard_map/ppermute | solution.py:189
  52.2 12.4 %collective-permute-start.6 = (bf16[1,32,64,128]{3,2,1,0:T(8,128)(2,1)S(1)}, bf16[1,32,64,128]{3,2,1,0:T(8,128)(2,1)S(1)}, u32[]{:S(2)}, u32[]{:S(2)}) collective-permute-start(bf16[1,32,64,128]{3,2,1,0:T(8,128)(2,1)S(1)} %fusion.23), channel_id=1, source_target_pairs={{0,16},{4,20},{8,24},{12,28},{1,17},{5,21},{9,25},{13,29},{2,18},{... | collective-permute-start | bytes 1572872 | tf_op jit(solution)/shard_map/ppermute | solution.py:14
  57.7 7.4 %copy-start.6 = (f32[256,32]{0,1:T(8,128)S(1)}, f32[256,32]{0,1:T(8,128)}, u32[]{:S(2)}) copy-start(f32[256,32]{0,1:T(8,128)} %param.19) | copy-start | bytes 98308
  57.7 7.4 %copy-start.11 = (f32[32]{0:T(128)S(1)}, f32[32]{0:T(128)}, u32[]{:S(2)}) copy-start(f32[32]{0:T(128)} %param.21) | copy-start | bytes 388
  68.8 2.0 copy-start.2
  70.9 0.8 copy-start.8
  88.2 23.4 %collective-permute-start.9 = (bf16[256,2048]{1,0:T(8,128)(2,1)}, bf16[256,2048]{1,0:T(8,128)(2,1)S(1)}, u32[]{:S(2)}, u32[]{:S(2)}) collective-permute-start(bf16[256,2048]{1,0:T(8,128)(2,1)} %multiply_convert_fusion.5), channel_id=1, source_target_pairs={{8,0},{16,8},{24,16},{9,1},{17,9},{25,17},{10,2},{18,10},{26,18},{... | collective-permute-start | bytes 3145736 | tf_op jit(solution)/shard_map/ppermute | solution.py:207
  89.5 23.4 %collective-permute-start.7 = (bf16[256,2048]{1,0:T(8,128)(2,1)}, bf16[256,2048]{1,0:T(8,128)(2,1)S(1)}, u32[]{:S(2)}, u32[]{:S(2)}) collective-permute-start(bf16[256,2048]{1,0:T(8,128)(2,1)} %multiply_convert_fusion.5), channel_id=1, source_target_pairs={{0,8},{8,16},{16,24},{1,9},{9,17},{17,25},{2,10},{10,18},{18,26},{... | collective-permute-start | bytes 3145736 | tf_op jit(solution)/shard_map/ppermute | solution.py:204
  111.6 22.8 %collective-permute-start.10 = (bf16[256,2048]{1,0:T(8,128)(2,1)S(1)}, bf16[256,2048]{1,0:T(8,128)(2,1)S(1)}, u32[]{:S(2)}, u32[]{:S(2)}) collective-permute-start(bf16[256,2048]{1,0:T(8,128)(2,1)S(1)} %collective-permute-done.9), channel_id=1, source_target_pairs={{8,0},{16,8},{9,1},{17,9},{10,2},{18,10},{11,3},{19,11},{12,4},{20... | collective-permute-start | bytes 3145736 | tf_op jit(solution)/shard_map/ppermute | solution.py:207
  112.9 21.5 %collective-permute-start.8 = (bf16[256,2048]{1,0:T(8,128)(2,1)S(1)}, bf16[256,2048]{1,0:T(8,128)(2,1)S(1)}, u32[]{:S(2)}, u32[]{:S(2)}) collective-permute-start(bf16[256,2048]{1,0:T(8,128)(2,1)S(1)} %collective-permute-done.7), channel_id=1, source_target_pairs={{8,16},{16,24},{9,17},{17,25},{10,18},{18,26},{11,19},{19,27},{12,... | collective-permute-start | bytes 3145736 | tf_op jit(solution)/shard_map/ppermute | solution.py:204
  134.6 22.0 %collective-permute-start.11 = (bf16[256,2048]{1,0:T(8,128)(2,1)S(1)}, bf16[256,2048]{1,0:T(8,128)(2,1)S(1)}, u32[]{:S(2)}, u32[]{:S(2)}) collective-permute-start(bf16[256,2048]{1,0:T(8,128)(2,1)S(1)} %broadcast_select_fusion.1), channel_id=1, source_target_pairs={{16,24},{8,0},{17,25},{9,1},{18,26},{10,2},{19,27},{11,3},{20,28},... | collective-permute-start | bytes 3145736 | tf_op jit(solution)/shard_map/ppermute | solution.py:211
  162.1 1.9 copy-start.1
  165.5 4.4 %collective-permute-start.12 = (f32[2,256,1024]{2,1,0:T(8,128)}, f32[2,256,1024]{2,1,0:T(8,128)S(1)}, u32[]{:S(2)}, u32[]{:S(2)}) collective-permute-start(f32[2,256,1024]{2,1,0:T(8,128)} %pad_maximum_fusion.1), channel_id=1, source_target_pairs={{0,1},{1,0},{2,3},{3,2},{4,5},{5,4},{6,7},{7,6},{8,9},{9,8},{10,11... | collective-permute-start | bytes 6291464 | tf_op jit(solution)/shard_map/ppermute | solution.py:241
  171.2 14.0 %collective-permute-start.13 = (bf16[1,256,1024]{2,1,0:T(8,128)(2,1)S(1)}, bf16[1,256,1024]{2,1,0:T(8,128)(2,1)S(1)}, u32[]{:S(2)}, u32[]{:S(2)}) collective-permute-start(bf16[1,256,1024]{2,1,0:T(8,128)(2,1)S(1)} %fusion.24), channel_id=1, source_target_pairs={{0,2},{1,3},{2,0},{3,1},{4,6},{5,7},{6,4},{7,5},{8,10},{9,11},{10,... | collective-permute-start | bytes 1572872 | tf_op jit(solution)/shard_map/ppermute | solution.py:241
  186.8 28.4 %collective-permute-start.14 = (bf16[256,1024]{1,0:T(8,128)(2,1)S(1)}, bf16[256,1024]{1,0:T(8,128)(2,1)S(1)}, u32[]{:S(2)}, u32[]{:S(2)}) collective-permute-start(bf16[256,1024]{1,0:T(8,128)(2,1)S(1)} %fusion.28), channel_id=1, source_target_pairs={{0,0},{1,8},{2,16},{3,24},{8,1},{9,9},{10,17},{11,25},{16,2},{17,1... | collective-permute-start | bytes 1572872 | tf_op jit(solution)/shard_map/ppermute | solution.py:251

commit v15 on v11

--- a/solution.py
+++ b/solution.py
@@ -71,19 +71,31 @@
 
 def on_link(part):
     decay, state = part
-    return (decay, state.astype(jnp.bfloat16))
+    heads = decay.shape[-1]
+    high = decay.astype(jnp.bfloat16)
+    low = (decay - high.astype(jnp.float32)).astype(jnp.bfloat16)
+    rows = jnp.concatenate([high, low], axis=0)
+    carrier = jnp.pad(rows, ((0, state.shape[-2] - 2), (0, state.shape[-1] - heads)))
+    return jnp.concatenate([state.astype(jnp.bfloat16), carrier[None, None]], axis=1)
+
+
+def off_link(packed):
+    heads = packed.shape[1] - 1
+    carrier = packed[0, heads].astype(jnp.float32)
+    decay = (carrier[0, :heads] + carrier[1, :heads])[None]
+    return (decay, packed[:, :heads])
 
 
 def prefix_states(dev_decay, dev_state, axis, count):
     own = (dev_decay, dev_state)
     if count == 1:
         return jnp.zeros_like(dev_state)
-    got = shifted(on_link(own), axis, 1, count)
+    got = off_link(shifted(on_link(own), axis, 1, count))
     before = got
     upto = combine(got, own)
     step = 2
     while step < count:
-        got = shifted(on_link(upto), axis, step, count)
+        got = off_link(shifted(on_link(upto), axis, step, count))
         before = combine(got, before)
         if step * 2 < count:
             upto = combine(got, upto)

time: 214 us -> 224 us (1.047)
  waiting for transfers between devices: 118 us -> 139 us
  starting transfers between devices: 40.6 us -> 29.2 us
    ppermute x2, waiting for transfers between devices: 0.01 us -> 18.7 us  [on_device(): lax.ppermute(going_right, outer_axis, [(s, s + 1) for s in range(step - 1...]
    ppermute x6 -> x4, waiting for transfers between devices: 21.2 us -> 30.2 us  [shifted(): lax.ppermute(value, axis, [(source, source + steps) for source in range(f...]
    ppermute x2, waiting for transfers between devices: 27.2 us -> 19 us  [on_device(): lax.ppermute(going_left, outer_axis, [(s, s - 1) for s in range(1, tp_cou...]
    ppermute x6 -> x4, starting transfers between devices: 23.7 us -> 17.7 us  [shifted(): lax.ppermute(value, axis, [(source, source + steps) for source in range(f...]
    ppermute x1, waiting for transfers between devices: 14.9 us -> 11.6 us  [on_device(): lax.ppermute(out_weight, inner_axis, [(s, (s + d) % inner_count) for s in...]
    ppermute x1, waiting for transfers between devices: 13.9 us -> 16.9 us  [on_device(): lax.ppermute(jnp.where(outer_at == tp_count - 2, going_right, going_left)...]
    ppermute x1, starting transfers between devices: 4.46 us -> 1.92 us  [on_device(): lax.ppermute(held[0].astype(jnp.bfloat16), (outer_axis, 'tp'), swap)]
    ppermute x1, waiting for transfers between devices: 22.7 us -> 25.1 us  [on_device(): lax.ppermute(held[0].astype(jnp.bfloat16), (outer_axis, 'tp'), swap)]
  transfers between devices with their start and end apart: 15 -> 13, of which waited for: 10 -> 11; matrix products, arithmetic and copies ran while one was open for 15% -> 14% of each run, Pallas kernels for 0% -> 0%
where the time goes in v15:
time: 224 us; the launch traced here: 223 us
  waiting for transfers between devices  139 us (62%)
  matrix products  30.4 us (14%)
  starting transfers between devices  29.2 us (13%)
  other arithmetic  15.4 us (7%)
  local copies, waits for them, and re-layouts  8.32 us (4%)
    ppermute x4, waiting for transfers between devices, shifted(): lax.ppermute(value, axis, [(source, source + steps) for source in range(f...  30.2 us
    ppermute x1, waiting for transfers between devices, on_device(): lax.ppermute(held[0].astype(jnp.bfloat16), (outer_axis, 'tp'), swap)  25.1 us
    dot_general x10, matrix products, times_weight(): jnp.dot(rows, piece, preferred_element_type=jnp.float32)  23.8 us
    ppermute x2, waiting for transfers between devices, on_device(): lax.ppermute(going_left, outer_axis, [(s, s - 1) for s in range(1, tp_cou...  19 us
    ppermute x2, waiting for transfers between devices, on_device(): lax.ppermute(going_right, outer_axis, [(s, s + 1) for s in range(step - 1...  18.7 us
    ppermute x2, waiting for transfers between devices, on_device(): lax.ppermute(sent if bit == 1 else sent.astype(jnp.bfloat16), 'tp', [(s,...  17.8 us
    ppermute x4, starting transfers between devices, shifted(): lax.ppermute(value, axis, [(source, source + steps) for source in range(f...  17.7 us
    ppermute x1, waiting for transfers between devices, on_device(): lax.ppermute(jnp.where(outer_at == tp_count - 2, going_right, going_left)...  16.9 us
  transfers between devices with their start and end apart: 13, of which 11 were waited for; matrix products, arithmetic and copies ran while one was open for 14% of the time, Pallas kernels for 0%

profile of v15, /device:TPU:2, one launch (start us, length us, event | category | flops | bytes accessed | tf_op | source)
XLA Modules:
  0.0 223.3 jit_solution(1610209902406032521)
XLA Ops:
  0.0 1.3 constant_dynamic-update-slice_fusion.5
  1.5 3.4 %collective-permute-start.1 = (bf16[3,2304]{1,0:T(4,128)(2,1)S(1)}, bf16[3,2304]{1,0:T(4,128)(2,1)S(1)}, u32[]{:S(2)}, u32[]{:S(2)}) collective-permute-start(bf16[3,2304]{1,0:T(4,128)(2,1)S(1)} %slice.135), channel_id=1, source_target_pairs={{0,4},{4,8},{8,12},{12,16},{16,20},{20,24},{24,28},{1,5},{5,9},{9,... | collective-permute-start | bytes 41480 | tf_op jit(solution)/shard_map/ppermute | solution.py:14
  4.9 0.6 reduce-window.6
  5.9 0.7 fusion.73
  8.3 1.5 multiply_convert_fusion.3
  9.9 1.6 slice_convert_fusion
  11.5 1.9 copy.27
  13.4 2.2 fusion.17
  15.8 3.5 %collective-permute-start.2 = (bf16[1,33,64,128]{3,2,1,0:T(8,128)(2,1)S(1)}, bf16[1,33,64,128]{3,2,1,0:T(8,128)(2,1)S(1)}, u32[]{:S(2)}, u32[]{:S(2)}) collective-permute-start(bf16[1,33,64,128]{3,2,1,0:T(8,128)(2,1)S(1)} %pad_maximum_fusion.3), channel_id=1, source_target_pairs={{0,4},{4,8},{8,12},{12,16},{16,20},{20,24},{24,28},{1,5},{5,9},{9,... | collective-permute-start | bytes 1622024 | tf_op jit(solution)/shard_map/ppermute | solution.py:14
  19.3 11.2 %collective-permute-done.2 = bf16[1,33,64,128]{3,2,1,0:T(8,128)(2,1)S(1)} collective-permute-done((bf16[1,33,64,128]{3,2,1,0:T(8,128)(2,1)S(1)}, bf16[1,33,64,128]{3,2,1,0:T(8,128)(2,1)S(1)}, u32[]{:S(2)}, u32[]{:S(2)}) %collective-permute-start.2) | collective-permute-done | bytes 540704 | tf_op jit(solution)/shard_map/ppermute | solution.py:14
  30.8 5.4 %collective-permute-start.3 = (bf16[1,33,64,128]{3,2,1,0:T(8,128)(2,1)S(1)}, bf16[1,33,64,128]{3,2,1,0:T(8,128)(2,1)S(1)}, u32[]{:S(2)}, u32[]{:S(2)}) collective-permute-start(bf16[1,33,64,128]{3,2,1,0:T(8,128)(2,1)S(1)} %pad_maximum_fusion.4), channel_id=1, source_target_pairs={{0,8},{4,12},{8,16},{12,20},{16,24},{20,28},{1,9},{5,13},{9,17},{1... | collective-permute-start | bytes 1622024 | tf_op jit(solution)/shard_map/ppermute | solution.py:14
  36.2 0.7 collective-permute-start
  36.9 9.6 %collective-permute-done.3 = bf16[1,33,64,128]{3,2,1,0:T(8,128)(2,1)S(1)} collective-permute-done((bf16[1,33,64,128]{3,2,1,0:T(8,128)(2,1)S(1)}, bf16[1,33,64,128]{3,2,1,0:T(8,128)(2,1)S(1)}, u32[]{:S(2)}, u32[]{:S(2)}) %collective-permute-start.3) | collective-permute-done | bytes 540704 | tf_op jit(solution)/shard_map/ppermute | solution.py:14
  46.9 5.4 %collective-permute-start.4 = (bf16[1,33,64,128]{3,2,1,0:T(8,128)(2,1)S(1)}, bf16[1,33,64,128]{3,2,1,0:T(8,128)(2,1)S(1)}, u32[]{:S(2)}, u32[]{:S(2)}) collective-permute-start(bf16[1,33,64,128]{3,2,1,0:T(8,128)(2,1)S(1)} %pad_maximum_fusion.5), channel_id=1, source_target_pairs={{0,16},{4,20},{8,24},{12,28},{1,17},{5,21},{9,25},{13,29},{2,18},{... | collective-permute-start | bytes 1622024 | tf_op jit(solution)/shard_map/ppermute | solution.py:14
  52.7 9.3 %collective-permute-done.4 = bf16[1,33,64,128]{3,2,1,0:T(8,128)(2,1)S(1)} collective-permute-done((bf16[1,33,64,128]{3,2,1,0:T(8,128)(2,1)S(1)}, bf16[1,33,64,128]{3,2,1,0:T(8,128)(2,1)S(1)}, u32[]{:S(2)}, u32[]{:S(2)}) %collective-permute-start.4) | collective-permute-done | bytes 540704 | tf_op jit(solution)/shard_map/ppermute | solution.py:14
  62.5 3.7 %fusion.14 = f32[256,1,32,64]{0,3,2,1:T(8,128)} fusion(f32[32,64,256]{2,1,0:T(8,128)S(1)} %fusion.29, f32[256,1,32,64]{0,3,2,1:T(8,128)S(1)} %bitcast.135, f32[32,256]{1,0:T(8,128)S(1)} %bitcast.143, f32[256,256]{1,0:T(8,128)S(1)} %fusion.43, pred[256,256]{1,0:T(8,128)(4,1)S(1)} %iota_compare_fusion.1, f32[32]{0:T(128)S(1)} %copy-done.14, ...), kind=kOutput, calls=%fused_computation.26 | convolution fusion | flops 279969792 | bytes 8814720 | tf_op jit(solution)/shard_map/while/body/eval_jaxpr/gjts,sgjp->tgjp/dot_general | solution.py:46
  66.2 2.0 copy.32
  68.3 0.8 multiply_reduce_fusion
  69.1 1.8 multiply_convert_fusion.5
  70.9 11.6 %collective-permute-done = bf16[2048,512]{1,0:T(8,128)(2,1)} collective-permute-done((bf16[2048,512]{1,0:T(8,128)(2,1)}, bf16[2048,512]{1,0:T(8,128)(2,1)}, u32[]{:S(2)}, u32[]{:S(2)}) %collective-permute-start) | collective-permute-done | bytes 2097184 | tf_op jit(solution)/shard_map/ppermute | solution.py:192
  82.5 3.5 %collective-permute-start.5 = (bf16[256,2048]{1,0:T(8,128)(2,1)}, bf16[256,2048]{1,0:T(8,128)(2,1)S(1)}, u32[]{:S(2)}, u32[]{:S(2)}) collective-permute-start(bf16[256,2048]{1,0:T(8,128)(2,1)} %multiply_convert_fusion.5), channel_id=1, source_target_pairs={{0,8},{8,16},{16,24},{1,9},{9,17},{17,25},{2,10},{10,18},{18,26},{... | collective-permute-start | bytes 3145736 | tf_op jit(solution)/shard_map/ppermute | solution.py:207
  86.0 1.3 collective-permute-start.7
  87.4 2.6 %fusion.76 = f32[256,512]{1,0:T(8,128)S(1)} fusion(bf16[256,2048]{1,0:T(8,128)(2,1)} %multiply_convert_fusion.5, bf16[2048,512]{1,0:T(8,128)(2,1)} %param.23), kind=kOutput, calls=%fused_computation.164 | convolution fusion | flops 536870912 | bytes 3670016 | tf_op jit(solution)/shard_map/dot_general | solution.py:200
  90.0 18.7 %collective-permute-done.5 = bf16[256,2048]{1,0:T(8,128)(2,1)S(1)} collective-permute-done((bf16[256,2048]{1,0:T(8,128)(2,1)}, bf16[256,2048]{1,0:T(8,128)(2,1)S(1)}, u32[]{:S(2)}, u32[]{:S(2)}) %collective-permute-start.5) | collective-permute-done | bytes 1048608 | tf_op jit(solution)/shard_map/ppermute | solution.py:207
  108.7 0.7 collective-permute-start.6
  109.4 3.3 %collective-permute-done.7 = bf16[256,2048]{1,0:T(8,128)(2,1)S(1)} collective-permute-done((bf16[256,2048]{1,0:T(8,128)(2,1)}, bf16[256,2048]{1,0:T(8,128)(2,1)S(1)}, u32[]{:S(2)}, u32[]{:S(2)}) %collective-permute-start.7) | collective-permute-done | bytes 1048608 | tf_op jit(solution)/shard_map/ppermute | solution.py:210
  112.8 1.3 collective-permute-start.8
  114.1 2.6 %fusion.77 = f32[256,512]{1,0:T(8,128)S(1)} fusion(bf16[256,2048]{1,0:T(8,128)(2,1)} %multiply_convert_fusion.5, bf16[2048,512]{1,0:T(8,128)(2,1)} %collective-permute-done), kind=kOutput, calls=%fused_computation.165 | convolution fusion | flops 536870912 | bytes 3670016 | tf_op jit(solution)/shard_map/dot_general | solution.py:200
  116.8 2.3 %convolution_bitcast_fusion.1 = f32[1,256,512]{2,1,0:T(8,128)S(1)} fusion(bf16[256,2048]{1,0:T(8,128)(2,1)S(1)} %collective-permute-done.7, bf16[2048,512]{1,0:T(8,128)(2,1)} %param.23), kind=kOutput, calls=%fused_computation.38 | convolution fusion | flops 536870912 | bytes 3670016 | tf_op jit(solution)/shard_map/dot_general | solution.py:200
  119.1 2.3 %convolution_bitcast_fusion = f32[1,256,512]{2,1,0:T(8,128)S(1)} fusion(bf16[256,2048]{1,0:T(8,128)(2,1)S(1)} %collective-permute-done.7, bf16[2048,512]{1,0:T(8,128)(2,1)} %collective-permute-done), kind=kOutput, calls=%fused_computation.37 | convolution fusion | flops 536870912 | bytes 3670016 | tf_op jit(solution)/shard_map/dot_general | solution.py:200
  121.4 2.3 %convolution_bitcast_fusion.5 = f32[1,256,512]{2,1,0:T(8,128)S(1)} fusion(bf16[256,2048]{1,0:T(8,128)(2,1)S(1)} %collective-permute-done.5, bf16[2048,512]{1,0:T(8,128)(2,1)} %param.23), kind=kOutput, calls=%fused_computation.42 | convolution fusion | flops 536870912 | bytes 3670016 | tf_op jit(solution)/shard_map/dot_general | solution.py:200
  123.7 15.6 %collective-permute-done.8 = bf16[256,2048]{1,0:T(8,128)(2,1)S(1)} collective-permute-done((bf16[256,2048]{1,0:T(8,128)(2,1)S(1)}, bf16[256,2048]{1,0:T(8,128)(2,1)S(1)}, u32[]{:S(2)}, u32[]{:S(2)}) %collective-permute-start.8) | collective-permute-done | bytes 1048608 | tf_op jit(solution)/shard_map/ppermute | solution.py:210
  139.4 1.5 collective-permute-start.9
  140.9 2.3 %convolution_bitcast_fusion.4 = f32[1,256,512]{2,1,0:T(8,128)S(1)} fusion(bf16[256,2048]{1,0:T(8,128)(2,1)S(1)} %collective-permute-done.5, bf16[2048,512]{1,0:T(8,128)(2,1)} %collective-permute-done), kind=kOutput, calls=%fused_computation.41 | convolution fusion | flops 536870912 | bytes 3670016 | tf_op jit(solution)/shard_map/dot_general | solution.py:200
  143.2 2.4 %fusion.37 = f32[256,512]{1,0:T(8,128)S(1)} fusion(bf16[2048,512]{1,0:T(8,128)(2,1)} %param.23, bf16[256,2048]{1,0:T(8,128)(2,1)S(1)} %collective-permute-done.6, bf16[256,2048]{1,0:T(8,128)(2,1)S(1)} %collective-permute-done.8, pred[]{:T(512)S(6)} %ge.33), kind=kOutput, calls=%fused_computation.80 | convolution fusion | flops 537395200 | bytes 4718593 | tf_op jit(solution)/shard_map/dot_general | solution.py:200
  145.6 2.4 %fusion.36 = f32[256,512]{1,0:T(8,128)S(1)} fusion(bf16[2048,512]{1,0:T(8,128)(2,1)} %collective-permute-done, bf16[256,2048]{1,0:T(8,128)(2,1)S(1)} %collective-permute-done.6, bf16[256,2048]{1,0:T(8,128)(2,1)S(1)} %collective-permute-done.8, pred[]{:T(512)S(6)} %ge.33), kind=kOutput, calls=%fused_computation.79 | convolution fusion | flops 537395200 | bytes 4718593 | tf_op jit(solution)/shard_map/dot_general | solution.py:200
  148.1 16.9 %collective-permute-done.9 = bf16[256,2048]{1,0:T(8,128)(2,1)S(1)} collective-permute-done((bf16[256,2048]{1,0:T(8,128)(2,1)S(1)}, bf16[256,2048]{1,0:T(8,128)(2,1)S(1)}, u32[]{:S(2)}, u32[]{:S(2)}) %collective-permute-start.9) | collective-permute-done | bytes 1048608 | tf_op jit(solution)/shard_map/ppermute | solution.py:214
  165.0 2.3 %convolution_bitcast_fusion.3 = f32[1,256,512]{2,1,0:T(8,128)S(1)} fusion(bf16[256,2048]{1,0:T(8,128)(2,1)S(1)} %collective-permute-done.9, bf16[2048,512]{1,0:T(8,128)(2,1)} %param.23), kind=kOutput, calls=%fused_computation.40 | convolution fusion | flops 536870912 | bytes 3670016 | tf_op jit(solution)/shard_map/dot_general | solution.py:200
  167.3 2.3 %convolution_bitcast_fusion.2 = f32[1,256,512]{2,1,0:T(8,128)S(1)} fusion(bf16[256,2048]{1,0:T(8,128)(2,1)S(1)} %collective-permute-done.9, bf16[2048,512]{1,0:T(8,128)(2,1)} %collective-permute-done), kind=kOutput, calls=%fused_computation.39 | convolution fusion | flops 536870912 | bytes 3670016 | tf_op jit(solution)/shard_map/dot_general | solution.py:200
  170.8 1.7 copy-done.1
  172.4 1.5 pad_maximum_fusion.1
  173.9 4.4 %collective-permute-done.10 = f32[2,256,1024]{2,1,0:T(8,128)S(1)} collective-permute-done((f32[2,256,1024]{2,1,0:T(8,128)}, f32[2,256,1024]{2,1,0:T(8,128)S(1)}, u32[]{:S(2)}, u32[]{:S(2)}) %collective-permute-start.10) | collective-permute-done | bytes 2097184 | tf_op jit(solution)/shard_map/ppermute | solution.py:244
  178.3 1.4 fusion.23
  180.2 13.5 %collective-permute-done.11 = bf16[1,256,1024]{2,1,0:T(8,128)(2,1)S(1)} collective-permute-done((bf16[1,256,1024]{2,1,0:T(8,128)(2,1)S(1)}, bf16[1,256,1024]{2,1,0:T(8,128)(2,1)S(1)}, u32[]{:S(2)}, u32[]{:S(2)}) %collective-permute-start.11) | collective-permute-done | bytes 524320 | tf_op jit(solution)/shard_map/ppermute | solution.py:244
  193.7 1.5 fusion.27
  195.1 1.9 collective-permute-start.12
  197.1 25.1 %collective-permute-done.12 = bf16[256,1024]{1,0:T(8,128)(2,1)S(1)} collective-permute-done((bf16[256,1024]{1,0:T(8,128)(2,1)S(1)}, bf16[256,1024]{1,0:T(8,128)(2,1)S(1)}, u32[]{:S(2)}, u32[]{:S(2)}) %collective-permute-start.12) | collective-permute-done | bytes 524320 | tf_op jit(solution)/shard_map/ppermute | solution.py:254
  222.4 0.9 pad_maximum_fusion.6
  (85 shorter events, 5.9 us)
Async XLA Ops:
  0.0 4.9 %copy-start = (f32[256,32]{0,1:T(8,128)S(1)}, f32[256,32]{0,1:T(8,128)}, u32[]{:S(2)}) copy-start(f32[256,32]{0,1:T(8,128)} %param.20) | copy-start | bytes 98308
  0.0 1.4 copy-start.4
  0.0 1.4 copy-start.5
  0.0 7.9 %copy-start.7 = (f32[4,2048]{1,0:T(4,128)S(1)}, f32[4,2048]{1,0:T(4,128)}, u32[]{:S(2)}) copy-start(f32[4,2048]{1,0:T(4,128)} %param.16) | copy-start | bytes 98308
  0.0 7.9 %copy-start.10 = (f32[4,128]{1,0:T(4,128)S(1)}, f32[4,128]{1,0:T(4,128)}, u32[]{:S(2)}) copy-start(f32[4,128]{1,0:T(4,128)} %param.17) | copy-start | bytes 6148
  0.0 7.9 %copy-start.11 = (f32[4,128]{1,0:T(4,128)S(1)}, f32[4,128]{1,0:T(4,128)}, u32[]{:S(2)}) copy-start(f32[4,128]{1,0:T(4,128)} %param.18) | copy-start | bytes 6148
  1.5 6.7 %collective-permute-start.1 = (bf16[3,2304]{1,0:T(4,128)(2,1)S(1)}, bf16[3,2304]{1,0:T(4,128)(2,1)S(1)}, u32[]{:S(2)}, u32[]{:S(2)}) collective-permute-start(bf16[3,2304]{1,0:T(4,128)(2,1)S(1)} %slice.135), channel_id=1, source_target_pairs={{0,4},{4,8},{8,12},{12,16},{16,20},{20,24},{24,28},{1,5},{5,9},{9,... | collective-permute-start | bytes 41480 | tf_op jit(solution)/shard_map/ppermute | solution.py:14
  7.2 0.7 copy-start.12
  15.6 14.9 %copy-start.13 = (f32[32]{0:T(128)S(1)}, f32[32]{0:T(128)}, u32[]{:S(2)}) copy-start(f32[32]{0:T(128)} %copy-done.12) | copy-start | bytes 388
  15.6 14.9 %copy-start.9 = (f32[32]{0:T(128)S(1)}, f32[32]{0:T(128)}, u32[]{:S(2)}) copy-start(f32[32]{0:T(128)} %get-tuple-element.78) | copy-start | bytes 388
  15.7 21.1 %copy-start.3 = (f32[1,256,1,32]{1,2,3,0:T(1,128)S(1)}, f32[1,256,1,32]{1,2,3,0:T(1,128)}, u32[]{:S(2)}) copy-start(f32[1,256,1,32]{1,2,3,0:T(1,128)} %get-tuple-element.56) | copy-start | bytes 98308
  15.8 14.7 %collective-permute-start.2 = (bf16[1,33,64,128]{3,2,1,0:T(8,128)(2,1)S(1)}, bf16[1,33,64,128]{3,2,1,0:T(8,128)(2,1)S(1)}, u32[]{:S(2)}, u32[]{:S(2)}) collective-permute-start(bf16[1,33,64,128]{3,2,1,0:T(8,128)(2,1)S(1)} %pad_maximum_fusion.3), channel_id=1, source_target_pairs={{0,4},{4,8},{8,12},{12,16},{16,20},{20,24},{24,28},{1,5},{5,9},{9,... | collective-permute-start | bytes 1622024 | tf_op jit(solution)/shard_map/ppermute | solution.py:14
  30.8 15.7 %collective-permute-start.3 = (bf16[1,33,64,128]{3,2,1,0:T(8,128)(2,1)S(1)}, bf16[1,33,64,128]{3,2,1,0:T(8,128)(2,1)S(1)}, u32[]{:S(2)}, u32[]{:S(2)}) collective-permute-start(bf16[1,33,64,128]{3,2,1,0:T(8,128)(2,1)S(1)} %pad_maximum_fusion.4), channel_id=1, source_target_pairs={{0,8},{4,12},{8,16},{12,20},{16,24},{20,28},{1,9},{5,13},{9,17},{1... | collective-permute-start | bytes 1622024 | tf_op jit(solution)/shard_map/ppermute | solution.py:14
  36.2 46.3 %collective-permute-start = (bf16[2048,512]{1,0:T(8,128)(2,1)}, bf16[2048,512]{1,0:T(8,128)(2,1)}, u32[]{:S(2)}, u32[]{:S(2)}) collective-permute-start(bf16[2048,512]{1,0:T(8,128)(2,1)} %param.23), channel_id=1, source_target_pairs={{0,4},{4,0},{1,5},{5,1},{2,6},{6,2},{3,7},{7,3},{8,12},{12,8},{9,1... | collective-permute-start | bytes 6291464 | tf_op jit(solution)/shard_map/ppermute | solution.py:192
  46.9 15.1 %collective-permute-start.4 = (bf16[1,33,64,128]{3,2,1,0:T(8,128)(2,1)S(1)}, bf16[1,33,64,128]{3,2,1,0:T(8,128)(2,1)S(1)}, u32[]{:S(2)}, u32[]{:S(2)}) collective-permute-start(bf16[1,33,64,128]{3,2,1,0:T(8,128)(2,1)S(1)} %pad_maximum_fusion.5), channel_id=1, source_target_pairs={{0,16},{4,20},{8,24},{12,28},{1,17},{5,21},{9,25},{13,29},{2,18},{... | collective-permute-start | bytes 1622024 | tf_op jit(solution)/shard_map/ppermute | solution.py:14
  52.4 10.1 %copy-start.6 = (f32[256,32]{0,1:T(8,128)S(1)}, f32[256,32]{0,1:T(8,128)}, u32[]{:S(2)}) copy-start(f32[256,32]{0,1:T(8,128)} %param.19) | copy-start | bytes 98308
  52.4 10.1 %copy-start.14 = (f32[32]{0:T(128)S(1)}, f32[32]{0:T(128)}, u32[]{:S(2)}) copy-start(f32[32]{0:T(128)} %param.21) | copy-start | bytes 388
  66.2 2.0 copy-start.2
  68.3 0.8 copy-start.8
  82.5 26.2 %collective-permute-start.5 = (bf16[256,2048]{1,0:T(8,128)(2,1)}, bf16[256,2048]{1,0:T(8,128)(2,1)S(1)}, u32[]{:S(2)}, u32[]{:S(2)}) collective-permute-start(bf16[256,2048]{1,0:T(8,128)(2,1)} %multiply_convert_fusion.5), channel_id=1, source_target_pairs={{0,8},{8,16},{16,24},{1,9},{9,17},{17,25},{2,10},{10,18},{18,26},{... | collective-permute-start | bytes 3145736 | tf_op jit(solution)/shard_map/ppermute | solution.py:207
  86.0 26.8 %collective-permute-start.7 = (bf16[256,2048]{1,0:T(8,128)(2,1)}, bf16[256,2048]{1,0:T(8,128)(2,1)S(1)}, u32[]{:S(2)}, u32[]{:S(2)}) collective-permute-start(bf16[256,2048]{1,0:T(8,128)(2,1)} %multiply_convert_fusion.5), channel_id=1, source_target_pairs={{8,0},{16,8},{24,16},{9,1},{17,9},{25,17},{10,2},{18,10},{26,18},{... | collective-permute-start | bytes 3145736 | tf_op jit(solution)/shard_map/ppermute | solution.py:210
  108.7 15.0 %collective-permute-start.6 = (bf16[256,2048]{1,0:T(8,128)(2,1)S(1)}, bf16[256,2048]{1,0:T(8,128)(2,1)S(1)}, u32[]{:S(2)}, u32[]{:S(2)}) collective-permute-start(bf16[256,2048]{1,0:T(8,128)(2,1)S(1)} %collective-permute-done.5), channel_id=1, source_target_pairs={{8,16},{16,24},{9,17},{17,25},{10,18},{18,26},{11,19},{19,27},{12,... | collective-permute-start | bytes 3145736 | tf_op jit(solution)/shard_map/ppermute | solution.py:207
  112.8 26.5 %collective-permute-start.8 = (bf16[256,2048]{1,0:T(8,128)(2,1)S(1)}, bf16[256,2048]{1,0:T(8,128)(2,1)S(1)}, u32[]{:S(2)}, u32[]{:S(2)}) collective-permute-start(bf16[256,2048]{1,0:T(8,128)(2,1)S(1)} %collective-permute-done.7), channel_id=1, source_target_pairs={{8,0},{16,8},{9,1},{17,9},{10,2},{18,10},{11,3},{19,11},{12,4},{20... | collective-permute-start | bytes 3145736 | tf_op jit(solution)/shard_map/ppermute | solution.py:210
  139.4 25.5 %collective-permute-start.9 = (bf16[256,2048]{1,0:T(8,128)(2,1)S(1)}, bf16[256,2048]{1,0:T(8,128)(2,1)S(1)}, u32[]{:S(2)}, u32[]{:S(2)}) collective-permute-start(bf16[256,2048]{1,0:T(8,128)(2,1)S(1)} %broadcast_select_fusion.1), channel_id=1, source_target_pairs={{16,24},{8,0},{17,25},{9,1},{18,26},{10,2},{19,27},{11,3},{20,28},... | collective-permute-start | bytes 3145736 | tf_op jit(solution)/shard_map/ppermute | solution.py:214
  170.5 1.9 copy-start.1
  173.9 4.4 %collective-permute-start.10 = (f32[2,256,1024]{2,1,0:T(8,128)}, f32[2,256,1024]{2,1,0:T(8,128)S(1)}, u32[]{:S(2)}, u32[]{:S(2)}) collective-permute-start(f32[2,256,1024]{2,1,0:T(8,128)} %pad_maximum_fusion.1), channel_id=1, source_target_pairs={{0,1},{1,0},{2,3},{3,2},{4,5},{5,4},{6,7},{7,6},{8,9},{9,8},{10,11... | collective-permute-start | bytes 6291464 | tf_op jit(solution)/shard_map/ppermute | solution.py:244
  179.6 14.0 %collective-permute-start.11 = (bf16[1,256,1024]{2,1,0:T(8,128)(2,1)S(1)}, bf16[1,256,1024]{2,1,0:T(8,128)(2,1)S(1)}, u32[]{:S(2)}, u32[]{:S(2)}) collective-permute-start(bf16[1,256,1024]{2,1,0:T(8,128)(2,1)S(1)} %fusion.23), channel_id=1, source_target_pairs={{0,2},{1,3},{2,0},{3,1},{4,6},{5,7},{6,4},{7,5},{8,10},{9,11},{10,... | collective-permute-start | bytes 1572872 | tf_op jit(solution)/shard_map/ppermute | solution.py:244
  195.1 27.0 %collective-permute-start.12 = (bf16[256,1024]{1,0:T(8,128)(2,1)S(1)}, bf16[256,1024]{1,0:T(8,128)(2,1)S(1)}, u32[]{:S(2)}, u32[]{:S(2)}) collective-permute-start(bf16[256,1024]{1,0:T(8,128)(2,1)S(1)} %fusion.27), channel_id=1, source_target_pairs={{0,0},{1,8},{2,16},{3,24},{8,1},{9,9},{10,17},{11,25},{16,2},{17,1... | collective-permute-start | bytes 1572872 | tf_op jit(solution)/shard_map/ppermute | solution.py:254

commit v16 on v12

--- a/solution.py
+++ b/solution.py
@@ -150,7 +150,7 @@
     dev_decay = jnp.prod(blk_decay, axis=0)
     if outer_axis is not None:
         inner_count = ctx_count // tp_count
-        split = out_weight.shape[1] // 2
+        split = out_weight.shape[1] // 4
         early, late = [], []
         for d in range(1, inner_count):
             pairs = [(s, (s + d) % inner_count) for s in range(inner_count)]

time: 235 us -> 224 us (0.953)
  starting transfers between devices: 54.8 us -> 49.7 us
  waiting for transfers between devices: 127 us -> 124 us
  matrix products: 22.8 us -> 20.4 us
    ppermute x1, waiting for transfers between devices: 12.7 us -> 1.22 us  [on_device(): early.append(lax.ppermute(out_weight[:, :split], inner_axis, pairs))]
    ppermute x2, waiting for transfers between devices: 33.8 us -> 37.4 us  [on_device(): lax.ppermute(going_left, outer_axis, [(s, s - 1) for s in range(1, tp_cou...]
    ppermute x2, starting transfers between devices: 17.1 us -> 13.8 us  [on_device(): lax.ppermute(going_right, outer_axis, [(s, s + 1) for s in range(step - 1...]
    ppermute x1, waiting for transfers between devices: 21 us -> 23.6 us  [on_device(): lax.ppermute(jnp.where(outer_at == tp_count - 2, going_right, going_left)...]
    ppermute x1, waiting for transfers between devices: 0.01 us -> 2.51 us  [on_device(): late.append(lax.ppermute(out_weight[:, split:], inner_axis, pairs))]
    dot_general x15, matrix products: 15.3 us -> 12.9 us  [times_weight(): jnp.dot(rows, piece, preferred_element_type=jnp.float32)]
  transfers between devices with their start and end apart: 16 -> 16, of which waited for: 10 -> 11; matrix products, arithmetic and copies ran while one was open for 16% -> 16% of each run, Pallas kernels for 0% -> 0%
where the time goes in v16:
time: 224 us; the launch traced here: 223 us
  waiting for transfers between devices  124 us (55%)
  starting transfers between devices  49.7 us (22%)
  matrix products  20.4 us (9%)
  other arithmetic  15.7 us (7%)
  local copies, waits for them, and re-layouts  12.7 us (6%)
    ppermute x2, waiting for transfers between devices, on_device(): lax.ppermute(going_left, outer_axis, [(s, s - 1) for s in range(1, tp_cou...  37.4 us
    ppermute x6, starting transfers between devices, shifted(): lax.ppermute(value, axis, [(source, source + steps) for source in range(f...  23.7 us
    ppermute x1, waiting for transfers between devices, on_device(): lax.ppermute(jnp.where(outer_at == tp_count - 2, going_right, going_left)...  23.6 us
    ppermute x1, waiting for transfers between devices, on_device(): lax.ppermute(held[0].astype(jnp.bfloat16), (outer_axis, 'tp'), swap)  23.4 us
    ppermute x2, waiting for transfers between devices, on_device(): lax.ppermute(sent if bit == 1 else sent.astype(jnp.bfloat16), 'tp', [(s,...  17.8 us
    ppermute x6, waiting for transfers between devices, shifted(): lax.ppermute(value, axis, [(source, source + steps) for source in range(f...  17.6 us
    ppermute x2, starting transfers between devices, on_device(): lax.ppermute(going_right, outer_axis, [(s, s + 1) for s in range(step - 1...  13.8 us
    dot_general x15, matrix products, times_weight(): jnp.dot(rows, piece, preferred_element_type=jnp.float32)  12.9 us
  transfers between devices with their start and end apart: 16, of which 11 were waited for; matrix products, arithmetic and copies ran while one was open for 16% of the time, Pallas kernels for 0%

profile of v16, /device:TPU:2, one launch (start us, length us, event | category | flops | bytes accessed | tf_op | source)
XLA Modules:
  0.0 223.0 jit_solution(3051816314760011560)
XLA Ops:
  0.0 1.3 constant_dynamic-update-slice_fusion.5
  1.5 3.4 %collective-permute-start.1 = (bf16[3,2304]{1,0:T(4,128)(2,1)S(1)}, bf16[3,2304]{1,0:T(4,128)(2,1)S(1)}, u32[]{:S(2)}, u32[]{:S(2)}) collective-permute-start(bf16[3,2304]{1,0:T(4,128)(2,1)S(1)} %slice.109), channel_id=1, source_target_pairs={{0,4},{4,8},{8,12},{12,16},{16,20},{20,24},{24,28},{1,5},{5,9},{9,... | collective-permute-start | bytes 41480 | tf_op jit(solution)/shard_map/ppermute | solution.py:14
  4.9 1.1 slice.80
  6.0 1.6 collective-permute-start
  9.8 1.5 multiply_convert_fusion.3
  11.3 1.0 copy-done.5
  12.3 1.6 slice_convert_fusion
  13.9 1.9 copy.40
  15.8 0.9 slice_convert_fusion.1
  16.8 1.4 fusion.18
  18.2 1.2 collective-permute-done
  19.5 3.5 %collective-permute-start.5 = (bf16[1,32,64,128]{3,2,1,0:T(8,128)(2,1)S(1)}, bf16[1,32,64,128]{3,2,1,0:T(8,128)(2,1)S(1)}, u32[]{:S(2)}, u32[]{:S(2)}) collective-permute-start(bf16[1,32,64,128]{3,2,1,0:T(8,128)(2,1)S(1)} %convert_element_type.96), channel_id=1, source_target_pairs={{0,4},{4,8},{8,12},{12,16},{16,20},{20,24},{24,28},{1,5},{5,9},{9,... | collective-permute-start | bytes 1572872 | tf_op jit(solution)/shard_map/ppermute | solution.py:14
  23.0 10.0 %collective-permute-done.5 = bf16[1,32,64,128]{3,2,1,0:T(8,128)(2,1)S(1)} collective-permute-done((bf16[1,32,64,128]{3,2,1,0:T(8,128)(2,1)S(1)}, bf16[1,32,64,128]{3,2,1,0:T(8,128)(2,1)S(1)}, u32[]{:S(2)}, u32[]{:S(2)}) %collective-permute-start.5) | collective-permute-done | bytes 524320 | tf_op jit(solution)/shard_map/ppermute | solution.py:14
  33.2 5.4 %collective-permute-start.6 = (bf16[1,32,64,128]{3,2,1,0:T(8,128)(2,1)S(1)}, bf16[1,32,64,128]{3,2,1,0:T(8,128)(2,1)S(1)}, u32[]{:S(2)}, u32[]{:S(2)}) collective-permute-start(bf16[1,32,64,128]{3,2,1,0:T(8,128)(2,1)S(1)} %fusion.27), channel_id=1, source_target_pairs={{0,8},{4,12},{8,16},{12,20},{16,24},{20,28},{1,9},{5,13},{9,17},{1... | collective-permute-start | bytes 1572872 | tf_op jit(solution)/shard_map/ppermute | solution.py:14
  38.6 2.5 %collective-permute-start.3 = (f32[1,32]{1,0:T(1,128)S(1)}, f32[1,32]{1,0:T(1,128)S(1)}, u32[]{:S(2)}, u32[]{:S(2)}) collective-permute-start(f32[1,32]{1,0:T(1,128)S(1)} %bitcast.135), channel_id=1, source_target_pairs={{0,4},{4,8},{8,12},{12,16},{16,20},{20,24},{24,28},{1,5},{5,9},{9,... | collective-permute-start | bytes 392 | tf_op jit(solution)/shard_map/ppermute | solution.py:14
  41.1 1.3 slice.97
  42.5 2.4 %collective-permute-start.2 = (bf16[2048,384]{1,0:T(8,128)(2,1)}, bf16[2048,384]{1,0:T(8,128)(2,1)S(1)}, u32[]{:S(2)}, u32[]{:S(2)}) collective-permute-start(bf16[2048,384]{1,0:T(8,128)(2,1)} %slice.97), channel_id=1, source_target_pairs={{0,4},{4,0},{1,5},{5,1},{2,6},{6,2},{3,7},{7,3},{8,12},{12,8},{9,1... | collective-permute-start | bytes 4718600 | tf_op jit(solution)/shard_map/ppermute | solution.py:158
  44.9 2.8 %collective-permute-done.6 = bf16[1,32,64,128]{3,2,1,0:T(8,128)(2,1)S(1)} collective-permute-done((bf16[1,32,64,128]{3,2,1,0:T(8,128)(2,1)S(1)}, bf16[1,32,64,128]{3,2,1,0:T(8,128)(2,1)S(1)}, u32[]{:S(2)}, u32[]{:S(2)}) %collective-permute-start.6) | collective-permute-done | bytes 524320 | tf_op jit(solution)/shard_map/ppermute | solution.py:14
  48.1 5.5 %collective-permute-start.7 = (bf16[1,32,64,128]{3,2,1,0:T(8,128)(2,1)S(1)}, bf16[1,32,64,128]{3,2,1,0:T(8,128)(2,1)S(1)}, u32[]{:S(2)}, u32[]{:S(2)}) collective-permute-start(bf16[1,32,64,128]{3,2,1,0:T(8,128)(2,1)S(1)} %fusion.23), channel_id=1, source_target_pairs={{0,16},{4,20},{8,24},{12,28},{1,17},{5,21},{9,25},{13,29},{2,18},{... | collective-permute-start | bytes 1572872 | tf_op jit(solution)/shard_map/ppermute | solution.py:14
  53.6 3.4 %collective-permute-start.4 = (f32[1,32]{1,0:T(1,128)S(1)}, f32[1,32]{1,0:T(1,128)S(1)}, u32[]{:S(2)}, u32[]{:S(2)}) collective-permute-start(f32[1,32]{1,0:T(1,128)S(1)} %bitcast_multiply_fusion.1), channel_id=1, source_target_pairs={{0,8},{4,12},{8,16},{12,20},{16,24},{20,28},{1,9},{5,13},{9,17},{1... | collective-permute-start | bytes 392 | tf_op jit(solution)/shard_map/ppermute | solution.py:14
  57.1 4.8 %collective-permute-done.4 = f32[1,32]{1,0:T(1,128)S(1)} collective-permute-done((f32[1,32]{1,0:T(1,128)S(1)}, f32[1,32]{1,0:T(1,128)S(1)}, u32[]{:S(2)}, u32[]{:S(2)}) %collective-permute-start.4) | collective-permute-done | bytes 160 | tf_op jit(solution)/shard_map/ppermute | solution.py:14
  61.9 1.1 fusion.40
  62.9 1.3 fusion.30
  64.3 3.7 %fusion.14 = f32[256,1,32,64]{0,3,2,1:T(8,128)} fusion(f32[32,64,256]{2,1,0:T(8,128)S(1)} %fusion.30, f32[256,1,32,64]{0,3,2,1:T(8,128)S(1)} %bitcast.123, f32[32,256]{1,0:T(8,128)S(1)} %bitcast.131, f32[256,256]{1,0:T(8,128)S(1)} %fusion.40, pred[256,256]{1,0:T(8,128)(4,1)S(1)} %iota_compare_fusion.1, f32[32]{0:T(128)S(1)} %copy-done.17, ...), kind=kOutput, calls=%fused_computation.26 | convolution fusion | flops 279969792 | bytes 8814720 | tf_op jit(solution)/shard_map/while/body/eval_jaxpr/gjts,sgjp->tgjp/dot_general | solution.py:46
  68.0 3.0 %copy.42 = f32[256,2048]{1,0:T(8,128)} copy(f32[256,2048]{0,1:T(8,128)} %bitcast.124) | data formatting | bytes 4194304 | tf_op jit(solution)/shard_map/reshape | solution.py:175
  71.0 2.5 %multiply_reduce_fusion = f32[256]{0:T(256)S(1)} fusion(f32[256,2048]{1,0:T(8,128)} %copy.42, bf16[256,2048]{1,0:T(8,128)(2,1)S(1)} %copy-done.6), kind=kLoop, calls=%fused_computation.28 | loop fusion | flops 4194048 | bytes 3146752 | tf_op jit(solution)/shard_map/reduce_sum | solution.py:177
  73.6 0.8 multiply_convert_fusion.5
  74.4 2.5 %collective-permute-done.2 = bf16[2048,384]{1,0:T(8,128)(2,1)S(1)} collective-permute-done((bf16[2048,384]{1,0:T(8,128)(2,1)}, bf16[2048,384]{1,0:T(8,128)(2,1)S(1)}, u32[]{:S(2)}, u32[]{:S(2)}) %collective-permute-start.2) | collective-permute-done | bytes 1572896 | tf_op jit(solution)/shard_map/ppermute | solution.py:158
  76.9 1.3 collective-permute-start.10
  78.3 12.9 %collective-permute-start.8 = (bf16[256,2048]{1,0:T(8,128)(2,1)S(1)}, bf16[256,2048]{1,0:T(8,128)(2,1)S(1)}, u32[]{:S(2)}, u32[]{:S(2)}) collective-permute-start(bf16[256,2048]{1,0:T(8,128)(2,1)S(1)} %multiply_convert_fusion.5), channel_id=1, source_target_pairs={{0,8},{8,16},{16,24},{1,9},{9,17},{17,25},{2,10},{10,18},{18,26},{... | collective-permute-start | bytes 3145736 | tf_op jit(solution)/shard_map/ppermute | solution.py:201
  93.2 19.3 %collective-permute-done.10 = bf16[256,2048]{1,0:T(8,128)(2,1)} collective-permute-done((bf16[256,2048]{1,0:T(8,128)(2,1)S(1)}, bf16[256,2048]{1,0:T(8,128)(2,1)}, u32[]{:S(2)}, u32[]{:S(2)}) %collective-permute-start.10) | collective-permute-done | bytes 1048608 | tf_op jit(solution)/shard_map/ppermute | solution.py:204
  112.4 1.3 collective-permute-start.11
  113.7 1.7 convolution_bitcast_fusion.6
  115.4 0.9 collective-permute-start.9
  116.3 1.9 convolution_bitcast_fusion.3
  119.0 1.9 convolution_bitcast_fusion
  121.6 18.1 %collective-permute-done.11 = bf16[256,2048]{1,0:T(8,128)(2,1)S(1)} collective-permute-done((bf16[256,2048]{1,0:T(8,128)(2,1)}, bf16[256,2048]{1,0:T(8,128)(2,1)S(1)}, u32[]{:S(2)}, u32[]{:S(2)}) %collective-permute-start.11) | collective-permute-done | bytes 1048608 | tf_op jit(solution)/shard_map/ppermute | solution.py:204
  139.9 1.3 collective-permute-start.12
  143.6 23.6 %collective-permute-done.12 = bf16[256,2048]{1,0:T(8,128)(2,1)S(1)} collective-permute-done((bf16[256,2048]{1,0:T(8,128)(2,1)S(1)}, bf16[256,2048]{1,0:T(8,128)(2,1)S(1)}, u32[]{:S(2)}, u32[]{:S(2)}) %collective-permute-start.12) | collective-permute-done | bytes 1048608 | tf_op jit(solution)/shard_map/ppermute | solution.py:208
  170.2 1.7 copy-done.2
  171.9 1.5 pad_maximum_fusion.1
  173.4 4.4 %collective-permute-done.13 = f32[2,256,1024]{2,1,0:T(8,128)S(1)} collective-permute-done((f32[2,256,1024]{2,1,0:T(8,128)}, f32[2,256,1024]{2,1,0:T(8,128)S(1)}, u32[]{:S(2)}, u32[]{:S(2)}) %collective-permute-start.13) | collective-permute-done | bytes 2097184 | tf_op jit(solution)/shard_map/ppermute | solution.py:238
  177.7 1.4 fusion.24
  179.7 13.4 %collective-permute-done.14 = bf16[1,256,1024]{2,1,0:T(8,128)(2,1)S(1)} collective-permute-done((bf16[1,256,1024]{2,1,0:T(8,128)(2,1)S(1)}, bf16[1,256,1024]{2,1,0:T(8,128)(2,1)S(1)}, u32[]{:S(2)}, u32[]{:S(2)}) %collective-permute-start.14) | collective-permute-done | bytes 524320 | tf_op jit(solution)/shard_map/ppermute | solution.py:238
  193.1 1.5 fusion.28
  194.6 3.8 %collective-permute-start.15 = (bf16[256,1024]{1,0:T(8,128)(2,1)S(1)}, bf16[256,1024]{1,0:T(8,128)(2,1)S(1)}, u32[]{:S(2)}, u32[]{:S(2)}) collective-permute-start(bf16[256,1024]{1,0:T(8,128)(2,1)S(1)} %fusion.28), channel_id=1, source_target_pairs={{0,0},{1,8},{2,16},{3,24},{8,1},{9,9},{10,17},{11,25},{16,2},{17,1... | collective-permute-start | bytes 1572872 | tf_op jit(solution)/shard_map/ppermute | solution.py:248
  198.4 23.4 %collective-permute-done.15 = bf16[256,1024]{1,0:T(8,128)(2,1)S(1)} collective-permute-done((bf16[256,1024]{1,0:T(8,128)(2,1)S(1)}, bf16[256,1024]{1,0:T(8,128)(2,1)S(1)}, u32[]{:S(2)}, u32[]{:S(2)}) %collective-permute-start.15) | collective-permute-done | bytes 524320 | tf_op jit(solution)/shard_map/ppermute | solution.py:248
  222.1 0.9 pad_maximum_fusion.3
  (93 shorter events, 12.5 us)
Async XLA Ops:
  0.0 7.6 %copy-start = (f32[256,32]{0,1:T(8,128)S(1)}, f32[256,32]{0,1:T(8,128)}, u32[]{:S(2)}) copy-start(f32[256,32]{0,1:T(8,128)} %param.20) | copy-start | bytes 98308
  0.0 1.4 copy-start.10
  0.0 1.4 copy-start.11
  0.0 9.3 %copy-start.13 = (f32[4,2048]{1,0:T(4,128)S(1)}, f32[4,2048]{1,0:T(4,128)}, u32[]{:S(2)}) copy-start(f32[4,2048]{1,0:T(4,128)} %param.16) | copy-start | bytes 98308
  0.0 9.4 %copy-start.15 = (f32[4,128]{1,0:T(4,128)S(1)}, f32[4,128]{1,0:T(4,128)}, u32[]{:S(2)}) copy-start(f32[4,128]{1,0:T(4,128)} %param.17) | copy-start | bytes 6148
  0.0 9.4 %copy-start.16 = (f32[4,128]{1,0:T(4,128)S(1)}, f32[4,128]{1,0:T(4,128)}, u32[]{:S(2)}) copy-start(f32[4,128]{1,0:T(4,128)} %param.18) | copy-start | bytes 6148
  1.5 8.1 %collective-permute-start.1 = (bf16[3,2304]{1,0:T(4,128)(2,1)S(1)}, bf16[3,2304]{1,0:T(4,128)(2,1)S(1)}, u32[]{:S(2)}, u32[]{:S(2)}) collective-permute-start(bf16[3,2304]{1,0:T(4,128)(2,1)S(1)} %slice.109), channel_id=1, source_target_pairs={{0,4},{4,8},{8,12},{12,16},{16,20},{20,24},{24,28},{1,5},{5,9},{9,... | collective-permute-start | bytes 41480 | tf_op jit(solution)/shard_map/ppermute | solution.py:14
  6.0 13.4 %collective-permute-start = (bf16[2048,128]{1,0:T(8,128)(2,1)S(1)}, bf16[2048,128]{1,0:T(8,128)(2,1)S(1)}, u32[]{:S(2)}, u32[]{:S(2)}) collective-permute-start(bf16[2048,128]{1,0:T(8,128)(2,1)S(1)} %slice.80), channel_id=1, source_target_pairs={{0,4},{4,0},{1,5},{5,1},{2,6},{6,2},{3,7},{7,3},{8,12},{12,8},{9,1... | collective-permute-start | bytes 1572872 | tf_op jit(solution)/shard_map/ppermute | solution.py:157
  11.3 1.0 copy-start.5
  13.9 2.9 %copy-start.12 = (f32[256,32]{0,1:T(8,128)S(1)}, f32[256,32]{0,1:T(8,128)}, u32[]{:S(2)}) copy-start(f32[256,32]{0,1:T(8,128)} %param.19) | copy-start | bytes 98308
  15.8 3.7 %copy-start.3 = (f32[256,2048]{0,1:T(8,128)}, f32[256,2048]{0,1:T(8,128)S(1)}, u32[]{:S(2)}) copy-start(f32[256,2048]{0,1:T(8,128)S(1)} %copy.40) | copy-start | bytes 6291460
  18.2 22.9 %copy-start.8 = (bf16[2048,512]{1,0:T(8,128)(2,1)S(1)}, bf16[2048,512]{1,0:T(8,128)(2,1)}, u32[]{:S(2)}) copy-start(bf16[2048,512]{1,0:T(8,128)(2,1)} %param.23) | copy-start | bytes 6291460
  19.5 13.5 %collective-permute-start.5 = (bf16[1,32,64,128]{3,2,1,0:T(8,128)(2,1)S(1)}, bf16[1,32,64,128]{3,2,1,0:T(8,128)(2,1)S(1)}, u32[]{:S(2)}, u32[]{:S(2)}) collective-permute-start(bf16[1,32,64,128]{3,2,1,0:T(8,128)(2,1)S(1)} %convert_element_type.96), channel_id=1, source_target_pairs={{0,4},{4,8},{8,12},{12,16},{16,20},{20,24},{24,28},{1,5},{5,9},{9,... | collective-permute-start | bytes 1572872 | tf_op jit(solution)/shard_map/ppermute | solution.py:14
  33.2 14.5 %collective-permute-start.6 = (bf16[1,32,64,128]{3,2,1,0:T(8,128)(2,1)S(1)}, bf16[1,32,64,128]{3,2,1,0:T(8,128)(2,1)S(1)}, u32[]{:S(2)}, u32[]{:S(2)}) collective-permute-start(bf16[1,32,64,128]{3,2,1,0:T(8,128)(2,1)S(1)} %fusion.27), channel_id=1, source_target_pairs={{0,8},{4,12},{8,16},{12,20},{16,24},{20,28},{1,9},{5,13},{9,17},{1... | collective-permute-start | bytes 1572872 | tf_op jit(solution)/shard_map/ppermute | solution.py:14
  38.6 6.3 %collective-permute-start.3 = (f32[1,32]{1,0:T(1,128)S(1)}, f32[1,32]{1,0:T(1,128)S(1)}, u32[]{:S(2)}, u32[]{:S(2)}) collective-permute-start(f32[1,32]{1,0:T(1,128)S(1)} %bitcast.135), channel_id=1, source_target_pairs={{0,4},{4,8},{8,12},{12,16},{16,20},{20,24},{24,28},{1,5},{5,9},{9,... | collective-permute-start | bytes 392 | tf_op jit(solution)/shard_map/ppermute | solution.py:14
  42.5 34.4 %collective-permute-start.2 = (bf16[2048,384]{1,0:T(8,128)(2,1)}, bf16[2048,384]{1,0:T(8,128)(2,1)S(1)}, u32[]{:S(2)}, u32[]{:S(2)}) collective-permute-start(bf16[2048,384]{1,0:T(8,128)(2,1)} %slice.97), channel_id=1, source_target_pairs={{0,4},{4,0},{1,5},{5,1},{2,6},{6,2},{3,7},{7,3},{8,12},{12,8},{9,1... | collective-permute-start | bytes 4718600 | tf_op jit(solution)/shard_map/ppermute | solution.py:158
  48.1 14.9 %collective-permute-start.7 = (bf16[1,32,64,128]{3,2,1,0:T(8,128)(2,1)S(1)}, bf16[1,32,64,128]{3,2,1,0:T(8,128)(2,1)S(1)}, u32[]{:S(2)}, u32[]{:S(2)}) collective-permute-start(bf16[1,32,64,128]{3,2,1,0:T(8,128)(2,1)S(1)} %fusion.23), channel_id=1, source_target_pairs={{0,16},{4,20},{8,24},{12,28},{1,17},{5,21},{9,25},{13,29},{2,18},{... | collective-permute-start | bytes 1572872 | tf_op jit(solution)/shard_map/ppermute | solution.py:14
  53.6 8.3 %collective-permute-start.4 = (f32[1,32]{1,0:T(1,128)S(1)}, f32[1,32]{1,0:T(1,128)S(1)}, u32[]{:S(2)}, u32[]{:S(2)}) collective-permute-start(f32[1,32]{1,0:T(1,128)S(1)} %bitcast_multiply_fusion.1), channel_id=1, source_target_pairs={{0,8},{4,12},{8,16},{12,20},{16,24},{20,28},{1,9},{5,13},{9,17},{1... | collective-permute-start | bytes 392 | tf_op jit(solution)/shard_map/ppermute | solution.py:14
  57.0 7.3 %copy-start.4 = (f32[256,2048]{0,1:T(8,128)S(1)}, f32[256,2048]{0,1:T(8,128)}, u32[]{:S(2)}) copy-start(f32[256,2048]{0,1:T(8,128)} %copy-done.3) | copy-start | bytes 6291460
  57.0 7.3 %copy-start.17 = (f32[32]{0:T(128)S(1)}, f32[32]{0:T(128)}, u32[]{:S(2)}) copy-start(f32[32]{0:T(128)} %param.21) | copy-start | bytes 388
  68.0 3.0 %copy-start.6 = (bf16[256,2048]{1,0:T(8,128)(2,1)S(1)}, bf16[256,2048]{1,0:T(8,128)(2,1)}, u32[]{:S(2)}) copy-start(bf16[256,2048]{1,0:T(8,128)(2,1)} %param.15) | copy-start | bytes 3145732
  68.0 5.5 %copy-start.14 = (f32[2048]{0:T(1024)S(1)}, f32[2048]{0:T(1024)}, u32[]{:S(2)}) copy-start(f32[2048]{0:T(1024)} %param.22) | copy-start | bytes 24580
  71.0 2.5 %copy-start.1 = (f32[256,2048]{1,0:T(8,128)S(1)}, f32[256,2048]{1,0:T(8,128)}, u32[]{:S(2)}) copy-start(f32[256,2048]{1,0:T(8,128)} %copy.42) | copy-start | bytes 6291460
  71.0 2.5 %copy-start.7 = (bf16[256,2048]{1,0:T(8,128)(2,1)S(1)}, bf16[256,2048]{1,0:T(8,128)(2,1)}, u32[]{:S(2)}) copy-start(bf16[256,2048]{1,0:T(8,128)(2,1)} %param.15) | copy-start | bytes 3145732
  76.9 35.5 %collective-permute-start.10 = (bf16[256,2048]{1,0:T(8,128)(2,1)S(1)}, bf16[256,2048]{1,0:T(8,128)(2,1)}, u32[]{:S(2)}, u32[]{:S(2)}) collective-permute-start(bf16[256,2048]{1,0:T(8,128)(2,1)S(1)} %multiply_convert_fusion.5), channel_id=1, source_target_pairs={{8,0},{16,8},{24,16},{9,1},{17,9},{25,17},{10,2},{18,10},{26,18},{... | collective-permute-start | bytes 3145736 | tf_op jit(solution)/shard_map/ppermute | solution.py:204
  78.3 14.1 %copy-start.9 = (bf16[2048,512]{1,0:T(8,128)(2,1)S(1)}, bf16[2048,512]{1,0:T(8,128)(2,1)}, u32[]{:S(2)}) copy-start(bf16[2048,512]{1,0:T(8,128)(2,1)} %param.23) | copy-start | bytes 6291460
  78.3 37.1 %collective-permute-start.8 = (bf16[256,2048]{1,0:T(8,128)(2,1)S(1)}, bf16[256,2048]{1,0:T(8,128)(2,1)S(1)}, u32[]{:S(2)}, u32[]{:S(2)}) collective-permute-start(bf16[256,2048]{1,0:T(8,128)(2,1)S(1)} %multiply_convert_fusion.5), channel_id=1, source_target_pairs={{0,8},{8,16},{16,24},{1,9},{9,17},{17,25},{2,10},{10,18},{18,26},{... | collective-permute-start | bytes 3145736 | tf_op jit(solution)/shard_map/ppermute | solution.py:201
  112.4 27.3 %collective-permute-start.11 = (bf16[256,2048]{1,0:T(8,128)(2,1)}, bf16[256,2048]{1,0:T(8,128)(2,1)S(1)}, u32[]{:S(2)}, u32[]{:S(2)}) collective-permute-start(bf16[256,2048]{1,0:T(8,128)(2,1)} %collective-permute-done.10), channel_id=1, source_target_pairs={{8,0},{16,8},{9,1},{17,9},{10,2},{18,10},{11,3},{19,11},{12,4},{20... | collective-permute-start | bytes 3145736 | tf_op jit(solution)/shard_map/ppermute | solution.py:204
  115.4 24.4 %collective-permute-start.9 = (bf16[256,2048]{1,0:T(8,128)(2,1)S(1)}, bf16[256,2048]{1,0:T(8,128)(2,1)S(1)}, u32[]{:S(2)}, u32[]{:S(2)}) collective-permute-start(bf16[256,2048]{1,0:T(8,128)(2,1)S(1)} %collective-permute-done.8), channel_id=1, source_target_pairs={{8,16},{16,24},{9,17},{17,25},{10,18},{18,26},{11,19},{19,27},{12,... | collective-permute-start | bytes 3145736 | tf_op jit(solution)/shard_map/ppermute | solution.py:201
  139.9 27.3 %collective-permute-start.12 = (bf16[256,2048]{1,0:T(8,128)(2,1)S(1)}, bf16[256,2048]{1,0:T(8,128)(2,1)S(1)}, u32[]{:S(2)}, u32[]{:S(2)}) collective-permute-start(bf16[256,2048]{1,0:T(8,128)(2,1)S(1)} %get-tuple-element.67), channel_id=1, source_target_pairs={{16,24},{8,0},{17,25},{9,1},{18,26},{10,2},{19,27},{11,3},{20,28},... | collective-permute-start | bytes 3145736 | tf_op jit(solution)/shard_map/ppermute | solution.py:208
  169.9 2.0 copy-start.2
  173.4 4.4 %collective-permute-start.13 = (f32[2,256,1024]{2,1,0:T(8,128)}, f32[2,256,1024]{2,1,0:T(8,128)S(1)}, u32[]{:S(2)}, u32[]{:S(2)}) collective-permute-start(f32[2,256,1024]{2,1,0:T(8,128)} %pad_maximum_fusion.1), channel_id=1, source_target_pairs={{0,1},{1,0},{2,3},{3,2},{4,5},{5,4},{6,7},{7,6},{8,9},{9,8},{10,11... | collective-permute-start | bytes 6291464 | tf_op jit(solution)/shard_map/ppermute | solution.py:238
  179.1 14.0 %collective-permute-start.14 = (bf16[1,256,1024]{2,1,0:T(8,128)(2,1)S(1)}, bf16[1,256,1024]{2,1,0:T(8,128)(2,1)S(1)}, u32[]{:S(2)}, u32[]{:S(2)}) collective-permute-start(bf16[1,256,1024]{2,1,0:T(8,128)(2,1)S(1)} %fusion.24), channel_id=1, source_target_pairs={{0,2},{1,3},{2,0},{3,1},{4,6},{5,7},{6,4},{7,5},{8,10},{9,11},{10,... | collective-permute-start | bytes 1572872 | tf_op jit(solution)/shard_map/ppermute | solution.py:238
  194.6 27.2 %collective-permute-start.15 = (bf16[256,1024]{1,0:T(8,128)(2,1)S(1)}, bf16[256,1024]{1,0:T(8,128)(2,1)S(1)}, u32[]{:S(2)}, u32[]{:S(2)}) collective-permute-start(bf16[256,1024]{1,0:T(8,128)(2,1)S(1)} %fusion.28), channel_id=1, source_target_pairs={{0,0},{1,8},{2,16},{3,24},{8,1},{9,9},{10,17},{11,25},{16,2},{17,1... | collective-permute-start | bytes 1572872 | tf_op jit(solution)/shard_map/ppermute | solution.py:248

commit v17 on v11

--- a/solution.py
+++ b/solution.py
@@ -205,7 +205,7 @@
         [(tp_count - 2, tp_count - 1), (1, 0)],
     )
     far_part = times_weight(far)
-    by_source = jnp.stack(
+    by_source = (
         [times_weight(hidden)]
         + [
             jnp.where(
@@ -220,8 +220,8 @@
     )
 
     def for_target(target):
-        return lax.dynamic_index_in_dim(
-            by_source, (outer_at - target + tp_count) % tp_count, 0, keepdims=False
+        return lax.select_n(
+            ((outer_at - target + tp_count) % tp_count).astype(jnp.int32), *by_source
         )
 
     held = {m: for_target(tp_at ^ m) for m in range(tp_count)}

time: 214 us -> 216 us (level)
  other arithmetic: 14.6 us -> 17.9 us
    ppermute x1, waiting for transfers between devices: 13.9 us -> 11.1 us  [on_device(): lax.ppermute(jnp.where(outer_at == tp_count - 2, going_right, going_left)...]
    ppermute x2, waiting for transfers between devices: 27.2 us -> 29.4 us  [on_device(): lax.ppermute(going_left, outer_axis, [(s, s - 1) for s in range(1, tp_cou...]
where the time goes in v17:
time: 216 us; the launch traced here: 215 us
  waiting for transfers between devices  118 us (55%)
  starting transfers between devices  40.5 us (19%)
  matrix products  31.3 us (14%)
  other arithmetic  17.9 us (8%)
  local copies, waits for them, and re-layouts  6.53 us (3%)
    ppermute x2, waiting for transfers between devices, on_device(): lax.ppermute(going_left, outer_axis, [(s, s - 1) for s in range(1, tp_cou...  29.4 us
    dot_general x10, matrix products, times_weight(): jnp.dot(rows, piece, preferred_element_type=jnp.float32)  24.7 us
    ppermute x6, starting transfers between devices, shifted(): lax.ppermute(value, axis, [(source, source + steps) for source in range(f...  23.7 us
    ppermute x1, waiting for transfers between devices, on_device(): lax.ppermute(held[0].astype(jnp.bfloat16), (outer_axis, 'tp'), swap)  22.8 us
    ppermute x6, waiting for transfers between devices, shifted(): lax.ppermute(value, axis, [(source, source + steps) for source in range(f...  21.2 us
    ppermute x2, waiting for transfers between devices, on_device(): lax.ppermute(sent if bit == 1 else sent.astype(jnp.bfloat16), 'tp', [(s,...  18.2 us
    ppermute x1, waiting for transfers between devices, on_device(): lax.ppermute(out_weight, inner_axis, [(s, (s + d) % inner_count) for s in...  14.9 us
    ppermute x1, waiting for transfers between devices, on_device(): lax.ppermute(jnp.where(outer_at == tp_count - 2, going_right, going_left)...  11.1 us
  transfers between devices with their start and end apart: 15, of which 10 were waited for; matrix products, arithmetic and copies ran while one was open for 15% of the time, Pallas kernels for 0%

profile of v17, /device:TPU:2, one launch (start us, length us, event | category | flops | bytes accessed | tf_op | source)
XLA Modules:
  0.0 214.6 jit_solution(1297493059708312700)
XLA Ops:
  0.0 1.3 constant_dynamic-update-slice_fusion.5
  1.5 3.4 %collective-permute-start.1 = (bf16[3,2304]{1,0:T(4,128)(2,1)S(1)}, bf16[3,2304]{1,0:T(4,128)(2,1)S(1)}, u32[]{:S(2)}, u32[]{:S(2)}) collective-permute-start(bf16[3,2304]{1,0:T(4,128)(2,1)S(1)} %slice.99), channel_id=1, source_target_pairs={{0,4},{4,8},{8,12},{12,16},{16,20},{20,24},{24,28},{1,5},{5,9},{9,... | collective-permute-start | bytes 41480 | tf_op jit(solution)/shard_map/ppermute | solution.py:14
  5.9 0.7 fusion.48
  7.7 1.5 multiply_convert_fusion.3
  9.3 1.6 slice_convert_fusion
  10.8 1.9 copy.27
  12.8 2.2 %fusion.17 = f32[32,64,128]{2,1,0:T(8,128)S(1)} fusion(f32[256,32]{0,1:T(8,128)S(1)} %bitcast.138, f32[256,128]{1,0:T(8,128)S(1)} %slice_convert_fusion.1, f32[32]{0:T(128)S(1)} %get-tuple-element.72, f32[256,32,64]{0,2,1:T(8,128)S(1)} %bitcast.112, f32[256,32]{0,1:T(8,128)} %param.19), kind=kOutput, calls=%fused_computation.31 | convolution fusion | flops 137625600 | bytes 3342464 | tf_op jit(solution)/shard_map/vmap(sgjp,sgjn->gjpn)/dot_general | solution.py:54
  15.1 3.5 %collective-permute-start.4 = (bf16[1,32,64,128]{3,2,1,0:T(8,128)(2,1)S(1)}, bf16[1,32,64,128]{3,2,1,0:T(8,128)(2,1)S(1)}, u32[]{:S(2)}, u32[]{:S(2)}) collective-permute-start(bf16[1,32,64,128]{3,2,1,0:T(8,128)(2,1)S(1)} %convert_bitcast_fusion), channel_id=1, source_target_pairs={{0,4},{4,8},{8,12},{12,16},{16,20},{20,24},{24,28},{1,5},{5,9},{9,... | collective-permute-start | bytes 1572872 | tf_op jit(solution)/shard_map/ppermute | solution.py:14
  18.5 10.8 %collective-permute-done.4 = bf16[1,32,64,128]{3,2,1,0:T(8,128)(2,1)S(1)} collective-permute-done((bf16[1,32,64,128]{3,2,1,0:T(8,128)(2,1)S(1)}, bf16[1,32,64,128]{3,2,1,0:T(8,128)(2,1)S(1)}, u32[]{:S(2)}, u32[]{:S(2)}) %collective-permute-start.4) | collective-permute-done | bytes 524320 | tf_op jit(solution)/shard_map/ppermute | solution.py:14
  29.6 5.4 %collective-permute-start.5 = (bf16[1,32,64,128]{3,2,1,0:T(8,128)(2,1)S(1)}, bf16[1,32,64,128]{3,2,1,0:T(8,128)(2,1)S(1)}, u32[]{:S(2)}, u32[]{:S(2)}) collective-permute-start(bf16[1,32,64,128]{3,2,1,0:T(8,128)(2,1)S(1)} %fusion.28), channel_id=1, source_target_pairs={{0,8},{4,12},{8,16},{12,20},{16,24},{20,28},{1,9},{5,13},{9,17},{1... | collective-permute-start | bytes 1572872 | tf_op jit(solution)/shard_map/ppermute | solution.py:14
  35.0 2.5 %collective-permute-start.2 = (f32[1,32]{1,0:T(1,128)S(1)}, f32[1,32]{1,0:T(1,128)S(1)}, u32[]{:S(2)}, u32[]{:S(2)}) collective-permute-start(f32[1,32]{1,0:T(1,128)S(1)} %bitcast.144), channel_id=1, source_target_pairs={{0,4},{4,8},{8,12},{12,16},{16,20},{20,24},{24,28},{1,5},{5,9},{9,... | collective-permute-start | bytes 392 | tf_op jit(solution)/shard_map/ppermute | solution.py:14
  37.5 2.5 %collective-permute-start = (bf16[2048,512]{1,0:T(8,128)(2,1)}, bf16[2048,512]{1,0:T(8,128)(2,1)}, u32[]{:S(2)}, u32[]{:S(2)}) collective-permute-start(bf16[2048,512]{1,0:T(8,128)(2,1)} %param.23), channel_id=1, source_target_pairs={{0,4},{4,0},{1,5},{5,1},{2,6},{6,2},{3,7},{7,3},{8,12},{12,8},{9,1... | collective-permute-start | bytes 6291464 | tf_op jit(solution)/shard_map/ppermute | solution.py:180
  40.0 4.5 %collective-permute-done.5 = bf16[1,32,64,128]{3,2,1,0:T(8,128)(2,1)S(1)} collective-permute-done((bf16[1,32,64,128]{3,2,1,0:T(8,128)(2,1)S(1)}, bf16[1,32,64,128]{3,2,1,0:T(8,128)(2,1)S(1)}, u32[]{:S(2)}, u32[]{:S(2)}) %collective-permute-start.5) | collective-permute-done | bytes 524320 | tf_op jit(solution)/shard_map/ppermute | solution.py:14
  44.9 6.0 %collective-permute-start.6 = (bf16[1,32,64,128]{3,2,1,0:T(8,128)(2,1)S(1)}, bf16[1,32,64,128]{3,2,1,0:T(8,128)(2,1)S(1)}, u32[]{:S(2)}, u32[]{:S(2)}) collective-permute-start(bf16[1,32,64,128]{3,2,1,0:T(8,128)(2,1)S(1)} %fusion.22), channel_id=1, source_target_pairs={{0,16},{4,20},{8,24},{12,28},{1,17},{5,21},{9,25},{13,29},{2,18},{... | collective-permute-start | bytes 1572872 | tf_op jit(solution)/shard_map/ppermute | solution.py:14
  50.9 3.0 %collective-permute-start.3 = (f32[1,32]{1,0:T(1,128)S(1)}, f32[1,32]{1,0:T(1,128)S(1)}, u32[]{:S(2)}, u32[]{:S(2)}) collective-permute-start(f32[1,32]{1,0:T(1,128)S(1)} %bitcast_multiply_fusion.1), channel_id=1, source_target_pairs={{0,8},{4,12},{8,16},{12,20},{16,24},{20,28},{1,9},{5,13},{9,17},{1... | collective-permute-start | bytes 392 | tf_op jit(solution)/shard_map/ppermute | solution.py:14
  53.9 5.9 %collective-permute-done.3 = f32[1,32]{1,0:T(1,128)S(1)} collective-permute-done((f32[1,32]{1,0:T(1,128)S(1)}, f32[1,32]{1,0:T(1,128)S(1)}, u32[]{:S(2)}, u32[]{:S(2)}) %collective-permute-start.3) | collective-permute-done | bytes 160 | tf_op jit(solution)/shard_map/ppermute | solution.py:14
  60.5 3.7 %fusion.14 = f32[256,1,32,64]{0,3,2,1:T(8,128)} fusion(f32[32,64,256]{2,1,0:T(8,128)S(1)} %fusion.30, f32[256,1,32,64]{0,3,2,1:T(8,128)S(1)} %bitcast.114, f32[32,256]{1,0:T(8,128)S(1)} %bitcast.140, f32[256,256]{1,0:T(8,128)S(1)} %fusion.41, pred[256,256]{1,0:T(8,128)(4,1)S(1)} %iota_compare_fusion.1, f32[32]{0:T(128)S(1)} %copy-done.18, ...), kind=kOutput, calls=%fused_computation.25 | convolution fusion | flops 279969792 | bytes 8814720 | tf_op jit(solution)/shard_map/while/body/eval_jaxpr/gjts,sgjp->tgjp/dot_general | solution.py:46
  64.2 2.0 copy.32
  66.3 0.8 multiply_reduce_fusion
  67.0 1.8 multiply_convert_fusion.5
  68.9 14.9 %collective-permute-done = bf16[2048,512]{1,0:T(8,128)(2,1)} collective-permute-done((bf16[2048,512]{1,0:T(8,128)(2,1)}, bf16[2048,512]{1,0:T(8,128)(2,1)}, u32[]{:S(2)}, u32[]{:S(2)}) %collective-permute-start) | collective-permute-done | bytes 2097184 | tf_op jit(solution)/shard_map/ppermute | solution.py:180
  83.8 1.3 collective-permute-start.9
  85.1 4.6 %collective-permute-start.7 = (bf16[256,2048]{1,0:T(8,128)(2,1)}, bf16[256,2048]{1,0:T(8,128)(2,1)S(1)}, u32[]{:S(2)}, u32[]{:S(2)}) collective-permute-start(bf16[256,2048]{1,0:T(8,128)(2,1)} %multiply_convert_fusion.5), channel_id=1, source_target_pairs={{0,8},{8,16},{16,24},{1,9},{9,17},{17,25},{2,10},{10,18},{18,26},{... | collective-permute-start | bytes 3145736 | tf_op jit(solution)/shard_map/ppermute | solution.py:195
  89.7 18.3 %collective-permute-done.9 = bf16[256,2048]{1,0:T(8,128)(2,1)S(1)} collective-permute-done((bf16[256,2048]{1,0:T(8,128)(2,1)}, bf16[256,2048]{1,0:T(8,128)(2,1)S(1)}, u32[]{:S(2)}, u32[]{:S(2)}) %collective-permute-start.9) | collective-permute-done | bytes 1048608 | tf_op jit(solution)/shard_map/ppermute | solution.py:198
  108.1 1.3 collective-permute-start.10
  109.4 0.7 collective-permute-start.8
  110.1 2.6 %fusion.50 = f32[256,512]{1,0:T(8,128)S(1)} fusion(bf16[256,2048]{1,0:T(8,128)(2,1)} %multiply_convert_fusion.5, bf16[2048,512]{1,0:T(8,128)(2,1)} %param.23), kind=kOutput, calls=%fused_computation.122 | convolution fusion | flops 536870912 | bytes 3670016 | tf_op jit(solution)/shard_map/dot_general | solution.py:188
  112.7 2.6 %fusion.51 = f32[256,512]{1,0:T(8,128)S(1)} fusion(bf16[256,2048]{1,0:T(8,128)(2,1)} %multiply_convert_fusion.5, bf16[2048,512]{1,0:T(8,128)(2,1)} %collective-permute-done), kind=kOutput, calls=%fused_computation.123 | convolution fusion | flops 536870912 | bytes 3670016 | tf_op jit(solution)/shard_map/dot_general | solution.py:188
  115.3 2.3 %fusion.56 = f32[256,512]{1,0:T(8,128)S(1)} fusion(bf16[256,2048]{1,0:T(8,128)(2,1)S(1)} %collective-permute-done.9, bf16[2048,512]{1,0:T(8,128)(2,1)} %param.23), kind=kOutput, calls=%fused_computation.128 | convolution fusion | flops 536870912 | bytes 3670016 | tf_op jit(solution)/shard_map/dot_general | solution.py:188
  117.7 2.5 %fusion.57 = f32[256,512]{1,0:T(8,128)S(1)} fusion(bf16[256,2048]{1,0:T(8,128)(2,1)S(1)} %collective-permute-done.9, bf16[2048,512]{1,0:T(8,128)(2,1)} %collective-permute-done), kind=kOutput, calls=%fused_computation.129 | convolution fusion | flops 536870912 | bytes 3670016 | tf_op jit(solution)/shard_map/dot_general | solution.py:188
  120.1 11.1 %collective-permute-done.10 = bf16[256,2048]{1,0:T(8,128)(2,1)S(1)} collective-permute-done((bf16[256,2048]{1,0:T(8,128)(2,1)S(1)}, bf16[256,2048]{1,0:T(8,128)(2,1)S(1)}, u32[]{:S(2)}, u32[]{:S(2)}) %collective-permute-start.10) | collective-permute-done | bytes 1048608 | tf_op jit(solution)/shard_map/ppermute | solution.py:198
  131.4 1.5 collective-permute-start.11
  132.9 2.3 %fusion.52 = f32[256,512]{1,0:T(8,128)S(1)} fusion(bf16[256,2048]{1,0:T(8,128)(2,1)S(1)} %collective-permute-done.7, bf16[2048,512]{1,0:T(8,128)(2,1)} %param.23), kind=kOutput, calls=%fused_computation.124 | convolution fusion | flops 536870912 | bytes 3670016 | tf_op jit(solution)/shard_map/dot_general | solution.py:188
  135.2 2.5 %fusion.53 = f32[256,512]{1,0:T(8,128)S(1)} fusion(bf16[256,2048]{1,0:T(8,128)(2,1)S(1)} %collective-permute-done.7, bf16[2048,512]{1,0:T(8,128)(2,1)} %collective-permute-done), kind=kOutput, calls=%fused_computation.125 | convolution fusion | flops 536870912 | bytes 3670016 | tf_op jit(solution)/shard_map/dot_general | solution.py:188
  137.7 2.6 %fusion.35 = f32[256,512]{1,0:T(8,128)S(1)} fusion(bf16[2048,512]{1,0:T(8,128)(2,1)} %param.23, bf16[256,2048]{1,0:T(8,128)(2,1)S(1)} %collective-permute-done.8, bf16[256,2048]{1,0:T(8,128)(2,1)S(1)} %collective-permute-done.10, pred[]{:T(512)S(6)} %ge.33), kind=kOutput, calls=%fused_computation.75 | convolution fusion | flops 537395200 | bytes 4718593 | tf_op jit(solution)/shard_map/dot_general | solution.py:188
  140.3 2.6 %fusion.34 = f32[256,512]{1,0:T(8,128)S(1)} fusion(bf16[2048,512]{1,0:T(8,128)(2,1)} %collective-permute-done, bf16[256,2048]{1,0:T(8,128)(2,1)S(1)} %collective-permute-done.8, bf16[256,2048]{1,0:T(8,128)(2,1)S(1)} %collective-permute-done.10, pred[]{:T(512)S(6)} %ge.33), kind=kOutput, calls=%fused_computation.74 | convolution fusion | flops 537395200 | bytes 4718593 | tf_op jit(solution)/shard_map/dot_general | solution.py:188
  142.9 11.1 %collective-permute-done.11 = bf16[256,2048]{1,0:T(8,128)(2,1)S(1)} collective-permute-done((bf16[256,2048]{1,0:T(8,128)(2,1)S(1)}, bf16[256,2048]{1,0:T(8,128)(2,1)S(1)}, u32[]{:S(2)}, u32[]{:S(2)}) %collective-permute-start.11) | collective-permute-done | bytes 1048608 | tf_op jit(solution)/shard_map/ppermute | solution.py:202
  154.0 2.3 %fusion.54 = f32[256,512]{1,0:T(8,128)S(1)} fusion(bf16[256,2048]{1,0:T(8,128)(2,1)S(1)} %collective-permute-done.11, bf16[2048,512]{1,0:T(8,128)(2,1)} %param.23), kind=kOutput, calls=%fused_computation.126 | convolution fusion | flops 536870912 | bytes 3670016 | tf_op jit(solution)/shard_map/dot_general | solution.py:188
  156.3 2.5 %fusion.55 = f32[256,512]{1,0:T(8,128)S(1)} fusion(bf16[256,2048]{1,0:T(8,128)(2,1)S(1)} %collective-permute-done.11, bf16[2048,512]{1,0:T(8,128)(2,1)} %collective-permute-done), kind=kOutput, calls=%fused_computation.127 | convolution fusion | flops 536870912 | bytes 3670016 | tf_op jit(solution)/shard_map/dot_general | solution.py:188
  158.8 0.6 select_select_fusion.1
  160.0 1.5 pad_maximum_fusion
  161.5 4.5 %collective-permute-done.12 = f32[2,256,1024]{2,1,0:T(8,128)} collective-permute-done((f32[2,256,1024]{2,1,0:T(8,128)}, f32[2,256,1024]{2,1,0:T(8,128)}, u32[]{:S(2)}, u32[]{:S(2)}) %collective-permute-start.12) | collective-permute-done | bytes 2097184 | tf_op jit(solution)/shard_map/ppermute | solution.py:232
  166.0 2.8 %fusion.23 = bf16[1,256,1024]{2,1,0:T(8,128)(2,1)} fusion(f32[2,256,1024]{2,1,0:T(8,128)} %collective-permute-done.12, f32[1,256,1024]{2,1,0:T(8,128)S(1)} %get-tuple-element.58, f32[1,256,1024]{2,1,0:T(8,128)S(1)} %get-tuple-element.57, f32[1,256,512]{2,1,0:T(8,128)} %bitcast.126, f32[1,256,512]{2,1,0:T(8,128)} %bitcast.123, ...), kind=kLoop, calls=%fused_computation.42 | loop fusion | flops 1835008 | bytes 5767171 | tf_op jit(solution)/shard_map/convert_element_type | solution.py:233
  169.3 13.7 %collective-permute-done.13 = bf16[1,256,1024]{2,1,0:T(8,128)(2,1)S(1)} collective-permute-done((bf16[1,256,1024]{2,1,0:T(8,128)(2,1)}, bf16[1,256,1024]{2,1,0:T(8,128)(2,1)S(1)}, u32[]{:S(2)}, u32[]{:S(2)}) %collective-permute-start.13) | collective-permute-done | bytes 524320 | tf_op jit(solution)/shard_map/ppermute | solution.py:232
  183.0 3.3 %fusion.26 = bf16[256,1024]{1,0:T(8,128)(2,1)S(1)} fusion(f32[2,256,1024]{2,1,0:T(8,128)} %collective-permute-done.12, f32[256,512]{1,0:T(8,128)S(1)} %fusion.51, f32[256,512]{1,0:T(8,128)S(1)} %fusion.50, f32[256,512]{1,0:T(8,128)} %copy-done.7, f32[256,512]{1,0:T(8,128)} %copy-done.6, f32[256,512]{1,0:T(8,128)} %copy-done.2, f32[256,512]{1,0:T(8,128)} %copy-done.1, ...), kind=kLoop, calls=%fused_computation.46 | loop fusion | flops 3670016 | bytes 7340037 | tf_op jit(solution)/shard_map/convert_element_type | solution.py:242
  186.2 4.4 %collective-permute-start.14 = (bf16[256,1024]{1,0:T(8,128)(2,1)S(1)}, bf16[256,1024]{1,0:T(8,128)(2,1)S(1)}, u32[]{:S(2)}, u32[]{:S(2)}) collective-permute-start(bf16[256,1024]{1,0:T(8,128)(2,1)S(1)} %fusion.26), channel_id=1, source_target_pairs={{0,0},{1,8},{2,16},{3,24},{8,1},{9,9},{10,17},{11,25},{16,2},{17,1... | collective-permute-start | bytes 1572872 | tf_op jit(solution)/shard_map/ppermute | solution.py:242
  190.7 22.8 %collective-permute-done.14 = bf16[256,1024]{1,0:T(8,128)(2,1)S(1)} collective-permute-done((bf16[256,1024]{1,0:T(8,128)(2,1)S(1)}, bf16[256,1024]{1,0:T(8,128)(2,1)S(1)}, u32[]{:S(2)}, u32[]{:S(2)}) %collective-permute-start.14) | collective-permute-done | bytes 524320 | tf_op jit(solution)/shard_map/ppermute | solution.py:242
  213.7 0.9 pad_maximum_fusion.5
  (83 shorter events, 5.0 us)
Async XLA Ops:
  0.0 4.9 %copy-start = (f32[256,32]{0,1:T(8,128)S(1)}, f32[256,32]{0,1:T(8,128)}, u32[]{:S(2)}) copy-start(f32[256,32]{0,1:T(8,128)} %param.20) | copy-start | bytes 98308
  0.0 1.4 copy-start.11
  0.0 1.4 copy-start.12
  0.0 7.3 %copy-start.14 = (f32[4,2048]{1,0:T(4,128)S(1)}, f32[4,2048]{1,0:T(4,128)}, u32[]{:S(2)}) copy-start(f32[4,2048]{1,0:T(4,128)} %param.16) | copy-start | bytes 98308
  0.0 7.3 %copy-start.16 = (f32[4,128]{1,0:T(4,128)S(1)}, f32[4,128]{1,0:T(4,128)}, u32[]{:S(2)}) copy-start(f32[4,128]{1,0:T(4,128)} %param.17) | copy-start | bytes 6148
  0.0 7.3 %copy-start.17 = (f32[4,128]{1,0:T(4,128)S(1)}, f32[4,128]{1,0:T(4,128)}, u32[]{:S(2)}) copy-start(f32[4,128]{1,0:T(4,128)} %param.18) | copy-start | bytes 6148
  1.5 6.1 %collective-permute-start.1 = (bf16[3,2304]{1,0:T(4,128)(2,1)S(1)}, bf16[3,2304]{1,0:T(4,128)(2,1)S(1)}, u32[]{:S(2)}, u32[]{:S(2)}) collective-permute-start(bf16[3,2304]{1,0:T(4,128)(2,1)S(1)} %slice.99), channel_id=1, source_target_pairs={{0,4},{4,8},{8,12},{12,16},{16,20},{20,24},{24,28},{1,5},{5,9},{9,... | collective-permute-start | bytes 41480 | tf_op jit(solution)/shard_map/ppermute | solution.py:14
  15.1 14.3 %collective-permute-start.4 = (bf16[1,32,64,128]{3,2,1,0:T(8,128)(2,1)S(1)}, bf16[1,32,64,128]{3,2,1,0:T(8,128)(2,1)S(1)}, u32[]{:S(2)}, u32[]{:S(2)}) collective-permute-start(bf16[1,32,64,128]{3,2,1,0:T(8,128)(2,1)S(1)} %convert_bitcast_fusion), channel_id=1, source_target_pairs={{0,4},{4,8},{8,12},{12,16},{16,20},{20,24},{24,28},{1,5},{5,9},{9,... | collective-permute-start | bytes 1572872 | tf_op jit(solution)/shard_map/ppermute | solution.py:14
  29.4 24.4 %copy-start.10 = (f32[1,256,1,32]{1,2,3,0:T(1,128)S(1)}, f32[1,256,1,32]{1,2,3,0:T(1,128)}, u32[]{:S(2)}) copy-start(f32[1,256,1,32]{1,2,3,0:T(1,128)} %get-tuple-element.59) | copy-start | bytes 98308
  29.6 14.9 %collective-permute-start.5 = (bf16[1,32,64,128]{3,2,1,0:T(8,128)(2,1)S(1)}, bf16[1,32,64,128]{3,2,1,0:T(8,128)(2,1)S(1)}, u32[]{:S(2)}, u32[]{:S(2)}) collective-permute-start(bf16[1,32,64,128]{3,2,1,0:T(8,128)(2,1)S(1)} %fusion.28), channel_id=1, source_target_pairs={{0,8},{4,12},{8,16},{12,20},{16,24},{20,28},{1,9},{5,13},{9,17},{1... | collective-permute-start | bytes 1572872 | tf_op jit(solution)/shard_map/ppermute | solution.py:14
  35.0 5.0 %collective-permute-start.2 = (f32[1,32]{1,0:T(1,128)S(1)}, f32[1,32]{1,0:T(1,128)S(1)}, u32[]{:S(2)}, u32[]{:S(2)}) collective-permute-start(f32[1,32]{1,0:T(1,128)S(1)} %bitcast.144), channel_id=1, source_target_pairs={{0,4},{4,8},{8,12},{12,16},{16,20},{20,24},{24,28},{1,5},{5,9},{9,... | collective-permute-start | bytes 392 | tf_op jit(solution)/shard_map/ppermute | solution.py:14
  37.5 46.3 %collective-permute-start = (bf16[2048,512]{1,0:T(8,128)(2,1)}, bf16[2048,512]{1,0:T(8,128)(2,1)}, u32[]{:S(2)}, u32[]{:S(2)}) collective-permute-start(bf16[2048,512]{1,0:T(8,128)(2,1)} %param.23), channel_id=1, source_target_pairs={{0,4},{4,0},{1,5},{5,1},{2,6},{6,2},{3,7},{7,3},{8,12},{12,8},{9,1... | collective-permute-start | bytes 6291464 | tf_op jit(solution)/shard_map/ppermute | solution.py:180
  44.9 15.1 %collective-permute-start.6 = (bf16[1,32,64,128]{3,2,1,0:T(8,128)(2,1)S(1)}, bf16[1,32,64,128]{3,2,1,0:T(8,128)(2,1)S(1)}, u32[]{:S(2)}, u32[]{:S(2)}) collective-permute-start(bf16[1,32,64,128]{3,2,1,0:T(8,128)(2,1)S(1)} %fusion.22), channel_id=1, source_target_pairs={{0,16},{4,20},{8,24},{12,28},{1,17},{5,21},{9,25},{13,29},{2,18},{... | collective-permute-start | bytes 1572872 | tf_op jit(solution)/shard_map/ppermute | solution.py:14
  50.9 8.9 %collective-permute-start.3 = (f32[1,32]{1,0:T(1,128)S(1)}, f32[1,32]{1,0:T(1,128)S(1)}, u32[]{:S(2)}, u32[]{:S(2)}) collective-permute-start(f32[1,32]{1,0:T(1,128)S(1)} %bitcast_multiply_fusion.1), channel_id=1, source_target_pairs={{0,8},{4,12},{8,16},{12,20},{16,24},{20,28},{1,9},{5,13},{9,17},{1... | collective-permute-start | bytes 392 | tf_op jit(solution)/shard_map/ppermute | solution.py:14
  53.8 6.6 %copy-start.13 = (f32[256,32]{0,1:T(8,128)S(1)}, f32[256,32]{0,1:T(8,128)}, u32[]{:S(2)}) copy-start(f32[256,32]{0,1:T(8,128)} %param.19) | copy-start | bytes 98308
  53.9 6.6 %copy-start.18 = (f32[32]{0:T(128)S(1)}, f32[32]{0:T(128)}, u32[]{:S(2)}) copy-start(f32[32]{0:T(128)} %param.21) | copy-start | bytes 388
  64.2 2.0 copy-start.3
  66.2 0.8 copy-start.15
  83.8 24.3 %collective-permute-start.9 = (bf16[256,2048]{1,0:T(8,128)(2,1)}, bf16[256,2048]{1,0:T(8,128)(2,1)S(1)}, u32[]{:S(2)}, u32[]{:S(2)}) collective-permute-start(bf16[256,2048]{1,0:T(8,128)(2,1)} %multiply_convert_fusion.5), channel_id=1, source_target_pairs={{8,0},{16,8},{24,16},{9,1},{17,9},{25,17},{10,2},{18,10},{26,18},{... | collective-permute-start | bytes 3145736 | tf_op jit(solution)/shard_map/ppermute | solution.py:198
  85.1 24.3 %collective-permute-start.7 = (bf16[256,2048]{1,0:T(8,128)(2,1)}, bf16[256,2048]{1,0:T(8,128)(2,1)S(1)}, u32[]{:S(2)}, u32[]{:S(2)}) collective-permute-start(bf16[256,2048]{1,0:T(8,128)(2,1)} %multiply_convert_fusion.5), channel_id=1, source_target_pairs={{0,8},{8,16},{16,24},{1,9},{9,17},{17,25},{2,10},{10,18},{18,26},{... | collective-permute-start | bytes 3145736 | tf_op jit(solution)/shard_map/ppermute | solution.py:195
  108.1 23.2 %collective-permute-start.10 = (bf16[256,2048]{1,0:T(8,128)(2,1)S(1)}, bf16[256,2048]{1,0:T(8,128)(2,1)S(1)}, u32[]{:S(2)}, u32[]{:S(2)}) collective-permute-start(bf16[256,2048]{1,0:T(8,128)(2,1)S(1)} %collective-permute-done.9), channel_id=1, source_target_pairs={{8,0},{16,8},{9,1},{17,9},{10,2},{18,10},{11,3},{19,11},{12,4},{20... | collective-permute-start | bytes 3145736 | tf_op jit(solution)/shard_map/ppermute | solution.py:198
  109.4 21.9 %collective-permute-start.8 = (bf16[256,2048]{1,0:T(8,128)(2,1)S(1)}, bf16[256,2048]{1,0:T(8,128)(2,1)S(1)}, u32[]{:S(2)}, u32[]{:S(2)}) collective-permute-start(bf16[256,2048]{1,0:T(8,128)(2,1)S(1)} %collective-permute-done.7), channel_id=1, source_target_pairs={{8,16},{16,24},{9,17},{17,25},{10,18},{18,26},{11,19},{19,27},{12,... | collective-permute-start | bytes 3145736 | tf_op jit(solution)/shard_map/ppermute | solution.py:195
  117.6 41.1 %copy-start.4 = (f32[256,512]{1,0:T(8,128)}, f32[256,512]{1,0:T(8,128)S(1)}, u32[]{:S(2)}) copy-start(f32[256,512]{1,0:T(8,128)S(1)} %fusion.56) | copy-start | bytes 1572868
  120.1 38.6 %copy-start.5 = (f32[256,512]{1,0:T(8,128)}, f32[256,512]{1,0:T(8,128)S(1)}, u32[]{:S(2)}) copy-start(f32[256,512]{1,0:T(8,128)S(1)} %fusion.57) | copy-start | bytes 1572868
  131.4 22.6 %collective-permute-start.11 = (bf16[256,2048]{1,0:T(8,128)(2,1)S(1)}, bf16[256,2048]{1,0:T(8,128)(2,1)S(1)}, u32[]{:S(2)}, u32[]{:S(2)}) collective-permute-start(bf16[256,2048]{1,0:T(8,128)(2,1)S(1)} %broadcast_select_fusion.1), channel_id=1, source_target_pairs={{16,24},{8,0},{17,25},{9,1},{18,26},{10,2},{19,27},{11,3},{20,28},... | collective-permute-start | bytes 3145736 | tf_op jit(solution)/shard_map/ppermute | solution.py:202
  135.2 23.6 %copy-start.6 = (f32[256,512]{1,0:T(8,128)}, f32[256,512]{1,0:T(8,128)S(1)}, u32[]{:S(2)}) copy-start(f32[256,512]{1,0:T(8,128)S(1)} %fusion.52) | copy-start | bytes 1572868
  137.7 21.1 %copy-start.7 = (f32[256,512]{1,0:T(8,128)}, f32[256,512]{1,0:T(8,128)S(1)}, u32[]{:S(2)}) copy-start(f32[256,512]{1,0:T(8,128)S(1)} %fusion.53) | copy-start | bytes 1572868
  140.3 19.3 %copy-start.1 = (f32[256,512]{1,0:T(8,128)}, f32[256,512]{1,0:T(8,128)S(1)}, u32[]{:S(2)}) copy-start(f32[256,512]{1,0:T(8,128)S(1)} %fusion.35) | copy-start | bytes 1572868
  142.8 16.7 %copy-start.2 = (f32[256,512]{1,0:T(8,128)}, f32[256,512]{1,0:T(8,128)S(1)}, u32[]{:S(2)}) copy-start(f32[256,512]{1,0:T(8,128)S(1)} %fusion.34) | copy-start | bytes 1572868
  156.2 3.1 %copy-start.8 = (f32[256,512]{1,0:T(8,128)}, f32[256,512]{1,0:T(8,128)S(1)}, u32[]{:S(2)}) copy-start(f32[256,512]{1,0:T(8,128)S(1)} %fusion.54) | copy-start | bytes 1572868
  158.7 0.8 copy-start.9
  161.5 4.5 %collective-permute-start.12 = (f32[2,256,1024]{2,1,0:T(8,128)}, f32[2,256,1024]{2,1,0:T(8,128)}, u32[]{:S(2)}, u32[]{:S(2)}) collective-permute-start(f32[2,256,1024]{2,1,0:T(8,128)} %pad_maximum_fusion), channel_id=1, source_target_pairs={{0,1},{1,0},{2,3},{3,2},{4,5},{5,4},{6,7},{7,6},{8,9},{9,8},{10,11... | collective-permute-start | bytes 6291464 | tf_op jit(solution)/shard_map/ppermute | solution.py:232
  168.8 14.2 %collective-permute-start.13 = (bf16[1,256,1024]{2,1,0:T(8,128)(2,1)}, bf16[1,256,1024]{2,1,0:T(8,128)(2,1)S(1)}, u32[]{:S(2)}, u32[]{:S(2)}) collective-permute-start(bf16[1,256,1024]{2,1,0:T(8,128)(2,1)} %fusion.23), channel_id=1, source_target_pairs={{0,2},{1,3},{2,0},{3,1},{4,6},{5,7},{6,4},{7,5},{8,10},{9,11},{10,... | collective-permute-start | bytes 1572872 | tf_op jit(solution)/shard_map/ppermute | solution.py:232
  186.2 27.2 %collective-permute-start.14 = (bf16[256,1024]{1,0:T(8,128)(2,1)S(1)}, bf16[256,1024]{1,0:T(8,128)(2,1)S(1)}, u32[]{:S(2)}, u32[]{:S(2)}) collective-permute-start(bf16[256,1024]{1,0:T(8,128)(2,1)S(1)} %fusion.26), channel_id=1, source_target_pairs={{0,0},{1,8},{2,16},{3,24},{8,1},{9,9},{10,17},{11,25},{16,2},{17,1... | collective-permute-start | bytes 1572872 | tf_op jit(solution)/shard_map/ppermute | solution.py:242

commit v18 on v11

--- a/solution.py
+++ b/solution.py
@@ -230,7 +230,7 @@
         going = sorted(m for m in held if m & bit)
         sent = jnp.stack([held[m] for m in going])
         got = lax.ppermute(
-            sent if bit == 1 else sent.astype(jnp.bfloat16),
+            sent.astype(jnp.bfloat16),
             "tp",
             [(s, s ^ bit) for s in range(tp_count)],
         )

time: 214 us -> 211 us (0.986)
  no operation moved by 1% of the time
where the time goes in v18:
time: 211 us; the launch traced here: 209 us
  waiting for transfers between devices  116 us (55%)
  starting transfers between devices  40.6 us (19%)
  matrix products  30.4 us (14%)
  other arithmetic  13.3 us (6%)
  local copies, waits for them, and re-layouts  8.18 us (4%)
    ppermute x2, waiting for transfers between devices, on_device(): lax.ppermute(going_left, outer_axis, [(s, s - 1) for s in range(1, tp_cou...  27.2 us
    dot_general x10, matrix products, times_weight(): jnp.dot(rows, piece, preferred_element_type=jnp.float32)  23.8 us
    ppermute x6, starting transfers between devices, shifted(): lax.ppermute(value, axis, [(source, source + steps) for source in range(f...  23.7 us
    ppermute x1, waiting for transfers between devices, on_device(): lax.ppermute(held[0].astype(jnp.bfloat16), (outer_axis, 'tp'), swap)  22.7 us
    ppermute x6, waiting for transfers between devices, shifted(): lax.ppermute(value, axis, [(source, source + steps) for source in range(f...  21.2 us
    ppermute x2, waiting for transfers between devices, on_device(): lax.ppermute(sent.astype(jnp.bfloat16), 'tp', [(s, s ^ bit) for s in rang...  16.1 us
    ppermute x1, waiting for transfers between devices, on_device(): lax.ppermute(out_weight, inner_axis, [(s, (s + d) % inner_count) for s in...  14.9 us
    ppermute x1, waiting for transfers between devices, on_device(): lax.ppermute(jnp.where(outer_at == tp_count - 2, going_right, going_left)...  13.9 us
  transfers between devices with their start and end apart: 15, of which 10 were waited for; matrix products, arithmetic and copies ran while one was open for 15% of the time, Pallas kernels for 0%

profile of v18, /device:TPU:2, one launch (start us, length us, event | category | flops | bytes accessed | tf_op | source)
XLA Modules:
  0.0 209.3 jit_solution(17012745988834256645)
XLA Ops:
  0.0 1.3 constant_dynamic-update-slice_fusion.5
  1.5 3.4 %collective-permute-start.1 = (bf16[3,2304]{1,0:T(4,128)(2,1)S(1)}, bf16[3,2304]{1,0:T(4,128)(2,1)S(1)}, u32[]{:S(2)}, u32[]{:S(2)}) collective-permute-start(bf16[3,2304]{1,0:T(4,128)(2,1)S(1)} %slice.99), channel_id=1, source_target_pairs={{0,4},{4,8},{8,12},{12,16},{16,20},{20,24},{24,28},{1,5},{5,9},{9,... | collective-permute-start | bytes 41480 | tf_op jit(solution)/shard_map/ppermute | solution.py:14
  5.9 0.7 fusion.44
  7.7 1.5 multiply_convert_fusion.3
  9.3 1.6 slice_convert_fusion
  10.9 1.9 copy.27
  12.8 2.2 %fusion.17 = f32[32,64,128]{2,1,0:T(8,128)S(1)} fusion(f32[256,32]{0,1:T(8,128)S(1)} %bitcast.117, f32[256,128]{1,0:T(8,128)S(1)} %slice_convert_fusion.1, f32[32]{0:T(128)S(1)} %get-tuple-element.73, f32[256,32,64]{0,2,1:T(8,128)S(1)} %bitcast.109, f32[256,32]{0,1:T(8,128)} %param.19), kind=kOutput, calls=%fused_computation.31 | convolution fusion | flops 137625600 | bytes 3342464 | tf_op jit(solution)/shard_map/vmap(sgjp,sgjn->gjpn)/dot_general | solution.py:54
  15.1 3.5 %collective-permute-start.4 = (bf16[1,32,64,128]{3,2,1,0:T(8,128)(2,1)S(1)}, bf16[1,32,64,128]{3,2,1,0:T(8,128)(2,1)S(1)}, u32[]{:S(2)}, u32[]{:S(2)}) collective-permute-start(bf16[1,32,64,128]{3,2,1,0:T(8,128)(2,1)S(1)} %convert_bitcast_fusion), channel_id=1, source_target_pairs={{0,4},{4,8},{8,12},{12,16},{16,20},{20,24},{24,28},{1,5},{5,9},{9,... | collective-permute-start | bytes 1572872 | tf_op jit(solution)/shard_map/ppermute | solution.py:14
  18.5 10.9 %collective-permute-done.4 = bf16[1,32,64,128]{3,2,1,0:T(8,128)(2,1)S(1)} collective-permute-done((bf16[1,32,64,128]{3,2,1,0:T(8,128)(2,1)S(1)}, bf16[1,32,64,128]{3,2,1,0:T(8,128)(2,1)S(1)}, u32[]{:S(2)}, u32[]{:S(2)}) %collective-permute-start.4) | collective-permute-done | bytes 524320 | tf_op jit(solution)/shard_map/ppermute | solution.py:14
  29.6 5.4 %collective-permute-start.5 = (bf16[1,32,64,128]{3,2,1,0:T(8,128)(2,1)S(1)}, bf16[1,32,64,128]{3,2,1,0:T(8,128)(2,1)S(1)}, u32[]{:S(2)}, u32[]{:S(2)}) collective-permute-start(bf16[1,32,64,128]{3,2,1,0:T(8,128)(2,1)S(1)} %fusion.23), channel_id=1, source_target_pairs={{0,8},{4,12},{8,16},{12,20},{16,24},{20,28},{1,9},{5,13},{9,17},{1... | collective-permute-start | bytes 1572872 | tf_op jit(solution)/shard_map/ppermute | solution.py:14
  35.0 2.5 %collective-permute-start.2 = (f32[1,32]{1,0:T(1,128)S(1)}, f32[1,32]{1,0:T(1,128)S(1)}, u32[]{:S(2)}, u32[]{:S(2)}) collective-permute-start(f32[1,32]{1,0:T(1,128)S(1)} %bitcast.123), channel_id=1, source_target_pairs={{0,4},{4,8},{8,12},{12,16},{16,20},{20,24},{24,28},{1,5},{5,9},{9,... | collective-permute-start | bytes 392 | tf_op jit(solution)/shard_map/ppermute | solution.py:14
  37.5 2.5 %collective-permute-start = (bf16[2048,512]{1,0:T(8,128)(2,1)}, bf16[2048,512]{1,0:T(8,128)(2,1)}, u32[]{:S(2)}, u32[]{:S(2)}) collective-permute-start(bf16[2048,512]{1,0:T(8,128)(2,1)} %param.23), channel_id=1, source_target_pairs={{0,4},{4,0},{1,5},{5,1},{2,6},{6,2},{3,7},{7,3},{8,12},{12,8},{9,1... | collective-permute-start | bytes 6291464 | tf_op jit(solution)/shard_map/ppermute | solution.py:180
  40.0 4.5 %collective-permute-done.5 = bf16[1,32,64,128]{3,2,1,0:T(8,128)(2,1)S(1)} collective-permute-done((bf16[1,32,64,128]{3,2,1,0:T(8,128)(2,1)S(1)}, bf16[1,32,64,128]{3,2,1,0:T(8,128)(2,1)S(1)}, u32[]{:S(2)}, u32[]{:S(2)}) %collective-permute-start.5) | collective-permute-done | bytes 524320 | tf_op jit(solution)/shard_map/ppermute | solution.py:14
  44.9 6.0 %collective-permute-start.6 = (bf16[1,32,64,128]{3,2,1,0:T(8,128)(2,1)S(1)}, bf16[1,32,64,128]{3,2,1,0:T(8,128)(2,1)S(1)}, u32[]{:S(2)}, u32[]{:S(2)}) collective-permute-start(bf16[1,32,64,128]{3,2,1,0:T(8,128)(2,1)S(1)} %fusion.22), channel_id=1, source_target_pairs={{0,16},{4,20},{8,24},{12,28},{1,17},{5,21},{9,25},{13,29},{2,18},{... | collective-permute-start | bytes 1572872 | tf_op jit(solution)/shard_map/ppermute | solution.py:14
  50.9 3.0 %collective-permute-start.3 = (f32[1,32]{1,0:T(1,128)S(1)}, f32[1,32]{1,0:T(1,128)S(1)}, u32[]{:S(2)}, u32[]{:S(2)}) collective-permute-start(f32[1,32]{1,0:T(1,128)S(1)} %bitcast_multiply_fusion.1), channel_id=1, source_target_pairs={{0,8},{4,12},{8,16},{12,20},{16,24},{20,28},{1,9},{5,13},{9,17},{1... | collective-permute-start | bytes 392 | tf_op jit(solution)/shard_map/ppermute | solution.py:14
  53.9 5.9 %collective-permute-done.3 = f32[1,32]{1,0:T(1,128)S(1)} collective-permute-done((f32[1,32]{1,0:T(1,128)S(1)}, f32[1,32]{1,0:T(1,128)S(1)}, u32[]{:S(2)}, u32[]{:S(2)}) %collective-permute-start.3) | collective-permute-done | bytes 160 | tf_op jit(solution)/shard_map/ppermute | solution.py:14
  60.5 3.7 %fusion.14 = f32[256,1,32,64]{0,3,2,1:T(8,128)} fusion(f32[32,64,256]{2,1,0:T(8,128)S(1)} %fusion.26, f32[256,1,32,64]{0,3,2,1:T(8,128)S(1)} %bitcast.111, f32[32,256]{1,0:T(8,128)S(1)} %bitcast.119, f32[256,256]{1,0:T(8,128)S(1)} %fusion.37, pred[256,256]{1,0:T(8,128)(4,1)S(1)} %iota_compare_fusion.1, f32[32]{0:T(128)S(1)} %copy-done.11, ...), kind=kOutput, calls=%fused_computation.25 | convolution fusion | flops 279969792 | bytes 8814720 | tf_op jit(solution)/shard_map/while/body/eval_jaxpr/gjts,sgjp->tgjp/dot_general | solution.py:46
  64.2 2.0 copy.32
  66.2 0.8 multiply_reduce_fusion
  67.0 1.8 multiply_convert_fusion.5
  68.9 14.9 %collective-permute-done = bf16[2048,512]{1,0:T(8,128)(2,1)} collective-permute-done((bf16[2048,512]{1,0:T(8,128)(2,1)}, bf16[2048,512]{1,0:T(8,128)(2,1)}, u32[]{:S(2)}, u32[]{:S(2)}) %collective-permute-start) | collective-permute-done | bytes 2097184 | tf_op jit(solution)/shard_map/ppermute | solution.py:180
  83.8 1.3 collective-permute-start.9
  85.1 4.6 %collective-permute-start.7 = (bf16[256,2048]{1,0:T(8,128)(2,1)}, bf16[256,2048]{1,0:T(8,128)(2,1)S(1)}, u32[]{:S(2)}, u32[]{:S(2)}) collective-permute-start(bf16[256,2048]{1,0:T(8,128)(2,1)} %multiply_convert_fusion.5), channel_id=1, source_target_pairs={{0,8},{8,16},{16,24},{1,9},{9,17},{17,25},{2,10},{10,18},{18,26},{... | collective-permute-start | bytes 3145736 | tf_op jit(solution)/shard_map/ppermute | solution.py:195
  89.7 2.6 %fusion.46 = f32[256,512]{1,0:T(8,128)S(1)} fusion(bf16[256,2048]{1,0:T(8,128)(2,1)} %multiply_convert_fusion.5, bf16[2048,512]{1,0:T(8,128)(2,1)} %param.23), kind=kOutput, calls=%fused_computation.120 | convolution fusion | flops 536870912 | bytes 3670016 | tf_op jit(solution)/shard_map/dot_general | solution.py:188
  92.4 15.7 %collective-permute-done.9 = bf16[256,2048]{1,0:T(8,128)(2,1)S(1)} collective-permute-done((bf16[256,2048]{1,0:T(8,128)(2,1)}, bf16[256,2048]{1,0:T(8,128)(2,1)S(1)}, u32[]{:S(2)}, u32[]{:S(2)}) %collective-permute-start.9) | collective-permute-done | bytes 1048608 | tf_op jit(solution)/shard_map/ppermute | solution.py:198
  108.1 1.3 collective-permute-start.10
  109.4 0.7 collective-permute-start.8
  110.1 2.6 %fusion.47 = f32[256,512]{1,0:T(8,128)S(1)} fusion(bf16[256,2048]{1,0:T(8,128)(2,1)} %multiply_convert_fusion.5, bf16[2048,512]{1,0:T(8,128)(2,1)} %collective-permute-done), kind=kOutput, calls=%fused_computation.121 | convolution fusion | flops 536870912 | bytes 3670016 | tf_op jit(solution)/shard_map/dot_general | solution.py:188
  112.8 2.3 %convolution_bitcast_fusion.1 = f32[1,256,512]{2,1,0:T(8,128)S(1)} fusion(bf16[256,2048]{1,0:T(8,128)(2,1)S(1)} %collective-permute-done.9, bf16[2048,512]{1,0:T(8,128)(2,1)} %param.23), kind=kOutput, calls=%fused_computation.37 | convolution fusion | flops 536870912 | bytes 3670016 | tf_op jit(solution)/shard_map/dot_general | solution.py:188
  115.1 2.3 %convolution_bitcast_fusion = f32[1,256,512]{2,1,0:T(8,128)S(1)} fusion(bf16[256,2048]{1,0:T(8,128)(2,1)S(1)} %collective-permute-done.9, bf16[2048,512]{1,0:T(8,128)(2,1)} %collective-permute-done), kind=kOutput, calls=%fused_computation.36 | convolution fusion | flops 536870912 | bytes 3670016 | tf_op jit(solution)/shard_map/dot_general | solution.py:188
  117.4 2.3 %convolution_bitcast_fusion.5 = f32[1,256,512]{2,1,0:T(8,128)S(1)} fusion(bf16[256,2048]{1,0:T(8,128)(2,1)S(1)} %collective-permute-done.7, bf16[2048,512]{1,0:T(8,128)(2,1)} %param.23), kind=kOutput, calls=%fused_computation.41 | convolution fusion | flops 536870912 | bytes 3670016 | tf_op jit(solution)/shard_map/dot_general | solution.py:188
  119.7 11.6 %collective-permute-done.10 = bf16[256,2048]{1,0:T(8,128)(2,1)S(1)} collective-permute-done((bf16[256,2048]{1,0:T(8,128)(2,1)S(1)}, bf16[256,2048]{1,0:T(8,128)(2,1)S(1)}, u32[]{:S(2)}, u32[]{:S(2)}) %collective-permute-start.10) | collective-permute-done | bytes 1048608 | tf_op jit(solution)/shard_map/ppermute | solution.py:198
  131.4 1.5 collective-permute-start.11
  132.9 2.3 %convolution_bitcast_fusion.4 = f32[1,256,512]{2,1,0:T(8,128)S(1)} fusion(bf16[256,2048]{1,0:T(8,128)(2,1)S(1)} %collective-permute-done.7, bf16[2048,512]{1,0:T(8,128)(2,1)} %collective-permute-done), kind=kOutput, calls=%fused_computation.40 | convolution fusion | flops 536870912 | bytes 3670016 | tf_op jit(solution)/shard_map/dot_general | solution.py:188
  135.2 2.4 %fusion.31 = f32[256,512]{1,0:T(8,128)S(1)} fusion(bf16[2048,512]{1,0:T(8,128)(2,1)} %param.23, bf16[256,2048]{1,0:T(8,128)(2,1)S(1)} %collective-permute-done.8, bf16[256,2048]{1,0:T(8,128)(2,1)S(1)} %collective-permute-done.10, pred[]{:T(512)S(6)} %ge.33), kind=kOutput, calls=%fused_computation.73 | convolution fusion | flops 537395200 | bytes 4718593 | tf_op jit(solution)/shard_map/dot_general | solution.py:188
  137.6 2.4 %fusion.30 = f32[256,512]{1,0:T(8,128)S(1)} fusion(bf16[2048,512]{1,0:T(8,128)(2,1)} %collective-permute-done, bf16[256,2048]{1,0:T(8,128)(2,1)S(1)} %collective-permute-done.8, bf16[256,2048]{1,0:T(8,128)(2,1)S(1)} %collective-permute-done.10, pred[]{:T(512)S(6)} %ge.33), kind=kOutput, calls=%fused_computation.72 | convolution fusion | flops 537395200 | bytes 4718593 | tf_op jit(solution)/shard_map/dot_general | solution.py:188
  140.0 13.9 %collective-permute-done.11 = bf16[256,2048]{1,0:T(8,128)(2,1)S(1)} collective-permute-done((bf16[256,2048]{1,0:T(8,128)(2,1)S(1)}, bf16[256,2048]{1,0:T(8,128)(2,1)S(1)}, u32[]{:S(2)}, u32[]{:S(2)}) %collective-permute-start.11) | collective-permute-done | bytes 1048608 | tf_op jit(solution)/shard_map/ppermute | solution.py:202
  154.0 2.3 %convolution_bitcast_fusion.3 = f32[1,256,512]{2,1,0:T(8,128)S(1)} fusion(bf16[256,2048]{1,0:T(8,128)(2,1)S(1)} %collective-permute-done.11, bf16[2048,512]{1,0:T(8,128)(2,1)} %param.23), kind=kOutput, calls=%fused_computation.39 | convolution fusion | flops 536870912 | bytes 3670016 | tf_op jit(solution)/shard_map/dot_general | solution.py:188
  156.3 2.3 %convolution_bitcast_fusion.2 = f32[1,256,512]{2,1,0:T(8,128)S(1)} fusion(bf16[256,2048]{1,0:T(8,128)(2,1)S(1)} %collective-permute-done.11, bf16[2048,512]{1,0:T(8,128)(2,1)} %collective-permute-done), kind=kOutput, calls=%fused_computation.38 | convolution fusion | flops 536870912 | bytes 3670016 | tf_op jit(solution)/shard_map/dot_general | solution.py:188
  159.8 1.7 copy-done.1
  161.4 2.7 %collective-permute-done.12 = bf16[2,256,1024]{2,1,0:T(8,128)(2,1)S(1)} collective-permute-done((bf16[2,256,1024]{2,1,0:T(8,128)(2,1)S(1)}, bf16[2,256,1024]{2,1,0:T(8,128)(2,1)S(1)}, u32[]{:S(2)}, u32[]{:S(2)}) %collective-permute-start.12) | collective-permute-done | bytes 1048608 | tf_op jit(solution)/shard_map/ppermute | solution.py:232
  164.1 1.4 add_convert_fusion.1
  165.5 0.6 collective-permute-start.13
  166.1 13.4 %collective-permute-done.13 = bf16[1,256,1024]{2,1,0:T(8,128)(2,1)S(1)} collective-permute-done((bf16[1,256,1024]{2,1,0:T(8,128)(2,1)S(1)}, bf16[1,256,1024]{2,1,0:T(8,128)(2,1)S(1)}, u32[]{:S(2)}, u32[]{:S(2)}) %collective-permute-start.13) | collective-permute-done | bytes 524320 | tf_op jit(solution)/shard_map/ppermute | solution.py:232
  179.5 1.5 fusion.24
  181.0 4.5 %collective-permute-start.14 = (bf16[256,1024]{1,0:T(8,128)(2,1)S(1)}, bf16[256,1024]{1,0:T(8,128)(2,1)S(1)}, u32[]{:S(2)}, u32[]{:S(2)}) collective-permute-start(bf16[256,1024]{1,0:T(8,128)(2,1)S(1)} %fusion.24), channel_id=1, source_target_pairs={{0,0},{1,8},{2,16},{3,24},{8,1},{9,9},{10,17},{11,25},{16,2},{17,1... | collective-permute-start | bytes 1572872 | tf_op jit(solution)/shard_map/ppermute | solution.py:242
  185.5 22.7 %collective-permute-done.14 = bf16[256,1024]{1,0:T(8,128)(2,1)S(1)} collective-permute-done((bf16[256,1024]{1,0:T(8,128)(2,1)S(1)}, bf16[256,1024]{1,0:T(8,128)(2,1)S(1)}, u32[]{:S(2)}, u32[]{:S(2)}) %collective-permute-start.14) | collective-permute-done | bytes 524320 | tf_op jit(solution)/shard_map/ppermute | solution.py:242
  208.5 0.9 pad_maximum_fusion.3
  (72 shorter events, 5.1 us)
Async XLA Ops:
  0.0 4.9 %copy-start = (f32[256,32]{0,1:T(8,128)S(1)}, f32[256,32]{0,1:T(8,128)}, u32[]{:S(2)}) copy-start(f32[256,32]{0,1:T(8,128)} %param.20) | copy-start | bytes 98308
  0.0 1.4 copy-start.4
  0.0 1.4 copy-start.5
  0.0 7.3 %copy-start.7 = (f32[4,2048]{1,0:T(4,128)S(1)}, f32[4,2048]{1,0:T(4,128)}, u32[]{:S(2)}) copy-start(f32[4,2048]{1,0:T(4,128)} %param.16) | copy-start | bytes 98308
  0.0 7.3 %copy-start.9 = (f32[4,128]{1,0:T(4,128)S(1)}, f32[4,128]{1,0:T(4,128)}, u32[]{:S(2)}) copy-start(f32[4,128]{1,0:T(4,128)} %param.17) | copy-start | bytes 6148
  0.0 7.3 %copy-start.10 = (f32[4,128]{1,0:T(4,128)S(1)}, f32[4,128]{1,0:T(4,128)}, u32[]{:S(2)}) copy-start(f32[4,128]{1,0:T(4,128)} %param.18) | copy-start | bytes 6148
  1.5 6.1 %collective-permute-start.1 = (bf16[3,2304]{1,0:T(4,128)(2,1)S(1)}, bf16[3,2304]{1,0:T(4,128)(2,1)S(1)}, u32[]{:S(2)}, u32[]{:S(2)}) collective-permute-start(bf16[3,2304]{1,0:T(4,128)(2,1)S(1)} %slice.99), channel_id=1, source_target_pairs={{0,4},{4,8},{8,12},{12,16},{16,20},{20,24},{24,28},{1,5},{5,9},{9,... | collective-permute-start | bytes 41480 | tf_op jit(solution)/shard_map/ppermute | solution.py:14
  15.1 14.3 %collective-permute-start.4 = (bf16[1,32,64,128]{3,2,1,0:T(8,128)(2,1)S(1)}, bf16[1,32,64,128]{3,2,1,0:T(8,128)(2,1)S(1)}, u32[]{:S(2)}, u32[]{:S(2)}) collective-permute-start(bf16[1,32,64,128]{3,2,1,0:T(8,128)(2,1)S(1)} %convert_bitcast_fusion), channel_id=1, source_target_pairs={{0,4},{4,8},{8,12},{12,16},{16,20},{20,24},{24,28},{1,5},{5,9},{9,... | collective-permute-start | bytes 1572872 | tf_op jit(solution)/shard_map/ppermute | solution.py:14
  29.4 24.4 %copy-start.3 = (f32[1,256,1,32]{1,2,3,0:T(1,128)S(1)}, f32[1,256,1,32]{1,2,3,0:T(1,128)}, u32[]{:S(2)}) copy-start(f32[1,256,1,32]{1,2,3,0:T(1,128)} %get-tuple-element.56) | copy-start | bytes 98308
  29.6 14.9 %collective-permute-start.5 = (bf16[1,32,64,128]{3,2,1,0:T(8,128)(2,1)S(1)}, bf16[1,32,64,128]{3,2,1,0:T(8,128)(2,1)S(1)}, u32[]{:S(2)}, u32[]{:S(2)}) collective-permute-start(bf16[1,32,64,128]{3,2,1,0:T(8,128)(2,1)S(1)} %fusion.23), channel_id=1, source_target_pairs={{0,8},{4,12},{8,16},{12,20},{16,24},{20,28},{1,9},{5,13},{9,17},{1... | collective-permute-start | bytes 1572872 | tf_op jit(solution)/shard_map/ppermute | solution.py:14
  35.0 5.0 %collective-permute-start.2 = (f32[1,32]{1,0:T(1,128)S(1)}, f32[1,32]{1,0:T(1,128)S(1)}, u32[]{:S(2)}, u32[]{:S(2)}) collective-permute-start(f32[1,32]{1,0:T(1,128)S(1)} %bitcast.123), channel_id=1, source_target_pairs={{0,4},{4,8},{8,12},{12,16},{16,20},{20,24},{24,28},{1,5},{5,9},{9,... | collective-permute-start | bytes 392 | tf_op jit(solution)/shard_map/ppermute | solution.py:14
  37.5 46.3 %collective-permute-start = (bf16[2048,512]{1,0:T(8,128)(2,1)}, bf16[2048,512]{1,0:T(8,128)(2,1)}, u32[]{:S(2)}, u32[]{:S(2)}) collective-permute-start(bf16[2048,512]{1,0:T(8,128)(2,1)} %param.23), channel_id=1, source_target_pairs={{0,4},{4,0},{1,5},{5,1},{2,6},{6,2},{3,7},{7,3},{8,12},{12,8},{9,1... | collective-permute-start | bytes 6291464 | tf_op jit(solution)/shard_map/ppermute | solution.py:180
  44.9 15.1 %collective-permute-start.6 = (bf16[1,32,64,128]{3,2,1,0:T(8,128)(2,1)S(1)}, bf16[1,32,64,128]{3,2,1,0:T(8,128)(2,1)S(1)}, u32[]{:S(2)}, u32[]{:S(2)}) collective-permute-start(bf16[1,32,64,128]{3,2,1,0:T(8,128)(2,1)S(1)} %fusion.22), channel_id=1, source_target_pairs={{0,16},{4,20},{8,24},{12,28},{1,17},{5,21},{9,25},{13,29},{2,18},{... | collective-permute-start | bytes 1572872 | tf_op jit(solution)/shard_map/ppermute | solution.py:14
  50.9 8.9 %collective-permute-start.3 = (f32[1,32]{1,0:T(1,128)S(1)}, f32[1,32]{1,0:T(1,128)S(1)}, u32[]{:S(2)}, u32[]{:S(2)}) collective-permute-start(f32[1,32]{1,0:T(1,128)S(1)} %bitcast_multiply_fusion.1), channel_id=1, source_target_pairs={{0,8},{4,12},{8,16},{12,20},{16,24},{20,28},{1,9},{5,13},{9,17},{1... | collective-permute-start | bytes 392 | tf_op jit(solution)/shard_map/ppermute | solution.py:14
  53.9 6.6 %copy-start.6 = (f32[256,32]{0,1:T(8,128)S(1)}, f32[256,32]{0,1:T(8,128)}, u32[]{:S(2)}) copy-start(f32[256,32]{0,1:T(8,128)} %param.19) | copy-start | bytes 98308
  53.9 6.6 %copy-start.11 = (f32[32]{0:T(128)S(1)}, f32[32]{0:T(128)}, u32[]{:S(2)}) copy-start(f32[32]{0:T(128)} %param.21) | copy-start | bytes 388
  64.2 2.0 copy-start.2
  66.2 0.8 copy-start.8
  83.8 24.3 %collective-permute-start.9 = (bf16[256,2048]{1,0:T(8,128)(2,1)}, bf16[256,2048]{1,0:T(8,128)(2,1)S(1)}, u32[]{:S(2)}, u32[]{:S(2)}) collective-permute-start(bf16[256,2048]{1,0:T(8,128)(2,1)} %multiply_convert_fusion.5), channel_id=1, source_target_pairs={{8,0},{16,8},{24,16},{9,1},{17,9},{25,17},{10,2},{18,10},{26,18},{... | collective-permute-start | bytes 3145736 | tf_op jit(solution)/shard_map/ppermute | solution.py:198
  85.1 24.3 %collective-permute-start.7 = (bf16[256,2048]{1,0:T(8,128)(2,1)}, bf16[256,2048]{1,0:T(8,128)(2,1)S(1)}, u32[]{:S(2)}, u32[]{:S(2)}) collective-permute-start(bf16[256,2048]{1,0:T(8,128)(2,1)} %multiply_convert_fusion.5), channel_id=1, source_target_pairs={{0,8},{8,16},{16,24},{1,9},{9,17},{17,25},{2,10},{10,18},{18,26},{... | collective-permute-start | bytes 3145736 | tf_op jit(solution)/shard_map/ppermute | solution.py:195
  108.1 23.2 %collective-permute-start.10 = (bf16[256,2048]{1,0:T(8,128)(2,1)S(1)}, bf16[256,2048]{1,0:T(8,128)(2,1)S(1)}, u32[]{:S(2)}, u32[]{:S(2)}) collective-permute-start(bf16[256,2048]{1,0:T(8,128)(2,1)S(1)} %collective-permute-done.9), channel_id=1, source_target_pairs={{8,0},{16,8},{9,1},{17,9},{10,2},{18,10},{11,3},{19,11},{12,4},{20... | collective-permute-start | bytes 3145736 | tf_op jit(solution)/shard_map/ppermute | solution.py:198
  109.4 21.9 %collective-permute-start.8 = (bf16[256,2048]{1,0:T(8,128)(2,1)S(1)}, bf16[256,2048]{1,0:T(8,128)(2,1)S(1)}, u32[]{:S(2)}, u32[]{:S(2)}) collective-permute-start(bf16[256,2048]{1,0:T(8,128)(2,1)S(1)} %collective-permute-done.7), channel_id=1, source_target_pairs={{8,16},{16,24},{9,17},{17,25},{10,18},{18,26},{11,19},{19,27},{12,... | collective-permute-start | bytes 3145736 | tf_op jit(solution)/shard_map/ppermute | solution.py:195
  131.4 22.6 %collective-permute-start.11 = (bf16[256,2048]{1,0:T(8,128)(2,1)S(1)}, bf16[256,2048]{1,0:T(8,128)(2,1)S(1)}, u32[]{:S(2)}, u32[]{:S(2)}) collective-permute-start(bf16[256,2048]{1,0:T(8,128)(2,1)S(1)} %broadcast_select_fusion.1), channel_id=1, source_target_pairs={{16,24},{8,0},{17,25},{9,1},{18,26},{10,2},{19,27},{11,3},{20,28},... | collective-permute-start | bytes 3145736 | tf_op jit(solution)/shard_map/ppermute | solution.py:202
  159.5 1.9 copy-start.1
  161.4 2.7 %collective-permute-start.12 = (bf16[2,256,1024]{2,1,0:T(8,128)(2,1)S(1)}, bf16[2,256,1024]{2,1,0:T(8,128)(2,1)S(1)}, u32[]{:S(2)}, u32[]{:S(2)}) collective-permute-start(bf16[2,256,1024]{2,1,0:T(8,128)(2,1)S(1)} %pad_maximum_fusion.2), channel_id=1, source_target_pairs={{0,1},{1,0},{2,3},{3,2},{4,5},{5,4},{6,7},{7,6},{8,9},{9,8},{10,11... | collective-permute-start | bytes 3145736 | tf_op jit(solution)/shard_map/ppermute | solution.py:232
  165.5 14.0 %collective-permute-start.13 = (bf16[1,256,1024]{2,1,0:T(8,128)(2,1)S(1)}, bf16[1,256,1024]{2,1,0:T(8,128)(2,1)S(1)}, u32[]{:S(2)}, u32[]{:S(2)}) collective-permute-start(bf16[1,256,1024]{2,1,0:T(8,128)(2,1)S(1)} %add_convert_fusion.1), channel_id=1, source_target_pairs={{0,2},{1,3},{2,0},{3,1},{4,6},{5,7},{6,4},{7,5},{8,10},{9,11},{10,... | collective-permute-start | bytes 1572872 | tf_op jit(solution)/shard_map/ppermute | solution.py:232
  181.0 27.2 %collective-permute-start.14 = (bf16[256,1024]{1,0:T(8,128)(2,1)S(1)}, bf16[256,1024]{1,0:T(8,128)(2,1)S(1)}, u32[]{:S(2)}, u32[]{:S(2)}) collective-permute-start(bf16[256,1024]{1,0:T(8,128)(2,1)S(1)} %fusion.24), channel_id=1, source_target_pairs={{0,0},{1,8},{2,16},{3,24},{8,1},{9,9},{10,17},{11,25},{16,2},{17,1... | collective-permute-start | bytes 1572872 | tf_op jit(solution)/shard_map/ppermute | solution.py:242

commit v19 on v18

--- a/solution.py
+++ b/solution.py
@@ -183,11 +183,10 @@
         for d in range(1, inner_count)
     ]
     weight_pieces, hidden = lax.optimization_barrier((weight_pieces, hidden))
+    weight_cat = jnp.concatenate(weight_pieces, axis=1)
+
     def times_weight(rows):
-        return jnp.concatenate(
-            [jnp.dot(rows, piece, preferred_element_type=jnp.float32) for piece in weight_pieces],
-            axis=1,
-        )
+        return jnp.dot(rows, weight_cat, preferred_element_type=jnp.float32)
 
     from_left, from_right = {}, {}
     going_right = going_left = hidden

time: 211 us -> 213 us (level)
  matrix products: 30.4 us -> 14.2 us
  waiting for transfers between devices: 116 us -> 130 us
  local copies, waits for them, and re-layouts: 8.18 us -> 14 us
    dot_general x10 -> x5, matrix products: 23.8 us -> 7.66 us  [times_weight(): return jnp.dot(rows, weight_cat, preferred_element_type=jnp.float32)]
    ppermute x2, waiting for transfers between devices: 27.2 us -> 36.4 us  [on_device(): lax.ppermute(going_left, outer_axis, [(s, s - 1) for s in range(1, tp_cou...]
    ppermute x1, waiting for transfers between devices: 13.9 us -> 17.1 us  [on_device(): lax.ppermute(jnp.where(outer_at == tp_count - 2, going_right, going_left)...]
    unnamed x31 -> x32, local copies, waits for them, and re-layouts: 3.08 us -> 6.12 us
  transfers between devices with their start and end apart: 15 -> 15, of which waited for: 10 -> 10; matrix products, arithmetic and copies ran while one was open for 15% -> 8% of each run, Pallas kernels for 0% -> 0%
where the time goes in v19:
time: 213 us; the launch traced here: 212 us
  waiting for transfers between devices  130 us (61%)
  starting transfers between devices  41.1 us (19%)
  matrix products  14.2 us (7%)
  local copies, waits for them, and re-layouts  14 us (7%)
  other arithmetic  11.8 us (6%)
    ppermute x2, waiting for transfers between devices, on_device(): lax.ppermute(going_left, outer_axis, [(s, s - 1) for s in range(1, tp_cou...  36.4 us
    ppermute x6, starting transfers between devices, shifted(): lax.ppermute(value, axis, [(source, source + steps) for source in range(f...  23.7 us
    ppermute x1, waiting for transfers between devices, on_device(): lax.ppermute(held[0].astype(jnp.bfloat16), (outer_axis, 'tp'), swap)  23.3 us
    ppermute x6, waiting for transfers between devices, shifted(): lax.ppermute(value, axis, [(source, source + steps) for source in range(f...  21.2 us
    ppermute x1, waiting for transfers between devices, on_device(): lax.ppermute(jnp.where(outer_at == tp_count - 2, going_right, going_left)...  17.1 us
    ppermute x2, waiting for transfers between devices, on_device(): lax.ppermute(sent.astype(jnp.bfloat16), 'tp', [(s, s ^ bit) for s in rang...  16.1 us
    ppermute x1, waiting for transfers between devices, on_device(): lax.ppermute(out_weight, inner_axis, [(s, (s + d) % inner_count) for s in...  15.9 us
    dot_general x5, matrix products, times_weight(): return jnp.dot(rows, weight_cat, preferred_element_type=jnp.float32)  7.66 us
  transfers between devices with their start and end apart: 15, of which 10 were waited for; matrix products, arithmetic and copies ran while one was open for 8% of the time, Pallas kernels for 0%

profile of v19, /device:TPU:2, one launch (start us, length us, event | category | flops | bytes accessed | tf_op | source)
XLA Modules:
  0.0 211.9 jit_solution(15949543934727389814)
XLA Ops:
  0.0 1.3 constant_dynamic-update-slice_fusion.5
  1.4 0.9 constant_dynamic-update-slice_fusion.4
  2.2 0.9 constant_dynamic-update-slice_fusion.3
  3.1 3.4 %collective-permute-start.1 = (bf16[3,2304]{1,0:T(4,128)(2,1)S(1)}, bf16[3,2304]{1,0:T(4,128)(2,1)S(1)}, u32[]{:S(2)}, u32[]{:S(2)}) collective-permute-start(bf16[3,2304]{1,0:T(4,128)(2,1)S(1)} %slice.99), channel_id=1, source_target_pairs={{0,4},{4,8},{8,12},{12,16},{16,20},{20,24},{24,28},{1,5},{5,9},{9,... | collective-permute-start | bytes 41480 | tf_op jit(solution)/shard_map/ppermute | solution.py:14
  6.6 0.6 reduce-window.6
  7.6 0.7 fusion.46
  9.4 1.5 multiply_convert_fusion.3
  10.9 1.6 slice_convert_fusion
  12.5 1.9 copy.27
  14.4 2.2 %fusion.17 = f32[32,64,128]{2,1,0:T(8,128)S(1)} fusion(f32[256,32]{0,1:T(8,128)S(1)} %bitcast.100, f32[256,128]{1,0:T(8,128)S(1)} %slice_convert_fusion.1, f32[32]{0:T(128)S(1)} %get-tuple-element.71, f32[256,32,64]{0,2,1:T(8,128)S(1)} %bitcast.92, f32[256,32]{0,1:T(8,128)} %param.19), kind=kOutput, calls=%fused_computation.31 | convolution fusion | flops 137625600 | bytes 3342464 | tf_op jit(solution)/shard_map/vmap(sgjp,sgjn->gjpn)/dot_general | solution.py:54
  16.7 3.5 %collective-permute-start.4 = (bf16[1,32,64,128]{3,2,1,0:T(8,128)(2,1)S(1)}, bf16[1,32,64,128]{3,2,1,0:T(8,128)(2,1)S(1)}, u32[]{:S(2)}, u32[]{:S(2)}) collective-permute-start(bf16[1,32,64,128]{3,2,1,0:T(8,128)(2,1)S(1)} %convert_bitcast_fusion), channel_id=1, source_target_pairs={{0,4},{4,8},{8,12},{12,16},{16,20},{20,24},{24,28},{1,5},{5,9},{9,... | collective-permute-start | bytes 1572872 | tf_op jit(solution)/shard_map/ppermute | solution.py:14
  20.2 10.8 %collective-permute-done.4 = bf16[1,32,64,128]{3,2,1,0:T(8,128)(2,1)S(1)} collective-permute-done((bf16[1,32,64,128]{3,2,1,0:T(8,128)(2,1)S(1)}, bf16[1,32,64,128]{3,2,1,0:T(8,128)(2,1)S(1)}, u32[]{:S(2)}, u32[]{:S(2)}) %collective-permute-start.4) | collective-permute-done | bytes 524320 | tf_op jit(solution)/shard_map/ppermute | solution.py:14
  31.2 5.4 %collective-permute-start.5 = (bf16[1,32,64,128]{3,2,1,0:T(8,128)(2,1)S(1)}, bf16[1,32,64,128]{3,2,1,0:T(8,128)(2,1)S(1)}, u32[]{:S(2)}, u32[]{:S(2)}) collective-permute-start(bf16[1,32,64,128]{3,2,1,0:T(8,128)(2,1)S(1)} %fusion.27), channel_id=1, source_target_pairs={{0,8},{4,12},{8,16},{12,20},{16,24},{20,28},{1,9},{5,13},{9,17},{1... | collective-permute-start | bytes 1572872 | tf_op jit(solution)/shard_map/ppermute | solution.py:14
  36.6 2.5 %collective-permute-start.2 = (f32[1,32]{1,0:T(1,128)S(1)}, f32[1,32]{1,0:T(1,128)S(1)}, u32[]{:S(2)}, u32[]{:S(2)}) collective-permute-start(f32[1,32]{1,0:T(1,128)S(1)} %bitcast.106), channel_id=1, source_target_pairs={{0,4},{4,8},{8,12},{12,16},{16,20},{20,24},{24,28},{1,5},{5,9},{9,... | collective-permute-start | bytes 392 | tf_op jit(solution)/shard_map/ppermute | solution.py:14
  39.2 2.5 %collective-permute-start = (bf16[2048,512]{1,0:T(8,128)(2,1)}, bf16[2048,512]{1,0:T(8,128)(2,1)}, u32[]{:S(2)}, u32[]{:S(2)}) collective-permute-start(bf16[2048,512]{1,0:T(8,128)(2,1)} %param.23), channel_id=1, source_target_pairs={{0,4},{4,0},{1,5},{5,1},{2,6},{6,2},{3,7},{7,3},{8,12},{12,8},{9,1... | collective-permute-start | bytes 6291464 | tf_op jit(solution)/shard_map/ppermute | solution.py:180
  41.7 4.5 %collective-permute-done.5 = bf16[1,32,64,128]{3,2,1,0:T(8,128)(2,1)S(1)} collective-permute-done((bf16[1,32,64,128]{3,2,1,0:T(8,128)(2,1)S(1)}, bf16[1,32,64,128]{3,2,1,0:T(8,128)(2,1)S(1)}, u32[]{:S(2)}, u32[]{:S(2)}) %collective-permute-start.5) | collective-permute-done | bytes 524320 | tf_op jit(solution)/shard_map/ppermute | solution.py:14
  46.5 6.0 %collective-permute-start.6 = (bf16[1,32,64,128]{3,2,1,0:T(8,128)(2,1)S(1)}, bf16[1,32,64,128]{3,2,1,0:T(8,128)(2,1)S(1)}, u32[]{:S(2)}, u32[]{:S(2)}) collective-permute-start(bf16[1,32,64,128]{3,2,1,0:T(8,128)(2,1)S(1)} %fusion.24), channel_id=1, source_target_pairs={{0,16},{4,20},{8,24},{12,28},{1,17},{5,21},{9,25},{13,29},{2,18},{... | collective-permute-start | bytes 1572872 | tf_op jit(solution)/shard_map/ppermute | solution.py:14
  52.5 3.0 %collective-permute-start.3 = (f32[1,32]{1,0:T(1,128)S(1)}, f32[1,32]{1,0:T(1,128)S(1)}, u32[]{:S(2)}, u32[]{:S(2)}) collective-permute-start(f32[1,32]{1,0:T(1,128)S(1)} %bitcast_multiply_fusion.1), channel_id=1, source_target_pairs={{0,8},{4,12},{8,16},{12,20},{16,24},{20,28},{1,9},{5,13},{9,17},{1... | collective-permute-start | bytes 392 | tf_op jit(solution)/shard_map/ppermute | solution.py:14
  55.5 5.9 %collective-permute-done.3 = f32[1,32]{1,0:T(1,128)S(1)} collective-permute-done((f32[1,32]{1,0:T(1,128)S(1)}, f32[1,32]{1,0:T(1,128)S(1)}, u32[]{:S(2)}, u32[]{:S(2)}) %collective-permute-start.3) | collective-permute-done | bytes 160 | tf_op jit(solution)/shard_map/ppermute | solution.py:14
  62.1 3.7 %fusion.14 = f32[256,1,32,64]{0,3,2,1:T(8,128)} fusion(f32[32,64,256]{2,1,0:T(8,128)S(1)} %fusion.30, f32[256,1,32,64]{0,3,2,1:T(8,128)S(1)} %bitcast.94, f32[32,256]{1,0:T(8,128)S(1)} %bitcast.102, f32[256,256]{1,0:T(8,128)S(1)} %fusion.39, pred[256,256]{1,0:T(8,128)(4,1)S(1)} %iota_compare_fusion.1, f32[32]{0:T(128)S(1)} %copy-done.11, ...), kind=kOutput, calls=%fused_computation.25 | convolution fusion | flops 279969792 | bytes 8814720 | tf_op jit(solution)/shard_map/while/body/eval_jaxpr/gjts,sgjp->tgjp/dot_general | solution.py:46
  65.9 2.0 copy.32
  67.9 0.8 multiply_reduce_fusion
  68.7 0.8 multiply_convert_fusion.5
  69.5 15.9 %collective-permute-done = bf16[2048,512]{1,0:T(8,128)(2,1)} collective-permute-done((bf16[2048,512]{1,0:T(8,128)(2,1)}, bf16[2048,512]{1,0:T(8,128)(2,1)}, u32[]{:S(2)}, u32[]{:S(2)}) %collective-permute-start) | collective-permute-done | bytes 2097184 | tf_op jit(solution)/shard_map/ppermute | solution.py:180
  85.4 1.3 collective-permute-start.9
  86.7 5.5 %collective-permute-start.7 = (bf16[256,2048]{1,0:T(8,128)(2,1)S(1)}, bf16[256,2048]{1,0:T(8,128)(2,1)}, u32[]{:S(2)}, u32[]{:S(2)}) collective-permute-start(bf16[256,2048]{1,0:T(8,128)(2,1)S(1)} %multiply_convert_fusion.5), channel_id=1, source_target_pairs={{0,8},{8,16},{16,24},{1,9},{9,17},{17,25},{2,10},{10,18},{18,26},{... | collective-permute-start | bytes 3145736 | tf_op jit(solution)/shard_map/ppermute | solution.py:194
  92.3 17.2 %collective-permute-done.9 = bf16[256,2048]{1,0:T(8,128)(2,1)S(1)} collective-permute-done((bf16[256,2048]{1,0:T(8,128)(2,1)S(1)}, bf16[256,2048]{1,0:T(8,128)(2,1)S(1)}, u32[]{:S(2)}, u32[]{:S(2)}) %collective-permute-start.9) | collective-permute-done | bytes 1048608 | tf_op jit(solution)/shard_map/ppermute | solution.py:197
  109.5 1.3 collective-permute-start.10
  110.8 0.7 collective-permute-start.8
  111.6 1.9 constant_dynamic-update-slice_fusion.7
  113.5 19.2 %collective-permute-done.10 = bf16[256,2048]{1,0:T(8,128)(2,1)S(1)} collective-permute-done((bf16[256,2048]{1,0:T(8,128)(2,1)S(1)}, bf16[256,2048]{1,0:T(8,128)(2,1)S(1)}, u32[]{:S(2)}, u32[]{:S(2)}) %collective-permute-start.10) | collective-permute-done | bytes 1048608 | tf_op jit(solution)/shard_map/ppermute | solution.py:197
  132.8 1.6 collective-permute-start.11
  134.4 1.9 constant_dynamic-update-slice_fusion.6
  136.4 1.3 convolution_bitcast_fusion.1
  137.7 1.3 convolution_bitcast_fusion
  139.0 17.1 %collective-permute-done.11 = bf16[256,2048]{1,0:T(8,128)(2,1)S(1)} collective-permute-done((bf16[256,2048]{1,0:T(8,128)(2,1)S(1)}, bf16[256,2048]{1,0:T(8,128)(2,1)S(1)}, u32[]{:S(2)}, u32[]{:S(2)}) %collective-permute-start.11) | collective-permute-done | bytes 1048608 | tf_op jit(solution)/shard_map/ppermute | solution.py:201
  156.0 1.3 fusion.48
  157.3 2.5 %fusion.19 = f32[1,256,1024]{2,1,0:T(8,128)S(1)} fusion(f32[256,1024]{1,0:T(8,128)S(1)} %fusion.48, bf16[256,2048]{1,0:T(8,128)(2,1)} %collective-permute-done.7, bf16[2048,1024]{1,0:T(8,128)(2,1)S(1)} %constant_dynamic-update-slice_fusion.6, pred[]{:T(512)S(6)} %ge.32), kind=kOutput, calls=%fused_computation.41 | convolution fusion | flops 1074003968 | bytes 7340033 | tf_op jit(solution)/shard_map/dot_general | solution.py:189
  159.9 1.3 fusion.18
  161.2 0.6 pad_maximum_fusion
  161.8 1.9 copy-done.1
  164.1 2.6 %collective-permute-done.12 = bf16[2,256,1024]{2,1,0:T(8,128)(2,1)S(1)} collective-permute-done((bf16[2,256,1024]{2,1,0:T(8,128)(2,1)S(1)}, bf16[2,256,1024]{2,1,0:T(8,128)(2,1)S(1)}, u32[]{:S(2)}, u32[]{:S(2)}) %collective-permute-start.12) | collective-permute-done | bytes 1048608 | tf_op jit(solution)/shard_map/ppermute | solution.py:231
  166.7 1.4 add_convert_fusion.1
  168.6 13.5 %collective-permute-done.13 = bf16[1,256,1024]{2,1,0:T(8,128)(2,1)S(1)} collective-permute-done((bf16[1,256,1024]{2,1,0:T(8,128)(2,1)S(1)}, bf16[1,256,1024]{2,1,0:T(8,128)(2,1)S(1)}, u32[]{:S(2)}, u32[]{:S(2)}) %collective-permute-start.13) | collective-permute-done | bytes 524320 | tf_op jit(solution)/shard_map/ppermute | solution.py:231
  182.1 1.5 fusion.28
  183.5 3.9 %collective-permute-start.14 = (bf16[256,1024]{1,0:T(8,128)(2,1)S(1)}, bf16[256,1024]{1,0:T(8,128)(2,1)S(1)}, u32[]{:S(2)}, u32[]{:S(2)}) collective-permute-start(bf16[256,1024]{1,0:T(8,128)(2,1)S(1)} %fusion.28), channel_id=1, source_target_pairs={{0,0},{1,8},{2,16},{3,24},{8,1},{9,9},{10,17},{11,25},{16,2},{17,1... | collective-permute-start | bytes 1572872 | tf_op jit(solution)/shard_map/ppermute | solution.py:241
  187.4 23.3 %collective-permute-done.14 = bf16[256,1024]{1,0:T(8,128)(2,1)S(1)} collective-permute-done((bf16[256,1024]{1,0:T(8,128)(2,1)S(1)}, bf16[256,1024]{1,0:T(8,128)(2,1)S(1)}, u32[]{:S(2)}, u32[]{:S(2)}) %collective-permute-start.14) | collective-permute-done | bytes 524320 | tf_op jit(solution)/shard_map/ppermute | solution.py:241
  211.0 0.9 pad_maximum_fusion.2
  (66 shorter events, 4.1 us)
Async XLA Ops:
  0.0 6.5 %copy-start = (f32[256,32]{0,1:T(8,128)S(1)}, f32[256,32]{0,1:T(8,128)}, u32[]{:S(2)}) copy-start(f32[256,32]{0,1:T(8,128)} %param.20) | copy-start | bytes 98308
  0.0 9.0 %copy-start.7 = (f32[4,2048]{1,0:T(4,128)S(1)}, f32[4,2048]{1,0:T(4,128)}, u32[]{:S(2)}) copy-start(f32[4,2048]{1,0:T(4,128)} %param.16) | copy-start | bytes 98308
  0.0 9.0 %copy-start.9 = (f32[4,128]{1,0:T(4,128)S(1)}, f32[4,128]{1,0:T(4,128)}, u32[]{:S(2)}) copy-start(f32[4,128]{1,0:T(4,128)} %param.17) | copy-start | bytes 6148
  0.0 9.0 %copy-start.10 = (f32[4,128]{1,0:T(4,128)S(1)}, f32[4,128]{1,0:T(4,128)}, u32[]{:S(2)}) copy-start(f32[4,128]{1,0:T(4,128)} %param.18) | copy-start | bytes 6148
  3.1 6.1 %collective-permute-start.1 = (bf16[3,2304]{1,0:T(4,128)(2,1)S(1)}, bf16[3,2304]{1,0:T(4,128)(2,1)S(1)}, u32[]{:S(2)}, u32[]{:S(2)}) collective-permute-start(bf16[3,2304]{1,0:T(4,128)(2,1)S(1)} %slice.99), channel_id=1, source_target_pairs={{0,4},{4,8},{8,12},{12,16},{16,20},{20,24},{24,28},{1,5},{5,9},{9,... | collective-permute-start | bytes 41480 | tf_op jit(solution)/shard_map/ppermute | solution.py:14
  16.7 14.3 %collective-permute-start.4 = (bf16[1,32,64,128]{3,2,1,0:T(8,128)(2,1)S(1)}, bf16[1,32,64,128]{3,2,1,0:T(8,128)(2,1)S(1)}, u32[]{:S(2)}, u32[]{:S(2)}) collective-permute-start(bf16[1,32,64,128]{3,2,1,0:T(8,128)(2,1)S(1)} %convert_bitcast_fusion), channel_id=1, source_target_pairs={{0,4},{4,8},{8,12},{12,16},{16,20},{20,24},{24,28},{1,5},{5,9},{9,... | collective-permute-start | bytes 1572872 | tf_op jit(solution)/shard_map/ppermute | solution.py:14
  31.0 24.5 %copy-start.5 = (f32[1,256,1,32]{1,2,3,0:T(1,128)S(1)}, f32[1,256,1,32]{1,2,3,0:T(1,128)}, u32[]{:S(2)}) copy-start(f32[1,256,1,32]{1,2,3,0:T(1,128)} %get-tuple-element.56) | copy-start | bytes 98308
  31.2 14.9 %collective-permute-start.5 = (bf16[1,32,64,128]{3,2,1,0:T(8,128)(2,1)S(1)}, bf16[1,32,64,128]{3,2,1,0:T(8,128)(2,1)S(1)}, u32[]{:S(2)}, u32[]{:S(2)}) collective-permute-start(bf16[1,32,64,128]{3,2,1,0:T(8,128)(2,1)S(1)} %fusion.27), channel_id=1, source_target_pairs={{0,8},{4,12},{8,16},{12,20},{16,24},{20,28},{1,9},{5,13},{9,17},{1... | collective-permute-start | bytes 1572872 | tf_op jit(solution)/shard_map/ppermute | solution.py:14
  36.6 5.0 %collective-permute-start.2 = (f32[1,32]{1,0:T(1,128)S(1)}, f32[1,32]{1,0:T(1,128)S(1)}, u32[]{:S(2)}, u32[]{:S(2)}) collective-permute-start(f32[1,32]{1,0:T(1,128)S(1)} %bitcast.106), channel_id=1, source_target_pairs={{0,4},{4,8},{8,12},{12,16},{16,20},{20,24},{24,28},{1,5},{5,9},{9,... | collective-permute-start | bytes 392 | tf_op jit(solution)/shard_map/ppermute | solution.py:14
  39.2 46.3 %collective-permute-start = (bf16[2048,512]{1,0:T(8,128)(2,1)}, bf16[2048,512]{1,0:T(8,128)(2,1)}, u32[]{:S(2)}, u32[]{:S(2)}) collective-permute-start(bf16[2048,512]{1,0:T(8,128)(2,1)} %param.23), channel_id=1, source_target_pairs={{0,4},{4,0},{1,5},{5,1},{2,6},{6,2},{3,7},{7,3},{8,12},{12,8},{9,1... | collective-permute-start | bytes 6291464 | tf_op jit(solution)/shard_map/ppermute | solution.py:180
  46.5 15.6 %copy-start.6 = (f32[256,32]{0,1:T(8,128)S(1)}, f32[256,32]{0,1:T(8,128)}, u32[]{:S(2)}) copy-start(f32[256,32]{0,1:T(8,128)} %param.19) | copy-start | bytes 98308
  46.5 15.6 %copy-start.11 = (f32[32]{0:T(128)S(1)}, f32[32]{0:T(128)}, u32[]{:S(2)}) copy-start(f32[32]{0:T(128)} %param.21) | copy-start | bytes 388
  46.5 15.1 %collective-permute-start.6 = (bf16[1,32,64,128]{3,2,1,0:T(8,128)(2,1)S(1)}, bf16[1,32,64,128]{3,2,1,0:T(8,128)(2,1)S(1)}, u32[]{:S(2)}, u32[]{:S(2)}) collective-permute-start(bf16[1,32,64,128]{3,2,1,0:T(8,128)(2,1)S(1)} %fusion.24), channel_id=1, source_target_pairs={{0,16},{4,20},{8,24},{12,28},{1,17},{5,21},{9,25},{13,29},{2,18},{... | collective-permute-start | bytes 1572872 | tf_op jit(solution)/shard_map/ppermute | solution.py:14
  52.5 8.9 %collective-permute-start.3 = (f32[1,32]{1,0:T(1,128)S(1)}, f32[1,32]{1,0:T(1,128)S(1)}, u32[]{:S(2)}, u32[]{:S(2)}) collective-permute-start(f32[1,32]{1,0:T(1,128)S(1)} %bitcast_multiply_fusion.1), channel_id=1, source_target_pairs={{0,8},{4,12},{8,16},{12,20},{16,24},{20,28},{1,9},{5,13},{9,17},{1... | collective-permute-start | bytes 392 | tf_op jit(solution)/shard_map/ppermute | solution.py:14
  65.9 2.0 copy-start.2
  67.9 0.8 copy-start.8
  69.5 17.2 %copy-start.3 = (bf16[256,2048]{1,0:T(8,128)(2,1)}, bf16[256,2048]{1,0:T(8,128)(2,1)S(1)}, u32[]{:S(2)}) copy-start(bf16[256,2048]{1,0:T(8,128)(2,1)S(1)} %multiply_convert_fusion.5) | copy-start | bytes 3145732
  85.4 24.1 %collective-permute-start.9 = (bf16[256,2048]{1,0:T(8,128)(2,1)S(1)}, bf16[256,2048]{1,0:T(8,128)(2,1)S(1)}, u32[]{:S(2)}, u32[]{:S(2)}) collective-permute-start(bf16[256,2048]{1,0:T(8,128)(2,1)S(1)} %multiply_convert_fusion.5), channel_id=1, source_target_pairs={{8,0},{16,8},{24,16},{9,1},{17,9},{25,17},{10,2},{18,10},{26,18},{... | collective-permute-start | bytes 3145736 | tf_op jit(solution)/shard_map/ppermute | solution.py:197
  86.7 24.1 %collective-permute-start.7 = (bf16[256,2048]{1,0:T(8,128)(2,1)S(1)}, bf16[256,2048]{1,0:T(8,128)(2,1)}, u32[]{:S(2)}, u32[]{:S(2)}) collective-permute-start(bf16[256,2048]{1,0:T(8,128)(2,1)S(1)} %multiply_convert_fusion.5), channel_id=1, source_target_pairs={{0,8},{8,16},{16,24},{1,9},{9,17},{17,25},{2,10},{10,18},{18,26},{... | collective-permute-start | bytes 3145736 | tf_op jit(solution)/shard_map/ppermute | solution.py:194
  109.5 23.2 %collective-permute-start.10 = (bf16[256,2048]{1,0:T(8,128)(2,1)S(1)}, bf16[256,2048]{1,0:T(8,128)(2,1)S(1)}, u32[]{:S(2)}, u32[]{:S(2)}) collective-permute-start(bf16[256,2048]{1,0:T(8,128)(2,1)S(1)} %collective-permute-done.9), channel_id=1, source_target_pairs={{8,0},{16,8},{9,1},{17,9},{10,2},{18,10},{11,3},{19,11},{12,4},{20... | collective-permute-start | bytes 3145736 | tf_op jit(solution)/shard_map/ppermute | solution.py:197
  110.8 21.9 %collective-permute-start.8 = (bf16[256,2048]{1,0:T(8,128)(2,1)}, bf16[256,2048]{1,0:T(8,128)(2,1)S(1)}, u32[]{:S(2)}, u32[]{:S(2)}) collective-permute-start(bf16[256,2048]{1,0:T(8,128)(2,1)} %collective-permute-done.7), channel_id=1, source_target_pairs={{8,16},{16,24},{9,17},{17,25},{10,18},{18,26},{11,19},{19,27},{12,... | collective-permute-start | bytes 3145736 | tf_op jit(solution)/shard_map/ppermute | solution.py:194
  132.8 3.5 %copy-start.4 = (bf16[256,2048]{1,0:T(8,128)(2,1)S(1)}, bf16[256,2048]{1,0:T(8,128)(2,1)}, u32[]{:S(2)}) copy-start(bf16[256,2048]{1,0:T(8,128)(2,1)} %copy-done.3) | copy-start | bytes 3145732
  132.8 23.2 %collective-permute-start.11 = (bf16[256,2048]{1,0:T(8,128)(2,1)S(1)}, bf16[256,2048]{1,0:T(8,128)(2,1)S(1)}, u32[]{:S(2)}, u32[]{:S(2)}) collective-permute-start(bf16[256,2048]{1,0:T(8,128)(2,1)S(1)} %broadcast_select_fusion), channel_id=1, source_target_pairs={{16,24},{8,0},{17,25},{9,1},{18,26},{10,2},{19,27},{11,3},{20,28},... | collective-permute-start | bytes 3145736 | tf_op jit(solution)/shard_map/ppermute | solution.py:201
  161.7 1.9 copy-start.1
  164.0 2.7 %collective-permute-start.12 = (bf16[2,256,1024]{2,1,0:T(8,128)(2,1)S(1)}, bf16[2,256,1024]{2,1,0:T(8,128)(2,1)S(1)}, u32[]{:S(2)}, u32[]{:S(2)}) collective-permute-start(bf16[2,256,1024]{2,1,0:T(8,128)(2,1)S(1)} %pad_maximum_fusion.1), channel_id=1, source_target_pairs={{0,1},{1,0},{2,3},{3,2},{4,5},{5,4},{6,7},{7,6},{8,9},{9,8},{10,11... | collective-permute-start | bytes 3145736 | tf_op jit(solution)/shard_map/ppermute | solution.py:231
  168.1 14.0 %collective-permute-start.13 = (bf16[1,256,1024]{2,1,0:T(8,128)(2,1)S(1)}, bf16[1,256,1024]{2,1,0:T(8,128)(2,1)S(1)}, u32[]{:S(2)}, u32[]{:S(2)}) collective-permute-start(bf16[1,256,1024]{2,1,0:T(8,128)(2,1)S(1)} %add_convert_fusion.1), channel_id=1, source_target_pairs={{0,2},{1,3},{2,0},{3,1},{4,6},{5,7},{6,4},{7,5},{8,10},{9,11},{10,... | collective-permute-start | bytes 1572872 | tf_op jit(solution)/shard_map/ppermute | solution.py:231
  183.5 27.2 %collective-permute-start.14 = (bf16[256,1024]{1,0:T(8,128)(2,1)S(1)}, bf16[256,1024]{1,0:T(8,128)(2,1)S(1)}, u32[]{:S(2)}, u32[]{:S(2)}) collective-permute-start(bf16[256,1024]{1,0:T(8,128)(2,1)S(1)} %fusion.28), channel_id=1, source_target_pairs={{0,0},{1,8},{2,16},{3,24},{8,1},{9,9},{10,17},{11,25},{16,2},{17,1... | collective-permute-start | bytes 1572872 | tf_op jit(solution)/shard_map/ppermute | solution.py:241

commit v20 on v18

--- a/solution.py
+++ b/solution.py
@@ -239,11 +239,11 @@
             held[m ^ bit] = held[m ^ bit] + got[index].astype(jnp.float32)
         bit *= 2
     swap = [(o * tp_count + t, t * tp_count + o) for o in range(tp_count) for t in range(tp_count)]
-    rotated = lax.ppermute(held[0].astype(jnp.bfloat16), (outer_axis, "tp"), swap)
+    final = held[0].astype(jnp.bfloat16)
     width = out_weight.shape[1]
-    pieces = jnp.stack([rotated[:, d * width : (d + 1) * width] for d in range(inner_count)])
+    pieces = jnp.stack([final[:, d * width : (d + 1) * width] for d in range(inner_count)])
     inner_at = lax.axis_index(inner_axis)
-    return jnp.concatenate(
+    ordered = jnp.concatenate(
         [
             lax.dynamic_index_in_dim(
                 pieces, (inner_at - place + inner_count) % inner_count, 0, keepdims=False
@@ -252,6 +252,7 @@
         ],
         axis=1,
     )
+    return lax.ppermute(ordered, (outer_axis, "tp"), swap)
 
 
 def solution(mesh):

time: 211 us -> 211 us (level)
  no operation moved by 1% of the time
where the time goes in v20:
time: 211 us; the launch traced here: 209 us
  waiting for transfers between devices  116 us (55%)
  starting transfers between devices  40.6 us (19%)
  matrix products  30.4 us (14%)
  other arithmetic  12.5 us (6%)
  local copies, waits for them, and re-layouts  8.97 us (4%)
    ppermute x2, waiting for transfers between devices, on_device(): lax.ppermute(going_left, outer_axis, [(s, s - 1) for s in range(1, tp_cou...  27.2 us
    dot_general x10, matrix products, times_weight(): jnp.dot(rows, piece, preferred_element_type=jnp.float32)  23.8 us
    ppermute x6, starting transfers between devices, shifted(): lax.ppermute(value, axis, [(source, source + steps) for source in range(f...  23.7 us
    ppermute x1, waiting for transfers between devices, on_device(): return lax.ppermute(ordered, (outer_axis, 'tp'), swap)  22.8 us
    ppermute x6, waiting for transfers between devices, shifted(): lax.ppermute(value, axis, [(source, source + steps) for source in range(f...  21.2 us
    ppermute x2, waiting for transfers between devices, on_device(): lax.ppermute(sent.astype(jnp.bfloat16), 'tp', [(s, s ^ bit) for s in rang...  16.1 us
    ppermute x1, waiting for transfers between devices, on_device(): lax.ppermute(out_weight, inner_axis, [(s, (s + d) % inner_count) for s in...  14.9 us
    ppermute x1, waiting for transfers between devices, on_device(): lax.ppermute(jnp.where(outer_at == tp_count - 2, going_right, going_left)...  13.9 us
  transfers between devices with their start and end apart: 15, of which 10 were waited for; matrix products, arithmetic and copies ran while one was open for 15% of the time, Pallas kernels for 0%

profile of v20, /device:TPU:2, one launch (start us, length us, event | category | flops | bytes accessed | tf_op | source)
XLA Modules:
  0.0 209.3 jit_solution(16287154280291180173)
XLA Ops:
  0.0 1.3 constant_dynamic-update-slice_fusion.5
  1.5 3.4 %collective-permute-start.1 = (bf16[3,2304]{1,0:T(4,128)(2,1)S(1)}, bf16[3,2304]{1,0:T(4,128)(2,1)S(1)}, u32[]{:S(2)}, u32[]{:S(2)}) collective-permute-start(bf16[3,2304]{1,0:T(4,128)(2,1)S(1)} %slice.99), channel_id=1, source_target_pairs={{0,4},{4,8},{8,12},{12,16},{16,20},{20,24},{24,28},{1,5},{5,9},{9,... | collective-permute-start | bytes 41480 | tf_op jit(solution)/shard_map/ppermute | solution.py:14
  5.9 0.7 fusion.44
  7.7 1.5 multiply_convert_fusion.3
  9.3 1.6 slice_convert_fusion
  10.9 1.9 copy.27
  12.8 2.2 %fusion.17 = f32[32,64,128]{2,1,0:T(8,128)S(1)} fusion(f32[256,32]{0,1:T(8,128)S(1)} %bitcast.117, f32[256,128]{1,0:T(8,128)S(1)} %slice_convert_fusion.1, f32[32]{0:T(128)S(1)} %get-tuple-element.73, f32[256,32,64]{0,2,1:T(8,128)S(1)} %bitcast.109, f32[256,32]{0,1:T(8,128)} %param.19), kind=kOutput, calls=%fused_computation.31 | convolution fusion | flops 137625600 | bytes 3342464 | tf_op jit(solution)/shard_map/vmap(sgjp,sgjn->gjpn)/dot_general | solution.py:54
  15.1 3.5 %collective-permute-start.4 = (bf16[1,32,64,128]{3,2,1,0:T(8,128)(2,1)S(1)}, bf16[1,32,64,128]{3,2,1,0:T(8,128)(2,1)S(1)}, u32[]{:S(2)}, u32[]{:S(2)}) collective-permute-start(bf16[1,32,64,128]{3,2,1,0:T(8,128)(2,1)S(1)} %convert_bitcast_fusion), channel_id=1, source_target_pairs={{0,4},{4,8},{8,12},{12,16},{16,20},{20,24},{24,28},{1,5},{5,9},{9,... | collective-permute-start | bytes 1572872 | tf_op jit(solution)/shard_map/ppermute | solution.py:14
  18.5 10.9 %collective-permute-done.4 = bf16[1,32,64,128]{3,2,1,0:T(8,128)(2,1)S(1)} collective-permute-done((bf16[1,32,64,128]{3,2,1,0:T(8,128)(2,1)S(1)}, bf16[1,32,64,128]{3,2,1,0:T(8,128)(2,1)S(1)}, u32[]{:S(2)}, u32[]{:S(2)}) %collective-permute-start.4) | collective-permute-done | bytes 524320 | tf_op jit(solution)/shard_map/ppermute | solution.py:14
  29.6 5.4 %collective-permute-start.5 = (bf16[1,32,64,128]{3,2,1,0:T(8,128)(2,1)S(1)}, bf16[1,32,64,128]{3,2,1,0:T(8,128)(2,1)S(1)}, u32[]{:S(2)}, u32[]{:S(2)}) collective-permute-start(bf16[1,32,64,128]{3,2,1,0:T(8,128)(2,1)S(1)} %fusion.23), channel_id=1, source_target_pairs={{0,8},{4,12},{8,16},{12,20},{16,24},{20,28},{1,9},{5,13},{9,17},{1... | collective-permute-start | bytes 1572872 | tf_op jit(solution)/shard_map/ppermute | solution.py:14
  35.0 2.5 %collective-permute-start.2 = (f32[1,32]{1,0:T(1,128)S(1)}, f32[1,32]{1,0:T(1,128)S(1)}, u32[]{:S(2)}, u32[]{:S(2)}) collective-permute-start(f32[1,32]{1,0:T(1,128)S(1)} %bitcast.123), channel_id=1, source_target_pairs={{0,4},{4,8},{8,12},{12,16},{16,20},{20,24},{24,28},{1,5},{5,9},{9,... | collective-permute-start | bytes 392 | tf_op jit(solution)/shard_map/ppermute | solution.py:14
  37.5 2.5 %collective-permute-start = (bf16[2048,512]{1,0:T(8,128)(2,1)}, bf16[2048,512]{1,0:T(8,128)(2,1)}, u32[]{:S(2)}, u32[]{:S(2)}) collective-permute-start(bf16[2048,512]{1,0:T(8,128)(2,1)} %param.23), channel_id=1, source_target_pairs={{0,4},{4,0},{1,5},{5,1},{2,6},{6,2},{3,7},{7,3},{8,12},{12,8},{9,1... | collective-permute-start | bytes 6291464 | tf_op jit(solution)/shard_map/ppermute | solution.py:180
  40.0 4.5 %collective-permute-done.5 = bf16[1,32,64,128]{3,2,1,0:T(8,128)(2,1)S(1)} collective-permute-done((bf16[1,32,64,128]{3,2,1,0:T(8,128)(2,1)S(1)}, bf16[1,32,64,128]{3,2,1,0:T(8,128)(2,1)S(1)}, u32[]{:S(2)}, u32[]{:S(2)}) %collective-permute-start.5) | collective-permute-done | bytes 524320 | tf_op jit(solution)/shard_map/ppermute | solution.py:14
  44.9 6.0 %collective-permute-start.6 = (bf16[1,32,64,128]{3,2,1,0:T(8,128)(2,1)S(1)}, bf16[1,32,64,128]{3,2,1,0:T(8,128)(2,1)S(1)}, u32[]{:S(2)}, u32[]{:S(2)}) collective-permute-start(bf16[1,32,64,128]{3,2,1,0:T(8,128)(2,1)S(1)} %fusion.22), channel_id=1, source_target_pairs={{0,16},{4,20},{8,24},{12,28},{1,17},{5,21},{9,25},{13,29},{2,18},{... | collective-permute-start | bytes 1572872 | tf_op jit(solution)/shard_map/ppermute | solution.py:14
  50.9 3.0 %collective-permute-start.3 = (f32[1,32]{1,0:T(1,128)S(1)}, f32[1,32]{1,0:T(1,128)S(1)}, u32[]{:S(2)}, u32[]{:S(2)}) collective-permute-start(f32[1,32]{1,0:T(1,128)S(1)} %bitcast_multiply_fusion.1), channel_id=1, source_target_pairs={{0,8},{4,12},{8,16},{12,20},{16,24},{20,28},{1,9},{5,13},{9,17},{1... | collective-permute-start | bytes 392 | tf_op jit(solution)/shard_map/ppermute | solution.py:14
  53.9 5.9 %collective-permute-done.3 = f32[1,32]{1,0:T(1,128)S(1)} collective-permute-done((f32[1,32]{1,0:T(1,128)S(1)}, f32[1,32]{1,0:T(1,128)S(1)}, u32[]{:S(2)}, u32[]{:S(2)}) %collective-permute-start.3) | collective-permute-done | bytes 160 | tf_op jit(solution)/shard_map/ppermute | solution.py:14
  60.5 3.7 %fusion.14 = f32[256,1,32,64]{0,3,2,1:T(8,128)} fusion(f32[32,64,256]{2,1,0:T(8,128)S(1)} %fusion.26, f32[256,1,32,64]{0,3,2,1:T(8,128)S(1)} %bitcast.111, f32[32,256]{1,0:T(8,128)S(1)} %bitcast.119, f32[256,256]{1,0:T(8,128)S(1)} %fusion.37, pred[256,256]{1,0:T(8,128)(4,1)S(1)} %iota_compare_fusion.1, f32[32]{0:T(128)S(1)} %copy-done.11, ...), kind=kOutput, calls=%fused_computation.25 | convolution fusion | flops 279969792 | bytes 8814720 | tf_op jit(solution)/shard_map/while/body/eval_jaxpr/gjts,sgjp->tgjp/dot_general | solution.py:46
  64.2 2.0 copy.32
  66.2 0.8 multiply_reduce_fusion
  67.0 1.8 multiply_convert_fusion.5
  68.9 14.9 %collective-permute-done = bf16[2048,512]{1,0:T(8,128)(2,1)} collective-permute-done((bf16[2048,512]{1,0:T(8,128)(2,1)}, bf16[2048,512]{1,0:T(8,128)(2,1)}, u32[]{:S(2)}, u32[]{:S(2)}) %collective-permute-start) | collective-permute-done | bytes 2097184 | tf_op jit(solution)/shard_map/ppermute | solution.py:180
  83.8 1.3 collective-permute-start.9
  85.1 4.6 %collective-permute-start.7 = (bf16[256,2048]{1,0:T(8,128)(2,1)}, bf16[256,2048]{1,0:T(8,128)(2,1)S(1)}, u32[]{:S(2)}, u32[]{:S(2)}) collective-permute-start(bf16[256,2048]{1,0:T(8,128)(2,1)} %multiply_convert_fusion.5), channel_id=1, source_target_pairs={{0,8},{8,16},{16,24},{1,9},{9,17},{17,25},{2,10},{10,18},{18,26},{... | collective-permute-start | bytes 3145736 | tf_op jit(solution)/shard_map/ppermute | solution.py:195
  89.7 2.6 %fusion.46 = f32[256,512]{1,0:T(8,128)S(1)} fusion(bf16[256,2048]{1,0:T(8,128)(2,1)} %multiply_convert_fusion.5, bf16[2048,512]{1,0:T(8,128)(2,1)} %param.23), kind=kOutput, calls=%fused_computation.120 | convolution fusion | flops 536870912 | bytes 3670016 | tf_op jit(solution)/shard_map/dot_general | solution.py:188
  92.4 15.7 %collective-permute-done.9 = bf16[256,2048]{1,0:T(8,128)(2,1)S(1)} collective-permute-done((bf16[256,2048]{1,0:T(8,128)(2,1)}, bf16[256,2048]{1,0:T(8,128)(2,1)S(1)}, u32[]{:S(2)}, u32[]{:S(2)}) %collective-permute-start.9) | collective-permute-done | bytes 1048608 | tf_op jit(solution)/shard_map/ppermute | solution.py:198
  108.1 1.3 collective-permute-start.10
  109.4 0.7 collective-permute-start.8
  110.1 2.6 %fusion.47 = f32[256,512]{1,0:T(8,128)S(1)} fusion(bf16[256,2048]{1,0:T(8,128)(2,1)} %multiply_convert_fusion.5, bf16[2048,512]{1,0:T(8,128)(2,1)} %collective-permute-done), kind=kOutput, calls=%fused_computation.121 | convolution fusion | flops 536870912 | bytes 3670016 | tf_op jit(solution)/shard_map/dot_general | solution.py:188
  112.8 2.3 %convolution_bitcast_fusion.1 = f32[1,256,512]{2,1,0:T(8,128)S(1)} fusion(bf16[256,2048]{1,0:T(8,128)(2,1)S(1)} %collective-permute-done.9, bf16[2048,512]{1,0:T(8,128)(2,1)} %param.23), kind=kOutput, calls=%fused_computation.37 | convolution fusion | flops 536870912 | bytes 3670016 | tf_op jit(solution)/shard_map/dot_general | solution.py:188
  115.1 2.3 %convolution_bitcast_fusion = f32[1,256,512]{2,1,0:T(8,128)S(1)} fusion(bf16[256,2048]{1,0:T(8,128)(2,1)S(1)} %collective-permute-done.9, bf16[2048,512]{1,0:T(8,128)(2,1)} %collective-permute-done), kind=kOutput, calls=%fused_computation.36 | convolution fusion | flops 536870912 | bytes 3670016 | tf_op jit(solution)/shard_map/dot_general | solution.py:188
  117.4 2.3 %convolution_bitcast_fusion.5 = f32[1,256,512]{2,1,0:T(8,128)S(1)} fusion(bf16[256,2048]{1,0:T(8,128)(2,1)S(1)} %collective-permute-done.7, bf16[2048,512]{1,0:T(8,128)(2,1)} %param.23), kind=kOutput, calls=%fused_computation.41 | convolution fusion | flops 536870912 | bytes 3670016 | tf_op jit(solution)/shard_map/dot_general | solution.py:188
  119.7 11.6 %collective-permute-done.10 = bf16[256,2048]{1,0:T(8,128)(2,1)S(1)} collective-permute-done((bf16[256,2048]{1,0:T(8,128)(2,1)S(1)}, bf16[256,2048]{1,0:T(8,128)(2,1)S(1)}, u32[]{:S(2)}, u32[]{:S(2)}) %collective-permute-start.10) | collective-permute-done | bytes 1048608 | tf_op jit(solution)/shard_map/ppermute | solution.py:198
  131.4 1.5 collective-permute-start.11
  132.9 2.3 %convolution_bitcast_fusion.4 = f32[1,256,512]{2,1,0:T(8,128)S(1)} fusion(bf16[256,2048]{1,0:T(8,128)(2,1)S(1)} %collective-permute-done.7, bf16[2048,512]{1,0:T(8,128)(2,1)} %collective-permute-done), kind=kOutput, calls=%fused_computation.40 | convolution fusion | flops 536870912 | bytes 3670016 | tf_op jit(solution)/shard_map/dot_general | solution.py:188
  135.2 2.4 %fusion.31 = f32[256,512]{1,0:T(8,128)S(1)} fusion(bf16[2048,512]{1,0:T(8,128)(2,1)} %param.23, bf16[256,2048]{1,0:T(8,128)(2,1)S(1)} %collective-permute-done.8, bf16[256,2048]{1,0:T(8,128)(2,1)S(1)} %collective-permute-done.10, pred[]{:T(512)S(6)} %ge.33), kind=kOutput, calls=%fused_computation.73 | convolution fusion | flops 537395200 | bytes 4718593 | tf_op jit(solution)/shard_map/dot_general | solution.py:188
  137.6 2.4 %fusion.30 = f32[256,512]{1,0:T(8,128)S(1)} fusion(bf16[2048,512]{1,0:T(8,128)(2,1)} %collective-permute-done, bf16[256,2048]{1,0:T(8,128)(2,1)S(1)} %collective-permute-done.8, bf16[256,2048]{1,0:T(8,128)(2,1)S(1)} %collective-permute-done.10, pred[]{:T(512)S(6)} %ge.33), kind=kOutput, calls=%fused_computation.72 | convolution fusion | flops 537395200 | bytes 4718593 | tf_op jit(solution)/shard_map/dot_general | solution.py:188
  140.0 13.9 %collective-permute-done.11 = bf16[256,2048]{1,0:T(8,128)(2,1)S(1)} collective-permute-done((bf16[256,2048]{1,0:T(8,128)(2,1)S(1)}, bf16[256,2048]{1,0:T(8,128)(2,1)S(1)}, u32[]{:S(2)}, u32[]{:S(2)}) %collective-permute-start.11) | collective-permute-done | bytes 1048608 | tf_op jit(solution)/shard_map/ppermute | solution.py:202
  154.0 2.3 %convolution_bitcast_fusion.3 = f32[1,256,512]{2,1,0:T(8,128)S(1)} fusion(bf16[256,2048]{1,0:T(8,128)(2,1)S(1)} %collective-permute-done.11, bf16[2048,512]{1,0:T(8,128)(2,1)} %param.23), kind=kOutput, calls=%fused_computation.39 | convolution fusion | flops 536870912 | bytes 3670016 | tf_op jit(solution)/shard_map/dot_general | solution.py:188
  156.3 2.3 %convolution_bitcast_fusion.2 = f32[1,256,512]{2,1,0:T(8,128)S(1)} fusion(bf16[256,2048]{1,0:T(8,128)(2,1)S(1)} %collective-permute-done.11, bf16[2048,512]{1,0:T(8,128)(2,1)} %collective-permute-done), kind=kOutput, calls=%fused_computation.38 | convolution fusion | flops 536870912 | bytes 3670016 | tf_op jit(solution)/shard_map/dot_general | solution.py:188
  159.8 1.7 copy-done.1
  161.4 2.7 %collective-permute-done.12 = bf16[2,256,1024]{2,1,0:T(8,128)(2,1)S(1)} collective-permute-done((bf16[2,256,1024]{2,1,0:T(8,128)(2,1)S(1)}, bf16[2,256,1024]{2,1,0:T(8,128)(2,1)S(1)}, u32[]{:S(2)}, u32[]{:S(2)}) %collective-permute-start.12) | collective-permute-done | bytes 1048608 | tf_op jit(solution)/shard_map/ppermute | solution.py:232
  164.1 1.4 add_convert_fusion.1
  165.5 0.6 collective-permute-start.13
  166.1 13.4 %collective-permute-done.13 = bf16[1,256,1024]{2,1,0:T(8,128)(2,1)S(1)} collective-permute-done((bf16[1,256,1024]{2,1,0:T(8,128)(2,1)S(1)}, bf16[1,256,1024]{2,1,0:T(8,128)(2,1)S(1)}, u32[]{:S(2)}, u32[]{:S(2)}) %collective-permute-start.13) | collective-permute-done | bytes 524320 | tf_op jit(solution)/shard_map/ppermute | solution.py:232
  179.5 1.5 fusion.24
  181.3 4.5 %collective-permute-start.14 = (bf16[256,1024]{1,0:T(8,128)(2,1)S(1)}, bf16[256,1024]{1,0:T(8,128)(2,1)S(1)}, u32[]{:S(2)}, u32[]{:S(2)}) collective-permute-start(bf16[256,1024]{1,0:T(8,128)(2,1)S(1)} %pad_maximum_fusion.3), channel_id=1, source_target_pairs={{0,0},{1,8},{2,16},{3,24},{8,1},{9,9},{10,17},{11,25},{16,2},{17,1... | collective-permute-start | bytes 1572872 | tf_op jit(solution)/shard_map/ppermute | solution.py:255
  185.8 22.8 %collective-permute-done.14 = bf16[256,1024]{1,0:T(8,128)(2,1)S(1)} collective-permute-done((bf16[256,1024]{1,0:T(8,128)(2,1)S(1)}, bf16[256,1024]{1,0:T(8,128)(2,1)S(1)}, u32[]{:S(2)}, u32[]{:S(2)}) %collective-permute-start.14) | collective-permute-done | bytes 524320 | tf_op jit(solution)/shard_map/ppermute | solution.py:255
  208.5 0.8 copy.49
  (73 shorter events, 5.2 us)
Async XLA Ops:
  0.0 4.9 %copy-start = (f32[256,32]{0,1:T(8,128)S(1)}, f32[256,32]{0,1:T(8,128)}, u32[]{:S(2)}) copy-start(f32[256,32]{0,1:T(8,128)} %param.20) | copy-start | bytes 98308
  0.0 1.4 copy-start.4
  0.0 1.4 copy-start.5
  0.0 7.3 %copy-start.7 = (f32[4,2048]{1,0:T(4,128)S(1)}, f32[4,2048]{1,0:T(4,128)}, u32[]{:S(2)}) copy-start(f32[4,2048]{1,0:T(4,128)} %param.16) | copy-start | bytes 98308
  0.0 7.3 %copy-start.9 = (f32[4,128]{1,0:T(4,128)S(1)}, f32[4,128]{1,0:T(4,128)}, u32[]{:S(2)}) copy-start(f32[4,128]{1,0:T(4,128)} %param.17) | copy-start | bytes 6148
  0.0 7.3 %copy-start.10 = (f32[4,128]{1,0:T(4,128)S(1)}, f32[4,128]{1,0:T(4,128)}, u32[]{:S(2)}) copy-start(f32[4,128]{1,0:T(4,128)} %param.18) | copy-start | bytes 6148
  1.5 6.1 %collective-permute-start.1 = (bf16[3,2304]{1,0:T(4,128)(2,1)S(1)}, bf16[3,2304]{1,0:T(4,128)(2,1)S(1)}, u32[]{:S(2)}, u32[]{:S(2)}) collective-permute-start(bf16[3,2304]{1,0:T(4,128)(2,1)S(1)} %slice.99), channel_id=1, source_target_pairs={{0,4},{4,8},{8,12},{12,16},{16,20},{20,24},{24,28},{1,5},{5,9},{9,... | collective-permute-start | bytes 41480 | tf_op jit(solution)/shard_map/ppermute | solution.py:14
  15.1 14.3 %collective-permute-start.4 = (bf16[1,32,64,128]{3,2,1,0:T(8,128)(2,1)S(1)}, bf16[1,32,64,128]{3,2,1,0:T(8,128)(2,1)S(1)}, u32[]{:S(2)}, u32[]{:S(2)}) collective-permute-start(bf16[1,32,64,128]{3,2,1,0:T(8,128)(2,1)S(1)} %convert_bitcast_fusion), channel_id=1, source_target_pairs={{0,4},{4,8},{8,12},{12,16},{16,20},{20,24},{24,28},{1,5},{5,9},{9,... | collective-permute-start | bytes 1572872 | tf_op jit(solution)/shard_map/ppermute | solution.py:14
  29.4 24.4 %copy-start.3 = (f32[1,256,1,32]{1,2,3,0:T(1,128)S(1)}, f32[1,256,1,32]{1,2,3,0:T(1,128)}, u32[]{:S(2)}) copy-start(f32[1,256,1,32]{1,2,3,0:T(1,128)} %get-tuple-element.56) | copy-start | bytes 98308
  29.6 14.9 %collective-permute-start.5 = (bf16[1,32,64,128]{3,2,1,0:T(8,128)(2,1)S(1)}, bf16[1,32,64,128]{3,2,1,0:T(8,128)(2,1)S(1)}, u32[]{:S(2)}, u32[]{:S(2)}) collective-permute-start(bf16[1,32,64,128]{3,2,1,0:T(8,128)(2,1)S(1)} %fusion.23), channel_id=1, source_target_pairs={{0,8},{4,12},{8,16},{12,20},{16,24},{20,28},{1,9},{5,13},{9,17},{1... | collective-permute-start | bytes 1572872 | tf_op jit(solution)/shard_map/ppermute | solution.py:14
  35.0 5.0 %collective-permute-start.2 = (f32[1,32]{1,0:T(1,128)S(1)}, f32[1,32]{1,0:T(1,128)S(1)}, u32[]{:S(2)}, u32[]{:S(2)}) collective-permute-start(f32[1,32]{1,0:T(1,128)S(1)} %bitcast.123), channel_id=1, source_target_pairs={{0,4},{4,8},{8,12},{12,16},{16,20},{20,24},{24,28},{1,5},{5,9},{9,... | collective-permute-start | bytes 392 | tf_op jit(solution)/shard_map/ppermute | solution.py:14
  37.5 46.3 %collective-permute-start = (bf16[2048,512]{1,0:T(8,128)(2,1)}, bf16[2048,512]{1,0:T(8,128)(2,1)}, u32[]{:S(2)}, u32[]{:S(2)}) collective-permute-start(bf16[2048,512]{1,0:T(8,128)(2,1)} %param.23), channel_id=1, source_target_pairs={{0,4},{4,0},{1,5},{5,1},{2,6},{6,2},{3,7},{7,3},{8,12},{12,8},{9,1... | collective-permute-start | bytes 6291464 | tf_op jit(solution)/shard_map/ppermute | solution.py:180
  44.9 15.1 %collective-permute-start.6 = (bf16[1,32,64,128]{3,2,1,0:T(8,128)(2,1)S(1)}, bf16[1,32,64,128]{3,2,1,0:T(8,128)(2,1)S(1)}, u32[]{:S(2)}, u32[]{:S(2)}) collective-permute-start(bf16[1,32,64,128]{3,2,1,0:T(8,128)(2,1)S(1)} %fusion.22), channel_id=1, source_target_pairs={{0,16},{4,20},{8,24},{12,28},{1,17},{5,21},{9,25},{13,29},{2,18},{... | collective-permute-start | bytes 1572872 | tf_op jit(solution)/shard_map/ppermute | solution.py:14
  50.9 8.9 %collective-permute-start.3 = (f32[1,32]{1,0:T(1,128)S(1)}, f32[1,32]{1,0:T(1,128)S(1)}, u32[]{:S(2)}, u32[]{:S(2)}) collective-permute-start(f32[1,32]{1,0:T(1,128)S(1)} %bitcast_multiply_fusion.1), channel_id=1, source_target_pairs={{0,8},{4,12},{8,16},{12,20},{16,24},{20,28},{1,9},{5,13},{9,17},{1... | collective-permute-start | bytes 392 | tf_op jit(solution)/shard_map/ppermute | solution.py:14
  53.9 6.6 %copy-start.6 = (f32[256,32]{0,1:T(8,128)S(1)}, f32[256,32]{0,1:T(8,128)}, u32[]{:S(2)}) copy-start(f32[256,32]{0,1:T(8,128)} %param.19) | copy-start | bytes 98308
  53.9 6.6 %copy-start.11 = (f32[32]{0:T(128)S(1)}, f32[32]{0:T(128)}, u32[]{:S(2)}) copy-start(f32[32]{0:T(128)} %param.21) | copy-start | bytes 388
  64.2 2.0 copy-start.2
  66.2 0.8 copy-start.8
  83.8 24.3 %collective-permute-start.9 = (bf16[256,2048]{1,0:T(8,128)(2,1)}, bf16[256,2048]{1,0:T(8,128)(2,1)S(1)}, u32[]{:S(2)}, u32[]{:S(2)}) collective-permute-start(bf16[256,2048]{1,0:T(8,128)(2,1)} %multiply_convert_fusion.5), channel_id=1, source_target_pairs={{8,0},{16,8},{24,16},{9,1},{17,9},{25,17},{10,2},{18,10},{26,18},{... | collective-permute-start | bytes 3145736 | tf_op jit(solution)/shard_map/ppermute | solution.py:198
  85.1 24.3 %collective-permute-start.7 = (bf16[256,2048]{1,0:T(8,128)(2,1)}, bf16[256,2048]{1,0:T(8,128)(2,1)S(1)}, u32[]{:S(2)}, u32[]{:S(2)}) collective-permute-start(bf16[256,2048]{1,0:T(8,128)(2,1)} %multiply_convert_fusion.5), channel_id=1, source_target_pairs={{0,8},{8,16},{16,24},{1,9},{9,17},{17,25},{2,10},{10,18},{18,26},{... | collective-permute-start | bytes 3145736 | tf_op jit(solution)/shard_map/ppermute | solution.py:195
  108.1 23.2 %collective-permute-start.10 = (bf16[256,2048]{1,0:T(8,128)(2,1)S(1)}, bf16[256,2048]{1,0:T(8,128)(2,1)S(1)}, u32[]{:S(2)}, u32[]{:S(2)}) collective-permute-start(bf16[256,2048]{1,0:T(8,128)(2,1)S(1)} %collective-permute-done.9), channel_id=1, source_target_pairs={{8,0},{16,8},{9,1},{17,9},{10,2},{18,10},{11,3},{19,11},{12,4},{20... | collective-permute-start | bytes 3145736 | tf_op jit(solution)/shard_map/ppermute | solution.py:198
  109.4 21.9 %collective-permute-start.8 = (bf16[256,2048]{1,0:T(8,128)(2,1)S(1)}, bf16[256,2048]{1,0:T(8,128)(2,1)S(1)}, u32[]{:S(2)}, u32[]{:S(2)}) collective-permute-start(bf16[256,2048]{1,0:T(8,128)(2,1)S(1)} %collective-permute-done.7), channel_id=1, source_target_pairs={{8,16},{16,24},{9,17},{17,25},{10,18},{18,26},{11,19},{19,27},{12,... | collective-permute-start | bytes 3145736 | tf_op jit(solution)/shard_map/ppermute | solution.py:195
  131.4 22.6 %collective-permute-start.11 = (bf16[256,2048]{1,0:T(8,128)(2,1)S(1)}, bf16[256,2048]{1,0:T(8,128)(2,1)S(1)}, u32[]{:S(2)}, u32[]{:S(2)}) collective-permute-start(bf16[256,2048]{1,0:T(8,128)(2,1)S(1)} %broadcast_select_fusion.1), channel_id=1, source_target_pairs={{16,24},{8,0},{17,25},{9,1},{18,26},{10,2},{19,27},{11,3},{20,28},... | collective-permute-start | bytes 3145736 | tf_op jit(solution)/shard_map/ppermute | solution.py:202
  159.5 1.9 copy-start.1
  161.4 2.7 %collective-permute-start.12 = (bf16[2,256,1024]{2,1,0:T(8,128)(2,1)S(1)}, bf16[2,256,1024]{2,1,0:T(8,128)(2,1)S(1)}, u32[]{:S(2)}, u32[]{:S(2)}) collective-permute-start(bf16[2,256,1024]{2,1,0:T(8,128)(2,1)S(1)} %pad_maximum_fusion.2), channel_id=1, source_target_pairs={{0,1},{1,0},{2,3},{3,2},{4,5},{5,4},{6,7},{7,6},{8,9},{9,8},{10,11... | collective-permute-start | bytes 3145736 | tf_op jit(solution)/shard_map/ppermute | solution.py:232
  165.5 14.0 %collective-permute-start.13 = (bf16[1,256,1024]{2,1,0:T(8,128)(2,1)S(1)}, bf16[1,256,1024]{2,1,0:T(8,128)(2,1)S(1)}, u32[]{:S(2)}, u32[]{:S(2)}) collective-permute-start(bf16[1,256,1024]{2,1,0:T(8,128)(2,1)S(1)} %add_convert_fusion.1), channel_id=1, source_target_pairs={{0,2},{1,3},{2,0},{3,1},{4,6},{5,7},{6,4},{7,5},{8,10},{9,11},{10,... | collective-permute-start | bytes 1572872 | tf_op jit(solution)/shard_map/ppermute | solution.py:232
  181.3 27.2 %collective-permute-start.14 = (bf16[256,1024]{1,0:T(8,128)(2,1)S(1)}, bf16[256,1024]{1,0:T(8,128)(2,1)S(1)}, u32[]{:S(2)}, u32[]{:S(2)}) collective-permute-start(bf16[256,1024]{1,0:T(8,128)(2,1)S(1)} %pad_maximum_fusion.3), channel_id=1, source_target_pairs={{0,0},{1,8},{2,16},{3,24},{8,1},{9,9},{10,17},{11,25},{16,2},{17,1... | collective-permute-start | bytes 1572872 | tf_op jit(solution)/shard_map/ppermute | solution.py:255

commit v21 on v18

--- a/solution.py
+++ b/solution.py
@@ -224,11 +224,25 @@
             by_source, (outer_at - target + tp_count) % tp_count, 0, keepdims=False
         )
 
+    by_source_low = by_source.astype(jnp.bfloat16)
     held = {m: for_target(tp_at ^ m) for m in range(tp_count)}
     bit = 1
     while bit < tp_count:
         going = sorted(m for m in held if m & bit)
-        sent = jnp.stack([held[m] for m in going])
+        if bit == 1:
+            sent = jnp.stack(
+                [
+                    lax.dynamic_index_in_dim(
+                        by_source_low,
+                        (outer_at - (tp_at ^ m) + tp_count) % tp_count,
+                        0,
+                        keepdims=False,
+                    )
+                    for m in going
+                ]
+            )
+        else:
+            sent = jnp.stack([held[m] for m in going])
         got = lax.ppermute(
             sent.astype(jnp.bfloat16),
             "tp",

time: 211 us -> 212 us (level)
  other arithmetic: 13.3 us -> 15.8 us
  transfers between devices with their start and end apart: 15 -> 15, of which waited for: 10 -> 10; matrix products, arithmetic and copies ran while one was open for 15% -> 16% of each run, Pallas kernels for 0% -> 0%
where the time goes in v21:
time: 212 us; the launch traced here: 210 us
  waiting for transfers between devices  115 us (54%)
  starting transfers between devices  40.6 us (19%)
  matrix products  30.4 us (14%)
  other arithmetic  15.8 us (7%)
  local copies, waits for them, and re-layouts  7.65 us (4%)
    ppermute x2, waiting for transfers between devices, on_device(): lax.ppermute(going_left, outer_axis, [(s, s - 1) for s in range(1, tp_cou...  27.2 us
    dot_general x10, matrix products, times_weight(): jnp.dot(rows, piece, preferred_element_type=jnp.float32)  23.8 us
    ppermute x6, starting transfers between devices, shifted(): lax.ppermute(value, axis, [(source, source + steps) for source in range(f...  23.7 us
    ppermute x1, waiting for transfers between devices, on_device(): lax.ppermute(held[0].astype(jnp.bfloat16), (outer_axis, 'tp'), swap)  22.9 us
    ppermute x6, waiting for transfers between devices, shifted(): lax.ppermute(value, axis, [(source, source + steps) for source in range(f...  21.2 us
    ppermute x2, waiting for transfers between devices, on_device(): lax.ppermute(sent.astype(jnp.bfloat16), 'tp', [(s, s ^ bit) for s in rang...  15.1 us
    ppermute x1, waiting for transfers between devices, on_device(): lax.ppermute(out_weight, inner_axis, [(s, (s + d) % inner_count) for s in...  14.9 us
    ppermute x1, waiting for transfers between devices, on_device(): lax.ppermute(jnp.where(outer_at == tp_count - 2, going_right, going_left)...  13.9 us
  transfers between devices with their start and end apart: 15, of which 10 were waited for; matrix products, arithmetic and copies ran while one was open for 16% of the time, Pallas kernels for 0%

profile of v21, /device:TPU:2, one launch (start us, length us, event | category | flops | bytes accessed | tf_op | source)
XLA Modules:
  0.0 210.5 jit_solution(3646580106742916609)
XLA Ops:
  0.0 1.3 constant_dynamic-update-slice_fusion.5
  1.5 3.4 %collective-permute-start.1 = (bf16[3,2304]{1,0:T(4,128)(2,1)S(1)}, bf16[3,2304]{1,0:T(4,128)(2,1)S(1)}, u32[]{:S(2)}, u32[]{:S(2)}) collective-permute-start(bf16[3,2304]{1,0:T(4,128)(2,1)S(1)} %slice.99), channel_id=1, source_target_pairs={{0,4},{4,8},{8,12},{12,16},{16,20},{20,24},{24,28},{1,5},{5,9},{9,... | collective-permute-start | bytes 41480 | tf_op jit(solution)/shard_map/ppermute | solution.py:14
  5.9 0.7 fusion.45
  7.7 1.5 multiply_convert_fusion.3
  9.3 1.6 slice_convert_fusion
  10.9 1.9 copy.27
  12.8 2.2 %fusion.17 = f32[32,64,128]{2,1,0:T(8,128)S(1)} fusion(f32[256,32]{0,1:T(8,128)S(1)} %bitcast.117, f32[256,128]{1,0:T(8,128)S(1)} %slice_convert_fusion.1, f32[32]{0:T(128)S(1)} %get-tuple-element.73, f32[256,32,64]{0,2,1:T(8,128)S(1)} %bitcast.109, f32[256,32]{0,1:T(8,128)} %param.19), kind=kOutput, calls=%fused_computation.31 | convolution fusion | flops 137625600 | bytes 3342464 | tf_op jit(solution)/shard_map/vmap(sgjp,sgjn->gjpn)/dot_general | solution.py:54
  15.1 3.5 %collective-permute-start.4 = (bf16[1,32,64,128]{3,2,1,0:T(8,128)(2,1)S(1)}, bf16[1,32,64,128]{3,2,1,0:T(8,128)(2,1)S(1)}, u32[]{:S(2)}, u32[]{:S(2)}) collective-permute-start(bf16[1,32,64,128]{3,2,1,0:T(8,128)(2,1)S(1)} %convert_bitcast_fusion), channel_id=1, source_target_pairs={{0,4},{4,8},{8,12},{12,16},{16,20},{20,24},{24,28},{1,5},{5,9},{9,... | collective-permute-start | bytes 1572872 | tf_op jit(solution)/shard_map/ppermute | solution.py:14
  18.6 10.8 %collective-permute-done.4 = bf16[1,32,64,128]{3,2,1,0:T(8,128)(2,1)S(1)} collective-permute-done((bf16[1,32,64,128]{3,2,1,0:T(8,128)(2,1)S(1)}, bf16[1,32,64,128]{3,2,1,0:T(8,128)(2,1)S(1)}, u32[]{:S(2)}, u32[]{:S(2)}) %collective-permute-start.4) | collective-permute-done | bytes 524320 | tf_op jit(solution)/shard_map/ppermute | solution.py:14
  29.6 5.4 %collective-permute-start.5 = (bf16[1,32,64,128]{3,2,1,0:T(8,128)(2,1)S(1)}, bf16[1,32,64,128]{3,2,1,0:T(8,128)(2,1)S(1)}, u32[]{:S(2)}, u32[]{:S(2)}) collective-permute-start(bf16[1,32,64,128]{3,2,1,0:T(8,128)(2,1)S(1)} %fusion.23), channel_id=1, source_target_pairs={{0,8},{4,12},{8,16},{12,20},{16,24},{20,28},{1,9},{5,13},{9,17},{1... | collective-permute-start | bytes 1572872 | tf_op jit(solution)/shard_map/ppermute | solution.py:14
  35.0 2.5 %collective-permute-start.2 = (f32[1,32]{1,0:T(1,128)S(1)}, f32[1,32]{1,0:T(1,128)S(1)}, u32[]{:S(2)}, u32[]{:S(2)}) collective-permute-start(f32[1,32]{1,0:T(1,128)S(1)} %bitcast.123), channel_id=1, source_target_pairs={{0,4},{4,8},{8,12},{12,16},{16,20},{20,24},{24,28},{1,5},{5,9},{9,... | collective-permute-start | bytes 392 | tf_op jit(solution)/shard_map/ppermute | solution.py:14
  37.5 2.5 %collective-permute-start = (bf16[2048,512]{1,0:T(8,128)(2,1)}, bf16[2048,512]{1,0:T(8,128)(2,1)}, u32[]{:S(2)}, u32[]{:S(2)}) collective-permute-start(bf16[2048,512]{1,0:T(8,128)(2,1)} %param.23), channel_id=1, source_target_pairs={{0,4},{4,0},{1,5},{5,1},{2,6},{6,2},{3,7},{7,3},{8,12},{12,8},{9,1... | collective-permute-start | bytes 6291464 | tf_op jit(solution)/shard_map/ppermute | solution.py:180
  40.1 4.5 %collective-permute-done.5 = bf16[1,32,64,128]{3,2,1,0:T(8,128)(2,1)S(1)} collective-permute-done((bf16[1,32,64,128]{3,2,1,0:T(8,128)(2,1)S(1)}, bf16[1,32,64,128]{3,2,1,0:T(8,128)(2,1)S(1)}, u32[]{:S(2)}, u32[]{:S(2)}) %collective-permute-start.5) | collective-permute-done | bytes 524320 | tf_op jit(solution)/shard_map/ppermute | solution.py:14
  44.9 6.0 %collective-permute-start.6 = (bf16[1,32,64,128]{3,2,1,0:T(8,128)(2,1)S(1)}, bf16[1,32,64,128]{3,2,1,0:T(8,128)(2,1)S(1)}, u32[]{:S(2)}, u32[]{:S(2)}) collective-permute-start(bf16[1,32,64,128]{3,2,1,0:T(8,128)(2,1)S(1)} %fusion.22), channel_id=1, source_target_pairs={{0,16},{4,20},{8,24},{12,28},{1,17},{5,21},{9,25},{13,29},{2,18},{... | collective-permute-start | bytes 1572872 | tf_op jit(solution)/shard_map/ppermute | solution.py:14
  50.9 3.0 %collective-permute-start.3 = (f32[1,32]{1,0:T(1,128)S(1)}, f32[1,32]{1,0:T(1,128)S(1)}, u32[]{:S(2)}, u32[]{:S(2)}) collective-permute-start(f32[1,32]{1,0:T(1,128)S(1)} %bitcast_multiply_fusion.1), channel_id=1, source_target_pairs={{0,8},{4,12},{8,16},{12,20},{16,24},{20,28},{1,9},{5,13},{9,17},{1... | collective-permute-start | bytes 392 | tf_op jit(solution)/shard_map/ppermute | solution.py:14
  53.9 5.9 %collective-permute-done.3 = f32[1,32]{1,0:T(1,128)S(1)} collective-permute-done((f32[1,32]{1,0:T(1,128)S(1)}, f32[1,32]{1,0:T(1,128)S(1)}, u32[]{:S(2)}, u32[]{:S(2)}) %collective-permute-start.3) | collective-permute-done | bytes 160 | tf_op jit(solution)/shard_map/ppermute | solution.py:14
  60.5 3.7 %fusion.14 = f32[256,1,32,64]{0,3,2,1:T(8,128)} fusion(f32[32,64,256]{2,1,0:T(8,128)S(1)} %fusion.26, f32[256,1,32,64]{0,3,2,1:T(8,128)S(1)} %bitcast.111, f32[32,256]{1,0:T(8,128)S(1)} %bitcast.119, f32[256,256]{1,0:T(8,128)S(1)} %fusion.37, pred[256,256]{1,0:T(8,128)(4,1)S(1)} %iota_compare_fusion.1, f32[32]{0:T(128)S(1)} %copy-done.12, ...), kind=kOutput, calls=%fused_computation.25 | convolution fusion | flops 279969792 | bytes 8814720 | tf_op jit(solution)/shard_map/while/body/eval_jaxpr/gjts,sgjp->tgjp/dot_general | solution.py:46
  64.2 2.0 copy.32
  66.3 0.8 multiply_reduce_fusion
  67.1 1.8 multiply_convert_fusion.5
  68.9 14.9 %collective-permute-done = bf16[2048,512]{1,0:T(8,128)(2,1)} collective-permute-done((bf16[2048,512]{1,0:T(8,128)(2,1)}, bf16[2048,512]{1,0:T(8,128)(2,1)}, u32[]{:S(2)}, u32[]{:S(2)}) %collective-permute-start) | collective-permute-done | bytes 2097184 | tf_op jit(solution)/shard_map/ppermute | solution.py:180
  83.8 1.3 collective-permute-start.9
  85.1 4.6 %collective-permute-start.7 = (bf16[256,2048]{1,0:T(8,128)(2,1)}, bf16[256,2048]{1,0:T(8,128)(2,1)S(1)}, u32[]{:S(2)}, u32[]{:S(2)}) collective-permute-start(bf16[256,2048]{1,0:T(8,128)(2,1)} %multiply_convert_fusion.5), channel_id=1, source_target_pairs={{0,8},{8,16},{16,24},{1,9},{9,17},{17,25},{2,10},{10,18},{18,26},{... | collective-permute-start | bytes 3145736 | tf_op jit(solution)/shard_map/ppermute | solution.py:195
  89.8 2.6 %fusion.47 = f32[256,512]{1,0:T(8,128)S(1)} fusion(bf16[256,2048]{1,0:T(8,128)(2,1)} %multiply_convert_fusion.5, bf16[2048,512]{1,0:T(8,128)(2,1)} %param.23), kind=kOutput, calls=%fused_computation.121 | convolution fusion | flops 536870912 | bytes 3670016 | tf_op jit(solution)/shard_map/dot_general | solution.py:188
  92.4 15.7 %collective-permute-done.9 = bf16[256,2048]{1,0:T(8,128)(2,1)S(1)} collective-permute-done((bf16[256,2048]{1,0:T(8,128)(2,1)}, bf16[256,2048]{1,0:T(8,128)(2,1)S(1)}, u32[]{:S(2)}, u32[]{:S(2)}) %collective-permute-start.9) | collective-permute-done | bytes 1048608 | tf_op jit(solution)/shard_map/ppermute | solution.py:198
  108.1 1.3 collective-permute-start.10
  109.4 0.7 collective-permute-start.8
  110.1 2.6 %fusion.48 = f32[256,512]{1,0:T(8,128)S(1)} fusion(bf16[256,2048]{1,0:T(8,128)(2,1)} %multiply_convert_fusion.5, bf16[2048,512]{1,0:T(8,128)(2,1)} %collective-permute-done), kind=kOutput, calls=%fused_computation.122 | convolution fusion | flops 536870912 | bytes 3670016 | tf_op jit(solution)/shard_map/dot_general | solution.py:188
  112.8 2.3 %convolution_bitcast_fusion.1 = f32[1,256,512]{2,1,0:T(8,128)S(1)} fusion(bf16[256,2048]{1,0:T(8,128)(2,1)S(1)} %collective-permute-done.9, bf16[2048,512]{1,0:T(8,128)(2,1)} %param.23), kind=kOutput, calls=%fused_computation.37 | convolution fusion | flops 536870912 | bytes 3670016 | tf_op jit(solution)/shard_map/dot_general | solution.py:188
  115.1 2.3 %convolution_bitcast_fusion = f32[1,256,512]{2,1,0:T(8,128)S(1)} fusion(bf16[256,2048]{1,0:T(8,128)(2,1)S(1)} %collective-permute-done.9, bf16[2048,512]{1,0:T(8,128)(2,1)} %collective-permute-done), kind=kOutput, calls=%fused_computation.36 | convolution fusion | flops 536870912 | bytes 3670016 | tf_op jit(solution)/shard_map/dot_general | solution.py:188
  117.4 2.3 %convolution_bitcast_fusion.5 = f32[1,256,512]{2,1,0:T(8,128)S(1)} fusion(bf16[256,2048]{1,0:T(8,128)(2,1)S(1)} %collective-permute-done.7, bf16[2048,512]{1,0:T(8,128)(2,1)} %param.23), kind=kOutput, calls=%fused_computation.41 | convolution fusion | flops 536870912 | bytes 3670016 | tf_op jit(solution)/shard_map/dot_general | solution.py:188
  119.7 11.6 %collective-permute-done.10 = bf16[256,2048]{1,0:T(8,128)(2,1)S(1)} collective-permute-done((bf16[256,2048]{1,0:T(8,128)(2,1)S(1)}, bf16[256,2048]{1,0:T(8,128)(2,1)S(1)}, u32[]{:S(2)}, u32[]{:S(2)}) %collective-permute-start.10) | collective-permute-done | bytes 1048608 | tf_op jit(solution)/shard_map/ppermute | solution.py:198
  131.4 1.5 collective-permute-start.11
  132.9 2.3 %convolution_bitcast_fusion.4 = f32[1,256,512]{2,1,0:T(8,128)S(1)} fusion(bf16[256,2048]{1,0:T(8,128)(2,1)S(1)} %collective-permute-done.7, bf16[2048,512]{1,0:T(8,128)(2,1)} %collective-permute-done), kind=kOutput, calls=%fused_computation.40 | convolution fusion | flops 536870912 | bytes 3670016 | tf_op jit(solution)/shard_map/dot_general | solution.py:188
  135.2 2.4 %fusion.31 = f32[256,512]{1,0:T(8,128)S(1)} fusion(bf16[2048,512]{1,0:T(8,128)(2,1)} %param.23, bf16[256,2048]{1,0:T(8,128)(2,1)S(1)} %collective-permute-done.8, bf16[256,2048]{1,0:T(8,128)(2,1)S(1)} %collective-permute-done.10, pred[]{:T(512)S(6)} %ge.33), kind=kOutput, calls=%fused_computation.71 | convolution fusion | flops 537395200 | bytes 4718593 | tf_op jit(solution)/shard_map/dot_general | solution.py:188
  137.6 2.4 %fusion.30 = f32[256,512]{1,0:T(8,128)S(1)} fusion(bf16[2048,512]{1,0:T(8,128)(2,1)} %collective-permute-done, bf16[256,2048]{1,0:T(8,128)(2,1)S(1)} %collective-permute-done.8, bf16[256,2048]{1,0:T(8,128)(2,1)S(1)} %collective-permute-done.10, pred[]{:T(512)S(6)} %ge.33), kind=kOutput, calls=%fused_computation.70 | convolution fusion | flops 537395200 | bytes 4718593 | tf_op jit(solution)/shard_map/dot_general | solution.py:188
  140.1 13.9 %collective-permute-done.11 = bf16[256,2048]{1,0:T(8,128)(2,1)S(1)} collective-permute-done((bf16[256,2048]{1,0:T(8,128)(2,1)S(1)}, bf16[256,2048]{1,0:T(8,128)(2,1)S(1)}, u32[]{:S(2)}, u32[]{:S(2)}) %collective-permute-start.11) | collective-permute-done | bytes 1048608 | tf_op jit(solution)/shard_map/ppermute | solution.py:202
  154.0 2.3 %convolution_bitcast_fusion.3 = f32[1,256,512]{2,1,0:T(8,128)S(1)} fusion(bf16[256,2048]{1,0:T(8,128)(2,1)S(1)} %collective-permute-done.11, bf16[2048,512]{1,0:T(8,128)(2,1)} %param.23), kind=kOutput, calls=%fused_computation.39 | convolution fusion | flops 536870912 | bytes 3670016 | tf_op jit(solution)/shard_map/dot_general | solution.py:188
  156.3 2.3 %convolution_bitcast_fusion.2 = f32[1,256,512]{2,1,0:T(8,128)S(1)} fusion(bf16[256,2048]{1,0:T(8,128)(2,1)S(1)} %collective-permute-done.11, bf16[2048,512]{1,0:T(8,128)(2,1)} %collective-permute-done), kind=kOutput, calls=%fused_computation.38 | convolution fusion | flops 536870912 | bytes 3670016 | tf_op jit(solution)/shard_map/dot_general | solution.py:188
  160.0 1.1 pad_maximum_fusion.2
  161.0 1.7 pad_maximum_fusion
  162.8 1.3 collective-permute-done.12
  164.7 1.2 add_convert_fusion.1
  166.5 13.8 %collective-permute-done.13 = bf16[1,256,1024]{2,1,0:T(8,128)(2,1)S(1)} collective-permute-done((bf16[1,256,1024]{2,1,0:T(8,128)(2,1)S(1)}, bf16[1,256,1024]{2,1,0:T(8,128)(2,1)S(1)}, u32[]{:S(2)}, u32[]{:S(2)}) %collective-permute-start.13) | collective-permute-done | bytes 524320 | tf_op jit(solution)/shard_map/ppermute | solution.py:246
  180.3 1.6 fusion.24
  181.9 4.5 %collective-permute-start.14 = (bf16[256,1024]{1,0:T(8,128)(2,1)S(1)}, bf16[256,1024]{1,0:T(8,128)(2,1)S(1)}, u32[]{:S(2)}, u32[]{:S(2)}) collective-permute-start(bf16[256,1024]{1,0:T(8,128)(2,1)S(1)} %fusion.24), channel_id=1, source_target_pairs={{0,0},{1,8},{2,16},{3,24},{8,1},{9,9},{10,17},{11,25},{16,2},{17,1... | collective-permute-start | bytes 1572872 | tf_op jit(solution)/shard_map/ppermute | solution.py:256
  186.4 22.9 %collective-permute-done.14 = bf16[256,1024]{1,0:T(8,128)(2,1)S(1)} collective-permute-done((bf16[256,1024]{1,0:T(8,128)(2,1)S(1)}, bf16[256,1024]{1,0:T(8,128)(2,1)S(1)}, u32[]{:S(2)}, u32[]{:S(2)}) %collective-permute-start.14) | collective-permute-done | bytes 524320 | tf_op jit(solution)/shard_map/ppermute | solution.py:256
  209.6 0.9 pad_maximum_fusion.3
  (75 shorter events, 6.6 us)
Async XLA Ops:
  0.0 4.9 %copy-start = (f32[256,32]{0,1:T(8,128)S(1)}, f32[256,32]{0,1:T(8,128)}, u32[]{:S(2)}) copy-start(f32[256,32]{0,1:T(8,128)} %param.20) | copy-start | bytes 98308
  0.0 1.4 copy-start.5
  0.0 1.4 copy-start.6
  0.0 7.3 %copy-start.8 = (f32[4,2048]{1,0:T(4,128)S(1)}, f32[4,2048]{1,0:T(4,128)}, u32[]{:S(2)}) copy-start(f32[4,2048]{1,0:T(4,128)} %param.16) | copy-start | bytes 98308
  0.0 7.3 %copy-start.10 = (f32[4,128]{1,0:T(4,128)S(1)}, f32[4,128]{1,0:T(4,128)}, u32[]{:S(2)}) copy-start(f32[4,128]{1,0:T(4,128)} %param.17) | copy-start | bytes 6148
  0.0 7.3 %copy-start.11 = (f32[4,128]{1,0:T(4,128)S(1)}, f32[4,128]{1,0:T(4,128)}, u32[]{:S(2)}) copy-start(f32[4,128]{1,0:T(4,128)} %param.18) | copy-start | bytes 6148
  1.5 6.1 %collective-permute-start.1 = (bf16[3,2304]{1,0:T(4,128)(2,1)S(1)}, bf16[3,2304]{1,0:T(4,128)(2,1)S(1)}, u32[]{:S(2)}, u32[]{:S(2)}) collective-permute-start(bf16[3,2304]{1,0:T(4,128)(2,1)S(1)} %slice.99), channel_id=1, source_target_pairs={{0,4},{4,8},{8,12},{12,16},{16,20},{20,24},{24,28},{1,5},{5,9},{9,... | collective-permute-start | bytes 41480 | tf_op jit(solution)/shard_map/ppermute | solution.py:14
  15.1 14.3 %collective-permute-start.4 = (bf16[1,32,64,128]{3,2,1,0:T(8,128)(2,1)S(1)}, bf16[1,32,64,128]{3,2,1,0:T(8,128)(2,1)S(1)}, u32[]{:S(2)}, u32[]{:S(2)}) collective-permute-start(bf16[1,32,64,128]{3,2,1,0:T(8,128)(2,1)S(1)} %convert_bitcast_fusion), channel_id=1, source_target_pairs={{0,4},{4,8},{8,12},{12,16},{16,20},{20,24},{24,28},{1,5},{5,9},{9,... | collective-permute-start | bytes 1572872 | tf_op jit(solution)/shard_map/ppermute | solution.py:14
  29.4 24.4 %copy-start.4 = (f32[1,256,1,32]{1,2,3,0:T(1,128)S(1)}, f32[1,256,1,32]{1,2,3,0:T(1,128)}, u32[]{:S(2)}) copy-start(f32[1,256,1,32]{1,2,3,0:T(1,128)} %get-tuple-element.56) | copy-start | bytes 98308
  29.6 14.9 %collective-permute-start.5 = (bf16[1,32,64,128]{3,2,1,0:T(8,128)(2,1)S(1)}, bf16[1,32,64,128]{3,2,1,0:T(8,128)(2,1)S(1)}, u32[]{:S(2)}, u32[]{:S(2)}) collective-permute-start(bf16[1,32,64,128]{3,2,1,0:T(8,128)(2,1)S(1)} %fusion.23), channel_id=1, source_target_pairs={{0,8},{4,12},{8,16},{12,20},{16,24},{20,28},{1,9},{5,13},{9,17},{1... | collective-permute-start | bytes 1572872 | tf_op jit(solution)/shard_map/ppermute | solution.py:14
  35.0 5.0 %collective-permute-start.2 = (f32[1,32]{1,0:T(1,128)S(1)}, f32[1,32]{1,0:T(1,128)S(1)}, u32[]{:S(2)}, u32[]{:S(2)}) collective-permute-start(f32[1,32]{1,0:T(1,128)S(1)} %bitcast.123), channel_id=1, source_target_pairs={{0,4},{4,8},{8,12},{12,16},{16,20},{20,24},{24,28},{1,5},{5,9},{9,... | collective-permute-start | bytes 392 | tf_op jit(solution)/shard_map/ppermute | solution.py:14
  37.5 46.3 %collective-permute-start = (bf16[2048,512]{1,0:T(8,128)(2,1)}, bf16[2048,512]{1,0:T(8,128)(2,1)}, u32[]{:S(2)}, u32[]{:S(2)}) collective-permute-start(bf16[2048,512]{1,0:T(8,128)(2,1)} %param.23), channel_id=1, source_target_pairs={{0,4},{4,0},{1,5},{5,1},{2,6},{6,2},{3,7},{7,3},{8,12},{12,8},{9,1... | collective-permute-start | bytes 6291464 | tf_op jit(solution)/shard_map/ppermute | solution.py:180
  44.9 15.1 %collective-permute-start.6 = (bf16[1,32,64,128]{3,2,1,0:T(8,128)(2,1)S(1)}, bf16[1,32,64,128]{3,2,1,0:T(8,128)(2,1)S(1)}, u32[]{:S(2)}, u32[]{:S(2)}) collective-permute-start(bf16[1,32,64,128]{3,2,1,0:T(8,128)(2,1)S(1)} %fusion.22), channel_id=1, source_target_pairs={{0,16},{4,20},{8,24},{12,28},{1,17},{5,21},{9,25},{13,29},{2,18},{... | collective-permute-start | bytes 1572872 | tf_op jit(solution)/shard_map/ppermute | solution.py:14
  50.9 8.9 %collective-permute-start.3 = (f32[1,32]{1,0:T(1,128)S(1)}, f32[1,32]{1,0:T(1,128)S(1)}, u32[]{:S(2)}, u32[]{:S(2)}) collective-permute-start(f32[1,32]{1,0:T(1,128)S(1)} %bitcast_multiply_fusion.1), channel_id=1, source_target_pairs={{0,8},{4,12},{8,16},{12,20},{16,24},{20,28},{1,9},{5,13},{9,17},{1... | collective-permute-start | bytes 392 | tf_op jit(solution)/shard_map/ppermute | solution.py:14
  53.9 6.6 %copy-start.7 = (f32[256,32]{0,1:T(8,128)S(1)}, f32[256,32]{0,1:T(8,128)}, u32[]{:S(2)}) copy-start(f32[256,32]{0,1:T(8,128)} %param.19) | copy-start | bytes 98308
  53.9 6.6 %copy-start.12 = (f32[32]{0:T(128)S(1)}, f32[32]{0:T(128)}, u32[]{:S(2)}) copy-start(f32[32]{0:T(128)} %param.21) | copy-start | bytes 388
  64.2 2.0 copy-start.3
  66.3 0.8 copy-start.9
  83.8 24.3 %collective-permute-start.9 = (bf16[256,2048]{1,0:T(8,128)(2,1)}, bf16[256,2048]{1,0:T(8,128)(2,1)S(1)}, u32[]{:S(2)}, u32[]{:S(2)}) collective-permute-start(bf16[256,2048]{1,0:T(8,128)(2,1)} %multiply_convert_fusion.5), channel_id=1, source_target_pairs={{8,0},{16,8},{24,16},{9,1},{17,9},{25,17},{10,2},{18,10},{26,18},{... | collective-permute-start | bytes 3145736 | tf_op jit(solution)/shard_map/ppermute | solution.py:198
  85.1 24.3 %collective-permute-start.7 = (bf16[256,2048]{1,0:T(8,128)(2,1)}, bf16[256,2048]{1,0:T(8,128)(2,1)S(1)}, u32[]{:S(2)}, u32[]{:S(2)}) collective-permute-start(bf16[256,2048]{1,0:T(8,128)(2,1)} %multiply_convert_fusion.5), channel_id=1, source_target_pairs={{0,8},{8,16},{16,24},{1,9},{9,17},{17,25},{2,10},{10,18},{18,26},{... | collective-permute-start | bytes 3145736 | tf_op jit(solution)/shard_map/ppermute | solution.py:195
  108.1 23.2 %collective-permute-start.10 = (bf16[256,2048]{1,0:T(8,128)(2,1)S(1)}, bf16[256,2048]{1,0:T(8,128)(2,1)S(1)}, u32[]{:S(2)}, u32[]{:S(2)}) collective-permute-start(bf16[256,2048]{1,0:T(8,128)(2,1)S(1)} %collective-permute-done.9), channel_id=1, source_target_pairs={{8,0},{16,8},{9,1},{17,9},{10,2},{18,10},{11,3},{19,11},{12,4},{20... | collective-permute-start | bytes 3145736 | tf_op jit(solution)/shard_map/ppermute | solution.py:198
  109.4 21.9 %collective-permute-start.8 = (bf16[256,2048]{1,0:T(8,128)(2,1)S(1)}, bf16[256,2048]{1,0:T(8,128)(2,1)S(1)}, u32[]{:S(2)}, u32[]{:S(2)}) collective-permute-start(bf16[256,2048]{1,0:T(8,128)(2,1)S(1)} %collective-permute-done.7), channel_id=1, source_target_pairs={{8,16},{16,24},{9,17},{17,25},{10,18},{18,26},{11,19},{19,27},{12,... | collective-permute-start | bytes 3145736 | tf_op jit(solution)/shard_map/ppermute | solution.py:195
  131.4 22.6 %collective-permute-start.11 = (bf16[256,2048]{1,0:T(8,128)(2,1)S(1)}, bf16[256,2048]{1,0:T(8,128)(2,1)S(1)}, u32[]{:S(2)}, u32[]{:S(2)}) collective-permute-start(bf16[256,2048]{1,0:T(8,128)(2,1)S(1)} %broadcast_select_fusion.1), channel_id=1, source_target_pairs={{16,24},{8,0},{17,25},{9,1},{18,26},{10,2},{19,27},{11,3},{20,28},... | collective-permute-start | bytes 3145736 | tf_op jit(solution)/shard_map/ppermute | solution.py:202
  158.9 1.0 copy-start.2
  161.0 3.0 %collective-permute-start.12 = (bf16[2,256,1024]{2,1,0:T(8,128)(2,1)}, bf16[2,256,1024]{2,1,0:T(8,128)(2,1)}, u32[]{:S(2)}, u32[]{:S(2)}) collective-permute-start(bf16[2,256,1024]{2,1,0:T(8,128)(2,1)} %pad_maximum_fusion.2), channel_id=1, source_target_pairs={{0,1},{1,0},{2,3},{3,2},{4,5},{5,4},{6,7},{7,6},{8,9},{9,8},{10,11... | collective-permute-start | bytes 3145736 | tf_op jit(solution)/shard_map/ppermute | solution.py:246
  162.8 1.9 copy-start.1
  165.9 14.4 %collective-permute-start.13 = (bf16[1,256,1024]{2,1,0:T(8,128)(2,1)S(1)}, bf16[1,256,1024]{2,1,0:T(8,128)(2,1)S(1)}, u32[]{:S(2)}, u32[]{:S(2)}) collective-permute-start(bf16[1,256,1024]{2,1,0:T(8,128)(2,1)S(1)} %add_convert_fusion.1), channel_id=1, source_target_pairs={{0,2},{1,3},{2,0},{3,1},{4,6},{5,7},{6,4},{7,5},{8,10},{9,11},{10,... | collective-permute-start | bytes 1572872 | tf_op jit(solution)/shard_map/ppermute | solution.py:246
  181.9 27.4 %collective-permute-start.14 = (bf16[256,1024]{1,0:T(8,128)(2,1)S(1)}, bf16[256,1024]{1,0:T(8,128)(2,1)S(1)}, u32[]{:S(2)}, u32[]{:S(2)}) collective-permute-start(bf16[256,1024]{1,0:T(8,128)(2,1)S(1)} %fusion.24), channel_id=1, source_target_pairs={{0,0},{1,8},{2,16},{3,24},{8,1},{9,9},{10,17},{11,25},{16,2},{17,1... | collective-permute-start | bytes 1572872 | tf_op jit(solution)/shard_map/ppermute | solution.py:256
